TPU v7x, 512 devices: a whole 4x4x16 slice. The times are simulated.
512 devices in a mesh: tm: 128 (over y, x, z_lo), batch: 4 (over z_hi, core).
Axes of the slice: x: 4, y: 4, z: 16 (z_hi: 2, z_lo: 8; z = z_hi * 8 + z_lo), core: 2. Of those that a mesh axis runs over, the one named last changes fastest.
Arguments:
- query_states: bfloat16 [4, 16384, 512], P('batch', 'tm'), may hold values from -8 to 8
- key_states: bfloat16 [4, 16384, 512], P('batch', 'tm'), may hold values from -8 to 8
- value_states: bfloat16 [4, 16384, 512], P('batch', 'tm'), may hold values from -6 to 6
- out_proj: bfloat16 [512, 1024], replicated, may hold values from -0.25 to 0.25
- grad_output: bfloat16 [4, 16384, 1024], P('batch', 'tm'), may hold values from -6 to 6
Outputs:
- output: bfloat16 [4, 16384, 1024], P('batch', 'tm')
- grad_query: bfloat16 [4, 16384, 512], P('batch', 'tm')
- grad_key: bfloat16 [4, 16384, 512], P('batch', 'tm')
- grad_value: bfloat16 [4, 16384, 512], P('batch', 'tm')
- grad_proj: float32 [512, 1024], P(('tm', 'batch'))
All inputs are finite; a program needn't handle non-finite values.
Results may differ from a plain program's by a relative error of at most 0.02.
Values may be sent and summed in bfloat16 or wider, within the bound.
No kernel may reach another device: no remote copies, remote signals or barrier semaphores. Data moves between devices by JAX's collectives and lax.ppermute only.
A program may use at most 128 MiB of HBM per device.

v0:
```python
import jax
import jax.numpy as jnp
import numpy as np
from jax import lax
from jax.sharding import PartitionSpec as P

HEADS = 8
HD = 64
R2 = 8
R3 = 16


def partner(value, axis, apart):
    mask = 2**apart
    pairs = [(source, source ^ mask) for source in range(lax.axis_size(axis))]
    return lax.ppermute(value, axis, pairs)


def offset_mask(dilation):
    return (np.arange(dilation)[:, None] == (np.arange(HEADS) % dilation)[None, :]).astype(
        np.float32
    )


def cover_table(row_count, dilation):
    return (np.arange(row_count) % dilation)[:, None] == (np.arange(HEADS) % dilation)[None, :]


def pick_rows(matrix, dilation):
    count = matrix.shape[0] // dilation
    blocks = matrix.reshape(count, dilation, HEADS, HD)
    chooser = jnp.asarray(offset_mask(dilation), matrix.dtype)[None, :, :, None]
    return jnp.sum(blocks * chooser, axis=1).reshape(count, HEADS * HD)


def pick_stats(matrix, dilation):
    count = matrix.shape[0] // dilation
    blocks = matrix.reshape(count, dilation, HEADS)
    chooser = jnp.asarray(offset_mask(dilation), matrix.dtype)[None, :, :]
    return jnp.sum(blocks * chooser, axis=1)


def spread_rows(values, dilation):
    chooser = jnp.asarray(offset_mask(dilation), values.dtype)[None, :, :, None]
    return (values[:, None] * chooser).reshape(values.shape[0] * dilation, HEADS, HD)


def spread_stats(values, dilation):
    chooser = jnp.asarray(offset_mask(dilation), values.dtype)[None, :, :]
    return (values[:, None] * chooser).reshape(values.shape[0] * dilation, HEADS)


def merge_levels(log_totals, coverage, partials):
    first_lse = log_totals[0]
    peak = first_lse
    for level_no in range(1, len(log_totals)):
        peak = jnp.maximum(peak, jnp.where(coverage[level_no], log_totals[level_no], first_lse))
    exponents = []
    for level_no in range(len(log_totals)):
        exponents.append(jnp.where(coverage[level_no], jnp.exp(log_totals[level_no] - peak), 0.0))
    denominator = exponents[0]
    for level_no in range(1, len(exponents)):
        denominator = denominator + exponents[level_no]
    weights = []
    merged = None
    for level_no in range(len(exponents)):
        weight_now = exponents[level_no] / denominator
        weights.append(weight_now)
        term = weight_now[:, :, None] * partials[level_no]
        merged = term if merged is None else merged + term
    return (merged, weights)


def gather_blocks(block, axis_pos, bit_order):
    for bit_pos in bit_order:
        block = jnp.concatenate([block, partner(block, "tm", bit_pos)], axis_pos)
    return block


def split_exact(values):
    high = lax.reduce_precision(values, exponent_bits=8, mantissa_bits=7)
    rest = values - high
    middle = lax.reduce_precision(rest, exponent_bits=8, mantissa_bits=7)
    low = rest - middle
    parts = jnp.concatenate([high, middle, low], -1)
    return parts.astype(jnp.bfloat16)


def join_exact(parts):
    width = parts.shape[-1] // 3
    as32 = parts.astype(jnp.float32)
    return as32[..., :width] + (as32[..., width : 2 * width] + as32[..., 2 * width :])


def by_parity(rows):
    return rows.reshape((rows.shape[0] // 2, 2) + rows.shape[1:]).swapaxes(0, 1)


def from_parity(rows):
    return rows.swapaxes(0, 1).reshape((rows.shape[0] * rows.shape[1],) + rows.shape[2:])


def pad_lanes(matrix, width):
    return jnp.pad(matrix, [(0, 0)] * (matrix.ndim - 1) + [(0, width - matrix.shape[-1])])


class HalvingSum:

    def __init__(self, matrix, bit_count):
        self.block = matrix.reshape((2,) * bit_count + matrix.shape[1:])
        self.dims = [bit_count - 1 - j for j in range(bit_count)]
        self.tail = matrix.shape[1:]

    def split(self, bit_pos, my_bit):
        self.axis_pos = self.dims.index(bit_pos)
        self.keep = lax.dynamic_index_in_dim(self.block, my_bit, self.axis_pos, keepdims=False)
        return lax.dynamic_index_in_dim(self.block, 1 - my_bit, self.axis_pos, keepdims=False)

    def absorb(self, received):
        self.block = self.keep + received
        self.dims.pop(self.axis_pos)

    def result(self):
        return self.block.reshape((1,) + self.tail)


def heads_view(matrix):
    return matrix.reshape(matrix.shape[0], HEADS, HD)


def attend(query_rows, key_rows, value_rows, inv_root):
    scores = (
        jnp.einsum(
            "qhd,khd->hqk",
            heads_view(query_rows),
            heads_view(key_rows),
            preferred_element_type=jnp.float32,
        )
        * inv_root
    )
    peak = jnp.max(scores, axis=2, keepdims=True)
    log_total = peak + jnp.log(jnp.sum(jnp.exp(scores - peak), axis=2, keepdims=True))
    weights_bf = jnp.exp(scores - log_total).astype(jnp.bfloat16)
    part_out = jnp.einsum(
        "hqk,khd->qhd", weights_bf, heads_view(value_rows), preferred_element_type=jnp.float32
    )
    return part_out, log_total[:, :, 0].T


def near_grad(query_rows, key_rows, value_rows, grad_rows, lse_rows, offset_rows, inv_root):
    scores = (
        jnp.einsum(
            "qhd,khd->hqk",
            heads_view(query_rows),
            heads_view(key_rows),
            preferred_element_type=jnp.float32,
        )
        * inv_root
    )
    prob_full = jnp.exp(scores - lse_rows.T[:, :, None])
    dprob = jnp.einsum(
        "qhd,khd->hqk",
        heads_view(grad_rows),
        heads_view(value_rows),
        preferred_element_type=jnp.float32,
    )
    dscore = (prob_full * (dprob - offset_rows.T[:, :, None])).astype(jnp.bfloat16)
    return (
        jnp.einsum("hqk,khd->qhd", dscore, heads_view(key_rows), preferred_element_type=jnp.float32)
        * inv_root
    )


def far_grad(query_group, grad_group, lse_group, offset_group, key_rows, value_rows, inv_root):
    scores_far = (
        jnp.einsum(
            "qhd,khd->hqk",
            heads_view(query_group),
            heads_view(key_rows),
            preferred_element_type=jnp.float32,
        )
        * inv_root
    )
    prob_far = jnp.exp(scores_far - lse_group.T[:, :, None])
    grad_v = jnp.einsum(
        "hqk,qhd->khd",
        prob_far.astype(jnp.bfloat16),
        heads_view(grad_group),
        preferred_element_type=jnp.float32,
    )
    dprob_far = jnp.einsum(
        "qhd,khd->hqk",
        heads_view(grad_group),
        heads_view(value_rows),
        preferred_element_type=jnp.float32,
    )
    dscore_far = (prob_far * (dprob_far - offset_group.T[:, :, None])).astype(jnp.bfloat16)
    grad_k = (
        jnp.einsum(
            "hqk,qhd->khd", dscore_far, heads_view(query_group), preferred_element_type=jnp.float32
        )
        * inv_root
    )
    return grad_k, grad_v


def on_device(query_states, key_states, value_states, out_proj, grad_output):
    queries = query_states[0]
    keys_all = key_states[0]
    values_all = value_states[0]
    upstream = grad_output[0]
    row_count = queries.shape[0]
    features = queries.shape[1]
    inv_root = HD ** (-0.5)
    devices = lax.axis_size("tm")
    bit_count = devices.bit_length() - 1
    top_bit = bit_count - 1
    near_first = {0: 0, 1: 2, 2: 1, 3: 4, 4: 3, 5: 5}
    low_bits = sorted(range(top_bit), key=lambda b: near_first.get(b, b))
    tm_index = lax.axis_index("tm")
    batch_index = lax.axis_index("batch")
    batch_count = lax.axis_size("batch")
    batch_bits = batch_count.bit_length() - 1
    wide = features + 128

    qkv = jnp.stack([by_parity(pick_rows(m, R2)) for m in (queries, keys_all, values_all)], 0)
    per_par = qkv.shape[2]
    own = qkv[:, :, None]
    for bit_pos in low_bits:
        if bit_pos == 0:
            other, other_qkv = partner(
                (own, jnp.stack([queries, keys_all, values_all], 0)), "tm", bit_pos
            )
        else:
            other = partner(own, "tm", bit_pos)
        own = jnp.concatenate([own, other], 2)
    far = partner(own[:, 0], "tm", top_bit)
    other_q = other_qkv[0]
    keys_one = jnp.concatenate([keys_all, other_qkv[1]], 0)
    values_one = jnp.concatenate([values_all, other_qkv[2]], 0)
    part_one, lse_one = attend(queries, keys_one, values_one, inv_root)
    q_seg2 = own[0].reshape(-1, features)
    k_seg2 = own[1].reshape(-1, features)
    v_seg2 = own[2].reshape(-1, features)
    q_seg3 = jnp.concatenate([own[0, 0], far[0]], 0).reshape(-1, features)
    k_seg3 = jnp.concatenate([own[1, 0], far[1]], 0).reshape(-1, features)
    v_seg3 = jnp.concatenate([own[2, 0], far[2]], 0).reshape(-1, features)
    q_two = qkv[0].reshape(-1, features)
    q_three = qkv[0, 0]
    part_two, lse_two = attend(q_two, k_seg2, v_seg2, inv_root)
    part_three, lse_three = attend(q_three, k_seg3, v_seg3, inv_root)

    partials = [
        spread_rows(part_one, 1),
        spread_rows(from_parity(part_two.reshape((2, per_par) + part_two.shape[1:])), R2),
        spread_rows(part_three, R3),
    ]
    log_totals = [
        spread_stats(lse_one, 1),
        spread_stats(from_parity(lse_two.reshape(2, per_par, HEADS)), R2),
        spread_stats(lse_three, R3),
    ]
    coverage = [cover_table(row_count, d) for d in (1, R2, R3)]
    merged, weights = merge_levels(log_totals, coverage, partials)
    attn = merged.reshape(row_count, features).astype(jnp.bfloat16)
    output = jnp.dot(attn, out_proj, preferred_element_type=jnp.float32).astype(jnp.bfloat16)
    grad_attn = lax.dot_general(
        upstream, out_proj, (((1,), (1,)), ((), ())), preferred_element_type=jnp.float32
    ).astype(jnp.bfloat16)
    proj_part = lax.dot_general(
        attn, upstream, (((0,), (0,)), ((), ())), preferred_element_type=jnp.float32
    )
    halving = HalvingSum(proj_part, bit_count + batch_bits)

    def batch_step(bit_pos):
        send = halving.split(bit_pos, batch_index // (1 << bit_pos) % 2)
        pairs = [(s, s ^ (1 << bit_pos)) for s in range(batch_count)]
        halving.absorb(lax.ppermute(send, "batch", pairs))

    def tm_send(bit_pos):
        return halving.split(bit_pos + batch_bits, tm_index // (1 << bit_pos) % 2)

    batch_step(0)

    grad_three = grad_attn.astype(jnp.float32).reshape(row_count, HEADS, HD)
    rowdot = jnp.sum(grad_three * merged, axis=2)

    def grad_of(weight_now, grad_rows):
        scaled = weight_now[:, :, None] * grad_rows.astype(jnp.float32).reshape(-1, HEADS, HD)
        return scaled.astype(jnp.bfloat16).reshape(-1, features)

    grad_one = grad_of(weights[0], grad_attn)
    offset_one = weights[0] * rowdot
    packed_one = jnp.concatenate([grad_one, split_exact(jnp.concatenate([lse_one, offset_one], 1))], 1)
    packed_one = pad_lanes(packed_one, wide)

    ga_par = by_parity(pick_rows(grad_attn, R2))
    w_two = by_parity(pick_stats(weights[1], R2))
    rd_two = by_parity(pick_stats(rowdot, R2))
    lse_two_par = lse_two.reshape(2, per_par, HEADS)
    w_three = pick_stats(weights[2], R3)
    no_level = jnp.zeros_like(w_three)
    lse3_par = jnp.stack([lse_three, no_level], 0)
    w3_par = jnp.stack([w_three, no_level], 0)
    stats_par = jnp.concatenate([lse_two_par, w_two, lse3_par, w3_par, rd_two], -1)
    packed = pad_lanes(jnp.concatenate([ga_par, split_exact(stats_par)], -1), wide)
    own_b = packed[:, None]
    for bit_pos in low_bits:
        if bit_pos == 0:
            other, received, other_one = partner(
                (own_b, tm_send(bit_pos), packed_one), "tm", bit_pos
            )
        else:
            other, received = partner((own_b, tm_send(bit_pos)), "tm", bit_pos)
        halving.absorb(received)
        own_b = jnp.concatenate([own_b, other], 1)
    far_b, received = partner((own_b[0], tm_send(top_bit)), "tm", top_bit)
    halving.absorb(received)
    for bit_pos in range(1, batch_bits):
        batch_step(bit_pos)
    grad_proj = halving.result()

    other_stats = join_exact(other_one[:, features : features + 6 * HEADS])
    total_q = spread_rows(
        near_grad(queries, keys_one, values_one, grad_one, lse_one, offset_one, inv_root), 1
    )
    k_g1, v_g1 = far_grad(
        jnp.concatenate([queries, other_q], 0),
        jnp.concatenate([grad_one, other_one[:, :features]], 0),
        jnp.concatenate([lse_one, other_stats[:, :HEADS]], 0),
        jnp.concatenate([offset_one, other_stats[:, HEADS:]], 0),
        keys_all,
        values_all,
        inv_root,
    )
    total_k = spread_rows(k_g1, 1)
    total_v = spread_rows(v_g1, 1)

    stat_w = 5 * HEADS

    def unpack(rows):
        rows = rows.reshape(-1, wide)
        stats = join_exact(rows[:, features : features + 3 * stat_w])
        return rows[:, :features], stats.reshape(-1, 5, HEADS)

    g_two = grad_of(w_two.reshape(-1, HEADS), ga_par.reshape(-1, features))
    c_two = w_two.reshape(-1, HEADS) * rd_two.reshape(-1, HEADS)
    grad_q2 = near_grad(q_two, k_seg2, v_seg2, g_two, lse_two, c_two, inv_root)
    ga_seg2, st_seg2 = unpack(own_b)
    k_g2, v_g2 = far_grad(
        q_seg2,
        grad_of(st_seg2[:, 1], ga_seg2),
        st_seg2[:, 0],
        st_seg2[:, 1] * st_seg2[:, 4],
        qkv[1].reshape(-1, features),
        qkv[2].reshape(-1, features),
        inv_root,
    )

    g_three = grad_of(w_three, ga_par[0])
    c_three = w_three * rd_two[0]
    grad_q3 = near_grad(q_three, k_seg3, v_seg3, g_three, lse_three, c_three, inv_root)
    ga_seg3, st_seg3 = unpack(jnp.concatenate([own_b[0], far_b], 0))
    k_g3, v_g3 = far_grad(
        q_seg3,
        grad_of(st_seg3[:, 3], ga_seg3),
        st_seg3[:, 2],
        st_seg3[:, 3] * st_seg3[:, 4],
        qkv[1, 0],
        qkv[2, 0],
        inv_root,
    )

    def level_two_rows(values):
        return spread_rows(from_parity(values.reshape((2, per_par) + values.shape[1:])), R2)

    total_q = total_q + level_two_rows(grad_q2) + spread_rows(grad_q3, R3)
    total_k = total_k + level_two_rows(k_g2) + spread_rows(k_g3, R3)
    total_v = total_v + level_two_rows(v_g2) + spread_rows(v_g3, R3)
    grad_query = total_q.reshape(row_count, features).astype(jnp.bfloat16)
    grad_key = total_k.reshape(row_count, features).astype(jnp.bfloat16)
    grad_value = total_v.reshape(row_count, features).astype(jnp.bfloat16)
    return (output[None], grad_query[None], grad_key[None], grad_value[None], grad_proj)


def solution(mesh):
    in_specs = (
        P("batch", "tm", None),
        P("batch", "tm", None),
        P("batch", "tm", None),
        P(),
        P("batch", "tm", None),
    )
    out_specs = (
        P("batch", "tm", None),
        P("batch", "tm", None),
        P("batch", "tm", None),
        P("batch", "tm", None),
        P(("tm", "batch"), None),
    )
    return jax.shard_map(
        on_device, mesh=mesh, in_specs=in_specs, out_specs=out_specs, check_vma=False
    )
```

profile of v0, /device:TPU:6, one launch (start us, length us, event | category | flops | bytes accessed | tf_op | source)
XLA Modules:
  0.0 408.5 jit_solution(11295394810474345798)
XLA Ops:
  5.1 3.8 collective-permute-start.1
  8.9 2.2 collective-permute-done.1
  11.1 9.1 %collective-permute-start.2 = (bf16[3,2,2,8,512]{4,3,1,0,2:T(8,128)(2,1)S(1)}, bf16[3,2,2,8,512]{4,3,1,0,2:T(8,128)(2,1)S(1)}, u32[]{:S(2)}, u32[]{:S(2)}) collective-permute-start(bf16[3,2,2,8,512]{4,3,1,0,2:T(8,128)(2,1)S(1)} %pad_maximum_fusion.21), channel_id=1, source_target_pairs={{0,16},{4,20},{8,24},{12,28},{16,0},{20,4},{24,8},{28,12},{32,48},... | collective-permute-start | bytes 294920 | tf_op jit(solution)/shard_map/ppermute | solution.py:16
  20.2 8.2 %collective-permute-done.2 = bf16[3,2,2,8,512]{4,3,1,0,2:T(8,128)(2,1)S(1)} collective-permute-done((bf16[3,2,2,8,512]{4,3,1,0,2:T(8,128)(2,1)S(1)}, bf16[3,2,2,8,512]{4,3,1,0,2:T(8,128)(2,1)S(1)}, u32[]{:S(2)}, u32[]{:S(2)}) %collective-permute-start.2) | collective-permute-done | bytes 98336 | tf_op jit(solution)/shard_map/ppermute | solution.py:16
  30.4 9.6 %collective-permute-done.3 = bf16[3,2,4,8,512]{4,3,1,0,2:T(8,128)(2,1)S(1)} collective-permute-done((bf16[3,2,4,8,512]{4,3,1,0,2:T(8,128)(2,1)S(1)}, bf16[3,2,4,8,512]{4,3,1,0,2:T(8,128)(2,1)S(1)}, u32[]{:S(2)}, u32[]{:S(2)}) %collective-permute-start.3) | collective-permute-done | bytes 196640 | tf_op jit(solution)/shard_map/ppermute | solution.py:16
  40.0 3.3 collective-permute-start.4
  46.2 8.0 %collective-permute-done.4 = bf16[3,2,8,8,512]{4,3,1,0,2:T(8,128)(2,1)S(1)} collective-permute-done((bf16[3,2,8,8,512]{4,3,1,0,2:T(8,128)(2,1)S(1)}, bf16[3,2,8,8,512]{4,3,1,0,2:T(8,128)(2,1)S(1)}, u32[]{:S(2)}, u32[]{:S(2)}) %collective-permute-start.4) | collective-permute-done | bytes 393248 | tf_op jit(solution)/shard_map/ppermute | solution.py:16
  55.3 2.6 collective-permute-start.5
  57.9 11.3 %collective-permute-done.5 = bf16[3,2,16,8,512]{4,3,1,0,2:T(8,128)(2,1)S(1)} collective-permute-done((bf16[3,2,16,8,512]{4,3,1,0,2:T(8,128)(2,1)S(1)}, bf16[3,2,16,8,512]{4,3,1,0,2:T(8,128)(2,1)S(1)}, u32[]{:S(2)}, u32[]{:S(2)}) %collective-permute-start.5) | collective-permute-done | bytes 786464 | tf_op jit(solution)/shard_map/ppermute | solution.py:16
  70.5 3.4 collective-permute-start.6
  74.0 8.7 %collective-permute-start = (bf16[3,128,512]{2,1,0:T(8,128)(2,1)S(1)}, bf16[3,128,512]{2,1,0:T(8,128)(2,1)S(1)}, u32[]{:S(2)}, u32[]{:S(2)}) collective-permute-start(bf16[3,128,512]{2,1,0:T(8,128)(2,1)S(1)} %pad_maximum_fusion.3), channel_id=1, source_target_pairs={{0,4},{4,0},{8,12},{12,8},{16,20},{20,16},{24,28},{28,24},{32,36},... | collective-permute-start | bytes 1179656 | tf_op jit(solution)/shard_map/ppermute | solution.py:16
  93.7 3.4 collective-permute-done.6
  97.1 2.7 constant_dynamic-update-slice_fusion.11
  99.8 2.8 copy_bitcast_fusion
  102.5 5.3 %collective-permute-start.7 = (bf16[3,64,8,512]{3,2,1,0:T(8,128)(2,1)}, bf16[3,64,8,512]{3,2,1,0:T(8,128)(2,1)}, u32[]{:S(2)}, u32[]{:S(2)}) collective-permute-start(bf16[3,64,8,512]{3,2,1,0:T(8,128)(2,1)} %copy_bitcast_fusion), channel_id=1, source_target_pairs={{0,256},{4,260},{8,264},{12,268},{16,272},{20,276},{24,280},{28,28... | collective-permute-start | bytes 4718600 | tf_op jit(solution)/shard_map/ppermute | solution.py:16
  107.8 3.5 fusion.134
  111.4 2.1 reshape_reshape_squeeze.6
  113.5 2.5 copy.761
  116.0 2.7 copy.771
  118.7 3.9 reshape_reshape_squeeze.14
  122.7 3.3 copy.772
  132.7 2.1 reshape_reshape_squeeze.15
  134.8 3.3 copy.818
  138.1 2.3 slice_bitcast_fusion.2
  140.4 2.3 slice_bitcast_fusion.1
  143.8 2.1 reshape_reshape.28
  145.9 2.5 copy.767
  152.5 3.9 reshape_reshape.29
  156.4 3.4 copy.776
  164.2 1.9 copy.781
  169.5 2.9 fusion.65
  192.2 19.0 %collective-permute-start.9 = (bf16[2,1,8,640]{3,2,0,1:T(8,128)(2,1)}, bf16[2,1,8,640]{3,2,0,1:T(8,128)(2,1)}, u32[]{:S(2)}, u32[]{:S(2)}) collective-permute-start(bf16[2,1,8,640]{3,2,0,1:T(8,128)(2,1)} %get-tuple-element.12), channel_id=1, source_target_pairs={{0,4},{4,0},{8,12},{12,8},{16,20},{20,16},{24,28},{28,24},{32,36},... | collective-permute-start | bytes 61448 | tf_op jit(solution)/shard_map/ppermute | solution.py:16
  214.3 1.9 fusion.55
  218.0 3.2 constant_dynamic-slice_fusion.3
  225.6 2.6 fusion.29
  229.9 1.9 mul.680
  231.9 2.4 fusion.17
  238.9 2.0 fusion.35
  248.7 8.3 %collective-permute-start.10 = (bf16[2,2,8,640]{3,2,0,1:T(8,128)(2,1)S(1)}, bf16[2,2,8,640]{3,2,0,1:T(8,128)(2,1)S(1)}, u32[]{:S(2)}, u32[]{:S(2)}) collective-permute-start(bf16[2,2,8,640]{3,2,0,1:T(8,128)(2,1)S(1)} %pad_maximum_fusion.24), channel_id=1, source_target_pairs={{0,16},{4,20},{8,24},{12,28},{16,0},{20,4},{24,8},{28,12},{32,48},... | collective-permute-start | bytes 122888 | tf_op jit(solution)/shard_map/ppermute | solution.py:16
  259.9 5.3 %collective-permute-start.11 = (bf16[2,4,8,640]{3,2,0,1:T(8,128)(2,1)S(1)}, bf16[2,4,8,640]{3,2,0,1:T(8,128)(2,1)S(1)}, u32[]{:S(2)}, u32[]{:S(2)}) collective-permute-start(bf16[2,4,8,640]{3,2,0,1:T(8,128)(2,1)S(1)} %pad_maximum_fusion.22), channel_id=1, source_target_pairs={{0,8},{4,12},{8,0},{12,4},{16,24},{20,28},{24,16},{28,20},{32,40},... | collective-permute-start | bytes 245768 | tf_op jit(solution)/shard_map/ppermute | solution.py:16
  268.5 3.3 collective-permute-start.12
  278.2 2.7 collective-permute-start.13
  284.3 4.2 %collective-permute-done.13 = bf16[2,16,8,640]{3,2,0,1:T(8,128)(2,1)} collective-permute-done((bf16[2,16,8,640]{3,2,0,1:T(8,128)(2,1)}, bf16[2,16,8,640]{3,2,0,1:T(8,128)(2,1)}, u32[]{:S(2)}, u32[]{:S(2)}) %collective-permute-start.13) | collective-permute-done | bytes 327712 | tf_op jit(solution)/shard_map/ppermute | solution.py:16
  290.4 2.9 collective-permute-start.14
  295.3 2.1 bitcast_add_fusion
  298.4 5.6 %collective-permute-start.17 = (f32[2,2,2,2,2,2,2,1024]{7,6,5,4,3,2,1,0:T(2,128)}, f32[2,2,2,2,2,2,2,1024]{7,6,5,4,3,2,1,0:T(2,128)}, u32[]{:S(2)}, u32[]{:S(2)}) collective-permute-start(f32[2,2,2,2,2,2,2,1024]{7,6,5,4,3,2,1,0:T(2,128)} %dynamic-slice_bitcast_fusion), channel_id=1, source_target_pairs={{0,4},{4,0},{8,12},{12,8},{16,20},{20,16},{24,28},{28,24},{32,36},... | collective-permute-start | bytes 1572872 | tf_op jit(solution)/shard_map/ppermute | solution.py:16
  303.9 2.8 collective-permute-done.14
  311.2 1.9 copy.815
  313.1 5.0 %collective-permute-start.15 = (bf16[64,8,640]{2,1,0:T(8,128)(2,1)}, bf16[64,8,640]{2,1,0:T(8,128)(2,1)}, u32[]{:S(2)}, u32[]{:S(2)}) collective-permute-start(bf16[64,8,640]{2,1,0:T(8,128)(2,1)} %slice_bitcast_fusion), channel_id=1, source_target_pairs={{0,256},{4,260},{8,264},{12,268},{16,272},{20,276},{24,280},{28,28... | collective-permute-start | bytes 1966088 | tf_op jit(solution)/shard_map/ppermute | solution.py:16
  318.1 2.3 fusion.11
  323.3 8.7 %collective-permute-start.18 = (f32[2,2,2,2,2,2,1024]{6,5,4,3,2,1,0:T(2,128)}, f32[2,2,2,2,2,2,1024]{6,5,4,3,2,1,0:T(2,128)}, u32[]{:S(2)}, u32[]{:S(2)}) collective-permute-start(f32[2,2,2,2,2,2,1024]{6,5,4,3,2,1,0:T(2,128)} %dynamic-slice_bitcast_fusion.1), channel_id=1, source_target_pairs={{0,16},{4,20},{8,24},{12,28},{16,0},{20,4},{24,8},{28,12},{32,48},... | collective-permute-start | bytes 786440 | tf_op jit(solution)/shard_map/ppermute | solution.py:16
  339.1 13.0 %collective-permute-done.18 = f32[2,2,2,2,2,2,1024]{6,5,4,3,2,1,0:T(2,128)} collective-permute-done((f32[2,2,2,2,2,2,1024]{6,5,4,3,2,1,0:T(2,128)}, f32[2,2,2,2,2,2,1024]{6,5,4,3,2,1,0:T(2,128)}, u32[]{:S(2)}, u32[]{:S(2)}) %collective-permute-start.18) | collective-permute-done | bytes 262176 | tf_op jit(solution)/shard_map/ppermute | solution.py:16
  353.2 1.9 collective-permute-start.19
  358.6 4.2 %collective-permute-done.19 = f32[2,2,2,2,2,1024]{5,4,3,2,1,0:T(2,128)S(1)} collective-permute-done((f32[2,2,2,2,2,1024]{5,4,3,2,1,0:T(2,128)S(1)}, f32[2,2,2,2,2,1024]{5,4,3,2,1,0:T(2,128)S(1)}, u32[]{:S(2)}, u32[]{:S(2)}) %collective-permute-start.19) | collective-permute-done | bytes 131104 | tf_op jit(solution)/shard_map/ppermute | solution.py:16
  362.9 3.3 collective-permute-start.20
  366.5 4.1 collective-permute-done.20
  371.2 2.7 collective-permute-start.21
  374.0 1.9 copy.825
  378.7 2.6 collective-permute-start.22
  381.9 2.8 collective-permute-done.22
  385.4 2.8 collective-permute-start.23
  389.0 3.5 collective-permute-done.23
  392.5 12.8 %collective-permute-start.24 = (f32[1024]{0:T(1024)S(1)}, f32[1024]{0:T(1024)S(1)}, u32[]{:S(2)}, u32[]{:S(2)}) collective-permute-start(f32[1024]{0:T(1024)S(1)} %bitcast.404), channel_id=1, source_target_pairs={{0,2},{1,3},{2,0},{3,1},{4,6},{5,7},{6,4},{7,5},{8,10},{9,11},{10,... | collective-permute-start | bytes 12296 | tf_op jit(solution)/shard_map/ppermute | solution.py:278
  405.3 2.6 add_convert_fusion
  (308 shorter events, 131.5 us)
Async XLA Ops:
  0.6 3.7 copy-start.49
  5.1 6.0 %collective-permute-start.1 = (bf16[3,2,1,8,512]{4,3,1,0,2:T(8,128)(2,1)S(1)}, bf16[3,2,1,8,512]{4,3,1,0,2:T(8,128)(2,1)S(1)}, u32[]{:S(2)}, u32[]{:S(2)}) collective-permute-start(bf16[3,2,1,8,512]{4,3,1,0,2:T(8,128)(2,1)S(1)} %bitcast.357), channel_id=1, source_target_pairs={{0,4},{4,0},{8,12},{12,8},{16,20},{20,16},{24,28},{28,24},{32,36},... | collective-permute-start | bytes 147464 | tf_op jit(solution)/shard_map/ppermute | solution.py:16
  11.1 17.4 %collective-permute-start.2 = (bf16[3,2,2,8,512]{4,3,1,0,2:T(8,128)(2,1)S(1)}, bf16[3,2,2,8,512]{4,3,1,0,2:T(8,128)(2,1)S(1)}, u32[]{:S(2)}, u32[]{:S(2)}) collective-permute-start(bf16[3,2,2,8,512]{4,3,1,0,2:T(8,128)(2,1)S(1)} %pad_maximum_fusion.21), channel_id=1, source_target_pairs={{0,16},{4,20},{8,24},{12,28},{16,0},{20,4},{24,8},{28,12},{32,48},... | collective-permute-start | bytes 294920 | tf_op jit(solution)/shard_map/ppermute | solution.py:16
  28.5 11.5 %collective-permute-start.3 = (bf16[3,2,4,8,512]{4,3,1,0,2:T(8,128)(2,1)S(1)}, bf16[3,2,4,8,512]{4,3,1,0,2:T(8,128)(2,1)S(1)}, u32[]{:S(2)}, u32[]{:S(2)}) collective-permute-start(bf16[3,2,4,8,512]{4,3,1,0,2:T(8,128)(2,1)S(1)} %pad_maximum_fusion.9), channel_id=1, source_target_pairs={{0,8},{4,12},{8,0},{12,4},{16,24},{20,28},{24,16},{28,20},{32,40},... | collective-permute-start | bytes 589832 | tf_op jit(solution)/shard_map/ppermute | solution.py:16
  40.0 14.2 %collective-permute-start.4 = (bf16[3,2,8,8,512]{4,3,1,0,2:T(8,128)(2,1)S(1)}, bf16[3,2,8,8,512]{4,3,1,0,2:T(8,128)(2,1)S(1)}, u32[]{:S(2)}, u32[]{:S(2)}) collective-permute-start(bf16[3,2,8,8,512]{4,3,1,0,2:T(8,128)(2,1)S(1)} %pad_maximum_fusion.4), channel_id=1, source_target_pairs={{0,64},{4,68},{8,72},{12,76},{16,80},{20,84},{24,88},{28,92},{32,9... | collective-permute-start | bytes 1179656 | tf_op jit(solution)/shard_map/ppermute | solution.py:16
  55.3 13.9 %collective-permute-start.5 = (bf16[3,2,16,8,512]{4,3,1,0,2:T(8,128)(2,1)S(1)}, bf16[3,2,16,8,512]{4,3,1,0,2:T(8,128)(2,1)S(1)}, u32[]{:S(2)}, u32[]{:S(2)}) collective-permute-start(bf16[3,2,16,8,512]{4,3,1,0,2:T(8,128)(2,1)S(1)} %get-tuple-element.41), channel_id=1, source_target_pairs={{0,32},{4,36},{8,40},{12,44},{16,48},{20,52},{24,56},{28,60},{32,0... | collective-permute-start | bytes 2359304 | tf_op jit(solution)/shard_map/ppermute | solution.py:16
  69.2 15.4 %copy-start.47 = (f32[8,8]{0,1:T(8,128)S(1)}, f32[8,8]{0,1:T(8,128)}, u32[]{:S(2)}) copy-start(f32[8,8]{0,1:T(8,128)} %constant.242.clone) | copy-start | bytes 772
  69.2 15.5 %copy-start.46 = (f32[16,8]{0,1:T(8,128)S(1)}, f32[16,8]{0,1:T(8,128)}, u32[]{:S(2)}) copy-start(f32[16,8]{0,1:T(8,128)} %constant.243.clone) | copy-start | bytes 1540
  70.5 26.6 %collective-permute-start.6 = (bf16[3,2,32,8,512]{4,3,1,0,2:T(8,128)(2,1)}, bf16[3,2,32,8,512]{4,3,1,0,2:T(8,128)(2,1)}, u32[]{:S(2)}, u32[]{:S(2)}) collective-permute-start(bf16[3,2,32,8,512]{4,3,1,0,2:T(8,128)(2,1)} %get-tuple-element.31), channel_id=1, source_target_pairs={{0,128},{4,132},{8,136},{12,140},{16,144},{20,148},{24,152},{28,15... | collective-permute-start | bytes 4718600 | tf_op jit(solution)/shard_map/ppermute | solution.py:16
  74.0 16.9 %collective-permute-start = (bf16[3,128,512]{2,1,0:T(8,128)(2,1)S(1)}, bf16[3,128,512]{2,1,0:T(8,128)(2,1)S(1)}, u32[]{:S(2)}, u32[]{:S(2)}) collective-permute-start(bf16[3,128,512]{2,1,0:T(8,128)(2,1)S(1)} %pad_maximum_fusion.3), channel_id=1, source_target_pairs={{0,4},{4,0},{8,12},{12,8},{16,20},{20,16},{24,28},{28,24},{32,36},... | collective-permute-start | bytes 1179656 | tf_op jit(solution)/shard_map/ppermute | solution.py:16
  82.8 9.8 %copy-start.23 = (bf16[1,128,512]{1,2,0:T(8,128)(2,1)}, bf16[1,128,512]{1,2,0:T(8,128)(2,1)S(1)}, u32[]{:S(2)}) copy-start(bf16[1,128,512]{1,2,0:T(8,128)(2,1)S(1)} %copy.754) | copy-start | bytes 393220
  82.9 9.6 %copy-start.16 = (bf16[1,128,512]{1,2,0:T(8,128)(2,1)}, bf16[1,128,512]{1,2,0:T(8,128)(2,1)S(1)}, u32[]{:S(2)}) copy-start(bf16[1,128,512]{1,2,0:T(8,128)(2,1)S(1)} %copy.756) | copy-start | bytes 393220
  84.8 84.8 %copy-start.37 = (f32[128,8]{0,1:T(8,128)}, f32[128,8]{0,1:T(8,128)S(1)}, u32[]{:S(2)}) copy-start(f32[128,8]{0,1:T(8,128)S(1)} %mul.643) | copy-start | bytes 12292
  84.9 8.1 %copy-start.33 = (bf16[2,8,512]{2,1,0:T(8,128)(2,1)}, bf16[2,8,512]{2,1,0:T(8,128)(2,1)S(1)}, u32[]{:S(2)}) copy-start(bf16[2,8,512]{2,1,0:T(8,128)(2,1)S(1)} %get-tuple-element.75) | copy-start | bytes 49156
  91.0 8.7 %copy-start.26 = (bf16[1,128,512]{1,2,0:T(8,128)(2,1)}, bf16[1,128,512]{1,2,0:T(8,128)(2,1)S(1)}, u32[]{:S(2)}) copy-start(bf16[1,128,512]{1,2,0:T(8,128)(2,1)S(1)} %copy.755) | copy-start | bytes 393220
  93.0 6.8 %copy-start.45 = (f32[8,128]{1,0:T(8,128)}, f32[8,128]{1,0:T(8,128)S(1)}, u32[]{:S(2)}) copy-start(f32[8,128]{1,0:T(8,128)S(1)} %get-tuple-element.98) | copy-start | bytes 12292
  102.5 37.9 %collective-permute-start.7 = (bf16[3,64,8,512]{3,2,1,0:T(8,128)(2,1)}, bf16[3,64,8,512]{3,2,1,0:T(8,128)(2,1)}, u32[]{:S(2)}, u32[]{:S(2)}) collective-permute-start(bf16[3,64,8,512]{3,2,1,0:T(8,128)(2,1)} %copy_bitcast_fusion), channel_id=1, source_target_pairs={{0,256},{4,260},{8,264},{12,268},{16,272},{20,276},{24,280},{28,28... | collective-permute-start | bytes 4718600 | tf_op jit(solution)/shard_map/ppermute | solution.py:16
  116.0 10.0 %copy-start.3 = (bf16[1024,8,64]{0,2,1:T(8,128)(2,1)}, bf16[1024,8,64]{0,2,1:T(8,128)(2,1)S(1)}, u32[]{:S(2)}) copy-start(bf16[1024,8,64]{0,2,1:T(8,128)(2,1)S(1)} %copy.761) | copy-start | bytes 3145732
  127.2 4.1 %copy-start.38 = (f32[8,16]{1,0:T(8,128)}, f32[8,16]{1,0:T(8,128)S(1)}, u32[]{:S(2)}) copy-start(f32[8,16]{1,0:T(8,128)S(1)} %log_add_fusion.1) | copy-start | bytes 1540
  167.5 11.8 %copy-start.40 = (f32[128,8]{0,1:T(8,128)}, f32[128,8]{0,1:T(8,128)S(1)}, u32[]{:S(2)}) copy-start(f32[128,8]{0,1:T(8,128)S(1)} %get-tuple-element.15) | copy-start | bytes 12292
  192.2 55.7 %collective-permute-start.9 = (bf16[2,1,8,640]{3,2,0,1:T(8,128)(2,1)}, bf16[2,1,8,640]{3,2,0,1:T(8,128)(2,1)}, u32[]{:S(2)}, u32[]{:S(2)}) collective-permute-start(bf16[2,1,8,640]{3,2,0,1:T(8,128)(2,1)} %get-tuple-element.12), channel_id=1, source_target_pairs={{0,4},{4,0},{8,12},{12,8},{16,20},{20,16},{24,28},{28,24},{32,36},... | collective-permute-start | bytes 61448 | tf_op jit(solution)/shard_map/ppermute | solution.py:16
  221.2 3.5 copy-start.35
  221.2 3.6 copy-start.27
  221.2 4.3 %copy-start.4 = (bf16[1024,8,64]{0,2,1:T(8,128)(2,1)S(1)}, bf16[1024,8,64]{0,2,1:T(8,128)(2,1)}, u32[]{:S(2)}) copy-start(bf16[1024,8,64]{0,2,1:T(8,128)(2,1)} %copy-done.3) | copy-start | bytes 3145732
  221.2 4.3 %copy-start.39 = (f32[8,16]{1,0:T(8,128)S(1)}, f32[8,16]{1,0:T(8,128)}, u32[]{:S(2)}) copy-start(f32[8,16]{1,0:T(8,128)} %copy-done.38) | copy-start | bytes 1540
  222.8 72.5 %collective-permute-start.16 = (f32[2,2,2,2,2,2,2,2,1024]{8,7,6,5,4,3,2,1,0:T(2,128)}, f32[2,2,2,2,2,2,2,2,1024]{8,7,6,5,4,3,2,1,0:T(2,128)}, u32[]{:S(2)}, u32[]{:S(2)}) collective-permute-start(f32[2,2,2,2,2,2,2,2,1024]{8,7,6,5,4,3,2,1,0:T(2,128)} %bitcast.326), channel_id=1, source_target_pairs={{0,1},{1,0},{2,3},{3,2},{4,5},{5,4},{6,7},{7,6},{8,9},{9,8},{10,11... | collective-permute-start | bytes 3145736 | tf_op jit(solution)/shard_map/ppermute | solution.py:278
  225.5 6.3 %copy-start.21 = (bf16[1,128,512]{1,2,0:T(8,128)(2,1)S(1)}, bf16[1,128,512]{1,2,0:T(8,128)(2,1)}, u32[]{:S(2)}) copy-start(bf16[1,128,512]{1,2,0:T(8,128)(2,1)} %copy.768) | copy-start | bytes 393220
  225.6 6.3 %copy-start.41 = (f32[128,8]{0,1:T(8,128)S(1)}, f32[128,8]{0,1:T(8,128)}, u32[]{:S(2)}) copy-start(f32[128,8]{0,1:T(8,128)} %copy-done.40) | copy-start | bytes 12292
  228.1 9.3 %copy-start.43 = (f32[8,8]{0,1:T(8,128)S(1)}, f32[8,8]{0,1:T(8,128)}, u32[]{:S(2)}) copy-start(f32[8,8]{0,1:T(8,128)} %multiply_reduce_fusion.6) | copy-start | bytes 772
  228.1 10.7 %copy-start.2 = (bf16[1024,8,64]{0,2,1:T(8,128)(2,1)S(1)}, bf16[1024,8,64]{0,2,1:T(8,128)(2,1)}, u32[]{:S(2)}) copy-start(bf16[1024,8,64]{0,2,1:T(8,128)(2,1)} %copy.776) | copy-start | bytes 3145732
  234.3 8.2 %copy-start.44 = (f32[8,128]{1,0:T(8,128)S(1)}, f32[8,128]{1,0:T(8,128)}, u32[]{:S(2)}) copy-start(f32[8,128]{1,0:T(8,128)} %get-tuple-element.19) | copy-start | bytes 12292
  234.3 8.2 %copy-start.48 = (f32[128,8]{0,1:T(8,128)S(1)}, f32[128,8]{0,1:T(8,128)}, u32[]{:S(2)}) copy-start(f32[128,8]{0,1:T(8,128)} %mul.657) | copy-start | bytes 12292
  234.3 8.2 %copy-start.15 = (bf16[128,512]{0,1:T(8,128)(2,1)S(1)}, bf16[128,512]{0,1:T(8,128)(2,1)}, u32[]{:S(2)}) copy-start(bf16[128,512]{0,1:T(8,128)(2,1)} %get-tuple-element.92) | copy-start | bytes 393220
  237.5 7.6 %copy-start.13 = (bf16[64,8,512]{2,1,0:T(8,128)(2,1)S(1)}, bf16[64,8,512]{2,1,0:T(8,128)(2,1)}, u32[]{:S(2)}) copy-start(bf16[64,8,512]{2,1,0:T(8,128)(2,1)} %get-tuple-element.23) | copy-start | bytes 1572868
  237.5 7.6 %copy-start.14 = (bf16[64,8,512]{2,1,0:T(8,128)(2,1)S(1)}, bf16[64,8,512]{2,1,0:T(8,128)(2,1)}, u32[]{:S(2)}) copy-start(bf16[64,8,512]{2,1,0:T(8,128)(2,1)} %get-tuple-element.28) | copy-start | bytes 1572868
  243.2 29.3 %collective-permute-start.8 = (bf16[128,640]{0,1:T(8,128)(2,1)}, bf16[128,640]{0,1:T(8,128)(2,1)}, u32[]{:S(2)}, u32[]{:S(2)}) collective-permute-start(bf16[128,640]{0,1:T(8,128)(2,1)} %fusion.74), channel_id=1, source_target_pairs={{0,4},{4,0},{8,12},{12,8},{16,20},{20,16},{24,28},{28,24},{32,36},... | collective-permute-start | bytes 491528 | tf_op jit(solution)/shard_map/ppermute | solution.py:16
  246.4 27.9 %copy-start.17 = (bf16[1,128,512]{1,2,0:T(8,128)(2,1)S(1)}, bf16[1,128,512]{1,2,0:T(8,128)(2,1)}, u32[]{:S(2)}) copy-start(bf16[1,128,512]{1,2,0:T(8,128)(2,1)} %copy-done.16) | copy-start | bytes 393220
  247.8 33.2 %copy-start.22 = (bf16[1,128,512]{1,2,0:T(8,128)(2,1)S(1)}, bf16[1,128,512]{1,2,0:T(8,128)(2,1)}, u32[]{:S(2)}) copy-start(bf16[1,128,512]{1,2,0:T(8,128)(2,1)} %copy.768) | copy-start | bytes 393220
  247.8 33.2 %copy-start.25 = (bf16[1,128,512]{1,2,0:T(8,128)(2,1)S(1)}, bf16[1,128,512]{1,2,0:T(8,128)(2,1)}, u32[]{:S(2)}) copy-start(bf16[1,128,512]{1,2,0:T(8,128)(2,1)} %copy.805) | copy-start | bytes 393220
  248.7 10.5 %collective-permute-start.10 = (bf16[2,2,8,640]{3,2,0,1:T(8,128)(2,1)S(1)}, bf16[2,2,8,640]{3,2,0,1:T(8,128)(2,1)S(1)}, u32[]{:S(2)}, u32[]{:S(2)}) collective-permute-start(bf16[2,2,8,640]{3,2,0,1:T(8,128)(2,1)S(1)} %pad_maximum_fusion.24), channel_id=1, source_target_pairs={{0,16},{4,20},{8,24},{12,28},{16,0},{20,4},{24,8},{28,12},{32,48},... | collective-permute-start | bytes 122888 | tf_op jit(solution)/shard_map/ppermute | solution.py:16
  259.9 7.8 %collective-permute-start.11 = (bf16[2,4,8,640]{3,2,0,1:T(8,128)(2,1)S(1)}, bf16[2,4,8,640]{3,2,0,1:T(8,128)(2,1)S(1)}, u32[]{:S(2)}, u32[]{:S(2)}) collective-permute-start(bf16[2,4,8,640]{3,2,0,1:T(8,128)(2,1)S(1)} %pad_maximum_fusion.22), channel_id=1, source_target_pairs={{0,8},{4,12},{8,0},{12,4},{16,24},{20,28},{24,16},{28,20},{32,40},... | collective-permute-start | bytes 245768 | tf_op jit(solution)/shard_map/ppermute | solution.py:16
  268.5 8.8 %collective-permute-start.12 = (bf16[2,8,8,640]{3,2,0,1:T(8,128)(2,1)S(1)}, bf16[2,8,8,640]{3,2,0,1:T(8,128)(2,1)S(1)}, u32[]{:S(2)}, u32[]{:S(2)}) collective-permute-start(bf16[2,8,8,640]{3,2,0,1:T(8,128)(2,1)S(1)} %pad_maximum_fusion.20), channel_id=1, source_target_pairs={{0,64},{4,68},{8,72},{12,76},{16,80},{20,84},{24,88},{28,92},{32,9... | collective-permute-start | bytes 491528 | tf_op jit(solution)/shard_map/ppermute | solution.py:16
  274.2 6.8 %copy-start.24 = (bf16[128,512]{0,1:T(8,128)(2,1)}, bf16[128,512]{0,1:T(8,128)(2,1)S(1)}, u32[]{:S(2)}) copy-start(bf16[128,512]{0,1:T(8,128)(2,1)S(1)} %slice.189) | copy-start | bytes 393220
  278.2 10.2 %collective-permute-start.13 = (bf16[2,16,8,640]{3,2,0,1:T(8,128)(2,1)}, bf16[2,16,8,640]{3,2,0,1:T(8,128)(2,1)}, u32[]{:S(2)}, u32[]{:S(2)}) collective-permute-start(bf16[2,16,8,640]{3,2,0,1:T(8,128)(2,1)} %get-tuple-element.53), channel_id=1, source_target_pairs={{0,32},{4,36},{8,40},{12,44},{16,48},{20,52},{24,56},{28,60},{32,0... | collective-permute-start | bytes 983048 | tf_op jit(solution)/shard_map/ppermute | solution.py:16
  282.4 12.9 %copy-start.7 = (f32[2,2,2,2,2,2,2,2,1,1024]{9,8,7,6,5,4,3,2,1,0:T(1,128)S(1)}, f32[2,2,2,2,2,2,2,2,1,1024]{9,8,7,6,5,4,3,2,1,0:T(1,128)}, u32[]{:S(2)}) copy-start(f32[2,2,2,2,2,2,2,2,1,1024]{9,8,7,6,5,4,3,2,1,0:T(1,128)} %get-tuple-element.26) | copy-start | bytes 3145732
  290.4 16.3 %collective-permute-start.14 = (bf16[2,32,8,640]{3,2,0,1:T(8,128)(2,1)}, bf16[2,32,8,640]{3,2,0,1:T(8,128)(2,1)}, u32[]{:S(2)}, u32[]{:S(2)}) collective-permute-start(bf16[2,32,8,640]{3,2,0,1:T(8,128)(2,1)} %get-tuple-element.42), channel_id=1, source_target_pairs={{0,128},{4,132},{8,136},{12,140},{16,144},{20,148},{24,152},{28,15... | collective-permute-start | bytes 1966088 | tf_op jit(solution)/shard_map/ppermute | solution.py:16
  295.3 11.4 %copy-start.10 = (bf16[2,64,8,640]{3,2,0,1:T(8,128)(2,1)S(1)}, bf16[2,64,8,640]{3,2,0,1:T(8,128)(2,1)}, u32[]{:S(2)}) copy-start(bf16[2,64,8,640]{3,2,0,1:T(8,128)(2,1)} %get-tuple-element.43) | copy-start | bytes 3932164
  297.4 10.6 %copy-start.8 = (f32[2,2,2,2,2,2,2,2,1024]{8,7,6,5,4,3,2,1,0:T(2,128)}, f32[2,2,2,2,2,2,2,2,1024]{8,7,6,5,4,3,2,1,0:T(2,128)S(1)}, u32[]{:S(2)}) copy-start(f32[2,2,2,2,2,2,2,2,1024]{8,7,6,5,4,3,2,1,0:T(2,128)S(1)} %bitcast_add_fusion) | copy-start | bytes 3145732
  298.4 22.0 %collective-permute-start.17 = (f32[2,2,2,2,2,2,2,1024]{7,6,5,4,3,2,1,0:T(2,128)}, f32[2,2,2,2,2,2,2,1024]{7,6,5,4,3,2,1,0:T(2,128)}, u32[]{:S(2)}, u32[]{:S(2)}) collective-permute-start(f32[2,2,2,2,2,2,2,1024]{7,6,5,4,3,2,1,0:T(2,128)} %dynamic-slice_bitcast_fusion), channel_id=1, source_target_pairs={{0,4},{4,0},{8,12},{12,8},{16,20},{20,16},{24,28},{28,24},{32,36},... | collective-permute-start | bytes 1572872 | tf_op jit(solution)/shard_map/ppermute | solution.py:16
  311.1 7.0 %copy-start.32 = (bf16[16,8,64]{2,1,0:T(8,128)(2,1)S(1)}, bf16[16,8,64]{2,1,0:T(8,128)(2,1)}, u32[]{:S(2)}) copy-start(bf16[16,8,64]{2,1,0:T(8,128)(2,1)} %reshape_reshape_squeeze_stack.11) | copy-start | bytes 49156
  313.1 7.3 %copy-start.9 = (f32[2,2,2,2,2,2,2,2,1024]{8,7,6,5,4,3,2,1,0:T(2,128)S(1)}, f32[2,2,2,2,2,2,2,2,1024]{8,7,6,5,4,3,2,1,0:T(2,128)}, u32[]{:S(2)}) copy-start(f32[2,2,2,2,2,2,2,2,1024]{8,7,6,5,4,3,2,1,0:T(2,128)} %copy-done.8) | copy-start | bytes 3145732
  313.1 18.9 %copy-start.29 = (bf16[16,8,64]{2,1,0:T(8,128)(2,1)S(1)}, bf16[16,8,64]{2,1,0:T(8,128)(2,1)}, u32[]{:S(2)}) copy-start(bf16[16,8,64]{2,1,0:T(8,128)(2,1)} %reshape_reshape_squeeze_stack.12) | copy-start | bytes 49156
  313.1 42.1 %collective-permute-start.15 = (bf16[64,8,640]{2,1,0:T(8,128)(2,1)}, bf16[64,8,640]{2,1,0:T(8,128)(2,1)}, u32[]{:S(2)}, u32[]{:S(2)}) collective-permute-start(bf16[64,8,640]{2,1,0:T(8,128)(2,1)} %slice_bitcast_fusion), channel_id=1, source_target_pairs={{0,256},{4,260},{8,264},{12,268},{16,272},{20,276},{24,280},{28,28... | collective-permute-start | bytes 1966088 | tf_op jit(solution)/shard_map/ppermute | solution.py:16
  323.3 28.7 %collective-permute-start.18 = (f32[2,2,2,2,2,2,1024]{6,5,4,3,2,1,0:T(2,128)}, f32[2,2,2,2,2,2,1024]{6,5,4,3,2,1,0:T(2,128)}, u32[]{:S(2)}, u32[]{:S(2)}) collective-permute-start(f32[2,2,2,2,2,2,1024]{6,5,4,3,2,1,0:T(2,128)} %dynamic-slice_bitcast_fusion.1), channel_id=1, source_target_pairs={{0,16},{4,20},{8,24},{12,28},{16,0},{20,4},{24,8},{28,12},{32,48},... | collective-permute-start | bytes 786440 | tf_op jit(solution)/shard_map/ppermute | solution.py:16
  338.1 17.1 %copy-start.11 = (bf16[64,8,640]{2,1,0:T(8,128)(2,1)S(1)}, bf16[64,8,640]{2,1,0:T(8,128)(2,1)}, u32[]{:S(2)}) copy-start(bf16[64,8,640]{2,1,0:T(8,128)(2,1)} %slice_bitcast_fusion) | copy-start | bytes 1966084
  353.2 9.6 %collective-permute-start.19 = (f32[2,2,2,2,2,1024]{5,4,3,2,1,0:T(2,128)S(1)}, f32[2,2,2,2,2,1024]{5,4,3,2,1,0:T(2,128)S(1)}, u32[]{:S(2)}, u32[]{:S(2)}) collective-permute-start(f32[2,2,2,2,2,1024]{5,4,3,2,1,0:T(2,128)S(1)} %dynamic-slice_bitcast_fusion.2), channel_id=1, source_target_pairs={{0,8},{4,12},{8,0},{12,4},{16,24},{20,28},{24,16},{28,20},{32,40},... | collective-permute-start | bytes 393224 | tf_op jit(solution)/shard_map/ppermute | solution.py:16
  358.1 8.1 %copy-start.42 = (bf16[8,8,64]{2,1,0:T(8,128)(2,1)S(1)}, bf16[8,8,64]{2,1,0:T(8,128)(2,1)}, u32[]{:S(2)}) copy-start(bf16[8,8,64]{2,1,0:T(8,128)(2,1)} %reshape_squeeze.30) | copy-start | bytes 24580
  362.9 7.7 %collective-permute-start.20 = (f32[2,2,2,2,1024]{4,3,2,1,0:T(2,128)S(1)}, f32[2,2,2,2,1024]{4,3,2,1,0:T(2,128)S(1)}, u32[]{:S(2)}, u32[]{:S(2)}) collective-permute-start(f32[2,2,2,2,1024]{4,3,2,1,0:T(2,128)S(1)} %dynamic-slice_bitcast_fusion.3), channel_id=1, source_target_pairs={{0,64},{4,68},{8,72},{12,76},{16,80},{20,84},{24,88},{28,92},{32,9... | collective-permute-start | bytes 196616 | tf_op jit(solution)/shard_map/ppermute | solution.py:16
  371.2 6.1 %collective-permute-start.21 = (f32[2,2,2,1024]{3,2,1,0:T(2,128)}, f32[2,2,2,1024]{3,2,1,0:T(2,128)}, u32[]{:S(2)}, u32[]{:S(2)}) collective-permute-start(f32[2,2,2,1024]{3,2,1,0:T(2,128)} %dynamic-slice_bitcast_fusion.4), channel_id=1, source_target_pairs={{0,32},{4,36},{8,40},{12,44},{16,48},{20,52},{24,56},{28,60},{32,0... | collective-permute-start | bytes 98312 | tf_op jit(solution)/shard_map/ppermute | solution.py:16
  374.0 7.4 %copy-start.36 = (bf16[8,8,64]{2,1,0:T(8,128)(2,1)S(1)}, bf16[8,8,64]{2,1,0:T(8,128)(2,1)}, u32[]{:S(2)}) copy-start(bf16[8,8,64]{2,1,0:T(8,128)(2,1)} %reshape_squeeze.31) | copy-start | bytes 24580
  378.7 5.9 %collective-permute-start.22 = (f32[2,2,1024]{2,1,0:T(2,128)}, f32[2,2,1024]{2,1,0:T(2,128)}, u32[]{:S(2)}, u32[]{:S(2)}) collective-permute-start(f32[2,2,1024]{2,1,0:T(2,128)} %dynamic-slice_bitcast_fusion.5), channel_id=1, source_target_pairs={{0,128},{4,132},{8,136},{12,140},{16,144},{20,148},{24,152},{28,15... | collective-permute-start | bytes 49160 | tf_op jit(solution)/shard_map/ppermute | solution.py:16
  385.4 7.0 %collective-permute-start.23 = (f32[2,1024]{1,0:T(2,128)S(1)}, f32[2,1024]{1,0:T(2,128)S(1)}, u32[]{:S(2)}, u32[]{:S(2)}) collective-permute-start(f32[2,1024]{1,0:T(2,128)S(1)} %dynamic-slice_bitcast_fusion.6), channel_id=1, source_target_pairs={{0,256},{4,260},{8,264},{12,268},{16,272},{20,276},{24,280},{28,28... | collective-permute-start | bytes 24584 | tf_op jit(solution)/shard_map/ppermute | solution.py:16
  388.8 19.7 %copy-start.1 = (bf16[512,1024]{1,0:T(8,128)(2,1)S(1)}, bf16[512,1024]{1,0:T(8,128)(2,1)}, u32[]{:S(2)}) copy-start(bf16[512,1024]{1,0:T(8,128)(2,1)} %param.33) | copy-start | bytes 3145732
  392.5 15.4 %collective-permute-start.24 = (f32[1024]{0:T(1024)S(1)}, f32[1024]{0:T(1024)S(1)}, u32[]{:S(2)}, u32[]{:S(2)}) collective-permute-start(f32[1024]{0:T(1024)S(1)} %bitcast.404), channel_id=1, source_target_pairs={{0,2},{1,3},{2,0},{3,1},{4,6},{5,7},{6,4},{7,5},{8,10},{9,11},{10,... | collective-permute-start | bytes 12296 | tf_op jit(solution)/shard_map/ppermute | solution.py:278
  (11 other events, 23.3 us)
where the time goes:
time: 412 us; the launch traced here: 409 us
  local copies, waits for them, and re-layouts  132 us (32%)
  starting transfers between devices  129 us (31%)
  waiting for transfers between devices  82.7 us (20%)
  other arithmetic  35.4 us (9%)
  matrix products  27.6 us (7%)
    ppermute x23, starting transfers between devices, partner(): return lax.ppermute(value, axis, pairs)  114 us
    ppermute x23, waiting for transfers between devices, partner(): return lax.ppermute(value, axis, pairs)  82.7 us
    another operation x18, local copies, waits for them, and re-layouts, heads_view(): return matrix.reshape(matrix.shape[0], HEADS, HD)  35.3 us
    mul x26, local copies, waits for them, and re-layouts, spread_rows(): values[:, None] * chooser  18 us
    unnamed x114, local copies, waits for them, and re-layouts  15 us
    ppermute x2, starting transfers between devices, batch_step(): halving.absorb(lax.ppermute(send, 'batch', pairs))  14.7 us
  transfers between devices with their start and end apart: 25, of which 17 were waited for; matrix products, arithmetic and copies ran while one was open for 31% of the time, Pallas kernels for 0%

commit v1 on v0

--- a/solution.py
+++ b/solution.py
@@ -104,24 +104,21 @@
     return jnp.pad(matrix, [(0, 0)] * (matrix.ndim - 1) + [(0, width - matrix.shape[-1])])
 
 
-class HalvingSum:
-
-    def __init__(self, matrix, bit_count):
-        self.block = matrix.reshape((2,) * bit_count + matrix.shape[1:])
-        self.dims = [bit_count - 1 - j for j in range(bit_count)]
-        self.tail = matrix.shape[1:]
-
-    def split(self, bit_pos, my_bit):
-        self.axis_pos = self.dims.index(bit_pos)
-        self.keep = lax.dynamic_index_in_dim(self.block, my_bit, self.axis_pos, keepdims=False)
-        return lax.dynamic_index_in_dim(self.block, 1 - my_bit, self.axis_pos, keepdims=False)
-
-    def absorb(self, received):
-        self.block = self.keep + received
-        self.dims.pop(self.axis_pos)
-
-    def result(self):
-        return self.block.reshape((1,) + self.tail)
+def scatter_sum(matrix, axes, bit_order):
+    index = lax.axis_index(axes)
+    bit_count = len(bit_order)
+    size = 1 << bit_count
+    block = matrix.reshape((2,) * bit_count + matrix.shape[1:])
+    dims = [bit_count - 1 - j for j in range(bit_count)]
+    for bit_pos in bit_order:
+        axis_pos = dims.index(bit_pos)
+        my_bit = index // (1 << bit_pos) % 2
+        keep = lax.dynamic_index_in_dim(block, my_bit, axis_pos, keepdims=False)
+        send = lax.dynamic_index_in_dim(block, 1 - my_bit, axis_pos, keepdims=False)
+        pairs = [(source, source ^ (1 << bit_pos)) for source in range(size)]
+        block = keep + lax.ppermute(send, axes, pairs)
+        dims.pop(axis_pos)
+    return block.reshape((1,) + matrix.shape[1:])
 
 
 def heads_view(matrix):
@@ -215,30 +212,20 @@
     devices = lax.axis_size("tm")
     bit_count = devices.bit_length() - 1
     top_bit = bit_count - 1
-    near_first = {0: 0, 1: 2, 2: 1, 3: 4, 4: 3, 5: 5}
+    near_first = {0: 3, 1: 1, 2: 0, 3: 4, 4: 2, 5: 5}
     low_bits = sorted(range(top_bit), key=lambda b: near_first.get(b, b))
-    tm_index = lax.axis_index("tm")
-    batch_index = lax.axis_index("batch")
-    batch_count = lax.axis_size("batch")
-    batch_bits = batch_count.bit_length() - 1
     wide = features + 128
 
-    qkv = jnp.stack([by_parity(pick_rows(m, R2)) for m in (queries, keys_all, values_all)], 0)
-    per_par = qkv.shape[2]
-    own = qkv[:, :, None]
-    for bit_pos in low_bits:
-        if bit_pos == 0:
-            other, other_qkv = partner(
-                (own, jnp.stack([queries, keys_all, values_all], 0)), "tm", bit_pos
-            )
-        else:
-            other = partner(own, "tm", bit_pos)
-        own = jnp.concatenate([own, other], 2)
-    far = partner(own[:, 0], "tm", top_bit)
+    other_qkv = partner(jnp.stack([queries, keys_all, values_all], 0), "tm", 0)
     other_q = other_qkv[0]
     keys_one = jnp.concatenate([keys_all, other_qkv[1]], 0)
     values_one = jnp.concatenate([values_all, other_qkv[2]], 0)
     part_one, lse_one = attend(queries, keys_one, values_one, inv_root)
+
+    qkv = jnp.stack([by_parity(pick_rows(m, R2)) for m in (queries, keys_all, values_all)], 0)
+    per_par = qkv.shape[2]
+    own = gather_blocks(qkv[:, :, None], 2, low_bits)
+    far = partner(own[:, 0], "tm", top_bit)
     q_seg2 = own[0].reshape(-1, features)
     k_seg2 = own[1].reshape(-1, features)
     v_seg2 = own[2].reshape(-1, features)
@@ -270,17 +257,8 @@
     proj_part = lax.dot_general(
         attn, upstream, (((0,), (0,)), ((), ())), preferred_element_type=jnp.float32
     )
-    halving = HalvingSum(proj_part, bit_count + batch_bits)
-
-    def batch_step(bit_pos):
-        send = halving.split(bit_pos, batch_index // (1 << bit_pos) % 2)
-        pairs = [(s, s ^ (1 << bit_pos)) for s in range(batch_count)]
-        halving.absorb(lax.ppermute(send, "batch", pairs))
-
-    def tm_send(bit_pos):
-        return halving.split(bit_pos + batch_bits, tm_index // (1 << bit_pos) % 2)
-
-    batch_step(0)
+    order = (0, 2, 5, 7, 3, 6, 8, 4, 1)
+    grad_proj = scatter_sum(proj_part, ("tm", "batch"), order)
 
     grad_three = grad_attn.astype(jnp.float32).reshape(row_count, HEADS, HD)
     rowdot = jnp.sum(grad_three * merged, axis=2)
@@ -292,7 +270,22 @@
     grad_one = grad_of(weights[0], grad_attn)
     offset_one = weights[0] * rowdot
     packed_one = jnp.concatenate([grad_one, split_exact(jnp.concatenate([lse_one, offset_one], 1))], 1)
-    packed_one = pad_lanes(packed_one, wide)
+    other_one = partner(pad_lanes(packed_one, wide), "tm", 0)
+    other_stats = join_exact(other_one[:, features : features + 6 * HEADS])
+    total_q = spread_rows(
+        near_grad(queries, keys_one, values_one, grad_one, lse_one, offset_one, inv_root), 1
+    )
+    k_g1, v_g1 = far_grad(
+        jnp.concatenate([queries, other_q], 0),
+        jnp.concatenate([grad_one, other_one[:, :features]], 0),
+        jnp.concatenate([lse_one, other_stats[:, :HEADS]], 0),
+        jnp.concatenate([offset_one, other_stats[:, HEADS:]], 0),
+        keys_all,
+        values_all,
+        inv_root,
+    )
+    total_k = spread_rows(k_g1, 1)
+    total_v = spread_rows(v_g1, 1)
 
     ga_par = by_parity(pick_rows(grad_attn, R2))
     w_two = by_parity(pick_stats(weights[1], R2))
@@ -304,38 +297,8 @@
     w3_par = jnp.stack([w_three, no_level], 0)
     stats_par = jnp.concatenate([lse_two_par, w_two, lse3_par, w3_par, rd_two], -1)
     packed = pad_lanes(jnp.concatenate([ga_par, split_exact(stats_par)], -1), wide)
-    own_b = packed[:, None]
-    for bit_pos in low_bits:
-        if bit_pos == 0:
-            other, received, other_one = partner(
-                (own_b, tm_send(bit_pos), packed_one), "tm", bit_pos
-            )
-        else:
-            other, received = partner((own_b, tm_send(bit_pos)), "tm", bit_pos)
-        halving.absorb(received)
-        own_b = jnp.concatenate([own_b, other], 1)
-    far_b, received = partner((own_b[0], tm_send(top_bit)), "tm", top_bit)
-    halving.absorb(received)
-    for bit_pos in range(1, batch_bits):
-        batch_step(bit_pos)
-    grad_proj = halving.result()
-
-    other_stats = join_exact(other_one[:, features : features + 6 * HEADS])
-    total_q = spread_rows(
-        near_grad(queries, keys_one, values_one, grad_one, lse_one, offset_one, inv_root), 1
-    )
-    k_g1, v_g1 = far_grad(
-        jnp.concatenate([queries, other_q], 0),
-        jnp.concatenate([grad_one, other_one[:, :features]], 0),
-        jnp.concatenate([lse_one, other_stats[:, :HEADS]], 0),
-        jnp.concatenate([offset_one, other_stats[:, HEADS:]], 0),
-        keys_all,
-        values_all,
-        inv_root,
-    )
-    total_k = spread_rows(k_g1, 1)
-    total_v = spread_rows(v_g1, 1)
-
+    own_b = gather_blocks(packed[:, None], 1, low_bits)
+    far_b = partner(own_b[0], "tm", top_bit)
     stat_w = 5 * HEADS
 
     def unpack(rows):

time: 412 us -> 389 us (0.944)
  starting transfers between devices: 129 us -> 93.6 us
  waiting for transfers between devices: 82.7 us -> 94.1 us
    ppermute x23 -> x16, starting transfers between devices: 114 us -> 67.8 us  [partner(): return lax.ppermute(value, axis, pairs)]
    ppermute x2 -> x9, waiting for transfers between devices: 0.01 us -> 26.9 us  [scatter_sum(): block = keep + lax.ppermute(send, axes, pairs)]
    ppermute x23 -> x16, waiting for transfers between devices: 82.7 us -> 67.2 us  [partner(): return lax.ppermute(value, axis, pairs)]
    ppermute x2 -> x9, starting transfers between devices: 14.7 us -> 25.9 us  [scatter_sum(): block = keep + lax.ppermute(send, axes, pairs)]
  transfers between devices with their start and end apart: 25 -> 25, of which waited for: 17 -> 17; matrix products, arithmetic and copies ran while one was open for 31% -> 33% of each run, Pallas kernels for 0% -> 0%
where the time goes in v1:
time: 389 us; the launch traced here: 385 us
  local copies, waits for them, and re-layouts  132 us (34%)
  waiting for transfers between devices  94.1 us (24%)
  starting transfers between devices  93.6 us (24%)
  other arithmetic  35.4 us (9%)
  matrix products  27.6 us (7%)
    ppermute x16, starting transfers between devices, partner(): return lax.ppermute(value, axis, pairs)  67.8 us
    ppermute x16, waiting for transfers between devices, partner(): return lax.ppermute(value, axis, pairs)  67.2 us
    another operation x18, local copies, waits for them, and re-layouts, heads_view(): return matrix.reshape(matrix.shape[0], HEADS, HD)  35.3 us
    ppermute x9, waiting for transfers between devices, scatter_sum(): block = keep + lax.ppermute(send, axes, pairs)  26.9 us
    ppermute x9, starting transfers between devices, scatter_sum(): block = keep + lax.ppermute(send, axes, pairs)  25.9 us
    mul x26, local copies, waits for them, and re-layouts, spread_rows(): values[:, None] * chooser  18 us
    unnamed x114, local copies, waits for them, and re-layouts  15 us
  transfers between devices with their start and end apart: 25, of which 17 were waited for; matrix products, arithmetic and copies ran while one was open for 33% of the time, Pallas kernels for 0%

profile of v1, /device:TPU:6, one launch (start us, length us, event | category | flops | bytes accessed | tf_op | source)
XLA Modules:
  0.0 384.6 jit_solution(14278987342150093086)
XLA Ops:
  5.1 9.1 %collective-permute-start.1 = (bf16[3,2,1,8,512]{4,3,1,0,2:T(8,128)(2,1)S(1)}, bf16[3,2,1,8,512]{4,3,1,0,2:T(8,128)(2,1)S(1)}, u32[]{:S(2)}, u32[]{:S(2)}) collective-permute-start(bf16[3,2,1,8,512]{4,3,1,0,2:T(8,128)(2,1)S(1)} %bitcast.357), channel_id=1, source_target_pairs={{0,16},{4,20},{8,24},{12,28},{16,0},{20,4},{24,8},{28,12},{32,48},... | collective-permute-start | bytes 147464 | tf_op jit(solution)/shard_map/ppermute | solution.py:16
  14.2 2.1 collective-permute-done.1
  16.3 5.3 %collective-permute-start.2 = (bf16[3,2,2,8,512]{4,3,1,0,2:T(8,128)(2,1)S(1)}, bf16[3,2,2,8,512]{4,3,1,0,2:T(8,128)(2,1)S(1)}, u32[]{:S(2)}, u32[]{:S(2)}) collective-permute-start(bf16[3,2,2,8,512]{4,3,1,0,2:T(8,128)(2,1)S(1)} %pad_maximum_fusion.21), channel_id=1, source_target_pairs={{0,8},{4,12},{8,0},{12,4},{16,24},{20,28},{24,16},{28,20},{32,40},... | collective-permute-start | bytes 294920 | tf_op jit(solution)/shard_map/ppermute | solution.py:16
  21.6 5.0 %collective-permute-done.2 = bf16[3,2,2,8,512]{4,3,1,0,2:T(8,128)(2,1)S(1)} collective-permute-done((bf16[3,2,2,8,512]{4,3,1,0,2:T(8,128)(2,1)S(1)}, bf16[3,2,2,8,512]{4,3,1,0,2:T(8,128)(2,1)S(1)}, u32[]{:S(2)}, u32[]{:S(2)}) %collective-permute-start.2) | collective-permute-done | bytes 98336 | tf_op jit(solution)/shard_map/ppermute | solution.py:16
  26.7 3.3 collective-permute-start.3
  30.0 5.7 %collective-permute-done.3 = bf16[3,2,4,8,512]{4,3,1,0,2:T(8,128)(2,1)S(1)} collective-permute-done((bf16[3,2,4,8,512]{4,3,1,0,2:T(8,128)(2,1)S(1)}, bf16[3,2,4,8,512]{4,3,1,0,2:T(8,128)(2,1)S(1)}, u32[]{:S(2)}, u32[]{:S(2)}) %collective-permute-start.3) | collective-permute-done | bytes 196640 | tf_op jit(solution)/shard_map/ppermute | solution.py:16
  35.8 3.8 collective-permute-start.4
  42.5 5.6 %collective-permute-done.4 = bf16[3,2,8,8,512]{4,3,1,0,2:T(8,128)(2,1)S(1)} collective-permute-done((bf16[3,2,8,8,512]{4,3,1,0,2:T(8,128)(2,1)S(1)}, bf16[3,2,8,8,512]{4,3,1,0,2:T(8,128)(2,1)S(1)}, u32[]{:S(2)}, u32[]{:S(2)}) %collective-permute-start.4) | collective-permute-done | bytes 393248 | tf_op jit(solution)/shard_map/ppermute | solution.py:16
  49.1 2.7 collective-permute-start.5
  51.8 17.0 %collective-permute-done.5 = bf16[3,2,16,8,512]{4,3,1,0,2:T(8,128)(2,1)S(1)} collective-permute-done((bf16[3,2,16,8,512]{4,3,1,0,2:T(8,128)(2,1)S(1)}, bf16[3,2,16,8,512]{4,3,1,0,2:T(8,128)(2,1)S(1)}, u32[]{:S(2)}, u32[]{:S(2)}) %collective-permute-start.5) | collective-permute-done | bytes 786464 | tf_op jit(solution)/shard_map/ppermute | solution.py:16
  70.1 3.5 collective-permute-start.6
  73.7 3.5 collective-permute-start
  88.2 17.9 %collective-permute-done.6 = bf16[3,2,32,8,512]{4,3,1,0,2:T(8,128)(2,1)} collective-permute-done((bf16[3,2,32,8,512]{4,3,1,0,2:T(8,128)(2,1)}, bf16[3,2,32,8,512]{4,3,1,0,2:T(8,128)(2,1)}, u32[]{:S(2)}, u32[]{:S(2)}) %collective-permute-start.6) | collective-permute-done | bytes 1572896 | tf_op jit(solution)/shard_map/ppermute | solution.py:16
  106.1 2.7 constant_dynamic-update-slice_fusion.11
  108.8 2.8 copy_bitcast_fusion
  111.6 5.3 %collective-permute-start.7 = (bf16[3,64,8,512]{3,2,1,0:T(8,128)(2,1)}, bf16[3,64,8,512]{3,2,1,0:T(8,128)(2,1)}, u32[]{:S(2)}, u32[]{:S(2)}) collective-permute-start(bf16[3,64,8,512]{3,2,1,0:T(8,128)(2,1)} %copy_bitcast_fusion), channel_id=1, source_target_pairs={{0,256},{4,260},{8,264},{12,268},{16,272},{20,276},{24,280},{28,28... | collective-permute-start | bytes 4718600 | tf_op jit(solution)/shard_map/ppermute | solution.py:16
  116.8 3.5 fusion.134
  120.4 2.1 reshape_reshape_squeeze.6
  122.5 2.5 copy.761
  125.0 2.7 copy.771
  127.8 3.9 %reshape_reshape_squeeze.14 = bf16[1024,8,64]{2,1,0:T(8,128)(2,1)} reshape(bf16[1,2,64,8,512]{4,3,2,1,0:T(8,128)(2,1)} %copy.771) | data formatting | bytes 2097152 | tf_op jit(solution)/shard_map/reshape;reshape;squeeze | solution.py:125
  131.7 3.3 copy.772
  141.7 2.1 reshape_reshape_squeeze.15
  143.8 3.3 copy.818
  147.1 2.3 slice_bitcast_fusion.2
  149.4 2.3 slice_bitcast_fusion.1
  152.9 2.1 reshape_reshape.28
  154.9 2.5 copy.767
  161.5 3.9 %reshape_reshape.29 = bf16[1024,8,64]{2,1,0:T(8,128)(2,1)} reshape(bf16[128,8,512]{2,1,0:T(8,128)(2,1)} %get-tuple-element.102) | data formatting | bytes 2097152 | tf_op jit(solution)/shard_map/reshape;reshape | solution.py:125
  165.4 3.4 copy.776
  173.2 1.9 copy.781
  178.5 2.9 fusion.65
  201.2 8.6 %collective-permute-start.9 = (bf16[2,1,8,640]{3,2,0,1:T(8,128)(2,1)}, bf16[2,1,8,640]{3,2,0,1:T(8,128)(2,1)}, u32[]{:S(2)}, u32[]{:S(2)}) collective-permute-start(bf16[2,1,8,640]{3,2,0,1:T(8,128)(2,1)} %get-tuple-element.12), channel_id=1, source_target_pairs={{0,16},{4,20},{8,24},{12,28},{16,0},{20,4},{24,8},{28,12},{32,48},... | collective-permute-start | bytes 61448 | tf_op jit(solution)/shard_map/ppermute | solution.py:16
  216.6 3.2 constant_dynamic-slice_fusion.3
  224.1 2.6 fusion.29
  228.5 1.9 mul.683
  230.4 2.4 fusion.17
  237.4 2.0 fusion.35
  241.8 3.4 collective-permute-start.8
  248.6 5.3 %collective-permute-start.10 = (bf16[2,2,8,640]{3,2,0,1:T(8,128)(2,1)S(1)}, bf16[2,2,8,640]{3,2,0,1:T(8,128)(2,1)S(1)}, u32[]{:S(2)}, u32[]{:S(2)}) collective-permute-start(bf16[2,2,8,640]{3,2,0,1:T(8,128)(2,1)S(1)} %pad_maximum_fusion.24), channel_id=1, source_target_pairs={{0,8},{4,12},{8,0},{12,4},{16,24},{20,28},{24,16},{28,20},{32,40},... | collective-permute-start | bytes 122888 | tf_op jit(solution)/shard_map/ppermute | solution.py:16
  257.5 3.3 collective-permute-start.11
  261.5 3.9 %collective-permute-done.11 = bf16[2,4,8,640]{3,2,0,1:T(8,128)(2,1)S(1)} collective-permute-done((bf16[2,4,8,640]{3,2,0,1:T(8,128)(2,1)S(1)}, bf16[2,4,8,640]{3,2,0,1:T(8,128)(2,1)S(1)}, u32[]{:S(2)}, u32[]{:S(2)}) %collective-permute-start.11) | collective-permute-done | bytes 81952 | tf_op jit(solution)/shard_map/ppermute | solution.py:16
  266.1 2.0 collective-permute-start.12
  274.2 2.7 collective-permute-start.13
  280.2 3.3 collective-permute-done.13
  285.4 2.6 collective-permute-start.14
  290.0 2.1 bitcast_add_fusion
  293.0 3.4 collective-permute-start.17
  296.5 4.1 %collective-permute-done.14 = bf16[2,32,8,640]{3,2,0,1:T(8,128)(2,1)} collective-permute-done((bf16[2,32,8,640]{3,2,0,1:T(8,128)(2,1)}, bf16[2,32,8,640]{3,2,0,1:T(8,128)(2,1)}, u32[]{:S(2)}, u32[]{:S(2)}) %collective-permute-start.14) | collective-permute-done | bytes 655392 | tf_op jit(solution)/shard_map/ppermute | solution.py:16
  305.0 1.9 copy.815
  307.0 3.5 collective-permute-start.15
  310.5 2.3 fusion.11
  315.7 2.7 collective-permute-start.18
  326.7 2.6 collective-permute-start.19
  333.7 5.8 %collective-permute-start.20 = (f32[2,2,2,2,1024]{4,3,2,1,0:T(2,128)S(1)}, f32[2,2,2,2,1024]{4,3,2,1,0:T(2,128)S(1)}, u32[]{:S(2)}, u32[]{:S(2)}) collective-permute-start(f32[2,2,2,2,1024]{4,3,2,1,0:T(2,128)S(1)} %dynamic-slice_bitcast_fusion.3), channel_id=1, source_target_pairs={{0,8},{1,9},{2,10},{3,11},{4,12},{5,13},{6,14},{7,15},{8,0},{9,1},... | collective-permute-start | bytes 196616 | tf_op jit(solution)/shard_map/ppermute | solution.py:119
  339.8 2.7 collective-permute-done.20
  343.1 3.0 collective-permute-start.21
  346.2 1.9 copy.825
  348.1 2.6 collective-permute-done.21
  352.1 2.5 collective-permute-start.22
  355.2 4.4 %collective-permute-done.22 = f32[2,2,1024]{2,1,0:T(2,128)} collective-permute-done((f32[2,2,1024]{2,1,0:T(2,128)}, f32[2,2,1024]{2,1,0:T(2,128)}, u32[]{:S(2)}, u32[]{:S(2)}) %collective-permute-start.22) | collective-permute-done | bytes 16416 | tf_op jit(solution)/shard_map/ppermute | solution.py:119
  363.1 6.7 %collective-permute-done.23 = f32[2,1024]{1,0:T(2,128)S(1)} collective-permute-done((f32[2,1024]{1,0:T(2,128)S(1)}, f32[2,1024]{1,0:T(2,128)S(1)}, u32[]{:S(2)}, u32[]{:S(2)}) %collective-permute-start.23) | collective-permute-done | bytes 8224 | tf_op jit(solution)/shard_map/ppermute | solution.py:119
  371.7 2.6 add_convert_fusion
  374.4 9.7 %collective-permute-done.24 = f32[1024]{0:T(1024)S(1)} collective-permute-done((f32[1024]{0:T(1024)S(1)}, f32[1024]{0:T(1024)S(1)}, u32[]{:S(2)}, u32[]{:S(2)}) %collective-permute-start.24) | collective-permute-done | bytes 4128 | tf_op jit(solution)/shard_map/ppermute | solution.py:119
  (308 shorter events, 131.2 us)
Async XLA Ops:
  0.6 3.7 copy-start.49
  5.1 11.2 %collective-permute-start.1 = (bf16[3,2,1,8,512]{4,3,1,0,2:T(8,128)(2,1)S(1)}, bf16[3,2,1,8,512]{4,3,1,0,2:T(8,128)(2,1)S(1)}, u32[]{:S(2)}, u32[]{:S(2)}) collective-permute-start(bf16[3,2,1,8,512]{4,3,1,0,2:T(8,128)(2,1)S(1)} %bitcast.357), channel_id=1, source_target_pairs={{0,16},{4,20},{8,24},{12,28},{16,0},{20,4},{24,8},{28,12},{32,48},... | collective-permute-start | bytes 147464 | tf_op jit(solution)/shard_map/ppermute | solution.py:16
  16.3 10.4 %collective-permute-start.2 = (bf16[3,2,2,8,512]{4,3,1,0,2:T(8,128)(2,1)S(1)}, bf16[3,2,2,8,512]{4,3,1,0,2:T(8,128)(2,1)S(1)}, u32[]{:S(2)}, u32[]{:S(2)}) collective-permute-start(bf16[3,2,2,8,512]{4,3,1,0,2:T(8,128)(2,1)S(1)} %pad_maximum_fusion.21), channel_id=1, source_target_pairs={{0,8},{4,12},{8,0},{12,4},{16,24},{20,28},{24,16},{28,20},{32,40},... | collective-permute-start | bytes 294920 | tf_op jit(solution)/shard_map/ppermute | solution.py:16
  26.7 9.1 %collective-permute-start.3 = (bf16[3,2,4,8,512]{4,3,1,0,2:T(8,128)(2,1)S(1)}, bf16[3,2,4,8,512]{4,3,1,0,2:T(8,128)(2,1)S(1)}, u32[]{:S(2)}, u32[]{:S(2)}) collective-permute-start(bf16[3,2,4,8,512]{4,3,1,0,2:T(8,128)(2,1)S(1)} %pad_maximum_fusion.9), channel_id=1, source_target_pairs={{0,64},{4,68},{8,72},{12,76},{16,80},{20,84},{24,88},{28,92},{32,9... | collective-permute-start | bytes 589832 | tf_op jit(solution)/shard_map/ppermute | solution.py:16
  35.8 12.2 %collective-permute-start.4 = (bf16[3,2,8,8,512]{4,3,1,0,2:T(8,128)(2,1)S(1)}, bf16[3,2,8,8,512]{4,3,1,0,2:T(8,128)(2,1)S(1)}, u32[]{:S(2)}, u32[]{:S(2)}) collective-permute-start(bf16[3,2,8,8,512]{4,3,1,0,2:T(8,128)(2,1)S(1)} %pad_maximum_fusion.4), channel_id=1, source_target_pairs={{0,4},{4,0},{8,12},{12,8},{16,20},{20,16},{24,28},{28,24},{32,36},... | collective-permute-start | bytes 1179656 | tf_op jit(solution)/shard_map/ppermute | solution.py:16
  49.1 19.7 %collective-permute-start.5 = (bf16[3,2,16,8,512]{4,3,1,0,2:T(8,128)(2,1)S(1)}, bf16[3,2,16,8,512]{4,3,1,0,2:T(8,128)(2,1)S(1)}, u32[]{:S(2)}, u32[]{:S(2)}) collective-permute-start(bf16[3,2,16,8,512]{4,3,1,0,2:T(8,128)(2,1)S(1)} %get-tuple-element.41), channel_id=1, source_target_pairs={{0,32},{4,36},{8,40},{12,44},{16,48},{20,52},{24,56},{28,60},{32,0... | collective-permute-start | bytes 2359304 | tf_op jit(solution)/shard_map/ppermute | solution.py:16
  68.8 10.3 %copy-start.47 = (f32[8,8]{0,1:T(8,128)S(1)}, f32[8,8]{0,1:T(8,128)}, u32[]{:S(2)}) copy-start(f32[8,8]{0,1:T(8,128)} %constant.249.clone) | copy-start | bytes 772
  68.8 10.4 %copy-start.46 = (f32[16,8]{0,1:T(8,128)S(1)}, f32[16,8]{0,1:T(8,128)}, u32[]{:S(2)}) copy-start(f32[16,8]{0,1:T(8,128)} %constant.250.clone) | copy-start | bytes 1540
  70.1 36.0 %collective-permute-start.6 = (bf16[3,2,32,8,512]{4,3,1,0,2:T(8,128)(2,1)}, bf16[3,2,32,8,512]{4,3,1,0,2:T(8,128)(2,1)}, u32[]{:S(2)}, u32[]{:S(2)}) collective-permute-start(bf16[3,2,32,8,512]{4,3,1,0,2:T(8,128)(2,1)} %get-tuple-element.31), channel_id=1, source_target_pairs={{0,128},{4,132},{8,136},{12,140},{16,144},{20,148},{24,152},{28,15... | collective-permute-start | bytes 4718600 | tf_op jit(solution)/shard_map/ppermute | solution.py:16
  73.7 11.7 %collective-permute-start = (bf16[3,128,512]{2,1,0:T(8,128)(2,1)S(1)}, bf16[3,128,512]{2,1,0:T(8,128)(2,1)S(1)}, u32[]{:S(2)}, u32[]{:S(2)}) collective-permute-start(bf16[3,128,512]{2,1,0:T(8,128)(2,1)S(1)} %pad_maximum_fusion.3), channel_id=1, source_target_pairs={{0,4},{4,0},{8,12},{12,8},{16,20},{20,16},{24,28},{28,24},{32,36},... | collective-permute-start | bytes 1179656 | tf_op jit(solution)/shard_map/ppermute | solution.py:16
  77.3 9.8 %copy-start.23 = (bf16[1,128,512]{1,2,0:T(8,128)(2,1)}, bf16[1,128,512]{1,2,0:T(8,128)(2,1)S(1)}, u32[]{:S(2)}) copy-start(bf16[1,128,512]{1,2,0:T(8,128)(2,1)S(1)} %copy.754) | copy-start | bytes 393220
  77.5 9.6 %copy-start.16 = (bf16[1,128,512]{1,2,0:T(8,128)(2,1)}, bf16[1,128,512]{1,2,0:T(8,128)(2,1)S(1)}, u32[]{:S(2)}) copy-start(bf16[1,128,512]{1,2,0:T(8,128)(2,1)S(1)} %copy.756) | copy-start | bytes 393220
  79.3 99.3 %copy-start.37 = (f32[128,8]{0,1:T(8,128)}, f32[128,8]{0,1:T(8,128)S(1)}, u32[]{:S(2)}) copy-start(f32[128,8]{0,1:T(8,128)S(1)} %mul.646) | copy-start | bytes 12292
  79.4 8.1 %copy-start.33 = (bf16[2,8,512]{2,1,0:T(8,128)(2,1)}, bf16[2,8,512]{2,1,0:T(8,128)(2,1)S(1)}, u32[]{:S(2)}) copy-start(bf16[2,8,512]{2,1,0:T(8,128)(2,1)S(1)} %get-tuple-element.75) | copy-start | bytes 49156
  85.6 23.2 %copy-start.26 = (bf16[1,128,512]{1,2,0:T(8,128)(2,1)}, bf16[1,128,512]{1,2,0:T(8,128)(2,1)S(1)}, u32[]{:S(2)}) copy-start(bf16[1,128,512]{1,2,0:T(8,128)(2,1)S(1)} %copy.755) | copy-start | bytes 393220
  87.5 21.3 %copy-start.45 = (f32[8,128]{1,0:T(8,128)}, f32[8,128]{1,0:T(8,128)S(1)}, u32[]{:S(2)}) copy-start(f32[8,128]{1,0:T(8,128)S(1)} %get-tuple-element.98) | copy-start | bytes 12292
  111.6 37.9 %collective-permute-start.7 = (bf16[3,64,8,512]{3,2,1,0:T(8,128)(2,1)}, bf16[3,64,8,512]{3,2,1,0:T(8,128)(2,1)}, u32[]{:S(2)}, u32[]{:S(2)}) collective-permute-start(bf16[3,64,8,512]{3,2,1,0:T(8,128)(2,1)} %copy_bitcast_fusion), channel_id=1, source_target_pairs={{0,256},{4,260},{8,264},{12,268},{16,272},{20,276},{24,280},{28,28... | collective-permute-start | bytes 4718600 | tf_op jit(solution)/shard_map/ppermute | solution.py:16
  125.0 10.0 %copy-start.3 = (bf16[1024,8,64]{0,2,1:T(8,128)(2,1)}, bf16[1024,8,64]{0,2,1:T(8,128)(2,1)S(1)}, u32[]{:S(2)}) copy-start(bf16[1024,8,64]{0,2,1:T(8,128)(2,1)S(1)} %copy.761) | copy-start | bytes 3145732
  136.2 4.1 %copy-start.38 = (f32[8,16]{1,0:T(8,128)}, f32[8,16]{1,0:T(8,128)S(1)}, u32[]{:S(2)}) copy-start(f32[8,16]{1,0:T(8,128)S(1)} %log_add_fusion.1) | copy-start | bytes 1540
  176.5 11.8 %copy-start.40 = (f32[128,8]{0,1:T(8,128)}, f32[128,8]{0,1:T(8,128)S(1)}, u32[]{:S(2)}) copy-start(f32[128,8]{0,1:T(8,128)S(1)} %get-tuple-element.15) | copy-start | bytes 12292
  201.2 46.7 %collective-permute-start.9 = (bf16[2,1,8,640]{3,2,0,1:T(8,128)(2,1)}, bf16[2,1,8,640]{3,2,0,1:T(8,128)(2,1)}, u32[]{:S(2)}, u32[]{:S(2)}) collective-permute-start(bf16[2,1,8,640]{3,2,0,1:T(8,128)(2,1)} %get-tuple-element.12), channel_id=1, source_target_pairs={{0,16},{4,20},{8,24},{12,28},{16,0},{20,4},{24,8},{28,12},{32,48},... | collective-permute-start | bytes 61448 | tf_op jit(solution)/shard_map/ppermute | solution.py:16
  219.8 3.6 copy-start.27
  219.8 4.3 %copy-start.4 = (bf16[1024,8,64]{0,2,1:T(8,128)(2,1)S(1)}, bf16[1024,8,64]{0,2,1:T(8,128)(2,1)}, u32[]{:S(2)}) copy-start(bf16[1024,8,64]{0,2,1:T(8,128)(2,1)} %copy-done.3) | copy-start | bytes 3145732
  219.8 4.3 %copy-start.39 = (f32[8,16]{1,0:T(8,128)S(1)}, f32[8,16]{1,0:T(8,128)}, u32[]{:S(2)}) copy-start(f32[8,16]{1,0:T(8,128)} %copy-done.38) | copy-start | bytes 1540
  221.3 68.7 %collective-permute-start.16 = (f32[2,2,2,2,2,2,2,2,1024]{8,7,6,5,4,3,2,1,0:T(2,128)}, f32[2,2,2,2,2,2,2,2,1024]{8,7,6,5,4,3,2,1,0:T(2,128)}, u32[]{:S(2)}, u32[]{:S(2)}) collective-permute-start(f32[2,2,2,2,2,2,2,2,1024]{8,7,6,5,4,3,2,1,0:T(2,128)} %bitcast.326), channel_id=1, source_target_pairs={{0,1},{1,0},{2,3},{3,2},{4,5},{5,4},{6,7},{7,6},{8,9},{9,8},{10,11... | collective-permute-start | bytes 3145736 | tf_op jit(solution)/shard_map/ppermute | solution.py:119
  224.1 6.3 %copy-start.21 = (bf16[1,128,512]{1,2,0:T(8,128)(2,1)S(1)}, bf16[1,128,512]{1,2,0:T(8,128)(2,1)}, u32[]{:S(2)}) copy-start(bf16[1,128,512]{1,2,0:T(8,128)(2,1)} %copy.768) | copy-start | bytes 393220
  224.1 6.3 %copy-start.41 = (f32[128,8]{0,1:T(8,128)S(1)}, f32[128,8]{0,1:T(8,128)}, u32[]{:S(2)}) copy-start(f32[128,8]{0,1:T(8,128)} %copy-done.40) | copy-start | bytes 12292
  226.7 9.3 %copy-start.43 = (f32[8,8]{0,1:T(8,128)S(1)}, f32[8,8]{0,1:T(8,128)}, u32[]{:S(2)}) copy-start(f32[8,8]{0,1:T(8,128)} %multiply_reduce_fusion.6) | copy-start | bytes 772
  226.7 10.7 %copy-start.2 = (bf16[1024,8,64]{0,2,1:T(8,128)(2,1)S(1)}, bf16[1024,8,64]{0,2,1:T(8,128)(2,1)}, u32[]{:S(2)}) copy-start(bf16[1024,8,64]{0,2,1:T(8,128)(2,1)} %copy.776) | copy-start | bytes 3145732
  232.9 8.2 %copy-start.44 = (f32[8,128]{1,0:T(8,128)S(1)}, f32[8,128]{1,0:T(8,128)}, u32[]{:S(2)}) copy-start(f32[8,128]{1,0:T(8,128)} %get-tuple-element.19) | copy-start | bytes 12292
  232.9 8.2 %copy-start.48 = (f32[128,8]{0,1:T(8,128)S(1)}, f32[128,8]{0,1:T(8,128)}, u32[]{:S(2)}) copy-start(f32[128,8]{0,1:T(8,128)} %mul.660) | copy-start | bytes 12292
  232.9 8.2 %copy-start.15 = (bf16[128,512]{0,1:T(8,128)(2,1)S(1)}, bf16[128,512]{0,1:T(8,128)(2,1)}, u32[]{:S(2)}) copy-start(bf16[128,512]{0,1:T(8,128)(2,1)} %get-tuple-element.92) | copy-start | bytes 393220
  236.0 9.1 %copy-start.13 = (bf16[64,8,512]{2,1,0:T(8,128)(2,1)S(1)}, bf16[64,8,512]{2,1,0:T(8,128)(2,1)}, u32[]{:S(2)}) copy-start(bf16[64,8,512]{2,1,0:T(8,128)(2,1)} %get-tuple-element.23) | copy-start | bytes 1572868
  236.0 9.1 %copy-start.14 = (bf16[64,8,512]{2,1,0:T(8,128)(2,1)S(1)}, bf16[64,8,512]{2,1,0:T(8,128)(2,1)}, u32[]{:S(2)}) copy-start(bf16[64,8,512]{2,1,0:T(8,128)(2,1)} %get-tuple-element.28) | copy-start | bytes 1572868
  241.8 27.1 %collective-permute-start.8 = (bf16[128,640]{0,1:T(8,128)(2,1)}, bf16[128,640]{0,1:T(8,128)(2,1)}, u32[]{:S(2)}, u32[]{:S(2)}) collective-permute-start(bf16[128,640]{0,1:T(8,128)(2,1)} %fusion.74), channel_id=1, source_target_pairs={{0,4},{4,0},{8,12},{12,8},{16,20},{20,16},{24,28},{28,24},{32,36},... | collective-permute-start | bytes 491528 | tf_op jit(solution)/shard_map/ppermute | solution.py:16
  246.3 24.1 %copy-start.17 = (bf16[1,128,512]{1,2,0:T(8,128)(2,1)S(1)}, bf16[1,128,512]{1,2,0:T(8,128)(2,1)}, u32[]{:S(2)}) copy-start(bf16[1,128,512]{1,2,0:T(8,128)(2,1)} %copy-done.16) | copy-start | bytes 393220
  247.8 29.1 %copy-start.22 = (bf16[1,128,512]{1,2,0:T(8,128)(2,1)S(1)}, bf16[1,128,512]{1,2,0:T(8,128)(2,1)}, u32[]{:S(2)}) copy-start(bf16[1,128,512]{1,2,0:T(8,128)(2,1)} %copy.768) | copy-start | bytes 393220
  247.8 29.1 %copy-start.25 = (bf16[1,128,512]{1,2,0:T(8,128)(2,1)S(1)}, bf16[1,128,512]{1,2,0:T(8,128)(2,1)}, u32[]{:S(2)}) copy-start(bf16[1,128,512]{1,2,0:T(8,128)(2,1)} %copy.805) | copy-start | bytes 393220
  248.6 8.1 %collective-permute-start.10 = (bf16[2,2,8,640]{3,2,0,1:T(8,128)(2,1)S(1)}, bf16[2,2,8,640]{3,2,0,1:T(8,128)(2,1)S(1)}, u32[]{:S(2)}, u32[]{:S(2)}) collective-permute-start(bf16[2,2,8,640]{3,2,0,1:T(8,128)(2,1)S(1)} %pad_maximum_fusion.24), channel_id=1, source_target_pairs={{0,8},{4,12},{8,0},{12,4},{16,24},{20,28},{24,16},{28,20},{32,40},... | collective-permute-start | bytes 122888 | tf_op jit(solution)/shard_map/ppermute | solution.py:16
  257.5 7.8 %collective-permute-start.11 = (bf16[2,4,8,640]{3,2,0,1:T(8,128)(2,1)S(1)}, bf16[2,4,8,640]{3,2,0,1:T(8,128)(2,1)S(1)}, u32[]{:S(2)}, u32[]{:S(2)}) collective-permute-start(bf16[2,4,8,640]{3,2,0,1:T(8,128)(2,1)S(1)} %pad_maximum_fusion.22), channel_id=1, source_target_pairs={{0,64},{4,68},{8,72},{12,76},{16,80},{20,84},{24,88},{28,92},{32,9... | collective-permute-start | bytes 245768 | tf_op jit(solution)/shard_map/ppermute | solution.py:16
  266.1 7.2 %collective-permute-start.12 = (bf16[2,8,8,640]{3,2,0,1:T(8,128)(2,1)S(1)}, bf16[2,8,8,640]{3,2,0,1:T(8,128)(2,1)S(1)}, u32[]{:S(2)}, u32[]{:S(2)}) collective-permute-start(bf16[2,8,8,640]{3,2,0,1:T(8,128)(2,1)S(1)} %pad_maximum_fusion.20), channel_id=1, source_target_pairs={{0,4},{4,0},{8,12},{12,8},{16,20},{20,16},{24,28},{28,24},{32,36},... | collective-permute-start | bytes 491528 | tf_op jit(solution)/shard_map/ppermute | solution.py:16
  270.5 6.5 %copy-start.24 = (bf16[128,512]{0,1:T(8,128)(2,1)}, bf16[128,512]{0,1:T(8,128)(2,1)S(1)}, u32[]{:S(2)}) copy-start(bf16[128,512]{0,1:T(8,128)(2,1)S(1)} %slice.189) | copy-start | bytes 393220
  274.2 9.3 %collective-permute-start.13 = (bf16[2,16,8,640]{3,2,0,1:T(8,128)(2,1)}, bf16[2,16,8,640]{3,2,0,1:T(8,128)(2,1)}, u32[]{:S(2)}, u32[]{:S(2)}) collective-permute-start(bf16[2,16,8,640]{3,2,0,1:T(8,128)(2,1)} %get-tuple-element.53), channel_id=1, source_target_pairs={{0,32},{4,36},{8,40},{12,44},{16,48},{20,52},{24,56},{28,60},{32,0... | collective-permute-start | bytes 983048 | tf_op jit(solution)/shard_map/ppermute | solution.py:16
  278.4 11.6 %copy-start.7 = (f32[2,2,2,2,2,2,2,2,1,1024]{9,8,7,6,5,4,3,2,1,0:T(1,128)S(1)}, f32[2,2,2,2,2,2,2,2,1,1024]{9,8,7,6,5,4,3,2,1,0:T(1,128)}, u32[]{:S(2)}) copy-start(f32[2,2,2,2,2,2,2,2,1,1024]{9,8,7,6,5,4,3,2,1,0:T(1,128)} %get-tuple-element.26) | copy-start | bytes 3145732
  285.4 15.1 %collective-permute-start.14 = (bf16[2,32,8,640]{3,2,0,1:T(8,128)(2,1)}, bf16[2,32,8,640]{3,2,0,1:T(8,128)(2,1)}, u32[]{:S(2)}, u32[]{:S(2)}) collective-permute-start(bf16[2,32,8,640]{3,2,0,1:T(8,128)(2,1)} %get-tuple-element.42), channel_id=1, source_target_pairs={{0,128},{4,132},{8,136},{12,140},{16,144},{20,148},{24,152},{28,15... | collective-permute-start | bytes 1966088 | tf_op jit(solution)/shard_map/ppermute | solution.py:16
  290.0 10.6 %copy-start.10 = (bf16[2,64,8,640]{3,2,0,1:T(8,128)(2,1)S(1)}, bf16[2,64,8,640]{3,2,0,1:T(8,128)(2,1)}, u32[]{:S(2)}) copy-start(bf16[2,64,8,640]{3,2,0,1:T(8,128)(2,1)} %get-tuple-element.43) | copy-start | bytes 3932164
  292.1 9.8 %copy-start.8 = (f32[2,2,2,2,2,2,2,2,1024]{8,7,6,5,4,3,2,1,0:T(2,128)}, f32[2,2,2,2,2,2,2,2,1024]{8,7,6,5,4,3,2,1,0:T(2,128)S(1)}, u32[]{:S(2)}) copy-start(f32[2,2,2,2,2,2,2,2,1024]{8,7,6,5,4,3,2,1,0:T(2,128)S(1)} %bitcast_add_fusion) | copy-start | bytes 3145732
  293.0 19.7 %collective-permute-start.17 = (f32[2,2,2,2,2,2,2,1024]{7,6,5,4,3,2,1,0:T(2,128)}, f32[2,2,2,2,2,2,2,1024]{7,6,5,4,3,2,1,0:T(2,128)}, u32[]{:S(2)}, u32[]{:S(2)}) collective-permute-start(f32[2,2,2,2,2,2,2,1024]{7,6,5,4,3,2,1,0:T(2,128)} %dynamic-slice_bitcast_fusion), channel_id=1, source_target_pairs={{0,4},{1,5},{2,6},{3,7},{4,0},{5,1},{6,2},{7,3},{8,12},{9,13},{10,... | collective-permute-start | bytes 1572872 | tf_op jit(solution)/shard_map/ppermute | solution.py:119
  305.0 5.5 %copy-start.32 = (bf16[16,8,64]{2,1,0:T(8,128)(2,1)S(1)}, bf16[16,8,64]{2,1,0:T(8,128)(2,1)}, u32[]{:S(2)}) copy-start(bf16[16,8,64]{2,1,0:T(8,128)(2,1)} %reshape_reshape_squeeze_stack.11) | copy-start | bytes 49156
  306.9 5.8 %copy-start.9 = (f32[2,2,2,2,2,2,2,2,1024]{8,7,6,5,4,3,2,1,0:T(2,128)S(1)}, f32[2,2,2,2,2,2,2,2,1024]{8,7,6,5,4,3,2,1,0:T(2,128)}, u32[]{:S(2)}) copy-start(f32[2,2,2,2,2,2,2,2,1024]{8,7,6,5,4,3,2,1,0:T(2,128)} %copy-done.8) | copy-start | bytes 3145732
  306.9 11.5 %copy-start.29 = (bf16[16,8,64]{2,1,0:T(8,128)(2,1)S(1)}, bf16[16,8,64]{2,1,0:T(8,128)(2,1)}, u32[]{:S(2)}) copy-start(bf16[16,8,64]{2,1,0:T(8,128)(2,1)} %reshape_reshape_squeeze_stack.12) | copy-start | bytes 49156
  307.0 22.4 %collective-permute-start.15 = (bf16[64,8,640]{2,1,0:T(8,128)(2,1)}, bf16[64,8,640]{2,1,0:T(8,128)(2,1)}, u32[]{:S(2)}, u32[]{:S(2)}) collective-permute-start(bf16[64,8,640]{2,1,0:T(8,128)(2,1)} %slice_bitcast_fusion), channel_id=1, source_target_pairs={{0,256},{4,260},{8,264},{12,268},{16,272},{20,276},{24,280},{28,28... | collective-permute-start | bytes 1966088 | tf_op jit(solution)/shard_map/ppermute | solution.py:16
  315.7 9.8 %collective-permute-start.18 = (f32[2,2,2,2,2,2,1024]{6,5,4,3,2,1,0:T(2,128)}, f32[2,2,2,2,2,2,1024]{6,5,4,3,2,1,0:T(2,128)}, u32[]{:S(2)}, u32[]{:S(2)}) collective-permute-start(f32[2,2,2,2,2,2,1024]{6,5,4,3,2,1,0:T(2,128)} %dynamic-slice_bitcast_fusion.1), channel_id=1, source_target_pairs={{0,32},{1,33},{2,34},{3,35},{4,36},{5,37},{6,38},{7,39},{8,40},{9,... | collective-permute-start | bytes 786440 | tf_op jit(solution)/shard_map/ppermute | solution.py:119
  324.6 4.8 %copy-start.11 = (bf16[64,8,640]{2,1,0:T(8,128)(2,1)S(1)}, bf16[64,8,640]{2,1,0:T(8,128)(2,1)}, u32[]{:S(2)}) copy-start(bf16[64,8,640]{2,1,0:T(8,128)(2,1)} %slice_bitcast_fusion) | copy-start | bytes 1966084
  326.7 6.9 %collective-permute-start.19 = (f32[2,2,2,2,2,1024]{5,4,3,2,1,0:T(2,128)S(1)}, f32[2,2,2,2,2,1024]{5,4,3,2,1,0:T(2,128)S(1)}, u32[]{:S(2)}, u32[]{:S(2)}) collective-permute-start(f32[2,2,2,2,2,1024]{5,4,3,2,1,0:T(2,128)S(1)} %dynamic-slice_bitcast_fusion.2), channel_id=1, source_target_pairs={{0,128},{1,129},{2,130},{3,131},{4,132},{5,133},{6,134},{7,135},{8... | collective-permute-start | bytes 393224 | tf_op jit(solution)/shard_map/ppermute | solution.py:119
  332.2 7.3 %copy-start.42 = (bf16[8,8,64]{2,1,0:T(8,128)(2,1)S(1)}, bf16[8,8,64]{2,1,0:T(8,128)(2,1)}, u32[]{:S(2)}) copy-start(bf16[8,8,64]{2,1,0:T(8,128)(2,1)} %reshape_squeeze.30) | copy-start | bytes 24580
  333.7 8.8 %collective-permute-start.20 = (f32[2,2,2,2,1024]{4,3,2,1,0:T(2,128)S(1)}, f32[2,2,2,2,1024]{4,3,2,1,0:T(2,128)S(1)}, u32[]{:S(2)}, u32[]{:S(2)}) collective-permute-start(f32[2,2,2,2,1024]{4,3,2,1,0:T(2,128)S(1)} %dynamic-slice_bitcast_fusion.3), channel_id=1, source_target_pairs={{0,8},{1,9},{2,10},{3,11},{4,12},{5,13},{6,14},{7,15},{8,0},{9,1},... | collective-permute-start | bytes 196616 | tf_op jit(solution)/shard_map/ppermute | solution.py:119
  343.1 7.6 %collective-permute-start.21 = (f32[2,2,2,1024]{3,2,1,0:T(2,128)}, f32[2,2,2,1024]{3,2,1,0:T(2,128)}, u32[]{:S(2)}, u32[]{:S(2)}) collective-permute-start(f32[2,2,2,1024]{3,2,1,0:T(2,128)} %dynamic-slice_bitcast_fusion.4), channel_id=1, source_target_pairs={{0,64},{1,65},{2,66},{3,67},{4,68},{5,69},{6,70},{7,71},{8,72},{9,... | collective-permute-start | bytes 98312 | tf_op jit(solution)/shard_map/ppermute | solution.py:119
  346.2 8.5 %copy-start.36 = (bf16[8,8,64]{2,1,0:T(8,128)(2,1)S(1)}, bf16[8,8,64]{2,1,0:T(8,128)(2,1)}, u32[]{:S(2)}) copy-start(bf16[8,8,64]{2,1,0:T(8,128)(2,1)} %reshape_squeeze.31) | copy-start | bytes 24580
  352.1 7.4 %collective-permute-start.22 = (f32[2,2,1024]{2,1,0:T(2,128)}, f32[2,2,1024]{2,1,0:T(2,128)}, u32[]{:S(2)}, u32[]{:S(2)}) collective-permute-start(f32[2,2,1024]{2,1,0:T(2,128)} %dynamic-slice_bitcast_fusion.5), channel_id=1, source_target_pairs={{0,256},{1,257},{2,258},{3,259},{4,260},{5,261},{6,262},{7,263},{8... | collective-permute-start | bytes 49160 | tf_op jit(solution)/shard_map/ppermute | solution.py:119
  354.7 4.9 %copy-start.31 = (f32[2,2,2,1024]{3,2,1,0:T(2,128)S(1)}, f32[2,2,2,1024]{3,2,1,0:T(2,128)}, u32[]{:S(2)}) copy-start(f32[2,2,2,1024]{3,2,1,0:T(2,128)} %copy-done.30) | copy-start | bytes 98308
  360.3 9.5 %collective-permute-start.23 = (f32[2,1024]{1,0:T(2,128)S(1)}, f32[2,1024]{1,0:T(2,128)S(1)}, u32[]{:S(2)}, u32[]{:S(2)}) collective-permute-start(f32[2,1024]{1,0:T(2,128)S(1)} %dynamic-slice_bitcast_fusion.6), channel_id=1, source_target_pairs={{0,16},{1,17},{2,18},{3,19},{4,20},{5,21},{6,22},{7,23},{8,24},{9,... | collective-permute-start | bytes 24584 | tf_op jit(solution)/shard_map/ppermute | solution.py:119
  362.9 21.8 %copy-start.1 = (bf16[512,1024]{1,0:T(8,128)(2,1)S(1)}, bf16[512,1024]{1,0:T(8,128)(2,1)}, u32[]{:S(2)}) copy-start(bf16[512,1024]{1,0:T(8,128)(2,1)} %param.33) | copy-start | bytes 3145732
  369.8 14.2 %collective-permute-start.24 = (f32[1024]{0:T(1024)S(1)}, f32[1024]{0:T(1024)S(1)}, u32[]{:S(2)}, u32[]{:S(2)}) collective-permute-start(f32[1024]{0:T(1024)S(1)} %bitcast.404), channel_id=1, source_target_pairs={{0,2},{1,3},{2,0},{3,1},{4,6},{5,7},{6,4},{7,5},{8,10},{9,11},{10,... | collective-permute-start | bytes 12296 | tf_op jit(solution)/shard_map/ppermute | solution.py:119
  (11 other events, 23.4 us)

commit v2 on v1

--- a/solution.py
+++ b/solution.py
@@ -104,20 +104,25 @@
     return jnp.pad(matrix, [(0, 0)] * (matrix.ndim - 1) + [(0, width - matrix.shape[-1])])
 
 
-def scatter_sum(matrix, axes, bit_order):
+def scatter_sum(matrix, axes, bit_groups):
     index = lax.axis_index(axes)
-    bit_count = len(bit_order)
+    bit_count = sum(len(group) for group in bit_groups)
     size = 1 << bit_count
     block = matrix.reshape((2,) * bit_count + matrix.shape[1:])
     dims = [bit_count - 1 - j for j in range(bit_count)]
-    for bit_pos in bit_order:
-        axis_pos = dims.index(bit_pos)
-        my_bit = index // (1 << bit_pos) % 2
-        keep = lax.dynamic_index_in_dim(block, my_bit, axis_pos, keepdims=False)
-        send = lax.dynamic_index_in_dim(block, 1 - my_bit, axis_pos, keepdims=False)
-        pairs = [(source, source ^ (1 << bit_pos)) for source in range(size)]
-        block = keep + lax.ppermute(send, axes, pairs)
-        dims.pop(axis_pos)
+    for group in bit_groups:
+        low, width = min(group), len(group)
+        axis_pos = dims.index(low + width - 1)
+        shape = block.shape
+        block = block.reshape(shape[:axis_pos] + (1 << width,) + shape[axis_pos + width :])
+        mine = index // (1 << low) % (1 << width)
+        total = lax.dynamic_index_in_dim(block, mine, axis_pos, keepdims=False)
+        for flip in range(1, 1 << width):
+            send = lax.dynamic_index_in_dim(block, mine ^ flip, axis_pos, keepdims=False)
+            pairs = [(source, source ^ (flip << low)) for source in range(size)]
+            total = total + lax.ppermute(send, axes, pairs)
+        block = total
+        del dims[axis_pos : axis_pos + width]
     return block.reshape((1,) + matrix.shape[1:])
 
 
@@ -257,7 +262,7 @@
     proj_part = lax.dot_general(
         attn, upstream, (((0,), (0,)), ((), ())), preferred_element_type=jnp.float32
     )
-    order = (0, 2, 5, 7, 3, 6, 8, 4, 1)
+    order = ((0,), (2,), (5, 6), (7, 8), (3,), (4,), (1,))
     grad_proj = scatter_sum(proj_part, ("tm", "batch"), order)
 
     grad_three = grad_attn.astype(jnp.float32).reshape(row_count, HEADS, HD)

time: 389 us -> 390 us (level)
  starting transfers between devices: 93.6 us -> 102 us
    ppermute x9 -> x11, starting transfers between devices: 25.9 us -> 33.8 us  [scatter_sum(): total = total + lax.ppermute(send, axes, pairs)]
    ppermute x9 -> x11, waiting for transfers between devices: 26.9 us -> 23.5 us  [scatter_sum(): total = total + lax.ppermute(send, axes, pairs)]
    unnamed x114 -> x118, local copies, waits for them, and re-layouts: 15 us -> 16 us
  transfers between devices with their start and end apart: 25 -> 27, of which waited for: 17 -> 17; matrix products, arithmetic and copies ran while one was open for 33% -> 30% of each run, Pallas kernels for 0% -> 0%
where the time goes in v2:
time: 390 us; the launch traced here: 384 us
  local copies, waits for them, and re-layouts  131 us (34%)
  starting transfers between devices  102 us (26%)
  waiting for transfers between devices  90.6 us (23%)
  other arithmetic  32.6 us (8%)
  matrix products  26.4 us (7%)
    ppermute x16, starting transfers between devices, partner(): return lax.ppermute(value, axis, pairs)  67.7 us
    ppermute x16, waiting for transfers between devices, partner(): return lax.ppermute(value, axis, pairs)  67.1 us
    another operation x18, local copies, waits for them, and re-layouts, heads_view(): return matrix.reshape(matrix.shape[0], HEADS, HD)  35.3 us
    ppermute x11, starting transfers between devices, scatter_sum(): total = total + lax.ppermute(send, axes, pairs)  33.8 us
    ppermute x11, waiting for transfers between devices, scatter_sum(): total = total + lax.ppermute(send, axes, pairs)  23.5 us
    mul x26, local copies, waits for them, and re-layouts, spread_rows(): values[:, None] * chooser  16.2 us
    unnamed x118, local copies, waits for them, and re-layouts  16 us
  transfers between devices with their start and end apart: 27, of which 17 were waited for; matrix products, arithmetic and copies ran while one was open for 30% of the time, Pallas kernels for 0%

profile of v2, /device:TPU:6, one launch (start us, length us, event | category | flops | bytes accessed | tf_op | source)
XLA Modules:
  0.0 383.6 jit_solution(9886863270165527661)
XLA Ops:
  5.1 9.1 %collective-permute-start.1 = (bf16[3,2,1,8,512]{4,3,1,0,2:T(8,128)(2,1)S(1)}, bf16[3,2,1,8,512]{4,3,1,0,2:T(8,128)(2,1)S(1)}, u32[]{:S(2)}, u32[]{:S(2)}) collective-permute-start(bf16[3,2,1,8,512]{4,3,1,0,2:T(8,128)(2,1)S(1)} %bitcast.369), channel_id=1, source_target_pairs={{0,16},{4,20},{8,24},{12,28},{16,0},{20,4},{24,8},{28,12},{32,48},... | collective-permute-start | bytes 147464 | tf_op jit(solution)/shard_map/ppermute | solution.py:16
  14.2 2.1 collective-permute-done.1
  16.3 5.3 %collective-permute-start.2 = (bf16[3,2,2,8,512]{4,3,1,0,2:T(8,128)(2,1)S(1)}, bf16[3,2,2,8,512]{4,3,1,0,2:T(8,128)(2,1)S(1)}, u32[]{:S(2)}, u32[]{:S(2)}) collective-permute-start(bf16[3,2,2,8,512]{4,3,1,0,2:T(8,128)(2,1)S(1)} %pad_maximum_fusion.21), channel_id=1, source_target_pairs={{0,8},{4,12},{8,0},{12,4},{16,24},{20,28},{24,16},{28,20},{32,40},... | collective-permute-start | bytes 294920 | tf_op jit(solution)/shard_map/ppermute | solution.py:16
  21.6 5.0 %collective-permute-done.2 = bf16[3,2,2,8,512]{4,3,1,0,2:T(8,128)(2,1)S(1)} collective-permute-done((bf16[3,2,2,8,512]{4,3,1,0,2:T(8,128)(2,1)S(1)}, bf16[3,2,2,8,512]{4,3,1,0,2:T(8,128)(2,1)S(1)}, u32[]{:S(2)}, u32[]{:S(2)}) %collective-permute-start.2) | collective-permute-done | bytes 98336 | tf_op jit(solution)/shard_map/ppermute | solution.py:16
  26.7 3.3 collective-permute-start.3
  30.0 5.7 %collective-permute-done.3 = bf16[3,2,4,8,512]{4,3,1,0,2:T(8,128)(2,1)S(1)} collective-permute-done((bf16[3,2,4,8,512]{4,3,1,0,2:T(8,128)(2,1)S(1)}, bf16[3,2,4,8,512]{4,3,1,0,2:T(8,128)(2,1)S(1)}, u32[]{:S(2)}, u32[]{:S(2)}) %collective-permute-start.3) | collective-permute-done | bytes 196640 | tf_op jit(solution)/shard_map/ppermute | solution.py:16
  35.8 3.8 collective-permute-start.4
  42.5 5.6 %collective-permute-done.4 = bf16[3,2,8,8,512]{4,3,1,0,2:T(8,128)(2,1)S(1)} collective-permute-done((bf16[3,2,8,8,512]{4,3,1,0,2:T(8,128)(2,1)S(1)}, bf16[3,2,8,8,512]{4,3,1,0,2:T(8,128)(2,1)S(1)}, u32[]{:S(2)}, u32[]{:S(2)}) %collective-permute-start.4) | collective-permute-done | bytes 393248 | tf_op jit(solution)/shard_map/ppermute | solution.py:16
  49.1 2.7 collective-permute-start.5
  51.8 17.0 %collective-permute-done.5 = bf16[3,2,16,8,512]{4,3,1,0,2:T(8,128)(2,1)S(1)} collective-permute-done((bf16[3,2,16,8,512]{4,3,1,0,2:T(8,128)(2,1)S(1)}, bf16[3,2,16,8,512]{4,3,1,0,2:T(8,128)(2,1)S(1)}, u32[]{:S(2)}, u32[]{:S(2)}) %collective-permute-start.5) | collective-permute-done | bytes 786464 | tf_op jit(solution)/shard_map/ppermute | solution.py:16
  70.2 3.5 collective-permute-start.6
  73.7 3.5 collective-permute-start
  88.3 17.8 %collective-permute-done.6 = bf16[3,2,32,8,512]{4,3,1,0,2:T(8,128)(2,1)} collective-permute-done((bf16[3,2,32,8,512]{4,3,1,0,2:T(8,128)(2,1)}, bf16[3,2,32,8,512]{4,3,1,0,2:T(8,128)(2,1)}, u32[]{:S(2)}, u32[]{:S(2)}) %collective-permute-start.6) | collective-permute-done | bytes 1572896 | tf_op jit(solution)/shard_map/ppermute | solution.py:16
  106.1 2.7 constant_dynamic-update-slice_fusion.11
  108.8 2.8 copy_bitcast_fusion
  111.6 5.3 %collective-permute-start.7 = (bf16[3,64,8,512]{3,2,1,0:T(8,128)(2,1)}, bf16[3,64,8,512]{3,2,1,0:T(8,128)(2,1)}, u32[]{:S(2)}, u32[]{:S(2)}) collective-permute-start(bf16[3,64,8,512]{3,2,1,0:T(8,128)(2,1)} %copy_bitcast_fusion), channel_id=1, source_target_pairs={{0,256},{4,260},{8,264},{12,268},{16,272},{20,276},{24,280},{28,28... | collective-permute-start | bytes 4718600 | tf_op jit(solution)/shard_map/ppermute | solution.py:16
  116.9 3.5 fusion.138
  120.5 2.1 reshape_reshape_squeeze.6
  122.6 2.5 copy.761
  125.1 2.7 copy.771
  127.8 3.9 %reshape_reshape_squeeze.14 = bf16[1024,8,64]{2,1,0:T(8,128)(2,1)} reshape(bf16[1,2,64,8,512]{4,3,2,1,0:T(8,128)(2,1)} %copy.771) | data formatting | bytes 2097152 | tf_op jit(solution)/shard_map/reshape;reshape;squeeze | solution.py:130
  131.7 3.3 copy.772
  141.7 2.1 reshape_reshape_squeeze.15
  143.8 3.3 copy.818
  147.1 2.3 slice_bitcast_fusion.2
  149.4 2.3 slice_bitcast_fusion.1
  152.8 2.1 reshape_reshape.28
  154.9 2.5 copy.767
  161.5 3.9 %reshape_reshape.29 = bf16[1024,8,64]{2,1,0:T(8,128)(2,1)} reshape(bf16[128,8,512]{2,1,0:T(8,128)(2,1)} %get-tuple-element.108) | data formatting | bytes 2097152 | tf_op jit(solution)/shard_map/reshape;reshape | solution.py:130
  165.4 3.4 copy.776
  173.3 2.0 copy.781
  178.6 2.9 fusion.65
  201.1 8.6 %collective-permute-start.9 = (bf16[2,1,8,640]{3,2,0,1:T(8,128)(2,1)}, bf16[2,1,8,640]{3,2,0,1:T(8,128)(2,1)}, u32[]{:S(2)}, u32[]{:S(2)}) collective-permute-start(bf16[2,1,8,640]{3,2,0,1:T(8,128)(2,1)} %get-tuple-element.12), channel_id=1, source_target_pairs={{0,16},{4,20},{8,24},{12,28},{16,0},{20,4},{24,8},{28,12},{32,48},... | collective-permute-start | bytes 61448 | tf_op jit(solution)/shard_map/ppermute | solution.py:16
  216.5 3.2 constant_dynamic-slice_fusion.3
  224.1 2.6 fusion.29
  230.3 2.4 fusion.17
  237.3 2.0 fusion.35
  241.7 3.4 collective-permute-start.8
  248.6 5.3 %collective-permute-start.10 = (bf16[2,2,8,640]{3,2,0,1:T(8,128)(2,1)S(1)}, bf16[2,2,8,640]{3,2,0,1:T(8,128)(2,1)S(1)}, u32[]{:S(2)}, u32[]{:S(2)}) collective-permute-start(bf16[2,2,8,640]{3,2,0,1:T(8,128)(2,1)S(1)} %pad_maximum_fusion.24), channel_id=1, source_target_pairs={{0,8},{4,12},{8,0},{12,4},{16,24},{20,28},{24,16},{28,20},{32,40},... | collective-permute-start | bytes 122888 | tf_op jit(solution)/shard_map/ppermute | solution.py:16
  257.4 3.3 collective-permute-start.11
  261.4 3.9 %collective-permute-done.11 = bf16[2,4,8,640]{3,2,0,1:T(8,128)(2,1)S(1)} collective-permute-done((bf16[2,4,8,640]{3,2,0,1:T(8,128)(2,1)S(1)}, bf16[2,4,8,640]{3,2,0,1:T(8,128)(2,1)S(1)}, u32[]{:S(2)}, u32[]{:S(2)}) %collective-permute-start.11) | collective-permute-done | bytes 81952 | tf_op jit(solution)/shard_map/ppermute | solution.py:16
  266.0 2.0 collective-permute-start.12
  274.1 2.7 collective-permute-start.13
  280.2 3.2 collective-permute-done.13
  285.3 2.6 collective-permute-start.14
  289.9 2.1 bitcast_add_fusion
  293.0 3.4 collective-permute-start.17
  296.4 4.0 %collective-permute-done.14 = bf16[2,32,8,640]{3,2,0,1:T(8,128)(2,1)} collective-permute-done((bf16[2,32,8,640]{3,2,0,1:T(8,128)(2,1)}, bf16[2,32,8,640]{3,2,0,1:T(8,128)(2,1)}, u32[]{:S(2)}, u32[]{:S(2)}) %collective-permute-start.14) | collective-permute-done | bytes 655392 | tf_op jit(solution)/shard_map/ppermute | solution.py:16
  306.8 2.1 slice_bitcast_fusion
  309.0 3.4 collective-permute-start.15
  314.0 2.7 collective-permute-start.18
  316.7 3.0 collective-permute-start.19
  319.8 4.7 %collective-permute-start.20 = (f32[2,2,2,2,2,1024]{5,4,3,2,1,0:T(2,128)S(1)}, f32[2,2,2,2,2,1024]{5,4,3,2,1,0:T(2,128)S(1)}, u32[]{:S(2)}, u32[]{:S(2)}) collective-permute-start(f32[2,2,2,2,2,1024]{5,4,3,2,1,0:T(2,128)S(1)} %get-tuple-element.34), channel_id=1, source_target_pairs={{0,96},{1,97},{2,98},{3,99},{4,100},{5,101},{6,102},{7,103},{8,104... | collective-permute-start | bytes 393224 | tf_op jit(solution)/shard_map/ppermute | solution.py:123
  325.1 2.7 collective-permute-done.20
  328.0 2.6 collective-permute-start.21
  330.6 4.8 %collective-permute-start.22 = (f32[2,2,2,1024]{3,2,1,0:T(2,128)S(1)}, f32[2,2,2,1024]{3,2,1,0:T(2,128)S(1)}, u32[]{:S(2)}, u32[]{:S(2)}) collective-permute-start(f32[2,2,2,1024]{3,2,1,0:T(2,128)S(1)} %get-tuple-element.59), channel_id=1, source_target_pairs={{0,256},{1,257},{2,258},{3,259},{4,260},{5,261},{6,262},{7,263},{8... | collective-permute-start | bytes 98312 | tf_op jit(solution)/shard_map/ppermute | solution.py:123
  335.4 3.1 collective-permute-start.23
  339.5 2.8 collective-permute-done.23
  342.4 3.8 collective-permute-start.24
  346.2 2.7 collective-permute-done.24
  352.8 5.6 %collective-permute-done.25 = f32[2,1024]{1,0:T(2,128)S(1)} collective-permute-done((f32[2,1024]{1,0:T(2,128)S(1)}, f32[2,1024]{1,0:T(2,128)S(1)}, u32[]{:S(2)}, u32[]{:S(2)}) %collective-permute-start.25) | collective-permute-done | bytes 8224 | tf_op jit(solution)/shard_map/ppermute | solution.py:123
  363.8 8.9 %collective-permute-done.26 = f32[1024]{0:T(1024)S(1)} collective-permute-done((f32[1024]{0:T(1024)S(1)}, f32[1024]{0:T(1024)S(1)}, u32[]{:S(2)}, u32[]{:S(2)}) %collective-permute-start.26) | collective-permute-done | bytes 4128 | tf_op jit(solution)/shard_map/ppermute | solution.py:123
  376.9 1.9 copy.825
  381.4 2.2 add_convert_fusion
  (312 shorter events, 130.0 us)
Async XLA Ops:
  0.6 3.7 copy-start.51
  0.7 3.3 copy-start.17
  5.1 11.2 %collective-permute-start.1 = (bf16[3,2,1,8,512]{4,3,1,0,2:T(8,128)(2,1)S(1)}, bf16[3,2,1,8,512]{4,3,1,0,2:T(8,128)(2,1)S(1)}, u32[]{:S(2)}, u32[]{:S(2)}) collective-permute-start(bf16[3,2,1,8,512]{4,3,1,0,2:T(8,128)(2,1)S(1)} %bitcast.369), channel_id=1, source_target_pairs={{0,16},{4,20},{8,24},{12,28},{16,0},{20,4},{24,8},{28,12},{32,48},... | collective-permute-start | bytes 147464 | tf_op jit(solution)/shard_map/ppermute | solution.py:16
  16.3 10.4 %collective-permute-start.2 = (bf16[3,2,2,8,512]{4,3,1,0,2:T(8,128)(2,1)S(1)}, bf16[3,2,2,8,512]{4,3,1,0,2:T(8,128)(2,1)S(1)}, u32[]{:S(2)}, u32[]{:S(2)}) collective-permute-start(bf16[3,2,2,8,512]{4,3,1,0,2:T(8,128)(2,1)S(1)} %pad_maximum_fusion.21), channel_id=1, source_target_pairs={{0,8},{4,12},{8,0},{12,4},{16,24},{20,28},{24,16},{28,20},{32,40},... | collective-permute-start | bytes 294920 | tf_op jit(solution)/shard_map/ppermute | solution.py:16
  26.7 9.1 %collective-permute-start.3 = (bf16[3,2,4,8,512]{4,3,1,0,2:T(8,128)(2,1)S(1)}, bf16[3,2,4,8,512]{4,3,1,0,2:T(8,128)(2,1)S(1)}, u32[]{:S(2)}, u32[]{:S(2)}) collective-permute-start(bf16[3,2,4,8,512]{4,3,1,0,2:T(8,128)(2,1)S(1)} %pad_maximum_fusion.9), channel_id=1, source_target_pairs={{0,64},{4,68},{8,72},{12,76},{16,80},{20,84},{24,88},{28,92},{32,9... | collective-permute-start | bytes 589832 | tf_op jit(solution)/shard_map/ppermute | solution.py:16
  35.8 12.2 %collective-permute-start.4 = (bf16[3,2,8,8,512]{4,3,1,0,2:T(8,128)(2,1)S(1)}, bf16[3,2,8,8,512]{4,3,1,0,2:T(8,128)(2,1)S(1)}, u32[]{:S(2)}, u32[]{:S(2)}) collective-permute-start(bf16[3,2,8,8,512]{4,3,1,0,2:T(8,128)(2,1)S(1)} %pad_maximum_fusion.4), channel_id=1, source_target_pairs={{0,4},{4,0},{8,12},{12,8},{16,20},{20,16},{24,28},{28,24},{32,36},... | collective-permute-start | bytes 1179656 | tf_op jit(solution)/shard_map/ppermute | solution.py:16
  49.1 19.7 %collective-permute-start.5 = (bf16[3,2,16,8,512]{4,3,1,0,2:T(8,128)(2,1)S(1)}, bf16[3,2,16,8,512]{4,3,1,0,2:T(8,128)(2,1)S(1)}, u32[]{:S(2)}, u32[]{:S(2)}) collective-permute-start(bf16[3,2,16,8,512]{4,3,1,0,2:T(8,128)(2,1)S(1)} %get-tuple-element.44), channel_id=1, source_target_pairs={{0,32},{4,36},{8,40},{12,44},{16,48},{20,52},{24,56},{28,60},{32,0... | collective-permute-start | bytes 2359304 | tf_op jit(solution)/shard_map/ppermute | solution.py:16
  68.8 10.3 %copy-start.49 = (f32[8,8]{0,1:T(8,128)S(1)}, f32[8,8]{0,1:T(8,128)}, u32[]{:S(2)}) copy-start(f32[8,8]{0,1:T(8,128)} %constant.210.clone) | copy-start | bytes 772
  68.8 10.4 %copy-start.48 = (f32[16,8]{0,1:T(8,128)S(1)}, f32[16,8]{0,1:T(8,128)}, u32[]{:S(2)}) copy-start(f32[16,8]{0,1:T(8,128)} %constant.211.clone) | copy-start | bytes 1540
  70.2 36.0 %collective-permute-start.6 = (bf16[3,2,32,8,512]{4,3,1,0,2:T(8,128)(2,1)}, bf16[3,2,32,8,512]{4,3,1,0,2:T(8,128)(2,1)}, u32[]{:S(2)}, u32[]{:S(2)}) collective-permute-start(bf16[3,2,32,8,512]{4,3,1,0,2:T(8,128)(2,1)} %get-tuple-element.31), channel_id=1, source_target_pairs={{0,128},{4,132},{8,136},{12,140},{16,144},{20,148},{24,152},{28,15... | collective-permute-start | bytes 4718600 | tf_op jit(solution)/shard_map/ppermute | solution.py:16
  73.7 11.7 %collective-permute-start = (bf16[3,128,512]{2,1,0:T(8,128)(2,1)S(1)}, bf16[3,128,512]{2,1,0:T(8,128)(2,1)S(1)}, u32[]{:S(2)}, u32[]{:S(2)}) collective-permute-start(bf16[3,128,512]{2,1,0:T(8,128)(2,1)S(1)} %pad_maximum_fusion.3), channel_id=1, source_target_pairs={{0,4},{4,0},{8,12},{12,8},{16,20},{20,16},{24,28},{28,24},{32,36},... | collective-permute-start | bytes 1179656 | tf_op jit(solution)/shard_map/ppermute | solution.py:16
  77.3 9.8 %copy-start.22 = (bf16[1,128,512]{1,2,0:T(8,128)(2,1)}, bf16[1,128,512]{1,2,0:T(8,128)(2,1)S(1)}, u32[]{:S(2)}) copy-start(bf16[1,128,512]{1,2,0:T(8,128)(2,1)S(1)} %copy.754) | copy-start | bytes 393220
  77.5 9.7 %copy-start.15 = (bf16[1,128,512]{1,2,0:T(8,128)(2,1)}, bf16[1,128,512]{1,2,0:T(8,128)(2,1)S(1)}, u32[]{:S(2)}) copy-start(bf16[1,128,512]{1,2,0:T(8,128)(2,1)S(1)} %copy.756) | copy-start | bytes 393220
  79.3 99.3 %copy-start.39 = (f32[128,8]{0,1:T(8,128)}, f32[128,8]{0,1:T(8,128)S(1)}, u32[]{:S(2)}) copy-start(f32[128,8]{0,1:T(8,128)S(1)} %mul.646) | copy-start | bytes 12292
  79.4 8.1 %copy-start.35 = (bf16[2,8,512]{2,1,0:T(8,128)(2,1)}, bf16[2,8,512]{2,1,0:T(8,128)(2,1)S(1)}, u32[]{:S(2)}) copy-start(bf16[2,8,512]{2,1,0:T(8,128)(2,1)S(1)} %get-tuple-element.81) | copy-start | bytes 49156
  85.6 23.2 %copy-start.30 = (bf16[1,128,512]{1,2,0:T(8,128)(2,1)}, bf16[1,128,512]{1,2,0:T(8,128)(2,1)S(1)}, u32[]{:S(2)}) copy-start(bf16[1,128,512]{1,2,0:T(8,128)(2,1)S(1)} %copy.755) | copy-start | bytes 393220
  87.5 21.3 %copy-start.47 = (f32[8,128]{1,0:T(8,128)}, f32[8,128]{1,0:T(8,128)S(1)}, u32[]{:S(2)}) copy-start(f32[8,128]{1,0:T(8,128)S(1)} %get-tuple-element.104) | copy-start | bytes 12292
  111.6 37.8 %collective-permute-start.7 = (bf16[3,64,8,512]{3,2,1,0:T(8,128)(2,1)}, bf16[3,64,8,512]{3,2,1,0:T(8,128)(2,1)}, u32[]{:S(2)}, u32[]{:S(2)}) collective-permute-start(bf16[3,64,8,512]{3,2,1,0:T(8,128)(2,1)} %copy_bitcast_fusion), channel_id=1, source_target_pairs={{0,256},{4,260},{8,264},{12,268},{16,272},{20,276},{24,280},{28,28... | collective-permute-start | bytes 4718600 | tf_op jit(solution)/shard_map/ppermute | solution.py:16
  125.1 10.0 %copy-start.4 = (bf16[1024,8,64]{0,2,1:T(8,128)(2,1)}, bf16[1024,8,64]{0,2,1:T(8,128)(2,1)S(1)}, u32[]{:S(2)}) copy-start(bf16[1024,8,64]{0,2,1:T(8,128)(2,1)S(1)} %copy.761) | copy-start | bytes 3145732
  136.3 4.1 %copy-start.40 = (f32[8,16]{1,0:T(8,128)}, f32[8,16]{1,0:T(8,128)S(1)}, u32[]{:S(2)}) copy-start(f32[8,16]{1,0:T(8,128)S(1)} %log_add_fusion.1) | copy-start | bytes 1540
  176.5 11.8 %copy-start.42 = (f32[128,8]{0,1:T(8,128)}, f32[128,8]{0,1:T(8,128)S(1)}, u32[]{:S(2)}) copy-start(f32[128,8]{0,1:T(8,128)S(1)} %get-tuple-element.15) | copy-start | bytes 12292
  201.1 46.6 %collective-permute-start.9 = (bf16[2,1,8,640]{3,2,0,1:T(8,128)(2,1)}, bf16[2,1,8,640]{3,2,0,1:T(8,128)(2,1)}, u32[]{:S(2)}, u32[]{:S(2)}) collective-permute-start(bf16[2,1,8,640]{3,2,0,1:T(8,128)(2,1)} %get-tuple-element.12), channel_id=1, source_target_pairs={{0,16},{4,20},{8,24},{12,28},{16,0},{20,4},{24,8},{28,12},{32,48},... | collective-permute-start | bytes 61448 | tf_op jit(solution)/shard_map/ppermute | solution.py:16
  219.7 3.6 copy-start.37
  219.7 3.6 copy-start.31
  219.7 4.3 %copy-start.5 = (bf16[1024,8,64]{0,2,1:T(8,128)(2,1)S(1)}, bf16[1024,8,64]{0,2,1:T(8,128)(2,1)}, u32[]{:S(2)}) copy-start(bf16[1024,8,64]{0,2,1:T(8,128)(2,1)} %copy-done.4) | copy-start | bytes 3145732
  219.7 4.3 %copy-start.41 = (f32[8,16]{1,0:T(8,128)S(1)}, f32[8,16]{1,0:T(8,128)}, u32[]{:S(2)}) copy-start(f32[8,16]{1,0:T(8,128)} %copy-done.40) | copy-start | bytes 1540
  221.3 68.6 %collective-permute-start.16 = (f32[2,2,2,2,2,2,2,2,1024]{8,7,6,5,4,3,2,1,0:T(2,128)}, f32[2,2,2,2,2,2,2,2,1024]{8,7,6,5,4,3,2,1,0:T(2,128)}, u32[]{:S(2)}, u32[]{:S(2)}) collective-permute-start(f32[2,2,2,2,2,2,2,2,1024]{8,7,6,5,4,3,2,1,0:T(2,128)} %bitcast.336), channel_id=1, source_target_pairs={{0,1},{1,0},{2,3},{3,2},{4,5},{5,4},{6,7},{7,6},{8,9},{9,8},{10,11... | collective-permute-start | bytes 3145736 | tf_op jit(solution)/shard_map/ppermute | solution.py:123
  224.0 6.3 %copy-start.20 = (bf16[1,128,512]{1,2,0:T(8,128)(2,1)S(1)}, bf16[1,128,512]{1,2,0:T(8,128)(2,1)}, u32[]{:S(2)}) copy-start(bf16[1,128,512]{1,2,0:T(8,128)(2,1)} %copy.768) | copy-start | bytes 393220
  224.1 6.3 %copy-start.43 = (f32[128,8]{0,1:T(8,128)S(1)}, f32[128,8]{0,1:T(8,128)}, u32[]{:S(2)}) copy-start(f32[128,8]{0,1:T(8,128)} %copy-done.42) | copy-start | bytes 12292
  226.6 9.3 %copy-start.45 = (f32[8,8]{0,1:T(8,128)S(1)}, f32[8,8]{0,1:T(8,128)}, u32[]{:S(2)}) copy-start(f32[8,8]{0,1:T(8,128)} %multiply_reduce_fusion.6) | copy-start | bytes 772
  226.6 10.7 %copy-start.2 = (bf16[1024,8,64]{0,2,1:T(8,128)(2,1)S(1)}, bf16[1024,8,64]{0,2,1:T(8,128)(2,1)}, u32[]{:S(2)}) copy-start(bf16[1024,8,64]{0,2,1:T(8,128)(2,1)} %copy.776) | copy-start | bytes 3145732
  232.8 8.2 %copy-start.46 = (f32[8,128]{1,0:T(8,128)S(1)}, f32[8,128]{1,0:T(8,128)}, u32[]{:S(2)}) copy-start(f32[8,128]{1,0:T(8,128)} %get-tuple-element.19) | copy-start | bytes 12292
  232.8 8.2 %copy-start.50 = (f32[128,8]{0,1:T(8,128)S(1)}, f32[128,8]{0,1:T(8,128)}, u32[]{:S(2)}) copy-start(f32[128,8]{0,1:T(8,128)} %mul.660) | copy-start | bytes 12292
  232.8 8.2 %copy-start.14 = (bf16[128,512]{0,1:T(8,128)(2,1)S(1)}, bf16[128,512]{0,1:T(8,128)(2,1)}, u32[]{:S(2)}) copy-start(bf16[128,512]{0,1:T(8,128)(2,1)} %get-tuple-element.98) | copy-start | bytes 393220
  236.0 9.1 %copy-start.12 = (bf16[64,8,512]{2,1,0:T(8,128)(2,1)S(1)}, bf16[64,8,512]{2,1,0:T(8,128)(2,1)}, u32[]{:S(2)}) copy-start(bf16[64,8,512]{2,1,0:T(8,128)(2,1)} %get-tuple-element.23) | copy-start | bytes 1572868
  236.0 9.1 %copy-start.13 = (bf16[64,8,512]{2,1,0:T(8,128)(2,1)S(1)}, bf16[64,8,512]{2,1,0:T(8,128)(2,1)}, u32[]{:S(2)}) copy-start(bf16[64,8,512]{2,1,0:T(8,128)(2,1)} %get-tuple-element.28) | copy-start | bytes 1572868
  241.7 27.1 %collective-permute-start.8 = (bf16[128,640]{0,1:T(8,128)(2,1)}, bf16[128,640]{0,1:T(8,128)(2,1)}, u32[]{:S(2)}, u32[]{:S(2)}) collective-permute-start(bf16[128,640]{0,1:T(8,128)(2,1)} %fusion.74), channel_id=1, source_target_pairs={{0,4},{4,0},{8,12},{12,8},{16,20},{20,16},{24,28},{28,24},{32,36},... | collective-permute-start | bytes 491528 | tf_op jit(solution)/shard_map/ppermute | solution.py:16
  246.3 24.1 %copy-start.16 = (bf16[1,128,512]{1,2,0:T(8,128)(2,1)S(1)}, bf16[1,128,512]{1,2,0:T(8,128)(2,1)}, u32[]{:S(2)}) copy-start(bf16[1,128,512]{1,2,0:T(8,128)(2,1)} %copy-done.15) | copy-start | bytes 393220
  247.7 29.1 %copy-start.21 = (bf16[1,128,512]{1,2,0:T(8,128)(2,1)S(1)}, bf16[1,128,512]{1,2,0:T(8,128)(2,1)}, u32[]{:S(2)}) copy-start(bf16[1,128,512]{1,2,0:T(8,128)(2,1)} %copy.768) | copy-start | bytes 393220
  247.7 29.1 %copy-start.24 = (bf16[1,128,512]{1,2,0:T(8,128)(2,1)S(1)}, bf16[1,128,512]{1,2,0:T(8,128)(2,1)}, u32[]{:S(2)}) copy-start(bf16[1,128,512]{1,2,0:T(8,128)(2,1)} %copy.805) | copy-start | bytes 393220
  248.6 8.1 %collective-permute-start.10 = (bf16[2,2,8,640]{3,2,0,1:T(8,128)(2,1)S(1)}, bf16[2,2,8,640]{3,2,0,1:T(8,128)(2,1)S(1)}, u32[]{:S(2)}, u32[]{:S(2)}) collective-permute-start(bf16[2,2,8,640]{3,2,0,1:T(8,128)(2,1)S(1)} %pad_maximum_fusion.24), channel_id=1, source_target_pairs={{0,8},{4,12},{8,0},{12,4},{16,24},{20,28},{24,16},{28,20},{32,40},... | collective-permute-start | bytes 122888 | tf_op jit(solution)/shard_map/ppermute | solution.py:16
  257.4 7.8 %collective-permute-start.11 = (bf16[2,4,8,640]{3,2,0,1:T(8,128)(2,1)S(1)}, bf16[2,4,8,640]{3,2,0,1:T(8,128)(2,1)S(1)}, u32[]{:S(2)}, u32[]{:S(2)}) collective-permute-start(bf16[2,4,8,640]{3,2,0,1:T(8,128)(2,1)S(1)} %pad_maximum_fusion.22), channel_id=1, source_target_pairs={{0,64},{4,68},{8,72},{12,76},{16,80},{20,84},{24,88},{28,92},{32,9... | collective-permute-start | bytes 245768 | tf_op jit(solution)/shard_map/ppermute | solution.py:16
  266.0 7.2 %collective-permute-start.12 = (bf16[2,8,8,640]{3,2,0,1:T(8,128)(2,1)S(1)}, bf16[2,8,8,640]{3,2,0,1:T(8,128)(2,1)S(1)}, u32[]{:S(2)}, u32[]{:S(2)}) collective-permute-start(bf16[2,8,8,640]{3,2,0,1:T(8,128)(2,1)S(1)} %pad_maximum_fusion.20), channel_id=1, source_target_pairs={{0,4},{4,0},{8,12},{12,8},{16,20},{20,16},{24,28},{28,24},{32,36},... | collective-permute-start | bytes 491528 | tf_op jit(solution)/shard_map/ppermute | solution.py:16
  270.4 6.4 %copy-start.23 = (bf16[128,512]{0,1:T(8,128)(2,1)}, bf16[128,512]{0,1:T(8,128)(2,1)S(1)}, u32[]{:S(2)}) copy-start(bf16[128,512]{0,1:T(8,128)(2,1)S(1)} %slice.189) | copy-start | bytes 393220
  274.1 9.3 %collective-permute-start.13 = (bf16[2,16,8,640]{3,2,0,1:T(8,128)(2,1)}, bf16[2,16,8,640]{3,2,0,1:T(8,128)(2,1)}, u32[]{:S(2)}, u32[]{:S(2)}) collective-permute-start(bf16[2,16,8,640]{3,2,0,1:T(8,128)(2,1)} %get-tuple-element.56), channel_id=1, source_target_pairs={{0,32},{4,36},{8,40},{12,44},{16,48},{20,52},{24,56},{28,60},{32,0... | collective-permute-start | bytes 983048 | tf_op jit(solution)/shard_map/ppermute | solution.py:16
  278.3 11.6 %copy-start.8 = (f32[2,2,2,2,2,2,2,2,1,1024]{9,8,7,6,5,4,3,2,1,0:T(1,128)S(1)}, f32[2,2,2,2,2,2,2,2,1,1024]{9,8,7,6,5,4,3,2,1,0:T(1,128)}, u32[]{:S(2)}) copy-start(f32[2,2,2,2,2,2,2,2,1,1024]{9,8,7,6,5,4,3,2,1,0:T(1,128)} %get-tuple-element.26) | copy-start | bytes 3145732
  285.3 15.1 %collective-permute-start.14 = (bf16[2,32,8,640]{3,2,0,1:T(8,128)(2,1)}, bf16[2,32,8,640]{3,2,0,1:T(8,128)(2,1)}, u32[]{:S(2)}, u32[]{:S(2)}) collective-permute-start(bf16[2,32,8,640]{3,2,0,1:T(8,128)(2,1)} %get-tuple-element.45), channel_id=1, source_target_pairs={{0,128},{4,132},{8,136},{12,140},{16,144},{20,148},{24,152},{28,15... | collective-permute-start | bytes 1966088 | tf_op jit(solution)/shard_map/ppermute | solution.py:16
  289.9 10.6 %copy-start.10 = (bf16[2,64,8,640]{3,2,0,1:T(8,128)(2,1)S(1)}, bf16[2,64,8,640]{3,2,0,1:T(8,128)(2,1)}, u32[]{:S(2)}) copy-start(bf16[2,64,8,640]{3,2,0,1:T(8,128)(2,1)} %get-tuple-element.46) | copy-start | bytes 3932164
  292.0 9.7 %copy-start.9 = (f32[2,2,2,2,2,2,2,2,1024]{8,7,6,5,4,3,2,1,0:T(2,128)}, f32[2,2,2,2,2,2,2,2,1024]{8,7,6,5,4,3,2,1,0:T(2,128)S(1)}, u32[]{:S(2)}) copy-start(f32[2,2,2,2,2,2,2,2,1024]{8,7,6,5,4,3,2,1,0:T(2,128)S(1)} %bitcast_add_fusion) | copy-start | bytes 3145732
  293.0 19.4 %collective-permute-start.17 = (f32[2,2,2,2,2,2,2,1024]{7,6,5,4,3,2,1,0:T(2,128)}, f32[2,2,2,2,2,2,2,1024]{7,6,5,4,3,2,1,0:T(2,128)}, u32[]{:S(2)}, u32[]{:S(2)}) collective-permute-start(f32[2,2,2,2,2,2,2,1024]{7,6,5,4,3,2,1,0:T(2,128)} %dynamic-slice_bitcast_fusion), channel_id=1, source_target_pairs={{0,4},{1,5},{2,6},{3,7},{4,0},{5,1},{6,2},{7,3},{8,12},{9,13},{10,... | collective-permute-start | bytes 1572872 | tf_op jit(solution)/shard_map/ppermute | solution.py:123
  306.8 31.6 %copy-start.3 = (bf16[1024,8,64]{0,2,1:T(8,128)(2,1)S(1)}, bf16[1024,8,64]{0,2,1:T(8,128)(2,1)}, u32[]{:S(2)}) copy-start(bf16[1024,8,64]{0,2,1:T(8,128)(2,1)} %copy.818) | copy-start | bytes 3145732
  306.8 31.6 %copy-start.34 = (bf16[16,8,64]{2,1,0:T(8,128)(2,1)S(1)}, bf16[16,8,64]{2,1,0:T(8,128)(2,1)}, u32[]{:S(2)}) copy-start(bf16[16,8,64]{2,1,0:T(8,128)(2,1)} %reshape_reshape_squeeze_stack.11) | copy-start | bytes 49156
  309.0 64.4 %collective-permute-start.15 = (bf16[64,8,640]{2,1,0:T(8,128)(2,1)}, bf16[64,8,640]{2,1,0:T(8,128)(2,1)}, u32[]{:S(2)}, u32[]{:S(2)}) collective-permute-start(bf16[64,8,640]{2,1,0:T(8,128)(2,1)} %slice_bitcast_fusion), channel_id=1, source_target_pairs={{0,256},{4,260},{8,264},{12,268},{16,272},{20,276},{24,280},{28,28... | collective-permute-start | bytes 1966088 | tf_op jit(solution)/shard_map/ppermute | solution.py:16
  313.9 37.0 %copy-start.33 = (bf16[16,8,64]{2,1,0:T(8,128)(2,1)S(1)}, bf16[16,8,64]{2,1,0:T(8,128)(2,1)}, u32[]{:S(2)}) copy-start(bf16[16,8,64]{2,1,0:T(8,128)(2,1)} %reshape_reshape_squeeze_stack.12) | copy-start | bytes 49156
  314.0 10.5 %collective-permute-start.18 = (f32[2,2,2,2,2,1024]{5,4,3,2,1,0:T(2,128)S(1)}, f32[2,2,2,2,2,1024]{5,4,3,2,1,0:T(2,128)S(1)}, u32[]{:S(2)}, u32[]{:S(2)}) collective-permute-start(f32[2,2,2,2,2,1024]{5,4,3,2,1,0:T(2,128)S(1)} %get-tuple-element.33), channel_id=1, source_target_pairs={{0,32},{1,33},{2,34},{3,35},{4,36},{5,37},{6,38},{7,39},{8,40},{9,... | collective-permute-start | bytes 393224 | tf_op jit(solution)/shard_map/ppermute | solution.py:123
  316.7 8.4 %collective-permute-start.19 = (f32[2,2,2,2,2,1024]{5,4,3,2,1,0:T(2,128)S(1)}, f32[2,2,2,2,2,1024]{5,4,3,2,1,0:T(2,128)S(1)}, u32[]{:S(2)}, u32[]{:S(2)}) collective-permute-start(f32[2,2,2,2,2,1024]{5,4,3,2,1,0:T(2,128)S(1)} %get-tuple-element.35), channel_id=1, source_target_pairs={{0,64},{1,65},{2,66},{3,67},{4,68},{5,69},{6,70},{7,71},{8,72},{9,... | collective-permute-start | bytes 393224 | tf_op jit(solution)/shard_map/ppermute | solution.py:123
  319.8 8.1 %collective-permute-start.20 = (f32[2,2,2,2,2,1024]{5,4,3,2,1,0:T(2,128)S(1)}, f32[2,2,2,2,2,1024]{5,4,3,2,1,0:T(2,128)S(1)}, u32[]{:S(2)}, u32[]{:S(2)}) collective-permute-start(f32[2,2,2,2,2,1024]{5,4,3,2,1,0:T(2,128)S(1)} %get-tuple-element.34), channel_id=1, source_target_pairs={{0,96},{1,97},{2,98},{3,99},{4,100},{5,101},{6,102},{7,103},{8,104... | collective-permute-start | bytes 393224 | tf_op jit(solution)/shard_map/ppermute | solution.py:123
  328.0 11.5 %collective-permute-start.21 = (f32[2,2,2,1024]{3,2,1,0:T(2,128)S(1)}, f32[2,2,2,1024]{3,2,1,0:T(2,128)S(1)}, u32[]{:S(2)}, u32[]{:S(2)}) collective-permute-start(f32[2,2,2,1024]{3,2,1,0:T(2,128)S(1)} %get-tuple-element.57), channel_id=1, source_target_pairs={{0,128},{1,129},{2,130},{3,131},{4,132},{5,133},{6,134},{7,135},{8... | collective-permute-start | bytes 98312 | tf_op jit(solution)/shard_map/ppermute | solution.py:123
  330.6 9.0 %collective-permute-start.22 = (f32[2,2,2,1024]{3,2,1,0:T(2,128)S(1)}, f32[2,2,2,1024]{3,2,1,0:T(2,128)S(1)}, u32[]{:S(2)}, u32[]{:S(2)}) collective-permute-start(f32[2,2,2,1024]{3,2,1,0:T(2,128)S(1)} %get-tuple-element.59), channel_id=1, source_target_pairs={{0,256},{1,257},{2,258},{3,259},{4,260},{5,261},{6,262},{7,263},{8... | collective-permute-start | bytes 98312 | tf_op jit(solution)/shard_map/ppermute | solution.py:123
  335.4 7.0 %collective-permute-start.23 = (f32[2,2,2,1024]{3,2,1,0:T(2,128)S(1)}, f32[2,2,2,1024]{3,2,1,0:T(2,128)S(1)}, u32[]{:S(2)}, u32[]{:S(2)}) collective-permute-start(f32[2,2,2,1024]{3,2,1,0:T(2,128)S(1)} %get-tuple-element.58), channel_id=1, source_target_pairs={{0,384},{1,385},{2,386},{3,387},{4,388},{5,389},{6,390},{7,391},{8... | collective-permute-start | bytes 98312 | tf_op jit(solution)/shard_map/ppermute | solution.py:123
  342.4 6.5 %collective-permute-start.24 = (f32[2,2,1024]{2,1,0:T(2,128)S(1)}, f32[2,2,1024]{2,1,0:T(2,128)S(1)}, u32[]{:S(2)}, u32[]{:S(2)}) collective-permute-start(f32[2,2,1024]{2,1,0:T(2,128)S(1)} %dynamic-slice_bitcast_fusion.7), channel_id=1, source_target_pairs={{0,8},{1,9},{2,10},{3,11},{4,12},{5,13},{6,14},{7,15},{8,0},{9,1},... | collective-permute-start | bytes 49160 | tf_op jit(solution)/shard_map/ppermute | solution.py:123
  349.0 9.5 %collective-permute-start.25 = (f32[2,1024]{1,0:T(2,128)S(1)}, f32[2,1024]{1,0:T(2,128)S(1)}, u32[]{:S(2)}, u32[]{:S(2)}) collective-permute-start(f32[2,1024]{1,0:T(2,128)S(1)} %dynamic-slice_bitcast_fusion.8), channel_id=1, source_target_pairs={{0,16},{1,17},{2,18},{3,19},{4,20},{5,21},{6,22},{7,23},{8,24},{9,... | collective-permute-start | bytes 24584 | tf_op jit(solution)/shard_map/ppermute | solution.py:123
  358.5 14.2 %collective-permute-start.26 = (f32[1024]{0:T(1024)S(1)}, f32[1024]{0:T(1024)S(1)}, u32[]{:S(2)}, u32[]{:S(2)}) collective-permute-start(f32[1024]{0:T(1024)S(1)} %bitcast.419), channel_id=1, source_target_pairs={{0,2},{1,3},{2,0},{3,1},{4,6},{5,7},{6,4},{7,5},{8,10},{9,11},{10,... | collective-permute-start | bytes 12296 | tf_op jit(solution)/shard_map/ppermute | solution.py:123
  380.4 3.2 copy-start.1
  (15 other events, 22.0 us)

commit v3 on v1

--- a/solution.py
+++ b/solution.py
@@ -71,9 +71,15 @@
     return (merged, weights)
 
 
-def gather_blocks(block, axis_pos, bit_order):
-    for bit_pos in bit_order:
-        block = jnp.concatenate([block, partner(block, "tm", bit_pos)], axis_pos)
+def gather_blocks(block, axis_pos, bit_groups):
+    devices = lax.axis_size("tm")
+    for group in bit_groups:
+        pieces = [block]
+        for flip in range(1, 1 << len(group)):
+            mask = sum(((flip >> t) & 1) << bit_pos for t, bit_pos in enumerate(group))
+            pairs = [(source, source ^ mask) for source in range(devices)]
+            pieces.append(lax.ppermute(block, "tm", pairs))
+        block = jnp.concatenate(pieces, axis_pos)
     return block
 
 
@@ -212,8 +218,7 @@
     devices = lax.axis_size("tm")
     bit_count = devices.bit_length() - 1
     top_bit = bit_count - 1
-    near_first = {0: 3, 1: 1, 2: 0, 3: 4, 4: 2, 5: 5}
-    low_bits = sorted(range(top_bit), key=lambda b: near_first.get(b, b))
+    low_bits = ((2,), (1,), (0,), (3, 4), (5,))
     wide = features + 128
 
     other_qkv = partner(jnp.stack([queries, keys_all, values_all], 0), "tm", 0)

time: 389 us -> 398 us (1.023)
  starting transfers between devices: 93.6 us -> 102 us
    ppermute x16 -> x4, waiting for transfers between devices: 67.2 us -> 0.01 us  [partner(): return lax.ppermute(value, axis, pairs)]
    ppermute x0 -> x14, starting transfers between devices: none -> 60 us  [gather_blocks(): pieces.append(lax.ppermute(block, 'tm', pairs))]
    ppermute x0 -> x14, waiting for transfers between devices: none -> 59.2 us  [gather_blocks(): pieces.append(lax.ppermute(block, 'tm', pairs))]
    ppermute x16 -> x4, starting transfers between devices: 67.8 us -> 18.1 us  [partner(): return lax.ppermute(value, axis, pairs)]
    ppermute x9, waiting for transfers between devices: 26.9 us -> 35.1 us  [scatter_sum(): block = keep + lax.ppermute(send, axes, pairs)]
    unnamed x114 -> x142, local copies, waits for them, and re-layouts: 15 us -> 16 us
  transfers between devices with their start and end apart: 25 -> 27, of which waited for: 17 -> 19; matrix products, arithmetic and copies ran while one was open for 33% -> 30% of each run, Pallas kernels for 0% -> 0%
where the time goes in v3:
time: 398 us; the launch traced here: 395 us
  local copies, waits for them, and re-layouts  134 us (34%)
  starting transfers between devices  102 us (26%)
  waiting for transfers between devices  94.3 us (24%)
  other arithmetic  36.5 us (9%)
  matrix products  26.5 us (7%)
    ppermute x14, starting transfers between devices, gather_blocks(): pieces.append(lax.ppermute(block, 'tm', pairs))  60 us
    ppermute x14, waiting for transfers between devices, gather_blocks(): pieces.append(lax.ppermute(block, 'tm', pairs))  59.2 us
    another operation x18, local copies, waits for them, and re-layouts, heads_view(): return matrix.reshape(matrix.shape[0], HEADS, HD)  35.1 us
    ppermute x9, waiting for transfers between devices, scatter_sum(): block = keep + lax.ppermute(send, axes, pairs)  35.1 us
    ppermute x9, starting transfers between devices, scatter_sum(): block = keep + lax.ppermute(send, axes, pairs)  23.7 us
    ppermute x4, starting transfers between devices, partner(): return lax.ppermute(value, axis, pairs)  18.1 us
    unnamed x142, local copies, waits for them, and re-layouts  16 us
    mul x26, local copies, waits for them, and re-layouts, spread_rows(): values[:, None] * chooser  14.3 us
  transfers between devices with their start and end apart: 27, of which 19 were waited for; matrix products, arithmetic and copies ran while one was open for 30% of the time, Pallas kernels for 0%

profile of v3, /device:TPU:6, one launch (start us, length us, event | category | flops | bytes accessed | tf_op | source)
XLA Modules:
  0.0 394.8 jit_solution(17572260441102174635)
XLA Ops:
  5.1 9.1 %collective-permute-start.1 = (bf16[3,2,1,8,512]{4,3,1,0,2:T(8,128)(2,1)S(1)}, bf16[3,2,1,8,512]{4,3,1,0,2:T(8,128)(2,1)S(1)}, u32[]{:S(2)}, u32[]{:S(2)}) collective-permute-start(bf16[3,2,1,8,512]{4,3,1,0,2:T(8,128)(2,1)S(1)} %bitcast.355), channel_id=1, source_target_pairs={{0,16},{4,20},{8,24},{12,28},{16,0},{20,4},{24,8},{28,12},{32,48},... | collective-permute-start | bytes 147464 | tf_op jit(solution)/shard_map/ppermute | solution.py:81
  14.2 2.1 collective-permute-done.1
  16.3 5.3 %collective-permute-start.2 = (bf16[3,2,2,8,512]{4,3,1,0,2:T(8,128)(2,1)S(1)}, bf16[3,2,2,8,512]{4,3,1,0,2:T(8,128)(2,1)S(1)}, u32[]{:S(2)}, u32[]{:S(2)}) collective-permute-start(bf16[3,2,2,8,512]{4,3,1,0,2:T(8,128)(2,1)S(1)} %pad_maximum_fusion.21), channel_id=1, source_target_pairs={{0,8},{4,12},{8,0},{12,4},{16,24},{20,28},{24,16},{28,20},{32,40},... | collective-permute-start | bytes 294920 | tf_op jit(solution)/shard_map/ppermute | solution.py:81
  21.6 5.0 %collective-permute-done.2 = bf16[3,2,2,8,512]{4,3,1,0,2:T(8,128)(2,1)S(1)} collective-permute-done((bf16[3,2,2,8,512]{4,3,1,0,2:T(8,128)(2,1)S(1)}, bf16[3,2,2,8,512]{4,3,1,0,2:T(8,128)(2,1)S(1)}, u32[]{:S(2)}, u32[]{:S(2)}) %collective-permute-start.2) | collective-permute-done | bytes 98336 | tf_op jit(solution)/shard_map/ppermute | solution.py:81
  26.7 2.6 collective-permute-start.3
  29.3 5.1 %collective-permute-done.3 = bf16[3,2,4,8,512]{4,3,1,0,2:T(8,128)(2,1)S(1)} collective-permute-done((bf16[3,2,4,8,512]{4,3,1,0,2:T(8,128)(2,1)S(1)}, bf16[3,2,4,8,512]{4,3,1,0,2:T(8,128)(2,1)S(1)}, u32[]{:S(2)}, u32[]{:S(2)}) %collective-permute-start.3) | collective-permute-done | bytes 196640 | tf_op jit(solution)/shard_map/ppermute | solution.py:81
  34.4 2.7 collective-permute-start.4
  37.8 4.5 %collective-permute-start.5 = (bf16[3,2,8,8,512]{4,3,1,0,2:T(8,128)(2,1)S(1)}, bf16[3,2,8,8,512]{4,3,1,0,2:T(8,128)(2,1)S(1)}, u32[]{:S(2)}, u32[]{:S(2)}) collective-permute-start(bf16[3,2,8,8,512]{4,3,1,0,2:T(8,128)(2,1)S(1)} %pad_maximum_fusion.4), channel_id=1, source_target_pairs={{0,64},{4,68},{8,72},{12,76},{16,80},{20,84},{24,88},{28,92},{32,9... | collective-permute-start | bytes 1179656 | tf_op jit(solution)/shard_map/ppermute | solution.py:81
  43.0 3.2 collective-permute-start.6
  49.4 4.6 %collective-permute-done.5 = bf16[3,2,8,8,512]{4,3,1,0,2:T(8,128)(2,1)S(1)} collective-permute-done((bf16[3,2,8,8,512]{4,3,1,0,2:T(8,128)(2,1)S(1)}, bf16[3,2,8,8,512]{4,3,1,0,2:T(8,128)(2,1)S(1)}, u32[]{:S(2)}, u32[]{:S(2)}) %collective-permute-start.5) | collective-permute-done | bytes 393248 | tf_op jit(solution)/shard_map/ppermute | solution.py:81
  55.1 5.1 %collective-permute-done.6 = bf16[3,2,8,8,512]{4,3,1,0,2:T(8,128)(2,1)S(1)} collective-permute-done((bf16[3,2,8,8,512]{4,3,1,0,2:T(8,128)(2,1)S(1)}, bf16[3,2,8,8,512]{4,3,1,0,2:T(8,128)(2,1)S(1)}, u32[]{:S(2)}, u32[]{:S(2)}) %collective-permute-start.6) | collective-permute-done | bytes 393248 | tf_op jit(solution)/shard_map/ppermute | solution.py:81
  61.2 4.2 %collective-permute-start.7 = (bf16[3,2,32,8,512]{4,3,1,0,2:T(8,128)(2,1)}, bf16[3,2,32,8,512]{4,3,1,0,2:T(8,128)(2,1)}, u32[]{:S(2)}, u32[]{:S(2)}) collective-permute-start(bf16[3,2,32,8,512]{4,3,1,0,2:T(8,128)(2,1)} %get-tuple-element.37), channel_id=1, source_target_pairs={{0,128},{4,132},{8,136},{12,140},{16,144},{20,148},{24,152},{28,15... | collective-permute-start | bytes 4718600 | tf_op jit(solution)/shard_map/ppermute | solution.py:81
  65.4 4.8 %collective-permute-start = (bf16[3,128,512]{2,1,0:T(8,128)(2,1)S(1)}, bf16[3,128,512]{2,1,0:T(8,128)(2,1)S(1)}, u32[]{:S(2)}, u32[]{:S(2)}) collective-permute-start(bf16[3,128,512]{2,1,0:T(8,128)(2,1)S(1)} %pad_maximum_fusion.3), channel_id=1, source_target_pairs={{0,4},{4,0},{8,12},{12,8},{16,20},{20,16},{24,28},{28,24},{32,36},... | collective-permute-start | bytes 1179656 | tf_op jit(solution)/shard_map/ppermute | solution.py:16
  81.4 17.3 %collective-permute-done.7 = bf16[3,2,32,8,512]{4,3,1,0,2:T(8,128)(2,1)} collective-permute-done((bf16[3,2,32,8,512]{4,3,1,0,2:T(8,128)(2,1)}, bf16[3,2,32,8,512]{4,3,1,0,2:T(8,128)(2,1)}, u32[]{:S(2)}, u32[]{:S(2)}) %collective-permute-start.7) | collective-permute-done | bytes 1572896 | tf_op jit(solution)/shard_map/ppermute | solution.py:81
  98.7 2.7 constant_dynamic-update-slice_fusion.7
  101.4 2.8 copy_bitcast_fusion
  104.2 5.4 %collective-permute-start.8 = (bf16[3,64,8,512]{3,2,1,0:T(8,128)(2,1)}, bf16[3,64,8,512]{3,2,1,0:T(8,128)(2,1)}, u32[]{:S(2)}, u32[]{:S(2)}) collective-permute-start(bf16[3,64,8,512]{3,2,1,0:T(8,128)(2,1)} %copy_bitcast_fusion), channel_id=1, source_target_pairs={{0,256},{4,260},{8,264},{12,268},{16,272},{20,276},{24,280},{28,28... | collective-permute-start | bytes 4718600 | tf_op jit(solution)/shard_map/ppermute | solution.py:16
  109.7 3.5 fusion.134
  113.3 2.1 reshape_reshape_squeeze.15
  115.3 3.3 copy.818
  120.0 2.1 reshape_reshape_squeeze.14
  122.1 2.5 copy.772
  124.6 2.7 copy.759
  127.3 3.9 reshape_reshape_squeeze.6
  131.2 3.3 copy.761
  142.4 2.3 slice_bitcast_fusion.2
  144.7 2.3 slice_bitcast_fusion.1
  148.1 2.1 reshape_reshape.28
  150.2 2.5 copy.767
  162.1 3.9 reshape_reshape.29
  166.0 3.3 copy.776
  173.8 2.3 fusion.65
  204.5 8.5 %collective-permute-start.10 = (bf16[2,1,8,640]{3,2,0,1:T(8,128)(2,1)}, bf16[2,1,8,640]{3,2,0,1:T(8,128)(2,1)}, u32[]{:S(2)}, u32[]{:S(2)}) collective-permute-start(bf16[2,1,8,640]{3,2,0,1:T(8,128)(2,1)} %get-tuple-element.12), channel_id=1, source_target_pairs={{0,16},{4,20},{8,24},{12,28},{16,0},{20,4},{24,8},{28,12},{32,48},... | collective-permute-start | bytes 61448 | tf_op jit(solution)/shard_map/ppermute | solution.py:81
  213.1 2.0 fusion.57
  216.8 2.4 fusion.17
  220.0 2.9 fusion.29
  224.1 5.9 %constant_dynamic-slice_fusion.3 = (f32[2,2,2,2,2,2,2,2,1,1024]{9,8,7,6,5,4,3,2,1,0:T(1,128)}, f32[2,2,2,2,2,2,2,2,1,1024]{9,8,7,6,5,4,3,2,1,0:T(1,128)}) fusion(f32[2,2,2,2,2,2,2,2,2,1024]{9,8,7,6,5,4,3,2,1,0:T(2,128)} %fusion.57, s32[]{:T(128)S(6)} %select_n.151, s32[]{:T(128)S(6)} %select_n.152), kind=kLoop, calls=%fused_computation.263 | loop fusion | bytes 4194312 | tf_op jit(solution)/shard_map/jit(dynamic_index_in_dim)/dynamic_slice | solution.py:122
  237.3 5.1 %collective-permute-start.9 = (bf16[128,640]{0,1:T(8,128)(2,1)}, bf16[128,640]{0,1:T(8,128)(2,1)}, u32[]{:S(2)}, u32[]{:S(2)}) collective-permute-start(bf16[128,640]{0,1:T(8,128)(2,1)} %fusion.74), channel_id=1, source_target_pairs={{0,4},{4,0},{8,12},{12,8},{16,20},{20,16},{24,28},{28,24},{32,36},... | collective-permute-start | bytes 491528 | tf_op jit(solution)/shard_map/ppermute | solution.py:16
  245.8 2.0 collective-permute-start.18
  248.6 5.3 %collective-permute-start.11 = (bf16[2,2,8,640]{3,2,0,1:T(8,128)(2,1)S(1)}, bf16[2,2,8,640]{3,2,0,1:T(8,128)(2,1)S(1)}, u32[]{:S(2)}, u32[]{:S(2)}) collective-permute-start(bf16[2,2,8,640]{3,2,0,1:T(8,128)(2,1)S(1)} %pad_maximum_fusion.24), channel_id=1, source_target_pairs={{0,8},{4,12},{8,0},{12,4},{16,24},{20,28},{24,16},{28,20},{32,40},... | collective-permute-start | bytes 122888 | tf_op jit(solution)/shard_map/ppermute | solution.py:81
  257.8 2.2 collective-permute-start.12
  260.6 3.5 collective-permute-done.12
  264.9 4.7 %collective-permute-start.15 = (bf16[2,8,8,640]{3,2,0,1:T(8,128)(2,1)S(1)}, bf16[2,8,8,640]{3,2,0,1:T(8,128)(2,1)S(1)}, u32[]{:S(2)}, u32[]{:S(2)}) collective-permute-start(bf16[2,8,8,640]{3,2,0,1:T(8,128)(2,1)S(1)} %pad_maximum_fusion.20), channel_id=1, source_target_pairs={{0,96},{4,100},{8,104},{12,108},{16,112},{20,116},{24,120},{28,124... | collective-permute-start | bytes 491528 | tf_op jit(solution)/shard_map/ppermute | solution.py:81
  271.5 3.2 collective-permute-start.13
  276.2 3.4 collective-permute-done.13
  281.9 2.6 collective-permute-start.16
  288.7 10.5 %collective-permute-done.16 = bf16[2,32,8,640]{3,2,0,1:T(8,128)(2,1)} collective-permute-done((bf16[2,32,8,640]{3,2,0,1:T(8,128)(2,1)}, bf16[2,32,8,640]{3,2,0,1:T(8,128)(2,1)}, u32[]{:S(2)}, u32[]{:S(2)}) %collective-permute-start.16) | collective-permute-done | bytes 655392 | tf_op jit(solution)/shard_map/ppermute | solution.py:81
  305.2 2.8 collective-permute-start.17
  309.6 2.1 bitcast_add_fusion
  312.8 2.4 collective-permute-start.19
  323.6 2.5 collective-permute-done.19
  328.2 2.7 collective-permute-start.20
  337.9 2.9 collective-permute-start.21
  340.9 3.9 collective-permute-done.21
  344.9 2.5 collective-permute-start.22
  347.6 4.9 %collective-permute-done.22 = f32[2,2,2,2,1024]{4,3,2,1,0:T(2,128)S(1)} collective-permute-done((f32[2,2,2,2,1024]{4,3,2,1,0:T(2,128)S(1)}, f32[2,2,2,2,1024]{4,3,2,1,0:T(2,128)S(1)}, u32[]{:S(2)}, u32[]{:S(2)}) %collective-permute-start.22) | collective-permute-done | bytes 65568 | tf_op jit(solution)/shard_map/ppermute | solution.py:125
  353.2 2.6 collective-permute-start.23
  357.7 3.1 collective-permute-done.23
  362.2 4.5 %collective-permute-start.24 = (f32[2,2,1024]{2,1,0:T(2,128)}, f32[2,2,1024]{2,1,0:T(2,128)}, u32[]{:S(2)}, u32[]{:S(2)}) collective-permute-start(f32[2,2,1024]{2,1,0:T(2,128)} %dynamic-slice_bitcast_fusion.5), channel_id=1, source_target_pairs={{0,256},{1,257},{2,258},{3,259},{4,260},{5,261},{6,262},{7,263},{8... | collective-permute-start | bytes 49160 | tf_op jit(solution)/shard_map/ppermute | solution.py:125
  367.3 2.3 collective-permute-done.24
  373.2 6.7 %collective-permute-done.25 = f32[2,1024]{1,0:T(2,128)S(1)} collective-permute-done((f32[2,1024]{1,0:T(2,128)S(1)}, f32[2,1024]{1,0:T(2,128)S(1)}, u32[]{:S(2)}, u32[]{:S(2)}) %collective-permute-start.25) | collective-permute-done | bytes 8224 | tf_op jit(solution)/shard_map/ppermute | solution.py:125
  379.9 2.1 collective-permute-start.26
  382.0 2.1 add_convert_fusion
  384.0 10.2 %collective-permute-done.26 = f32[1024]{0:T(1024)S(1)} collective-permute-done((f32[1024]{0:T(1024)S(1)}, f32[1024]{0:T(1024)S(1)}, u32[]{:S(2)}, u32[]{:S(2)}) %collective-permute-start.26) | collective-permute-done | bytes 4128 | tf_op jit(solution)/shard_map/ppermute | solution.py:125
  (340 shorter events, 139.5 us)
Async XLA Ops:
  0.6 3.7 copy-start.62
  5.1 11.2 %collective-permute-start.1 = (bf16[3,2,1,8,512]{4,3,1,0,2:T(8,128)(2,1)S(1)}, bf16[3,2,1,8,512]{4,3,1,0,2:T(8,128)(2,1)S(1)}, u32[]{:S(2)}, u32[]{:S(2)}) collective-permute-start(bf16[3,2,1,8,512]{4,3,1,0,2:T(8,128)(2,1)S(1)} %bitcast.355), channel_id=1, source_target_pairs={{0,16},{4,20},{8,24},{12,28},{16,0},{20,4},{24,8},{28,12},{32,48},... | collective-permute-start | bytes 147464 | tf_op jit(solution)/shard_map/ppermute | solution.py:81
  16.3 10.4 %collective-permute-start.2 = (bf16[3,2,2,8,512]{4,3,1,0,2:T(8,128)(2,1)S(1)}, bf16[3,2,2,8,512]{4,3,1,0,2:T(8,128)(2,1)S(1)}, u32[]{:S(2)}, u32[]{:S(2)}) collective-permute-start(bf16[3,2,2,8,512]{4,3,1,0,2:T(8,128)(2,1)S(1)} %pad_maximum_fusion.21), channel_id=1, source_target_pairs={{0,8},{4,12},{8,0},{12,4},{16,24},{20,28},{24,16},{28,20},{32,40},... | collective-permute-start | bytes 294920 | tf_op jit(solution)/shard_map/ppermute | solution.py:81
  26.7 7.7 %collective-permute-start.3 = (bf16[3,2,4,8,512]{4,3,1,0,2:T(8,128)(2,1)S(1)}, bf16[3,2,4,8,512]{4,3,1,0,2:T(8,128)(2,1)S(1)}, u32[]{:S(2)}, u32[]{:S(2)}) collective-permute-start(bf16[3,2,4,8,512]{4,3,1,0,2:T(8,128)(2,1)S(1)} %pad_maximum_fusion.9), channel_id=1, source_target_pairs={{0,4},{4,0},{8,12},{12,8},{16,20},{20,16},{24,28},{28,24},{32,36},... | collective-permute-start | bytes 589832 | tf_op jit(solution)/shard_map/ppermute | solution.py:81
  34.4 13.9 %collective-permute-start.4 = (bf16[3,2,8,8,512]{4,3,1,0,2:T(8,128)(2,1)S(1)}, bf16[3,2,8,8,512]{4,3,1,0,2:T(8,128)(2,1)S(1)}, u32[]{:S(2)}, u32[]{:S(2)}) collective-permute-start(bf16[3,2,8,8,512]{4,3,1,0,2:T(8,128)(2,1)S(1)} %pad_maximum_fusion.4), channel_id=1, source_target_pairs={{0,32},{4,36},{8,40},{12,44},{16,48},{20,52},{24,56},{28,60},{32,0... | collective-permute-start | bytes 1179656 | tf_op jit(solution)/shard_map/ppermute | solution.py:81
  37.8 16.2 %collective-permute-start.5 = (bf16[3,2,8,8,512]{4,3,1,0,2:T(8,128)(2,1)S(1)}, bf16[3,2,8,8,512]{4,3,1,0,2:T(8,128)(2,1)S(1)}, u32[]{:S(2)}, u32[]{:S(2)}) collective-permute-start(bf16[3,2,8,8,512]{4,3,1,0,2:T(8,128)(2,1)S(1)} %pad_maximum_fusion.4), channel_id=1, source_target_pairs={{0,64},{4,68},{8,72},{12,76},{16,80},{20,84},{24,88},{28,92},{32,9... | collective-permute-start | bytes 1179656 | tf_op jit(solution)/shard_map/ppermute | solution.py:81
  43.0 17.3 %collective-permute-start.6 = (bf16[3,2,8,8,512]{4,3,1,0,2:T(8,128)(2,1)S(1)}, bf16[3,2,8,8,512]{4,3,1,0,2:T(8,128)(2,1)S(1)}, u32[]{:S(2)}, u32[]{:S(2)}) collective-permute-start(bf16[3,2,8,8,512]{4,3,1,0,2:T(8,128)(2,1)S(1)} %pad_maximum_fusion.4), channel_id=1, source_target_pairs={{0,96},{4,100},{8,104},{12,108},{16,112},{20,116},{24,120},{28,124... | collective-permute-start | bytes 1179656 | tf_op jit(solution)/shard_map/ppermute | solution.py:81
  60.2 11.2 %copy-start.54 = (f32[16,8]{0,1:T(8,128)S(1)}, f32[16,8]{0,1:T(8,128)}, u32[]{:S(2)}) copy-start(f32[16,8]{0,1:T(8,128)} %constant.250.clone) | copy-start | bytes 1540
  60.2 11.3 %copy-start.53 = (f32[8,8]{0,1:T(8,128)S(1)}, f32[8,8]{0,1:T(8,128)}, u32[]{:S(2)}) copy-start(f32[8,8]{0,1:T(8,128)} %constant.249.clone) | copy-start | bytes 772
  61.2 37.5 %collective-permute-start.7 = (bf16[3,2,32,8,512]{4,3,1,0,2:T(8,128)(2,1)}, bf16[3,2,32,8,512]{4,3,1,0,2:T(8,128)(2,1)}, u32[]{:S(2)}, u32[]{:S(2)}) collective-permute-start(bf16[3,2,32,8,512]{4,3,1,0,2:T(8,128)(2,1)} %get-tuple-element.37), channel_id=1, source_target_pairs={{0,128},{4,132},{8,136},{12,140},{16,144},{20,148},{24,152},{28,15... | collective-permute-start | bytes 4718600 | tf_op jit(solution)/shard_map/ppermute | solution.py:81
  65.4 13.2 %collective-permute-start = (bf16[3,128,512]{2,1,0:T(8,128)(2,1)S(1)}, bf16[3,128,512]{2,1,0:T(8,128)(2,1)S(1)}, u32[]{:S(2)}, u32[]{:S(2)}) collective-permute-start(bf16[3,128,512]{2,1,0:T(8,128)(2,1)S(1)} %pad_maximum_fusion.3), channel_id=1, source_target_pairs={{0,4},{4,0},{8,12},{12,8},{16,20},{20,16},{24,28},{28,24},{32,36},... | collective-permute-start | bytes 1179656 | tf_op jit(solution)/shard_map/ppermute | solution.py:16
  70.6 9.7 %copy-start.14 = (bf16[1,128,512]{1,2,0:T(8,128)(2,1)}, bf16[1,128,512]{1,2,0:T(8,128)(2,1)S(1)}, u32[]{:S(2)}) copy-start(bf16[1,128,512]{1,2,0:T(8,128)(2,1)S(1)} %copy.756) | copy-start | bytes 393220
  70.7 9.6 %copy-start.20 = (bf16[1,128,512]{1,2,0:T(8,128)(2,1)}, bf16[1,128,512]{1,2,0:T(8,128)(2,1)S(1)}, u32[]{:S(2)}) copy-start(bf16[1,128,512]{1,2,0:T(8,128)(2,1)S(1)} %copy.754) | copy-start | bytes 393220
  71.7 102.1 %copy-start.42 = (f32[128,8]{0,1:T(8,128)}, f32[128,8]{0,1:T(8,128)S(1)}, u32[]{:S(2)}) copy-start(f32[128,8]{0,1:T(8,128)S(1)} %mul.636) | copy-start | bytes 12292
  80.3 21.1 %copy-start.31 = (bf16[1,128,512]{1,2,0:T(8,128)(2,1)}, bf16[1,128,512]{1,2,0:T(8,128)(2,1)S(1)}, u32[]{:S(2)}) copy-start(bf16[1,128,512]{1,2,0:T(8,128)(2,1)S(1)} %copy.755) | copy-start | bytes 393220
  80.7 20.7 %copy-start.51 = (f32[8,128]{1,0:T(8,128)}, f32[8,128]{1,0:T(8,128)S(1)}, u32[]{:S(2)}) copy-start(f32[8,128]{1,0:T(8,128)S(1)} %get-tuple-element.91) | copy-start | bytes 12292
  104.2 40.4 %collective-permute-start.8 = (bf16[3,64,8,512]{3,2,1,0:T(8,128)(2,1)}, bf16[3,64,8,512]{3,2,1,0:T(8,128)(2,1)}, u32[]{:S(2)}, u32[]{:S(2)}) collective-permute-start(bf16[3,64,8,512]{3,2,1,0:T(8,128)(2,1)} %copy_bitcast_fusion), channel_id=1, source_target_pairs={{0,256},{4,260},{8,264},{12,268},{16,272},{20,276},{24,280},{28,28... | collective-permute-start | bytes 4718600 | tf_op jit(solution)/shard_map/ppermute | solution.py:16
  124.6 14.3 %copy-start.4 = (bf16[1024,8,64]{0,2,1:T(8,128)(2,1)}, bf16[1024,8,64]{0,2,1:T(8,128)(2,1)S(1)}, u32[]{:S(2)}) copy-start(bf16[1024,8,64]{0,2,1:T(8,128)(2,1)S(1)} %copy.772) | copy-start | bytes 3145732
  158.7 17.3 %copy-start.45 = (f32[128,8]{0,1:T(8,128)}, f32[128,8]{0,1:T(8,128)S(1)}, u32[]{:S(2)}) copy-start(f32[128,8]{0,1:T(8,128)S(1)} %get-tuple-element.15) | copy-start | bytes 12292
  181.4 4.2 %copy-start.48 = (f32[8,8]{0,1:T(8,128)}, f32[8,8]{0,1:T(8,128)S(1)}, u32[]{:S(2)}) copy-start(f32[8,8]{0,1:T(8,128)S(1)} %multiply_reduce_fusion.6) | copy-start | bytes 772
  200.9 12.2 %copy-start.33 = (bf16[1,128,1024]{2,1,0:T(8,128)(2,1)S(1)}, bf16[1,128,1024]{2,1,0:T(8,128)(2,1)}, u32[]{:S(2)}) copy-start(bf16[1,128,1024]{2,1,0:T(8,128)(2,1)} %param.34) | copy-start | bytes 786436
  204.5 43.3 %collective-permute-start.10 = (bf16[2,1,8,640]{3,2,0,1:T(8,128)(2,1)}, bf16[2,1,8,640]{3,2,0,1:T(8,128)(2,1)}, u32[]{:S(2)}, u32[]{:S(2)}) collective-permute-start(bf16[2,1,8,640]{3,2,0,1:T(8,128)(2,1)} %get-tuple-element.12), channel_id=1, source_target_pairs={{0,16},{4,20},{8,24},{12,28},{16,0},{20,4},{24,8},{28,12},{32,48},... | collective-permute-start | bytes 61448 | tf_op jit(solution)/shard_map/ppermute | solution.py:81
  216.2 3.8 copy-start.44
  224.1 5.9 %copy-start.13 = (bf16[128,512]{0,1:T(8,128)(2,1)S(1)}, bf16[128,512]{0,1:T(8,128)(2,1)}, u32[]{:S(2)}) copy-start(bf16[128,512]{0,1:T(8,128)(2,1)} %get-tuple-element.85) | copy-start | bytes 393220
  224.1 5.9 %copy-start.58 = (bf16[128,16]{0,1:T(8,128)(2,1)S(1)}, bf16[128,16]{0,1:T(8,128)(2,1)}, u32[]{:S(2)}) copy-start(bf16[128,16]{0,1:T(8,128)(2,1)} %get-tuple-element.75) | copy-start | bytes 12292
  224.1 5.9 %copy-start.59 = (bf16[128,16]{0,1:T(8,128)(2,1)S(1)}, bf16[128,16]{0,1:T(8,128)(2,1)}, u32[]{:S(2)}) copy-start(bf16[128,16]{0,1:T(8,128)(2,1)} %get-tuple-element.76) | copy-start | bytes 12292
  224.1 5.9 %copy-start.60 = (bf16[128,16]{0,1:T(8,128)(2,1)S(1)}, bf16[128,16]{0,1:T(8,128)(2,1)}, u32[]{:S(2)}) copy-start(bf16[128,16]{0,1:T(8,128)(2,1)} %get-tuple-element.77) | copy-start | bytes 12292
  224.1 7.9 %copy-start.7 = (bf16[128,8,512]{2,1,0:T(8,128)(2,1)S(1)}, bf16[128,8,512]{2,1,0:T(8,128)(2,1)}, u32[]{:S(2)}) copy-start(bf16[128,8,512]{2,1,0:T(8,128)(2,1)} %pad_maximum_fusion.2) | copy-start | bytes 3145732
  236.4 7.9 %copy-start.10 = (f32[2,2,2,2,2,2,2,2,1,1024]{9,8,7,6,5,4,3,2,1,0:T(1,128)S(1)}, f32[2,2,2,2,2,2,2,2,1,1024]{9,8,7,6,5,4,3,2,1,0:T(1,128)}, u32[]{:S(2)}) copy-start(f32[2,2,2,2,2,2,2,2,1,1024]{9,8,7,6,5,4,3,2,1,0:T(1,128)} %get-tuple-element.27) | copy-start | bytes 3145732
  237.3 38.1 %collective-permute-start.9 = (bf16[128,640]{0,1:T(8,128)(2,1)}, bf16[128,640]{0,1:T(8,128)(2,1)}, u32[]{:S(2)}, u32[]{:S(2)}) collective-permute-start(bf16[128,640]{0,1:T(8,128)(2,1)} %fusion.74), channel_id=1, source_target_pairs={{0,4},{4,0},{8,12},{12,8},{16,20},{20,16},{24,28},{28,24},{32,36},... | collective-permute-start | bytes 491528 | tf_op jit(solution)/shard_map/ppermute | solution.py:16
  245.8 38.7 %copy-start.15 = (bf16[1,128,512]{1,2,0:T(8,128)(2,1)S(1)}, bf16[1,128,512]{1,2,0:T(8,128)(2,1)}, u32[]{:S(2)}) copy-start(bf16[1,128,512]{1,2,0:T(8,128)(2,1)} %copy-done.14) | copy-start | bytes 393220
  245.8 38.7 %copy-start.21 = (bf16[1,128,512]{1,2,0:T(8,128)(2,1)S(1)}, bf16[1,128,512]{1,2,0:T(8,128)(2,1)}, u32[]{:S(2)}) copy-start(bf16[1,128,512]{1,2,0:T(8,128)(2,1)} %copy-done.20) | copy-start | bytes 393220
  245.8 38.7 %copy-start.22 = (bf16[1,128,512]{1,2,0:T(8,128)(2,1)S(1)}, bf16[1,128,512]{1,2,0:T(8,128)(2,1)}, u32[]{:S(2)}) copy-start(bf16[1,128,512]{1,2,0:T(8,128)(2,1)} %copy.805) | copy-start | bytes 393220
  245.8 63.8 %collective-permute-start.18 = (f32[2,2,2,2,2,2,2,2,1024]{8,7,6,5,4,3,2,1,0:T(2,128)}, f32[2,2,2,2,2,2,2,2,1024]{8,7,6,5,4,3,2,1,0:T(2,128)}, u32[]{:S(2)}, u32[]{:S(2)}) collective-permute-start(f32[2,2,2,2,2,2,2,2,1024]{8,7,6,5,4,3,2,1,0:T(2,128)} %bitcast.324), channel_id=1, source_target_pairs={{0,1},{1,0},{2,3},{3,2},{4,5},{5,4},{6,7},{7,6},{8,9},{9,8},{10,11... | collective-permute-start | bytes 3145736 | tf_op jit(solution)/shard_map/ppermute | solution.py:125
  248.6 8.4 %collective-permute-start.11 = (bf16[2,2,8,640]{3,2,0,1:T(8,128)(2,1)S(1)}, bf16[2,2,8,640]{3,2,0,1:T(8,128)(2,1)S(1)}, u32[]{:S(2)}, u32[]{:S(2)}) collective-permute-start(bf16[2,2,8,640]{3,2,0,1:T(8,128)(2,1)S(1)} %pad_maximum_fusion.24), channel_id=1, source_target_pairs={{0,8},{4,12},{8,0},{12,4},{16,24},{20,28},{24,16},{28,20},{32,40},... | collective-permute-start | bytes 122888 | tf_op jit(solution)/shard_map/ppermute | solution.py:81
  257.8 6.3 %collective-permute-start.12 = (bf16[2,4,8,640]{3,2,0,1:T(8,128)(2,1)S(1)}, bf16[2,4,8,640]{3,2,0,1:T(8,128)(2,1)S(1)}, u32[]{:S(2)}, u32[]{:S(2)}) collective-permute-start(bf16[2,4,8,640]{3,2,0,1:T(8,128)(2,1)S(1)} %pad_maximum_fusion.22), channel_id=1, source_target_pairs={{0,4},{4,0},{8,12},{12,8},{16,20},{20,16},{24,28},{28,24},{32,36},... | collective-permute-start | bytes 245768 | tf_op jit(solution)/shard_map/ppermute | solution.py:81
  264.9 16.3 %collective-permute-start.15 = (bf16[2,8,8,640]{3,2,0,1:T(8,128)(2,1)S(1)}, bf16[2,8,8,640]{3,2,0,1:T(8,128)(2,1)S(1)}, u32[]{:S(2)}, u32[]{:S(2)}) collective-permute-start(bf16[2,8,8,640]{3,2,0,1:T(8,128)(2,1)S(1)} %pad_maximum_fusion.20), channel_id=1, source_target_pairs={{0,96},{4,100},{8,104},{12,108},{16,112},{20,116},{24,120},{28,124... | collective-permute-start | bytes 491528 | tf_op jit(solution)/shard_map/ppermute | solution.py:81
  269.6 10.8 %collective-permute-start.14 = (bf16[2,8,8,640]{3,2,0,1:T(8,128)(2,1)S(1)}, bf16[2,8,8,640]{3,2,0,1:T(8,128)(2,1)S(1)}, u32[]{:S(2)}, u32[]{:S(2)}) collective-permute-start(bf16[2,8,8,640]{3,2,0,1:T(8,128)(2,1)S(1)} %pad_maximum_fusion.20), channel_id=1, source_target_pairs={{0,64},{4,68},{8,72},{12,76},{16,80},{20,84},{24,88},{28,92},{32,9... | collective-permute-start | bytes 491528 | tf_op jit(solution)/shard_map/ppermute | solution.py:81
  271.5 8.1 %collective-permute-start.13 = (bf16[2,8,8,640]{3,2,0,1:T(8,128)(2,1)S(1)}, bf16[2,8,8,640]{3,2,0,1:T(8,128)(2,1)S(1)}, u32[]{:S(2)}, u32[]{:S(2)}) collective-permute-start(bf16[2,8,8,640]{3,2,0,1:T(8,128)(2,1)S(1)} %pad_maximum_fusion.20), channel_id=1, source_target_pairs={{0,32},{4,36},{8,40},{12,44},{16,48},{20,52},{24,56},{28,60},{32,0... | collective-permute-start | bytes 491528 | tf_op jit(solution)/shard_map/ppermute | solution.py:81
  281.9 17.3 %collective-permute-start.16 = (bf16[2,32,8,640]{3,2,0,1:T(8,128)(2,1)}, bf16[2,32,8,640]{3,2,0,1:T(8,128)(2,1)}, u32[]{:S(2)}, u32[]{:S(2)}) collective-permute-start(bf16[2,32,8,640]{3,2,0,1:T(8,128)(2,1)} %get-tuple-element.49), channel_id=1, source_target_pairs={{0,128},{4,132},{8,136},{12,140},{16,144},{20,148},{24,152},{28,15... | collective-permute-start | bytes 1966088 | tf_op jit(solution)/shard_map/ppermute | solution.py:81
  305.2 25.8 %collective-permute-start.17 = (bf16[64,8,640]{2,1,0:T(8,128)(2,1)}, bf16[64,8,640]{2,1,0:T(8,128)(2,1)}, u32[]{:S(2)}, u32[]{:S(2)}) collective-permute-start(bf16[64,8,640]{2,1,0:T(8,128)(2,1)} %slice_bitcast_fusion), channel_id=1, source_target_pairs={{0,256},{4,260},{8,264},{12,268},{16,272},{20,276},{24,280},{28,28... | collective-permute-start | bytes 1966088 | tf_op jit(solution)/shard_map/ppermute | solution.py:16
  309.6 5.6 %copy-start.3 = (bf16[1024,8,64]{0,2,1:T(8,128)(2,1)S(1)}, bf16[1024,8,64]{0,2,1:T(8,128)(2,1)}, u32[]{:S(2)}) copy-start(bf16[1024,8,64]{0,2,1:T(8,128)(2,1)} %copy.818) | copy-start | bytes 3145732
  309.6 5.6 %copy-start.38 = (bf16[16,8,64]{2,1,0:T(8,128)(2,1)S(1)}, bf16[16,8,64]{2,1,0:T(8,128)(2,1)}, u32[]{:S(2)}) copy-start(bf16[16,8,64]{2,1,0:T(8,128)(2,1)} %reshape_reshape_squeeze_stack.11) | copy-start | bytes 49156
  312.8 13.3 %collective-permute-start.19 = (f32[2,2,2,2,2,2,2,1024]{7,6,5,4,3,2,1,0:T(2,128)}, f32[2,2,2,2,2,2,2,1024]{7,6,5,4,3,2,1,0:T(2,128)}, u32[]{:S(2)}, u32[]{:S(2)}) collective-permute-start(f32[2,2,2,2,2,2,2,1024]{7,6,5,4,3,2,1,0:T(2,128)} %dynamic-slice_bitcast_fusion), channel_id=1, source_target_pairs={{0,4},{1,5},{2,6},{3,7},{4,0},{5,1},{6,2},{7,3},{8,12},{9,13},{10,... | collective-permute-start | bytes 1572872 | tf_op jit(solution)/shard_map/ppermute | solution.py:125
  321.7 4.4 %copy-start.9 = (f32[2,2,2,2,2,2,2,2,1024]{8,7,6,5,4,3,2,1,0:T(2,128)S(1)}, f32[2,2,2,2,2,2,2,2,1024]{8,7,6,5,4,3,2,1,0:T(2,128)}, u32[]{:S(2)}) copy-start(f32[2,2,2,2,2,2,2,2,1024]{8,7,6,5,4,3,2,1,0:T(2,128)} %copy-done.8) | copy-start | bytes 3145732
  328.2 8.6 %collective-permute-start.20 = (f32[2,2,2,2,2,2,1024]{6,5,4,3,2,1,0:T(2,128)}, f32[2,2,2,2,2,2,1024]{6,5,4,3,2,1,0:T(2,128)}, u32[]{:S(2)}, u32[]{:S(2)}) collective-permute-start(f32[2,2,2,2,2,2,1024]{6,5,4,3,2,1,0:T(2,128)} %dynamic-slice_bitcast_fusion.1), channel_id=1, source_target_pairs={{0,32},{1,33},{2,34},{3,35},{4,36},{5,37},{6,38},{7,39},{8,40},{9,... | collective-permute-start | bytes 786440 | tf_op jit(solution)/shard_map/ppermute | solution.py:125
  333.7 7.2 %copy-start.30 = (f32[1024,40]{0,1:T(8,128)S(1)}, f32[1024,40]{0,1:T(8,128)}, u32[]{:S(2)}) copy-start(f32[1024,40]{0,1:T(8,128)} %copy.824) | copy-start | bytes 491524
  335.3 12.1 %copy-start.47 = (bf16[8,8,64]{2,1,0:T(8,128)(2,1)S(1)}, bf16[8,8,64]{2,1,0:T(8,128)(2,1)}, u32[]{:S(2)}) copy-start(bf16[8,8,64]{2,1,0:T(8,128)(2,1)} %reshape_squeeze.30) | copy-start | bytes 24580
  337.9 6.9 %collective-permute-start.21 = (f32[2,2,2,2,2,1024]{5,4,3,2,1,0:T(2,128)S(1)}, f32[2,2,2,2,2,1024]{5,4,3,2,1,0:T(2,128)S(1)}, u32[]{:S(2)}, u32[]{:S(2)}) collective-permute-start(f32[2,2,2,2,2,1024]{5,4,3,2,1,0:T(2,128)S(1)} %dynamic-slice_bitcast_fusion.2), channel_id=1, source_target_pairs={{0,128},{1,129},{2,130},{3,131},{4,132},{5,133},{6,134},{7,135},{8... | collective-permute-start | bytes 393224 | tf_op jit(solution)/shard_map/ppermute | solution.py:125
  344.9 7.6 %collective-permute-start.22 = (f32[2,2,2,2,1024]{4,3,2,1,0:T(2,128)S(1)}, f32[2,2,2,2,1024]{4,3,2,1,0:T(2,128)S(1)}, u32[]{:S(2)}, u32[]{:S(2)}) collective-permute-start(f32[2,2,2,2,1024]{4,3,2,1,0:T(2,128)S(1)} %dynamic-slice_bitcast_fusion.3), channel_id=1, source_target_pairs={{0,8},{1,9},{2,10},{3,11},{4,12},{5,13},{6,14},{7,15},{8,0},{9,1},... | collective-permute-start | bytes 196616 | tf_op jit(solution)/shard_map/ppermute | solution.py:125
  353.2 7.6 %collective-permute-start.23 = (f32[2,2,2,1024]{3,2,1,0:T(2,128)}, f32[2,2,2,1024]{3,2,1,0:T(2,128)}, u32[]{:S(2)}, u32[]{:S(2)}) collective-permute-start(f32[2,2,2,1024]{3,2,1,0:T(2,128)} %dynamic-slice_bitcast_fusion.4), channel_id=1, source_target_pairs={{0,64},{1,65},{2,66},{3,67},{4,68},{5,69},{6,70},{7,71},{8,72},{9,... | collective-permute-start | bytes 98312 | tf_op jit(solution)/shard_map/ppermute | solution.py:125
  355.8 11.0 %copy-start.41 = (bf16[8,8,64]{2,1,0:T(8,128)(2,1)S(1)}, bf16[8,8,64]{2,1,0:T(8,128)(2,1)}, u32[]{:S(2)}) copy-start(bf16[8,8,64]{2,1,0:T(8,128)(2,1)} %reshape_squeeze.31) | copy-start | bytes 24580
  361.6 5.2 %copy-start.36 = (f32[2,2,2,1024]{3,2,1,0:T(2,128)}, f32[2,2,2,1024]{3,2,1,0:T(2,128)S(1)}, u32[]{:S(2)}) copy-start(f32[2,2,2,1024]{3,2,1,0:T(2,128)S(1)} %bitcast_add_fusion.5) | copy-start | bytes 98308
  362.2 7.4 %collective-permute-start.24 = (f32[2,2,1024]{2,1,0:T(2,128)}, f32[2,2,1024]{2,1,0:T(2,128)}, u32[]{:S(2)}, u32[]{:S(2)}) collective-permute-start(f32[2,2,1024]{2,1,0:T(2,128)} %dynamic-slice_bitcast_fusion.5), channel_id=1, source_target_pairs={{0,256},{1,257},{2,258},{3,259},{4,260},{5,261},{6,262},{7,263},{8... | collective-permute-start | bytes 49160 | tf_op jit(solution)/shard_map/ppermute | solution.py:125
  370.4 9.5 %collective-permute-start.25 = (f32[2,1024]{1,0:T(2,128)S(1)}, f32[2,1024]{1,0:T(2,128)S(1)}, u32[]{:S(2)}, u32[]{:S(2)}) collective-permute-start(f32[2,1024]{1,0:T(2,128)S(1)} %dynamic-slice_bitcast_fusion.6), channel_id=1, source_target_pairs={{0,16},{1,17},{2,18},{3,19},{4,20},{5,21},{6,22},{7,23},{8,24},{9,... | collective-permute-start | bytes 24584 | tf_op jit(solution)/shard_map/ppermute | solution.py:125
  372.7 9.2 %copy-start.23 = (f32[1,128,512]{2,1,0:T(8,128)S(1)}, f32[1,128,512]{2,1,0:T(8,128)}, u32[]{:S(2)}) copy-start(f32[1,128,512]{2,1,0:T(8,128)} %mul.683) | copy-start | bytes 786436
  372.7 9.2 %copy-start.24 = (f32[1,128,512]{2,1,0:T(8,128)S(1)}, f32[1,128,512]{2,1,0:T(8,128)}, u32[]{:S(2)}) copy-start(f32[1,128,512]{2,1,0:T(8,128)} %mul.698) | copy-start | bytes 786436
  372.7 9.2 %copy-start.25 = (f32[1,128,512]{2,1,0:T(8,128)S(1)}, f32[1,128,512]{2,1,0:T(8,128)}, u32[]{:S(2)}) copy-start(f32[1,128,512]{2,1,0:T(8,128)} %mul.723) | copy-start | bytes 786436
  372.7 9.3 %copy-start.26 = (f32[1,128,512]{2,1,0:T(8,128)S(1)}, f32[1,128,512]{2,1,0:T(8,128)}, u32[]{:S(2)}) copy-start(f32[1,128,512]{2,1,0:T(8,128)} %mul.751) | copy-start | bytes 786436
  372.7 9.2 %copy-start.27 = (f32[1,128,512]{2,1,0:T(8,128)S(1)}, f32[1,128,512]{2,1,0:T(8,128)}, u32[]{:S(2)}) copy-start(f32[1,128,512]{2,1,0:T(8,128)} %copy.797) | copy-start | bytes 786436
  372.7 9.2 %copy-start.28 = (f32[1,128,512]{2,1,0:T(8,128)S(1)}, f32[1,128,512]{2,1,0:T(8,128)}, u32[]{:S(2)}) copy-start(f32[1,128,512]{2,1,0:T(8,128)} %copy.804) | copy-start | bytes 786436
  372.7 9.2 %copy-start.29 = (f32[1,128,512]{2,1,0:T(8,128)S(1)}, f32[1,128,512]{2,1,0:T(8,128)}, u32[]{:S(2)}) copy-start(f32[1,128,512]{2,1,0:T(8,128)} %copy.798) | copy-start | bytes 786436
  379.9 15.0 %copy-start.1 = (bf16[512,1024]{1,0:T(8,128)(2,1)S(1)}, bf16[512,1024]{1,0:T(8,128)(2,1)}, u32[]{:S(2)}) copy-start(bf16[512,1024]{1,0:T(8,128)(2,1)} %param.33) | copy-start | bytes 3145732
  379.9 14.3 %collective-permute-start.26 = (f32[1024]{0:T(1024)S(1)}, f32[1024]{0:T(1024)S(1)}, u32[]{:S(2)}, u32[]{:S(2)}) collective-permute-start(f32[1024]{0:T(1024)S(1)} %bitcast.402), channel_id=1, source_target_pairs={{0,2},{1,3},{2,0},{3,1},{4,6},{5,7},{6,4},{7,5},{8,10},{9,11},{10,... | collective-permute-start | bytes 12296 | tf_op jit(solution)/shard_map/ppermute | solution.py:125
  (26 other events, 63.8 us)

commit v4 on v1

--- a/solution.py
+++ b/solution.py
@@ -77,6 +77,21 @@
     return block
 
 
+def gather_with_rider(block, axis_pos, bit_order, rider):
+    lanes = block.shape[-1]
+    for bit_pos in bit_order:
+        if bit_pos == 0:
+            rows = block.size // lanes
+            message = jnp.concatenate([block.reshape(rows, lanes), rider.reshape(-1, lanes)], 0)
+            got = partner(message, "tm", bit_pos)
+            other = got[:rows].reshape(block.shape)
+            rider_back = got[rows:].reshape(rider.shape)
+        else:
+            other = partner(block, "tm", bit_pos)
+        block = jnp.concatenate([block, other], axis_pos)
+    return block, rider_back
+
+
 def split_exact(values):
     high = lax.reduce_precision(values, exponent_bits=8, mantissa_bits=7)
     rest = values - high
@@ -216,16 +231,16 @@
     low_bits = sorted(range(top_bit), key=lambda b: near_first.get(b, b))
     wide = features + 128
 
-    other_qkv = partner(jnp.stack([queries, keys_all, values_all], 0), "tm", 0)
+    qkv = jnp.stack([by_parity(pick_rows(m, R2)) for m in (queries, keys_all, values_all)], 0)
+    per_par = qkv.shape[2]
+    own, other_qkv = gather_with_rider(
+        qkv[:, :, None], 2, low_bits, jnp.stack([queries, keys_all, values_all], 0)
+    )
+    far = partner(own[:, 0], "tm", top_bit)
     other_q = other_qkv[0]
     keys_one = jnp.concatenate([keys_all, other_qkv[1]], 0)
     values_one = jnp.concatenate([values_all, other_qkv[2]], 0)
     part_one, lse_one = attend(queries, keys_one, values_one, inv_root)
-
-    qkv = jnp.stack([by_parity(pick_rows(m, R2)) for m in (queries, keys_all, values_all)], 0)
-    per_par = qkv.shape[2]
-    own = gather_blocks(qkv[:, :, None], 2, low_bits)
-    far = partner(own[:, 0], "tm", top_bit)
     q_seg2 = own[0].reshape(-1, features)
     k_seg2 = own[1].reshape(-1, features)
     v_seg2 = own[2].reshape(-1, features)
@@ -270,22 +285,6 @@
     grad_one = grad_of(weights[0], grad_attn)
     offset_one = weights[0] * rowdot
     packed_one = jnp.concatenate([grad_one, split_exact(jnp.concatenate([lse_one, offset_one], 1))], 1)
-    other_one = partner(pad_lanes(packed_one, wide), "tm", 0)
-    other_stats = join_exact(other_one[:, features : features + 6 * HEADS])
-    total_q = spread_rows(
-        near_grad(queries, keys_one, values_one, grad_one, lse_one, offset_one, inv_root), 1
-    )
-    k_g1, v_g1 = far_grad(
-        jnp.concatenate([queries, other_q], 0),
-        jnp.concatenate([grad_one, other_one[:, :features]], 0),
-        jnp.concatenate([lse_one, other_stats[:, :HEADS]], 0),
-        jnp.concatenate([offset_one, other_stats[:, HEADS:]], 0),
-        keys_all,
-        values_all,
-        inv_root,
-    )
-    total_k = spread_rows(k_g1, 1)
-    total_v = spread_rows(v_g1, 1)
 
     ga_par = by_parity(pick_rows(grad_attn, R2))
     w_two = by_parity(pick_stats(weights[1], R2))
@@ -297,7 +296,22 @@
     w3_par = jnp.stack([w_three, no_level], 0)
     stats_par = jnp.concatenate([lse_two_par, w_two, lse3_par, w3_par, rd_two], -1)
     packed = pad_lanes(jnp.concatenate([ga_par, split_exact(stats_par)], -1), wide)
-    own_b = gather_blocks(packed[:, None], 1, low_bits)
+    own_b, other_one = gather_with_rider(packed[:, None], 1, low_bits, pad_lanes(packed_one, wide))
+    other_stats = join_exact(other_one[:, features : features + 6 * HEADS])
+    total_q = spread_rows(
+        near_grad(queries, keys_one, values_one, grad_one, lse_one, offset_one, inv_root), 1
+    )
+    k_g1, v_g1 = far_grad(
+        jnp.concatenate([queries, other_q], 0),
+        jnp.concatenate([grad_one, other_one[:, :features]], 0),
+        jnp.concatenate([lse_one, other_stats[:, :HEADS]], 0),
+        jnp.concatenate([offset_one, other_stats[:, HEADS:]], 0),
+        keys_all,
+        values_all,
+        inv_root,
+    )
+    total_k = spread_rows(k_g1, 1)
+    total_v = spread_rows(v_g1, 1)
     far_b = partner(own_b[0], "tm", top_bit)
     stat_w = 5 * HEADS
 

time: 389 us -> 381 us (0.979)
  local copies, waits for them, and re-layouts: 132 us -> 117 us
  waiting for transfers between devices: 94.1 us -> 108 us
  starting transfers between devices: 93.6 us -> 89.5 us
    ppermute x16 -> x14, waiting for transfers between devices: 67.2 us -> 81.1 us  [partner(): return lax.ppermute(value, axis, pairs)]
    ppermute x16 -> x14, starting transfers between devices: 67.8 us -> 64.5 us  [partner(): return lax.ppermute(value, axis, pairs)]
    unnamed x114 -> x139, local copies, waits for them, and re-layouts: 15 us -> 15.3 us
  transfers between devices with their start and end apart: 25 -> 23, of which waited for: 17 -> 18; matrix products, arithmetic and copies ran while one was open for 33% -> 27% of each run, Pallas kernels for 0% -> 0%
where the time goes in v4:
time: 381 us; the launch traced here: 378 us
  local copies, waits for them, and re-layouts  117 us (31%)
  waiting for transfers between devices  108 us (28%)
  starting transfers between devices  89.5 us (23%)
  other arithmetic  34.2 us (9%)
  matrix products  27 us (7%)
    ppermute x14, waiting for transfers between devices, partner(): return lax.ppermute(value, axis, pairs)  81.1 us
    ppermute x14, starting transfers between devices, partner(): return lax.ppermute(value, axis, pairs)  64.5 us
    another operation x18, local copies, waits for them, and re-layouts, heads_view(): return matrix.reshape(matrix.shape[0], HEADS, HD)  37.9 us
    ppermute x9, waiting for transfers between devices, scatter_sum(): block = keep + lax.ppermute(send, axes, pairs)  27.2 us
    ppermute x9, starting transfers between devices, scatter_sum(): block = keep + lax.ppermute(send, axes, pairs)  24.9 us
    unnamed x139, local copies, waits for them, and re-layouts  15.3 us
    mul x26, local copies, waits for them, and re-layouts, spread_rows(): values[:, None] * chooser  14.3 us
  transfers between devices with their start and end apart: 23, of which 18 were waited for; matrix products, arithmetic and copies ran while one was open for 27% of the time, Pallas kernels for 0%

profile of v4, /device:TPU:6, one launch (start us, length us, event | category | flops | bytes accessed | tf_op | source)
XLA Modules:
  0.0 378.1 jit_solution(16134627524191614090)
XLA Ops:
  5.1 9.1 %collective-permute-start = (bf16[3,2,1,8,512]{4,3,1,0,2:T(8,128)(2,1)S(1)}, bf16[3,2,1,8,512]{4,3,1,0,2:T(8,128)(2,1)S(1)}, u32[]{:S(2)}, u32[]{:S(2)}) collective-permute-start(bf16[3,2,1,8,512]{4,3,1,0,2:T(8,128)(2,1)S(1)} %bitcast.382), channel_id=1, source_target_pairs={{0,16},{4,20},{8,24},{12,28},{16,0},{20,4},{24,8},{28,12},{32,48},... | collective-permute-start | bytes 147464 | tf_op jit(solution)/shard_map/ppermute | solution.py:16
  14.2 2.1 collective-permute-done
  16.3 5.3 %collective-permute-start.1 = (bf16[3,2,2,8,512]{4,3,1,0,2:T(8,128)(2,1)S(1)}, bf16[3,2,2,8,512]{4,3,1,0,2:T(8,128)(2,1)S(1)}, u32[]{:S(2)}, u32[]{:S(2)}) collective-permute-start(bf16[3,2,2,8,512]{4,3,1,0,2:T(8,128)(2,1)S(1)} %pad_maximum_fusion.23), channel_id=1, source_target_pairs={{0,8},{4,12},{8,0},{12,4},{16,24},{20,28},{24,16},{28,20},{32,40},... | collective-permute-start | bytes 294920 | tf_op jit(solution)/shard_map/ppermute | solution.py:16
  21.6 5.0 %collective-permute-done.1 = bf16[3,2,2,8,512]{4,3,1,0,2:T(8,128)(2,1)S(1)} collective-permute-done((bf16[3,2,2,8,512]{4,3,1,0,2:T(8,128)(2,1)S(1)}, bf16[3,2,2,8,512]{4,3,1,0,2:T(8,128)(2,1)S(1)}, u32[]{:S(2)}, u32[]{:S(2)}) %collective-permute-start.1) | collective-permute-done | bytes 98336 | tf_op jit(solution)/shard_map/ppermute | solution.py:16
  26.7 3.3 collective-permute-start.2
  30.1 5.7 %collective-permute-done.2 = bf16[3,2,4,8,512]{4,3,1,0,2:T(8,128)(2,1)S(1)} collective-permute-done((bf16[3,2,4,8,512]{4,3,1,0,2:T(8,128)(2,1)S(1)}, bf16[3,2,4,8,512]{4,3,1,0,2:T(8,128)(2,1)S(1)}, u32[]{:S(2)}, u32[]{:S(2)}) %collective-permute-start.2) | collective-permute-done | bytes 196640 | tf_op jit(solution)/shard_map/ppermute | solution.py:16
  35.9 3.8 collective-permute-start.3
  42.6 14.0 %collective-permute-done.3 = bf16[768,512]{1,0:T(8,128)(2,1)S(1)} collective-permute-done((bf16[768,512]{1,0:T(8,128)(2,1)S(1)}, bf16[768,512]{1,0:T(8,128)(2,1)S(1)}, u32[]{:S(2)}, u32[]{:S(2)}) %collective-permute-start.3) | collective-permute-done | bytes 786464 | tf_op jit(solution)/shard_map/ppermute | solution.py:16
  57.6 2.9 collective-permute-start.4
  60.4 17.0 %collective-permute-done.4 = bf16[3,2,16,8,512]{4,3,2,1,0:T(8,128)(2,1)S(1)} collective-permute-done((bf16[3,2,16,8,512]{4,3,2,1,0:T(8,128)(2,1)S(1)}, bf16[3,2,16,8,512]{4,3,2,1,0:T(8,128)(2,1)S(1)}, u32[]{:S(2)}, u32[]{:S(2)}) %collective-permute-start.4) | collective-permute-done | bytes 786464 | tf_op jit(solution)/shard_map/ppermute | solution.py:16
  78.7 3.5 collective-permute-start.5
  93.9 20.8 %collective-permute-done.5 = bf16[3,2,32,8,512]{4,3,2,1,0:T(8,128)(2,1)} collective-permute-done((bf16[3,2,32,8,512]{4,3,2,1,0:T(8,128)(2,1)}, bf16[3,2,32,8,512]{4,3,2,1,0:T(8,128)(2,1)}, u32[]{:S(2)}, u32[]{:S(2)}) %collective-permute-start.5) | collective-permute-done | bytes 1572896 | tf_op jit(solution)/shard_map/ppermute | solution.py:16
  114.7 2.8 constant_dynamic-update-slice_fusion.9
  117.5 2.7 slice_bitcast_fusion
  120.2 5.3 %collective-permute-start.6 = (bf16[3,64,8,512]{3,2,1,0:T(8,128)(2,1)}, bf16[3,64,8,512]{3,2,1,0:T(8,128)(2,1)}, u32[]{:S(2)}, u32[]{:S(2)}) collective-permute-start(bf16[3,64,8,512]{3,2,1,0:T(8,128)(2,1)} %slice_bitcast_fusion), channel_id=1, source_target_pairs={{0,256},{4,260},{8,264},{12,268},{16,272},{20,276},{24,280},{28,28... | collective-permute-start | bytes 4718600 | tf_op jit(solution)/shard_map/ppermute | solution.py:16
  125.5 3.5 fusion.133
  129.0 2.1 reshape_reshape_squeeze.6
  131.0 2.5 copy.1008
  133.6 4.2 %reshape_reshape_squeeze.14 = bf16[1024,8,64]{2,1,0:T(8,128)(2,1)} reshape(bf16[1,2,64,8,512]{4,3,2,1,0:T(8,128)(2,1)} %get-tuple-element.19) | data formatting | bytes 2097152 | tf_op jit(solution)/shard_map/reshape;reshape;squeeze | solution.py:140
  137.7 3.3 copy.1017
  146.4 3.9 %reshape_reshape_squeeze.15 = bf16[1024,8,64]{2,1,0:T(8,128)(2,1)} reshape(bf16[1,2,64,8,512]{4,3,2,1,0:T(8,128)(2,1)} %get-tuple-element.18) | data formatting | bytes 2097152 | tf_op jit(solution)/shard_map/reshape;reshape;squeeze | solution.py:140
  150.2 3.3 copy.1075
  153.6 2.3 slice_bitcast_fusion.3
  156.7 2.3 slice_bitcast_fusion.2
  160.2 2.1 reshape_reshape.28
  162.3 2.5 copy.1013
  169.5 3.9 %reshape_reshape.29 = bf16[1024,8,64]{2,1,0:T(8,128)(2,1)} reshape(bf16[128,8,512]{2,1,0:T(8,128)(2,1)} %get-tuple-element.101) | data formatting | bytes 2097152 | tf_op jit(solution)/shard_map/reshape;reshape | solution.py:140
  173.3 3.4 copy.1020
  181.2 2.0 copy.1025
  186.5 2.8 fusion.65
  196.5 1.9 fusion.55
  200.2 3.2 constant_dynamic-slice_fusion.3
  205.1 2.0 collective-permute-start.14
  212.9 8.4 %collective-permute-start.7 = (bf16[2,1,8,640]{3,2,0,1:T(8,128)(2,1)}, bf16[2,1,8,640]{3,2,0,1:T(8,128)(2,1)}, u32[]{:S(2)}, u32[]{:S(2)}) collective-permute-start(bf16[2,1,8,640]{3,2,0,1:T(8,128)(2,1)} %fusion.129), channel_id=1, source_target_pairs={{0,16},{4,20},{8,24},{12,28},{16,0},{20,4},{24,8},{28,12},{32,48},... | collective-permute-start | bytes 61448 | tf_op jit(solution)/shard_map/ppermute | solution.py:16
  221.9 3.0 fusion.29
  226.1 2.4 fusion.17
  228.6 2.1 fusion.35
  233.4 5.7 %collective-permute-start.8 = (bf16[2,2,8,640]{3,2,0,1:T(8,128)(2,1)}, bf16[2,2,8,640]{3,2,0,1:T(8,128)(2,1)S(1)}, u32[]{:S(2)}, u32[]{:S(2)}) collective-permute-start(bf16[2,2,8,640]{3,2,0,1:T(8,128)(2,1)} %pad_maximum_fusion.26), channel_id=1, source_target_pairs={{0,8},{4,12},{8,0},{12,4},{16,24},{20,28},{24,16},{28,20},{32,40},... | collective-permute-start | bytes 122888 | tf_op jit(solution)/shard_map/ppermute | solution.py:16
  246.0 3.3 collective-permute-start.9
  250.7 3.2 collective-permute-done.9
  255.8 2.8 collective-permute-start.10
  260.0 6.1 %collective-permute-done.10 = bf16[256,640]{0,1:T(8,128)(2,1)S(1)} collective-permute-done((bf16[256,640]{0,1:T(8,128)(2,1)S(1)}, bf16[256,640]{0,1:T(8,128)(2,1)S(1)}, u32[]{:S(2)}, u32[]{:S(2)}) %collective-permute-start.10) | collective-permute-done | bytes 327712 | tf_op jit(solution)/shard_map/ppermute | solution.py:16
  267.1 2.7 collective-permute-start.11
  274.0 2.8 collective-permute-done.11
  278.7 3.7 collective-permute-start.12
  285.2 2.1 bitcast_add_fusion
  288.2 2.8 collective-permute-start.15
  291.0 3.5 collective-permute-done.12
  302.3 2.7 collective-permute-start.16
  306.7 3.9 %collective-permute-done.16 = f32[2,2,2,2,2,2,1024]{6,5,4,3,2,1,0:T(2,128)S(1)} collective-permute-done((f32[2,2,2,2,2,2,1024]{6,5,4,3,2,1,0:T(2,128)S(1)}, f32[2,2,2,2,2,2,1024]{6,5,4,3,2,1,0:T(2,128)S(1)}, u32[]{:S(2)}, u32[]{:S(2)}) %collective-permute-start.16) | collective-permute-done | bytes 262176 | tf_op jit(solution)/shard_map/ppermute | solution.py:134
  310.8 2.5 collective-permute-start.17
  314.2 3.5 collective-permute-done.17
  317.7 3.9 %collective-permute-start.18 = (f32[2,2,2,2,1024]{4,3,2,1,0:T(2,128)S(1)}, f32[2,2,2,2,1024]{4,3,2,1,0:T(2,128)S(1)}, u32[]{:S(2)}, u32[]{:S(2)}) collective-permute-start(f32[2,2,2,2,1024]{4,3,2,1,0:T(2,128)S(1)} %dynamic-slice_bitcast_fusion.3), channel_id=1, source_target_pairs={{0,8},{1,9},{2,10},{3,11},{4,12},{5,13},{6,14},{7,15},{8,0},{9,1},... | collective-permute-start | bytes 196616 | tf_op jit(solution)/shard_map/ppermute | solution.py:134
  322.4 1.9 copy.1072
  324.4 4.8 %collective-permute-start.13 = (bf16[64,8,640]{2,1,0:T(8,128)(2,1)}, bf16[64,8,640]{2,1,0:T(8,128)(2,1)}, u32[]{:S(2)}, u32[]{:S(2)}) collective-permute-start(bf16[64,8,640]{2,1,0:T(8,128)(2,1)} %slice_bitcast_fusion.1), channel_id=1, source_target_pairs={{0,256},{4,260},{8,264},{12,268},{16,272},{20,276},{24,280},{28,28... | collective-permute-start | bytes 1966088 | tf_op jit(solution)/shard_map/ppermute | solution.py:16
  329.2 3.3 collective-permute-start.19
  332.6 2.3 fusion.11
  336.6 2.6 collective-permute-start.20
  339.9 3.8 collective-permute-done.20
  343.7 3.2 collective-permute-start.21
  348.9 4.3 %collective-permute-done.21 = f32[2,1024]{1,0:T(2,128)S(1)} collective-permute-done((f32[2,1024]{1,0:T(2,128)S(1)}, f32[2,1024]{1,0:T(2,128)S(1)}, u32[]{:S(2)}, u32[]{:S(2)}) %collective-permute-start.21) | collective-permute-done | bytes 8224 | tf_op jit(solution)/shard_map/ppermute | solution.py:134
  358.4 9.0 %collective-permute-done.22 = f32[1024]{0:T(1024)S(1)} collective-permute-done((f32[1024]{0:T(1024)S(1)}, f32[1024]{0:T(1024)S(1)}, u32[]{:S(2)}, u32[]{:S(2)}) %collective-permute-start.22) | collective-permute-done | bytes 4128 | tf_op jit(solution)/shard_map/ppermute | solution.py:134
  371.5 1.9 copy.1082
  375.9 2.2 add_convert_fusion
  (334 shorter events, 111.3 us)
Async XLA Ops:
  0.6 3.7 copy-start.62
  0.7 3.3 copy-start.16
  5.1 11.2 %collective-permute-start = (bf16[3,2,1,8,512]{4,3,1,0,2:T(8,128)(2,1)S(1)}, bf16[3,2,1,8,512]{4,3,1,0,2:T(8,128)(2,1)S(1)}, u32[]{:S(2)}, u32[]{:S(2)}) collective-permute-start(bf16[3,2,1,8,512]{4,3,1,0,2:T(8,128)(2,1)S(1)} %bitcast.382), channel_id=1, source_target_pairs={{0,16},{4,20},{8,24},{12,28},{16,0},{20,4},{24,8},{28,12},{32,48},... | collective-permute-start | bytes 147464 | tf_op jit(solution)/shard_map/ppermute | solution.py:16
  16.3 10.4 %collective-permute-start.1 = (bf16[3,2,2,8,512]{4,3,1,0,2:T(8,128)(2,1)S(1)}, bf16[3,2,2,8,512]{4,3,1,0,2:T(8,128)(2,1)S(1)}, u32[]{:S(2)}, u32[]{:S(2)}) collective-permute-start(bf16[3,2,2,8,512]{4,3,1,0,2:T(8,128)(2,1)S(1)} %pad_maximum_fusion.23), channel_id=1, source_target_pairs={{0,8},{4,12},{8,0},{12,4},{16,24},{20,28},{24,16},{28,20},{32,40},... | collective-permute-start | bytes 294920 | tf_op jit(solution)/shard_map/ppermute | solution.py:16
  26.7 9.1 %collective-permute-start.2 = (bf16[3,2,4,8,512]{4,3,1,0,2:T(8,128)(2,1)S(1)}, bf16[3,2,4,8,512]{4,3,1,0,2:T(8,128)(2,1)S(1)}, u32[]{:S(2)}, u32[]{:S(2)}) collective-permute-start(bf16[3,2,4,8,512]{4,3,1,0,2:T(8,128)(2,1)S(1)} %pad_maximum_fusion.11), channel_id=1, source_target_pairs={{0,64},{4,68},{8,72},{12,76},{16,80},{20,84},{24,88},{28,92},{32,9... | collective-permute-start | bytes 589832 | tf_op jit(solution)/shard_map/ppermute | solution.py:16
  35.9 20.6 %collective-permute-start.3 = (bf16[768,512]{1,0:T(8,128)(2,1)S(1)}, bf16[768,512]{1,0:T(8,128)(2,1)S(1)}, u32[]{:S(2)}, u32[]{:S(2)}) collective-permute-start(bf16[768,512]{1,0:T(8,128)(2,1)S(1)} %pad_maximum_fusion.3), channel_id=1, source_target_pairs={{0,4},{4,0},{8,12},{12,8},{16,20},{20,16},{24,28},{28,24},{32,36},... | collective-permute-start | bytes 2359304 | tf_op jit(solution)/shard_map/ppermute | solution.py:16
  57.6 27.1 %copy-start.49 = (f32[8,8]{0,1:T(8,128)S(1)}, f32[8,8]{0,1:T(8,128)}, u32[]{:S(2)}) copy-start(f32[8,8]{0,1:T(8,128)} %constant.249.clone) | copy-start | bytes 772
  57.6 27.2 %copy-start.48 = (f32[16,8]{0,1:T(8,128)S(1)}, f32[16,8]{0,1:T(8,128)}, u32[]{:S(2)}) copy-start(f32[16,8]{0,1:T(8,128)} %constant.250.clone) | copy-start | bytes 1540
  57.6 19.8 %collective-permute-start.4 = (bf16[3,2,16,8,512]{4,3,2,1,0:T(8,128)(2,1)S(1)}, bf16[3,2,16,8,512]{4,3,2,1,0:T(8,128)(2,1)S(1)}, u32[]{:S(2)}, u32[]{:S(2)}) collective-permute-start(bf16[3,2,16,8,512]{4,3,2,1,0:T(8,128)(2,1)S(1)} %get-tuple-element.39), channel_id=1, source_target_pairs={{0,32},{4,36},{8,40},{12,44},{16,48},{20,52},{24,56},{28,60},{32,0... | collective-permute-start | bytes 2359304 | tf_op jit(solution)/shard_map/ppermute | solution.py:16
  78.7 36.0 %collective-permute-start.5 = (bf16[3,2,32,8,512]{4,3,2,1,0:T(8,128)(2,1)}, bf16[3,2,32,8,512]{4,3,2,1,0:T(8,128)(2,1)}, u32[]{:S(2)}, u32[]{:S(2)}) collective-permute-start(bf16[3,2,32,8,512]{4,3,2,1,0:T(8,128)(2,1)} %get-tuple-element.32), channel_id=1, source_target_pairs={{0,128},{4,132},{8,136},{12,140},{16,144},{20,148},{24,152},{28,15... | collective-permute-start | bytes 4718600 | tf_op jit(solution)/shard_map/ppermute | solution.py:16
  82.3 10.4 %copy-start.21 = (bf16[1,128,512]{1,2,0:T(8,128)(2,1)}, bf16[1,128,512]{1,2,0:T(8,128)(2,1)S(1)}, u32[]{:S(2)}) copy-start(bf16[1,128,512]{1,2,0:T(8,128)(2,1)S(1)} %copy.989) | copy-start | bytes 393220
  82.5 10.3 %copy-start.14 = (bf16[1,128,512]{1,2,0:T(8,128)(2,1)}, bf16[1,128,512]{1,2,0:T(8,128)(2,1)S(1)}, u32[]{:S(2)}) copy-start(bf16[1,128,512]{1,2,0:T(8,128)(2,1)S(1)} %copy.993) | copy-start | bytes 393220
  84.8 6.2 %copy-start.41 = (f32[128,8]{0,1:T(8,128)}, f32[128,8]{0,1:T(8,128)S(1)}, u32[]{:S(2)}) copy-start(f32[128,8]{0,1:T(8,128)S(1)} %mul.636) | copy-start | bytes 12292
  84.9 6.1 %copy-start.42 = (f32[128,8]{0,1:T(8,128)}, f32[128,8]{0,1:T(8,128)S(1)}, u32[]{:S(2)}) copy-start(f32[128,8]{0,1:T(8,128)S(1)} %mul.646) | copy-start | bytes 12292
  91.2 26.2 %copy-start.29 = (bf16[128,512]{0,1:T(8,128)(2,1)}, bf16[128,512]{0,1:T(8,128)(2,1)S(1)}, u32[]{:S(2)}) copy-start(bf16[128,512]{0,1:T(8,128)(2,1)S(1)} %copy.992) | copy-start | bytes 393220
  93.1 24.3 %copy-start.47 = (f32[8,128]{1,0:T(8,128)}, f32[8,128]{1,0:T(8,128)S(1)}, u32[]{:S(2)}) copy-start(f32[8,128]{1,0:T(8,128)S(1)} %get-tuple-element.97) | copy-start | bytes 12292
  120.2 36.5 %collective-permute-start.6 = (bf16[3,64,8,512]{3,2,1,0:T(8,128)(2,1)}, bf16[3,64,8,512]{3,2,1,0:T(8,128)(2,1)}, u32[]{:S(2)}, u32[]{:S(2)}) collective-permute-start(bf16[3,64,8,512]{3,2,1,0:T(8,128)(2,1)} %slice_bitcast_fusion), channel_id=1, source_target_pairs={{0,256},{4,260},{8,264},{12,268},{16,272},{20,276},{24,280},{28,28... | collective-permute-start | bytes 4718600 | tf_op jit(solution)/shard_map/ppermute | solution.py:16
  133.6 7.5 %copy-start.3 = (bf16[1024,8,64]{0,2,1:T(8,128)(2,1)}, bf16[1024,8,64]{0,2,1:T(8,128)(2,1)S(1)}, u32[]{:S(2)}) copy-start(bf16[1024,8,64]{0,2,1:T(8,128)(2,1)S(1)} %copy.1008) | copy-start | bytes 3145732
  137.7 3.3 copy-start.38
  142.3 4.1 %copy-start.43 = (f32[8,16]{1,0:T(8,128)}, f32[8,16]{1,0:T(8,128)S(1)}, u32[]{:S(2)}) copy-start(f32[8,16]{1,0:T(8,128)S(1)} %log_add_fusion.1) | copy-start | bytes 1540
  203.4 3.7 copy-start.32
  203.4 3.7 copy-start.33
  203.5 3.7 copy-start.51
  205.1 21.1 %copy-start.19 = (bf16[1,128,512]{1,2,0:T(8,128)(2,1)S(1)}, bf16[1,128,512]{1,2,0:T(8,128)(2,1)}, u32[]{:S(2)}) copy-start(bf16[1,128,512]{1,2,0:T(8,128)(2,1)} %copy.1014) | copy-start | bytes 393220
  205.1 80.1 %collective-permute-start.14 = (f32[2,2,2,2,2,2,2,2,1024]{8,7,6,5,4,3,2,1,0:T(2,128)}, f32[2,2,2,2,2,2,2,2,1024]{8,7,6,5,4,3,2,1,0:T(2,128)}, u32[]{:S(2)}, u32[]{:S(2)}) collective-permute-start(f32[2,2,2,2,2,2,2,2,1024]{8,7,6,5,4,3,2,1,0:T(2,128)} %bitcast.348), channel_id=1, source_target_pairs={{0,1},{1,0},{2,3},{3,2},{4,5},{5,4},{6,7},{7,6},{8,9},{9,8},{10,11... | collective-permute-start | bytes 3145736 | tf_op jit(solution)/shard_map/ppermute | solution.py:134
  210.0 11.2 %copy-start.45 = (f32[8,8]{0,1:T(8,128)}, f32[8,8]{0,1:T(8,128)S(1)}, u32[]{:S(2)}) copy-start(f32[8,8]{0,1:T(8,128)S(1)} %multiply_reduce_fusion.6) | copy-start | bytes 772
  212.2 9.1 %copy-start.52 = (bf16[2,8,40]{2,1,0:T(8,128)(2,1)}, bf16[2,8,40]{2,1,0:T(8,128)(2,1)S(1)}, u32[]{:S(2)}) copy-start(bf16[2,8,40]{2,1,0:T(8,128)(2,1)S(1)} %get-tuple-element.84) | copy-start | bytes 3844
  212.2 9.1 %copy-start.54 = (bf16[2,8,40]{2,1,0:T(8,128)(2,1)}, bf16[2,8,40]{2,1,0:T(8,128)(2,1)S(1)}, u32[]{:S(2)}) copy-start(bf16[2,8,40]{2,1,0:T(8,128)(2,1)S(1)} %get-tuple-element.85) | copy-start | bytes 3844
  212.2 9.1 %copy-start.56 = (bf16[2,8,40]{2,1,0:T(8,128)(2,1)}, bf16[2,8,40]{2,1,0:T(8,128)(2,1)S(1)}, u32[]{:S(2)}) copy-start(bf16[2,8,40]{2,1,0:T(8,128)(2,1)S(1)} %get-tuple-element.86) | copy-start | bytes 3844
  212.9 19.1 %collective-permute-start.7 = (bf16[2,1,8,640]{3,2,0,1:T(8,128)(2,1)}, bf16[2,1,8,640]{3,2,0,1:T(8,128)(2,1)}, u32[]{:S(2)}, u32[]{:S(2)}) collective-permute-start(bf16[2,1,8,640]{3,2,0,1:T(8,128)(2,1)} %fusion.129), channel_id=1, source_target_pairs={{0,16},{4,20},{8,24},{12,28},{16,0},{20,4},{24,8},{28,12},{32,48},... | collective-permute-start | bytes 61448 | tf_op jit(solution)/shard_map/ppermute | solution.py:16
  221.9 6.7 %copy-start.2 = (bf16[1024,8,64]{0,2,1:T(8,128)(2,1)S(1)}, bf16[1024,8,64]{0,2,1:T(8,128)(2,1)}, u32[]{:S(2)}) copy-start(bf16[1024,8,64]{0,2,1:T(8,128)(2,1)} %copy.1020) | copy-start | bytes 3145732
  230.6 8.5 %copy-start.53 = (bf16[2,8,40]{2,1,0:T(8,128)(2,1)S(1)}, bf16[2,8,40]{2,1,0:T(8,128)(2,1)}, u32[]{:S(2)}) copy-start(bf16[2,8,40]{2,1,0:T(8,128)(2,1)} %copy-done.52) | copy-start | bytes 3844
  230.6 8.5 %copy-start.55 = (bf16[2,8,40]{2,1,0:T(8,128)(2,1)S(1)}, bf16[2,8,40]{2,1,0:T(8,128)(2,1)}, u32[]{:S(2)}) copy-start(bf16[2,8,40]{2,1,0:T(8,128)(2,1)} %copy-done.54) | copy-start | bytes 3844
  230.6 8.5 %copy-start.57 = (bf16[2,8,40]{2,1,0:T(8,128)(2,1)S(1)}, bf16[2,8,40]{2,1,0:T(8,128)(2,1)}, u32[]{:S(2)}) copy-start(bf16[2,8,40]{2,1,0:T(8,128)(2,1)} %copy-done.56) | copy-start | bytes 3844
  230.7 9.2 %copy-start.30 = (f32[2,8,8,64]{3,1,0,2:T(8,128)S(1)}, f32[2,8,8,64]{3,1,0,2:T(8,128)}, u32[]{:S(2)}) copy-start(f32[2,8,8,64]{3,1,0,2:T(8,128)} %fusion.29) | copy-start | bytes 98308
  230.7 10.1 %copy-start.31 = (f32[8,64,128]{2,1,0:T(8,128)S(1)}, f32[8,64,128]{2,1,0:T(8,128)}, u32[]{:S(2)}) copy-start(f32[8,64,128]{2,1,0:T(8,128)} %fusion.17) | copy-start | bytes 786436
  230.7 10.9 %copy-start.36 = (f32[8,8,64]{2,0,1:T(8,128)S(1)}, f32[8,8,64]{2,0,1:T(8,128)}, u32[]{:S(2)}) copy-start(f32[8,8,64]{2,0,1:T(8,128)} %fusion.35) | copy-start | bytes 49156
  233.4 11.8 %collective-permute-start.8 = (bf16[2,2,8,640]{3,2,0,1:T(8,128)(2,1)}, bf16[2,2,8,640]{3,2,0,1:T(8,128)(2,1)S(1)}, u32[]{:S(2)}, u32[]{:S(2)}) collective-permute-start(bf16[2,2,8,640]{3,2,0,1:T(8,128)(2,1)} %pad_maximum_fusion.26), channel_id=1, source_target_pairs={{0,8},{4,12},{8,0},{12,4},{16,24},{20,28},{24,16},{28,20},{32,40},... | collective-permute-start | bytes 122888 | tf_op jit(solution)/shard_map/ppermute | solution.py:16
  245.1 24.8 %copy-start.46 = (f32[8,128]{1,0:T(8,128)S(1)}, f32[8,128]{1,0:T(8,128)}, u32[]{:S(2)}) copy-start(f32[8,128]{1,0:T(8,128)} %get-tuple-element.17) | copy-start | bytes 12292
  245.1 24.8 %copy-start.15 = (bf16[1,128,512]{1,2,0:T(8,128)(2,1)S(1)}, bf16[1,128,512]{1,2,0:T(8,128)(2,1)}, u32[]{:S(2)}) copy-start(bf16[1,128,512]{1,2,0:T(8,128)(2,1)} %copy-done.14) | copy-start | bytes 393220
  245.2 24.8 %copy-start.22 = (bf16[1,128,512]{1,2,0:T(8,128)(2,1)S(1)}, bf16[1,128,512]{1,2,0:T(8,128)(2,1)}, u32[]{:S(2)}) copy-start(bf16[1,128,512]{1,2,0:T(8,128)(2,1)} %copy-done.21) | copy-start | bytes 393220
  245.2 24.8 %copy-start.23 = (bf16[128,512]{0,1:T(8,128)(2,1)S(1)}, bf16[128,512]{0,1:T(8,128)(2,1)}, u32[]{:S(2)}) copy-start(bf16[128,512]{0,1:T(8,128)(2,1)} %copy.1049) | copy-start | bytes 393220
  246.0 7.8 %collective-permute-start.9 = (bf16[2,4,8,640]{3,2,0,1:T(8,128)(2,1)S(1)}, bf16[2,4,8,640]{3,2,0,1:T(8,128)(2,1)S(1)}, u32[]{:S(2)}, u32[]{:S(2)}) collective-permute-start(bf16[2,4,8,640]{3,2,0,1:T(8,128)(2,1)S(1)} %pad_maximum_fusion.24), channel_id=1, source_target_pairs={{0,64},{4,68},{8,72},{12,76},{16,80},{20,84},{24,88},{28,92},{32,9... | collective-permute-start | bytes 245768 | tf_op jit(solution)/shard_map/ppermute | solution.py:16
  254.8 15.9 %copy-start.58 = (f32[128,8]{0,1:T(8,128)S(1)}, f32[128,8]{0,1:T(8,128)}, u32[]{:S(2)}) copy-start(f32[128,8]{0,1:T(8,128)} %mul.660) | copy-start | bytes 12292
  254.8 15.9 %copy-start.20 = (bf16[1,128,512]{1,2,0:T(8,128)(2,1)S(1)}, bf16[1,128,512]{1,2,0:T(8,128)(2,1)}, u32[]{:S(2)}) copy-start(bf16[1,128,512]{1,2,0:T(8,128)(2,1)} %copy.1014) | copy-start | bytes 393220
  255.8 10.3 %collective-permute-start.10 = (bf16[256,640]{0,1:T(8,128)(2,1)S(1)}, bf16[256,640]{0,1:T(8,128)(2,1)S(1)}, u32[]{:S(2)}, u32[]{:S(2)}) collective-permute-start(bf16[256,640]{0,1:T(8,128)(2,1)S(1)} %pad_maximum_fusion.6), channel_id=1, source_target_pairs={{0,4},{4,0},{8,12},{12,8},{16,20},{20,16},{24,28},{28,24},{32,36},... | collective-permute-start | bytes 983048 | tf_op jit(solution)/shard_map/ppermute | solution.py:16
  267.1 9.7 %collective-permute-start.11 = (bf16[2,16,8,640]{3,2,1,0:T(8,128)(2,1)}, bf16[2,16,8,640]{3,2,1,0:T(8,128)(2,1)}, u32[]{:S(2)}, u32[]{:S(2)}) collective-permute-start(bf16[2,16,8,640]{3,2,1,0:T(8,128)(2,1)} %get-tuple-element.51), channel_id=1, source_target_pairs={{0,32},{4,36},{8,40},{12,44},{16,48},{20,52},{24,56},{28,60},{32,0... | collective-permute-start | bytes 983048 | tf_op jit(solution)/shard_map/ppermute | solution.py:16
  272.1 13.1 %copy-start.6 = (f32[2,2,2,2,2,2,2,2,1,1024]{9,8,7,6,5,4,3,2,1,0:T(1,128)S(1)}, f32[2,2,2,2,2,2,2,2,1,1024]{9,8,7,6,5,4,3,2,1,0:T(1,128)}, u32[]{:S(2)}) copy-start(f32[2,2,2,2,2,2,2,2,1,1024]{9,8,7,6,5,4,3,2,1,0:T(1,128)} %get-tuple-element.24) | copy-start | bytes 3145732
  278.7 15.8 %collective-permute-start.12 = (bf16[2,32,8,640]{3,2,1,0:T(8,128)(2,1)}, bf16[2,32,8,640]{3,2,1,0:T(8,128)(2,1)}, u32[]{:S(2)}, u32[]{:S(2)}) collective-permute-start(bf16[2,32,8,640]{3,2,1,0:T(8,128)(2,1)} %get-tuple-element.40), channel_id=1, source_target_pairs={{0,128},{4,132},{8,136},{12,140},{16,144},{20,148},{24,152},{28,15... | collective-permute-start | bytes 1966088 | tf_op jit(solution)/shard_map/ppermute | solution.py:16
  285.2 9.3 %copy-start.7 = (bf16[2,64,8,640]{3,2,1,0:T(8,128)(2,1)S(1)}, bf16[2,64,8,640]{3,2,1,0:T(8,128)(2,1)}, u32[]{:S(2)}) copy-start(bf16[2,64,8,640]{3,2,1,0:T(8,128)(2,1)} %get-tuple-element.41) | copy-start | bytes 3932164
  288.2 12.7 %collective-permute-start.15 = (f32[2,2,2,2,2,2,2,1024]{7,6,5,4,3,2,1,0:T(2,128)}, f32[2,2,2,2,2,2,2,1024]{7,6,5,4,3,2,1,0:T(2,128)}, u32[]{:S(2)}, u32[]{:S(2)}) collective-permute-start(f32[2,2,2,2,2,2,2,1024]{7,6,5,4,3,2,1,0:T(2,128)} %dynamic-slice_bitcast_fusion), channel_id=1, source_target_pairs={{0,4},{1,5},{2,6},{3,7},{4,0},{5,1},{6,2},{7,3},{8,12},{9,13},{10,... | collective-permute-start | bytes 1572872 | tf_op jit(solution)/shard_map/ppermute | solution.py:134
  296.8 8.3 %copy-start.9 = (bf16[2,64,8,640]{3,2,1,0:T(8,128)(2,1)S(1)}, bf16[2,64,8,640]{3,2,1,0:T(8,128)(2,1)}, u32[]{:S(2)}) copy-start(bf16[2,64,8,640]{3,2,1,0:T(8,128)(2,1)} %copy-done.8) | copy-start | bytes 3932164
  302.3 8.3 %collective-permute-start.16 = (f32[2,2,2,2,2,2,1024]{6,5,4,3,2,1,0:T(2,128)S(1)}, f32[2,2,2,2,2,2,1024]{6,5,4,3,2,1,0:T(2,128)S(1)}, u32[]{:S(2)}, u32[]{:S(2)}) collective-permute-start(f32[2,2,2,2,2,2,1024]{6,5,4,3,2,1,0:T(2,128)S(1)} %dynamic-slice_bitcast_fusion.1), channel_id=1, source_target_pairs={{0,32},{1,33},{2,34},{3,35},{4,36},{5,37},{6,38},{7,39},{8,40},{9,... | collective-permute-start | bytes 786440 | tf_op jit(solution)/shard_map/ppermute | solution.py:134
  310.8 6.9 %collective-permute-start.17 = (f32[2,2,2,2,2,1024]{5,4,3,2,1,0:T(2,128)S(1)}, f32[2,2,2,2,2,1024]{5,4,3,2,1,0:T(2,128)S(1)}, u32[]{:S(2)}, u32[]{:S(2)}) collective-permute-start(f32[2,2,2,2,2,1024]{5,4,3,2,1,0:T(2,128)S(1)} %dynamic-slice_bitcast_fusion.2), channel_id=1, source_target_pairs={{0,128},{1,129},{2,130},{3,131},{4,132},{5,133},{6,134},{7,135},{8... | collective-permute-start | bytes 393224 | tf_op jit(solution)/shard_map/ppermute | solution.py:134
  317.7 11.4 %collective-permute-start.18 = (f32[2,2,2,2,1024]{4,3,2,1,0:T(2,128)S(1)}, f32[2,2,2,2,1024]{4,3,2,1,0:T(2,128)S(1)}, u32[]{:S(2)}, u32[]{:S(2)}) collective-permute-start(f32[2,2,2,2,1024]{4,3,2,1,0:T(2,128)S(1)} %dynamic-slice_bitcast_fusion.3), channel_id=1, source_target_pairs={{0,8},{1,9},{2,10},{3,11},{4,12},{5,13},{6,14},{7,15},{8,0},{9,1},... | collective-permute-start | bytes 196616 | tf_op jit(solution)/shard_map/ppermute | solution.py:134
  322.4 10.1 %copy-start.37 = (bf16[16,8,64]{2,1,0:T(8,128)(2,1)S(1)}, bf16[16,8,64]{2,1,0:T(8,128)(2,1)}, u32[]{:S(2)}) copy-start(bf16[16,8,64]{2,1,0:T(8,128)(2,1)} %reshape_reshape_squeeze_stack.11) | copy-start | bytes 49156
  324.3 22.6 %copy-start.35 = (bf16[16,8,64]{2,1,0:T(8,128)(2,1)S(1)}, bf16[16,8,64]{2,1,0:T(8,128)(2,1)}, u32[]{:S(2)}) copy-start(bf16[16,8,64]{2,1,0:T(8,128)(2,1)} %reshape_reshape_squeeze_stack.12) | copy-start | bytes 49156
  324.4 43.7 %collective-permute-start.13 = (bf16[64,8,640]{2,1,0:T(8,128)(2,1)}, bf16[64,8,640]{2,1,0:T(8,128)(2,1)}, u32[]{:S(2)}, u32[]{:S(2)}) collective-permute-start(bf16[64,8,640]{2,1,0:T(8,128)(2,1)} %slice_bitcast_fusion.1), channel_id=1, source_target_pairs={{0,256},{4,260},{8,264},{12,268},{16,272},{20,276},{24,280},{28,28... | collective-permute-start | bytes 1966088 | tf_op jit(solution)/shard_map/ppermute | solution.py:16
  329.2 7.3 %collective-permute-start.19 = (f32[2,2,2,1024]{3,2,1,0:T(2,128)S(1)}, f32[2,2,2,1024]{3,2,1,0:T(2,128)S(1)}, u32[]{:S(2)}, u32[]{:S(2)}) collective-permute-start(f32[2,2,2,1024]{3,2,1,0:T(2,128)S(1)} %dynamic-slice_bitcast_fusion.4), channel_id=1, source_target_pairs={{0,64},{1,65},{2,66},{3,67},{4,68},{5,69},{6,70},{7,71},{8,72},{9,... | collective-permute-start | bytes 98312 | tf_op jit(solution)/shard_map/ppermute | solution.py:134
  336.6 7.1 %collective-permute-start.20 = (f32[2,2,1024]{2,1,0:T(2,128)S(1)}, f32[2,2,1024]{2,1,0:T(2,128)S(1)}, u32[]{:S(2)}, u32[]{:S(2)}) collective-permute-start(f32[2,2,1024]{2,1,0:T(2,128)S(1)} %dynamic-slice_bitcast_fusion.5), channel_id=1, source_target_pairs={{0,256},{1,257},{2,258},{3,259},{4,260},{5,261},{6,262},{7,263},{8... | collective-permute-start | bytes 49160 | tf_op jit(solution)/shard_map/ppermute | solution.py:134
  343.7 9.5 %collective-permute-start.21 = (f32[2,1024]{1,0:T(2,128)S(1)}, f32[2,1024]{1,0:T(2,128)S(1)}, u32[]{:S(2)}, u32[]{:S(2)}) collective-permute-start(f32[2,1024]{1,0:T(2,128)S(1)} %dynamic-slice_bitcast_fusion.6), channel_id=1, source_target_pairs={{0,16},{1,17},{2,18},{3,19},{4,20},{5,21},{6,22},{7,23},{8,24},{9,... | collective-permute-start | bytes 24584 | tf_op jit(solution)/shard_map/ppermute | solution.py:134
  353.2 14.2 %collective-permute-start.22 = (f32[1024]{0:T(1024)S(1)}, f32[1024]{0:T(1024)S(1)}, u32[]{:S(2)}, u32[]{:S(2)}) collective-permute-start(f32[1024]{0:T(1024)S(1)} %bitcast.432), channel_id=1, source_target_pairs={{0,2},{1,3},{2,0},{3,1},{4,6},{5,7},{6,4},{7,5},{8,10},{9,11},{10,... | collective-permute-start | bytes 12296 | tf_op jit(solution)/shard_map/ppermute | solution.py:134
  356.6 11.5 %copy-start.10 = (bf16[64,8,640]{2,1,0:T(8,128)(2,1)S(1)}, bf16[64,8,640]{2,1,0:T(8,128)(2,1)}, u32[]{:S(2)}) copy-start(bf16[64,8,640]{2,1,0:T(8,128)(2,1)} %slice_bitcast_fusion.1) | copy-start | bytes 1966084
  374.9 3.2 copy-start.1
  (22 other events, 33.8 us)

commit v5 on v4

--- a/solution.py
+++ b/solution.py
@@ -233,20 +233,23 @@
 
     qkv = jnp.stack([by_parity(pick_rows(m, R2)) for m in (queries, keys_all, values_all)], 0)
     per_par = qkv.shape[2]
+    far = partner(qkv[:, 0], "tm", top_bit)
     own, other_qkv = gather_with_rider(
-        qkv[:, :, None], 2, low_bits, jnp.stack([queries, keys_all, values_all], 0)
-    )
-    far = partner(own[:, 0], "tm", top_bit)
+        jnp.concatenate([qkv, far[:, None]], 1)[:, :, None],
+        2,
+        low_bits,
+        jnp.stack([queries, keys_all, values_all], 0),
+    )
     other_q = other_qkv[0]
     keys_one = jnp.concatenate([keys_all, other_qkv[1]], 0)
     values_one = jnp.concatenate([values_all, other_qkv[2]], 0)
     part_one, lse_one = attend(queries, keys_one, values_one, inv_root)
-    q_seg2 = own[0].reshape(-1, features)
-    k_seg2 = own[1].reshape(-1, features)
-    v_seg2 = own[2].reshape(-1, features)
-    q_seg3 = jnp.concatenate([own[0, 0], far[0]], 0).reshape(-1, features)
-    k_seg3 = jnp.concatenate([own[1, 0], far[1]], 0).reshape(-1, features)
-    v_seg3 = jnp.concatenate([own[2, 0], far[2]], 0).reshape(-1, features)
+    q_seg2 = own[0, :2].reshape(-1, features)
+    k_seg2 = own[1, :2].reshape(-1, features)
+    v_seg2 = own[2, :2].reshape(-1, features)
+    q_seg3 = own[0, ::2].reshape(-1, features)
+    k_seg3 = own[1, ::2].reshape(-1, features)
+    v_seg3 = own[2, ::2].reshape(-1, features)
     q_two = qkv[0].reshape(-1, features)
     q_three = qkv[0, 0]
     part_two, lse_two = attend(q_two, k_seg2, v_seg2, inv_root)
@@ -296,7 +299,10 @@
     w3_par = jnp.stack([w_three, no_level], 0)
     stats_par = jnp.concatenate([lse_two_par, w_two, lse3_par, w3_par, rd_two], -1)
     packed = pad_lanes(jnp.concatenate([ga_par, split_exact(stats_par)], -1), wide)
-    own_b, other_one = gather_with_rider(packed[:, None], 1, low_bits, pad_lanes(packed_one, wide))
+    far_b = partner(packed[0], "tm", top_bit)
+    own_b, other_one = gather_with_rider(
+        jnp.concatenate([packed, far_b[None]], 0)[:, None], 1, low_bits, pad_lanes(packed_one, wide)
+    )
     other_stats = join_exact(other_one[:, features : features + 6 * HEADS])
     total_q = spread_rows(
         near_grad(queries, keys_one, values_one, grad_one, lse_one, offset_one, inv_root), 1
@@ -312,7 +318,6 @@
     )
     total_k = spread_rows(k_g1, 1)
     total_v = spread_rows(v_g1, 1)
-    far_b = partner(own_b[0], "tm", top_bit)
     stat_w = 5 * HEADS
 
     def unpack(rows):
@@ -323,7 +328,7 @@
     g_two = grad_of(w_two.reshape(-1, HEADS), ga_par.reshape(-1, features))
     c_two = w_two.reshape(-1, HEADS) * rd_two.reshape(-1, HEADS)
     grad_q2 = near_grad(q_two, k_seg2, v_seg2, g_two, lse_two, c_two, inv_root)
-    ga_seg2, st_seg2 = unpack(own_b)
+    ga_seg2, st_seg2 = unpack(own_b[:2])
     k_g2, v_g2 = far_grad(
         q_seg2,
         grad_of(st_seg2[:, 1], ga_seg2),
@@ -337,7 +342,7 @@
     g_three = grad_of(w_three, ga_par[0])
     c_three = w_three * rd_two[0]
     grad_q3 = near_grad(q_three, k_seg3, v_seg3, g_three, lse_three, c_three, inv_root)
-    ga_seg3, st_seg3 = unpack(jnp.concatenate([own_b[0], far_b], 0))
+    ga_seg3, st_seg3 = unpack(own_b[::2])
     k_g3, v_g3 = far_grad(
         q_seg3,
         grad_of(st_seg3[:, 3], ga_seg3),

time: 381 us -> 410 us (1.076)
  waiting for transfers between devices: 108 us -> 146 us
  other arithmetic: 34.2 us -> 26.5 us
    ppermute x14, waiting for transfers between devices: 81.1 us -> 114 us  [partner(): return lax.ppermute(value, axis, pairs)]
    squeeze x4 -> x1, local copies, waits for them, and re-layouts: 8.21 us -> 0.6 us  [on_device(): far_b = partner(packed[0], 'tm', top_bit)]
    ppermute x9, starting transfers between devices: 24.9 us -> 31 us  [scatter_sum(): block = keep + lax.ppermute(send, axes, pairs)]
    ppermute x14, starting transfers between devices: 64.5 us -> 60.1 us  [partner(): return lax.ppermute(value, axis, pairs)]
    ppermute x9, waiting for transfers between devices: 27.2 us -> 31.4 us  [scatter_sum(): block = keep + lax.ppermute(send, axes, pairs)]
    unnamed x139 -> x126, local copies, waits for them, and re-layouts: 15.3 us -> 16.5 us
  transfers between devices with their start and end apart: 23 -> 23, of which waited for: 18 -> 18; matrix products, arithmetic and copies ran while one was open for 27% -> 13% of each run, Pallas kernels for 0% -> 0%
where the time goes in v5:
time: 410 us; the launch traced here: 407 us
  waiting for transfers between devices  146 us (36%)
  local copies, waits for them, and re-layouts  115 us (28%)
  starting transfers between devices  91.1 us (22%)
  matrix products  26.5 us (6%)
  other arithmetic  26.5 us (6%)
    ppermute x14, waiting for transfers between devices, partner(): return lax.ppermute(value, axis, pairs)  114 us
    ppermute x14, starting transfers between devices, partner(): return lax.ppermute(value, axis, pairs)  60.1 us
    another operation x18, local copies, waits for them, and re-layouts, heads_view(): return matrix.reshape(matrix.shape[0], HEADS, HD)  35.7 us
    ppermute x9, waiting for transfers between devices, scatter_sum(): block = keep + lax.ppermute(send, axes, pairs)  31.4 us
    ppermute x9, starting transfers between devices, scatter_sum(): block = keep + lax.ppermute(send, axes, pairs)  31 us
    unnamed x126, local copies, waits for them, and re-layouts  16.5 us
    mul x26, local copies, waits for them, and re-layouts, spread_rows(): values[:, None] * chooser  15.3 us
    concatenate x6, local copies, waits for them, and re-layouts, gather_with_rider(): block = jnp.concatenate([block, other], axis_pos)  8.31 us
  transfers between devices with their start and end apart: 23, of which 18 were waited for; matrix products, arithmetic and copies ran while one was open for 13% of the time, Pallas kernels for 0%

profile of v5, /device:TPU:6, one launch (start us, length us, event | category | flops | bytes accessed | tf_op | source)
XLA Modules:
  0.0 407.3 jit_solution(750789855951981741)
XLA Ops:
  5.7 5.1 %collective-permute-start = (bf16[3,8,512]{2,1,0:T(8,128)(2,1)S(1)}, bf16[3,8,512]{2,1,0:T(8,128)(2,1)S(1)}, u32[]{:S(2)}, u32[]{:S(2)}) collective-permute-start(bf16[3,8,512]{2,1,0:T(8,128)(2,1)S(1)} %bitcast.427), channel_id=1, source_target_pairs={{0,256},{4,260},{8,264},{12,268},{16,272},{20,276},{24,280},{28,28... | collective-permute-start | bytes 73736 | tf_op jit(solution)/shard_map/ppermute | solution.py:16
  10.8 2.1 collective-permute-done
  13.1 9.1 %collective-permute-start.1 = (bf16[3,3,1,8,512]{4,3,1,0,2:T(8,128)(2,1)S(1)}, bf16[3,3,1,8,512]{4,3,1,0,2:T(8,128)(2,1)S(1)}, u32[]{:S(2)}, u32[]{:S(2)}) collective-permute-start(bf16[3,3,1,8,512]{4,3,1,0,2:T(8,128)(2,1)S(1)} %bitcast.364), channel_id=1, source_target_pairs={{0,16},{4,20},{8,24},{12,28},{16,0},{20,4},{24,8},{28,12},{32,48},... | collective-permute-start | bytes 221192 | tf_op jit(solution)/shard_map/ppermute | solution.py:16
  22.2 6.4 %collective-permute-done.1 = bf16[3,3,1,8,512]{4,3,1,0,2:T(8,128)(2,1)S(1)} collective-permute-done((bf16[3,3,1,8,512]{4,3,1,0,2:T(8,128)(2,1)S(1)}, bf16[3,3,1,8,512]{4,3,1,0,2:T(8,128)(2,1)S(1)}, u32[]{:S(2)}, u32[]{:S(2)}) %collective-permute-start.1) | collective-permute-done | bytes 73760 | tf_op jit(solution)/shard_map/ppermute | solution.py:16
  28.6 1.9 collective-permute-start.2
  30.6 7.4 %collective-permute-done.2 = bf16[3,3,2,8,512]{4,3,1,0,2:T(8,128)(2,1)S(1)} collective-permute-done((bf16[3,3,2,8,512]{4,3,1,0,2:T(8,128)(2,1)S(1)}, bf16[3,3,2,8,512]{4,3,1,0,2:T(8,128)(2,1)S(1)}, u32[]{:S(2)}, u32[]{:S(2)}) %collective-permute-start.2) | collective-permute-done | bytes 147488 | tf_op jit(solution)/shard_map/ppermute | solution.py:16
  38.0 3.3 collective-permute-start.3
  41.4 6.7 %collective-permute-done.3 = bf16[3,3,4,8,512]{4,3,1,0,2:T(8,128)(2,1)S(1)} collective-permute-done((bf16[3,3,4,8,512]{4,3,1,0,2:T(8,128)(2,1)S(1)}, bf16[3,3,4,8,512]{4,3,1,0,2:T(8,128)(2,1)S(1)}, u32[]{:S(2)}, u32[]{:S(2)}) %collective-permute-start.3) | collective-permute-done | bytes 294944 | tf_op jit(solution)/shard_map/ppermute | solution.py:16
  48.3 3.9 collective-permute-start.4
  55.3 17.9 %collective-permute-done.4 = bf16[960,512]{1,0:T(8,128)(2,1)S(1)} collective-permute-done((bf16[960,512]{1,0:T(8,128)(2,1)S(1)}, bf16[960,512]{1,0:T(8,128)(2,1)S(1)}, u32[]{:S(2)}, u32[]{:S(2)}) %collective-permute-start.4) | collective-permute-done | bytes 983072 | tf_op jit(solution)/shard_map/ppermute | solution.py:16
  74.4 2.7 collective-permute-start.5
  77.1 25.5 %collective-permute-done.5 = bf16[3,3,16,8,512]{4,3,2,1,0:T(8,128)(2,1)S(1)} collective-permute-done((bf16[3,3,16,8,512]{4,3,2,1,0:T(8,128)(2,1)S(1)}, bf16[3,3,16,8,512]{4,3,2,1,0:T(8,128)(2,1)S(1)}, u32[]{:S(2)}, u32[]{:S(2)}) %collective-permute-start.5) | collective-permute-done | bytes 1179680 | tf_op jit(solution)/shard_map/ppermute | solution.py:16
  104.3 3.7 collective-permute-start.6
  119.7 37.5 %collective-permute-done.6 = bf16[3,3,32,8,512]{4,3,2,1,0:T(8,128)(2,1)} collective-permute-done((bf16[3,3,32,8,512]{4,3,2,1,0:T(8,128)(2,1)}, bf16[3,3,32,8,512]{4,3,2,1,0:T(8,128)(2,1)}, u32[]{:S(2)}, u32[]{:S(2)}) %collective-permute-start.6) | collective-permute-done | bytes 2359328 | tf_op jit(solution)/shard_map/ppermute | solution.py:16
  157.1 3.3 constant_dynamic-update-slice_fusion.7
  160.4 5.2 %fusion.133 = (bf16[1,2,64,8,512]{4,3,2,1,0:T(8,128)(2,1)}, bf16[1,2,64,8,512]{4,3,2,1,0:T(8,128)(2,1)}, bf16[1,2,64,8,512]{4,3,2,1,0:T(8,128)(2,1)}, bf16[1,2,6...) fusion(bf16[3,3,64,8,512]{4,3,2,1,0:T(8,128)(2,1)} %constant_dynamic-upda, ...), kind=kLoop, calls=%fused_computation.287 | loop fusion | bytes 12582912 | tf_op jit(solution)/shard_map/slice | solution.py:247
  165.6 2.1 reshape_reshape_squeeze.12
  167.7 2.5 copy.1148
  171.6 3.9 reshape_reshape_squeeze.28
  175.6 3.4 copy.1156
  182.6 3.9 reshape_reshape_squeeze.13
  186.5 2.5 copy.1152
  198.1 3.9 reshape_reshape_squeeze.29
  202.0 3.4 copy.1159
  208.0 1.9 mul.644
  209.9 1.9 copy.1164
  215.1 2.8 fusion.65
  227.0 1.9 fusion.55
  230.6 3.3 constant_dynamic-slice_fusion.3
  235.6 2.0 collective-permute-start.14
  242.6 5.1 %collective-permute-start.7 = (bf16[8,640]{1,0:T(8,128)(2,1)}, bf16[8,640]{1,0:T(8,128)(2,1)}, u32[]{:S(2)}, u32[]{:S(2)}) collective-permute-start(bf16[8,640]{1,0:T(8,128)(2,1)} %slice_bitcast_fusion.6), channel_id=1, source_target_pairs={{0,256},{4,260},{8,264},{12,268},{16,272},{20,276},{24,280},{28,28... | collective-permute-start | bytes 30728 | tf_op jit(solution)/shard_map/ppermute | solution.py:16
  247.7 2.9 fusion.29
  250.6 2.5 fusion.17
  255.4 8.3 %collective-permute-start.8 = (bf16[3,1,8,640]{3,2,0,1:T(8,128)(2,1)S(1)}, bf16[3,1,8,640]{3,2,0,1:T(8,128)(2,1)S(1)}, u32[]{:S(2)}, u32[]{:S(2)}) collective-permute-start(bf16[3,1,8,640]{3,2,0,1:T(8,128)(2,1)S(1)} %fusion.129), channel_id=1, source_target_pairs={{0,16},{4,20},{8,24},{12,28},{16,0},{20,4},{24,8},{28,12},{32,48},... | collective-permute-start | bytes 92168 | tf_op jit(solution)/shard_map/ppermute | solution.py:16
  267.5 2.3 copy.1214
  273.0 5.3 %collective-permute-start.9 = (bf16[3,2,8,640]{3,2,0,1:T(8,128)(2,1)S(1)}, bf16[3,2,8,640]{3,2,0,1:T(8,128)(2,1)S(1)}, u32[]{:S(2)}, u32[]{:S(2)}) collective-permute-start(bf16[3,2,8,640]{3,2,0,1:T(8,128)(2,1)S(1)} %pad_maximum_fusion.23), channel_id=1, source_target_pairs={{0,8},{4,12},{8,0},{12,4},{16,24},{20,28},{24,16},{28,20},{32,40},... | collective-permute-start | bytes 184328 | tf_op jit(solution)/shard_map/ppermute | solution.py:16
  279.7 2.0 collective-permute-done.9
  282.5 3.3 collective-permute-start.10
  287.2 3.5 collective-permute-done.10
  292.6 2.3 collective-permute-start.11
  295.0 2.1 bitcast_add_fusion
  297.9 3.8 collective-permute-start.15
  303.2 5.4 %collective-permute-done.11 = bf16[320,640]{0,1:T(8,128)(2,1)S(1)} collective-permute-done((bf16[320,640]{0,1:T(8,128)(2,1)S(1)}, bf16[320,640]{0,1:T(8,128)(2,1)S(1)}, u32[]{:S(2)}, u32[]{:S(2)}) %collective-permute-start.11) | collective-permute-done | bytes 409632 | tf_op jit(solution)/shard_map/ppermute | solution.py:16
  310.5 2.8 collective-permute-start.12
  313.4 2.2 collective-permute-done.15
  316.0 2.7 collective-permute-start.16
  319.6 7.6 %collective-permute-done.16 = f32[2,2,2,2,2,2,1024]{6,5,4,3,2,1,0:T(2,128)S(1)} collective-permute-done((f32[2,2,2,2,2,2,1024]{6,5,4,3,2,1,0:T(2,128)S(1)}, f32[2,2,2,2,2,2,1024]{6,5,4,3,2,1,0:T(2,128)S(1)}, u32[]{:S(2)}, u32[]{:S(2)}) %collective-permute-start.16) | collective-permute-done | bytes 262176 | tf_op jit(solution)/shard_map/ppermute | solution.py:134
  327.4 2.6 collective-permute-start.17
  330.0 4.2 %collective-permute-done.17 = f32[2,2,2,2,2,1024]{5,4,3,2,1,0:T(2,128)S(1)} collective-permute-done((f32[2,2,2,2,2,1024]{5,4,3,2,1,0:T(2,128)S(1)}, f32[2,2,2,2,2,1024]{5,4,3,2,1,0:T(2,128)S(1)}, u32[]{:S(2)}, u32[]{:S(2)}) %collective-permute-start.17) | collective-permute-done | bytes 131104 | tf_op jit(solution)/shard_map/ppermute | solution.py:134
  334.3 4.5 %collective-permute-start.18 = (f32[2,2,2,2,1024]{4,3,2,1,0:T(2,128)S(1)}, f32[2,2,2,2,1024]{4,3,2,1,0:T(2,128)S(1)}, u32[]{:S(2)}, u32[]{:S(2)}) collective-permute-start(f32[2,2,2,2,1024]{4,3,2,1,0:T(2,128)S(1)} %dynamic-slice_bitcast_fusion.3), channel_id=1, source_target_pairs={{0,8},{1,9},{2,10},{3,11},{4,12},{5,13},{6,14},{7,15},{8,0},{9,1},... | collective-permute-start | bytes 196616 | tf_op jit(solution)/shard_map/ppermute | solution.py:134
  338.8 3.3 collective-permute-done.18
  342.1 3.3 collective-permute-start.19
  347.2 2.2 collective-permute-done.19
  349.5 2.4 collective-permute-start.20
  353.0 3.3 collective-permute-start.13
  356.9 2.4 collective-permute-start.21
  360.0 6.3 %collective-permute-done.21 = f32[2,1024]{1,0:T(2,128)S(1)} collective-permute-done((f32[2,1024]{1,0:T(2,128)S(1)}, f32[2,1024]{1,0:T(2,128)S(1)}, u32[]{:S(2)}, u32[]{:S(2)}) %collective-permute-start.21) | collective-permute-done | bytes 8224 | tf_op jit(solution)/shard_map/ppermute | solution.py:134
  366.4 7.3 %collective-permute-start.22 = (f32[1024]{0:T(1024)S(1)}, f32[1024]{0:T(1024)S(1)}, u32[]{:S(2)}, u32[]{:S(2)}) collective-permute-start(f32[1024]{0:T(1024)S(1)} %bitcast.433), channel_id=1, source_target_pairs={{0,2},{1,3},{2,0},{3,1},{4,6},{5,7},{6,4},{7,5},{8,10},{9,11},{10,... | collective-permute-start | bytes 12296 | tf_op jit(solution)/shard_map/ppermute | solution.py:134
  375.6 5.0 %collective-permute-done.22 = f32[1024]{0:T(1024)S(1)} collective-permute-done((f32[1024]{0:T(1024)S(1)}, f32[1024]{0:T(1024)S(1)}, u32[]{:S(2)}, u32[]{:S(2)}) %collective-permute-start.22) | collective-permute-done | bytes 4128 | tf_op jit(solution)/shard_map/ppermute | solution.py:134
  381.2 2.2 constant_dynamic-update-slice_fusion.21
  383.4 1.9 fusion.134
  390.4 1.9 copy.1211
  397.9 1.9 copy.1221
  405.0 2.2 add_convert_fusion
  (318 shorter events, 102.9 us)
Async XLA Ops:
  0.6 3.7 copy-start.55
  0.7 3.1 copy-start.13
  0.7 3.3 copy-start.12
  2.0 2.1 copy-start.14
  5.7 7.2 %collective-permute-start = (bf16[3,8,512]{2,1,0:T(8,128)(2,1)S(1)}, bf16[3,8,512]{2,1,0:T(8,128)(2,1)S(1)}, u32[]{:S(2)}, u32[]{:S(2)}) collective-permute-start(bf16[3,8,512]{2,1,0:T(8,128)(2,1)S(1)} %bitcast.427), channel_id=1, source_target_pairs={{0,256},{4,260},{8,264},{12,268},{16,272},{20,276},{24,280},{28,28... | collective-permute-start | bytes 73736 | tf_op jit(solution)/shard_map/ppermute | solution.py:16
  13.1 15.5 %collective-permute-start.1 = (bf16[3,3,1,8,512]{4,3,1,0,2:T(8,128)(2,1)S(1)}, bf16[3,3,1,8,512]{4,3,1,0,2:T(8,128)(2,1)S(1)}, u32[]{:S(2)}, u32[]{:S(2)}) collective-permute-start(bf16[3,3,1,8,512]{4,3,1,0,2:T(8,128)(2,1)S(1)} %bitcast.364), channel_id=1, source_target_pairs={{0,16},{4,20},{8,24},{12,28},{16,0},{20,4},{24,8},{28,12},{32,48},... | collective-permute-start | bytes 221192 | tf_op jit(solution)/shard_map/ppermute | solution.py:16
  28.6 9.3 %collective-permute-start.2 = (bf16[3,3,2,8,512]{4,3,1,0,2:T(8,128)(2,1)S(1)}, bf16[3,3,2,8,512]{4,3,1,0,2:T(8,128)(2,1)S(1)}, u32[]{:S(2)}, u32[]{:S(2)}) collective-permute-start(bf16[3,3,2,8,512]{4,3,1,0,2:T(8,128)(2,1)S(1)} %pad_maximum_fusion.20), channel_id=1, source_target_pairs={{0,8},{4,12},{8,0},{12,4},{16,24},{20,28},{24,16},{28,20},{32,40},... | collective-permute-start | bytes 442376 | tf_op jit(solution)/shard_map/ppermute | solution.py:16
  38.0 10.1 %collective-permute-start.3 = (bf16[3,3,4,8,512]{4,3,1,0,2:T(8,128)(2,1)S(1)}, bf16[3,3,4,8,512]{4,3,1,0,2:T(8,128)(2,1)S(1)}, u32[]{:S(2)}, u32[]{:S(2)}) collective-permute-start(bf16[3,3,4,8,512]{4,3,1,0,2:T(8,128)(2,1)S(1)} %pad_maximum_fusion.4), channel_id=1, source_target_pairs={{0,64},{4,68},{8,72},{12,76},{16,80},{20,84},{24,88},{28,92},{32,9... | collective-permute-start | bytes 884744 | tf_op jit(solution)/shard_map/ppermute | solution.py:16
  48.3 24.9 %collective-permute-start.4 = (bf16[960,512]{1,0:T(8,128)(2,1)S(1)}, bf16[960,512]{1,0:T(8,128)(2,1)S(1)}, u32[]{:S(2)}, u32[]{:S(2)}) collective-permute-start(bf16[960,512]{1,0:T(8,128)(2,1)S(1)} %pad_maximum_fusion), channel_id=1, source_target_pairs={{0,4},{4,0},{8,12},{12,8},{16,20},{20,16},{24,28},{28,24},{32,36},... | collective-permute-start | bytes 2949128 | tf_op jit(solution)/shard_map/ppermute | solution.py:16
  74.4 28.2 %collective-permute-start.5 = (bf16[3,3,16,8,512]{4,3,2,1,0:T(8,128)(2,1)S(1)}, bf16[3,3,16,8,512]{4,3,2,1,0:T(8,128)(2,1)S(1)}, u32[]{:S(2)}, u32[]{:S(2)}) collective-permute-start(bf16[3,3,16,8,512]{4,3,2,1,0:T(8,128)(2,1)S(1)} %get-tuple-element.35), channel_id=1, source_target_pairs={{0,32},{4,36},{8,40},{12,44},{16,48},{20,52},{24,56},{28,60},{32,0... | collective-permute-start | bytes 3538952 | tf_op jit(solution)/shard_map/ppermute | solution.py:16
  102.6 7.9 %copy-start.52 = (f32[8,8]{0,1:T(8,128)S(1)}, f32[8,8]{0,1:T(8,128)}, u32[]{:S(2)}) copy-start(f32[8,8]{0,1:T(8,128)} %constant.249.clone) | copy-start | bytes 772
  102.6 8.0 %copy-start.51 = (f32[16,8]{0,1:T(8,128)S(1)}, f32[16,8]{0,1:T(8,128)}, u32[]{:S(2)}) copy-start(f32[16,8]{0,1:T(8,128)} %constant.250.clone) | copy-start | bytes 1540
  102.6 8.1 %copy-start.40 = (bf16[16,8,64]{2,1,0:T(8,128)(2,1)S(1)}, bf16[16,8,64]{2,1,0:T(8,128)(2,1)}, u32[]{:S(2)}) copy-start(bf16[16,8,64]{2,1,0:T(8,128)(2,1)} %get-tuple-element.7) | copy-start | bytes 49156
  104.3 52.8 %collective-permute-start.6 = (bf16[3,3,32,8,512]{4,3,2,1,0:T(8,128)(2,1)}, bf16[3,3,32,8,512]{4,3,2,1,0:T(8,128)(2,1)}, u32[]{:S(2)}, u32[]{:S(2)}) collective-permute-start(bf16[3,3,32,8,512]{4,3,2,1,0:T(8,128)(2,1)} %get-tuple-element.28), channel_id=1, source_target_pairs={{0,128},{4,132},{8,136},{12,140},{16,144},{20,148},{24,152},{28,15... | collective-permute-start | bytes 7077896 | tf_op jit(solution)/shard_map/ppermute | solution.py:16
  108.1 10.5 %copy-start.16 = (bf16[1,128,512]{1,2,0:T(8,128)(2,1)}, bf16[1,128,512]{1,2,0:T(8,128)(2,1)S(1)}, u32[]{:S(2)}) copy-start(bf16[1,128,512]{1,2,0:T(8,128)(2,1)S(1)} %copy.1128) | copy-start | bytes 393220
  108.2 10.3 %copy-start.10 = (bf16[1,128,512]{1,2,0:T(8,128)(2,1)}, bf16[1,128,512]{1,2,0:T(8,128)(2,1)S(1)}, u32[]{:S(2)}) copy-start(bf16[1,128,512]{1,2,0:T(8,128)(2,1)S(1)} %copy.1133) | copy-start | bytes 393220
  110.6 8.3 %copy-start.45 = (f32[128,8]{0,1:T(8,128)}, f32[128,8]{0,1:T(8,128)S(1)}, u32[]{:S(2)}) copy-start(f32[128,8]{0,1:T(8,128)S(1)} %mul.646) | copy-start | bytes 12292
  110.8 3.6 copy-start.43
  117.0 40.2 %copy-start.24 = (bf16[128,512]{0,1:T(8,128)(2,1)}, bf16[128,512]{0,1:T(8,128)(2,1)S(1)}, u32[]{:S(2)}) copy-start(bf16[128,512]{0,1:T(8,128)(2,1)S(1)} %copy.1132) | copy-start | bytes 393220
  118.9 41.5 %copy-start.50 = (f32[8,128]{1,0:T(8,128)}, f32[8,128]{1,0:T(8,128)S(1)}, u32[]{:S(2)}) copy-start(f32[8,128]{1,0:T(8,128)S(1)} %get-tuple-element.96) | copy-start | bytes 12292
  167.7 2.5 copy-start.41
  170.2 5.3 %copy-start.3 = (bf16[1024,8,64]{0,2,1:T(8,128)(2,1)}, bf16[1024,8,64]{0,2,1:T(8,128)(2,1)S(1)}, u32[]{:S(2)}) copy-start(bf16[1024,8,64]{0,2,1:T(8,128)(2,1)S(1)} %copy.1148) | copy-start | bytes 3145732
  171.6 7.3 %copy-start.46 = (f32[8,16]{1,0:T(8,128)}, f32[8,16]{1,0:T(8,128)S(1)}, u32[]{:S(2)}) copy-start(f32[8,16]{1,0:T(8,128)S(1)} %log_add_fusion.1) | copy-start | bytes 1540
  226.9 3.0 copy-start.34
  233.9 3.7 copy-start.32
  233.9 3.7 copy-start.33
  233.9 3.7 copy-start.53
  233.9 4.1 %copy-start.31 = (f32[16,8,64]{2,1,0:T(8,128)S(1)}, f32[16,8,64]{2,1,0:T(8,128)}, u32[]{:S(2)}) copy-start(f32[16,8,64]{2,1,0:T(8,128)} %reshape.499) | copy-start | bytes 98308
  233.9 4.3 %copy-start.42 = (f32[8,16,8]{1,0,2:T(8,128)S(1)}, f32[8,16,8]{1,0,2:T(8,128)}, u32[]{:S(2)}) copy-start(f32[8,16,8]{1,0,2:T(8,128)} %reshape.483) | copy-start | bytes 12292
  233.9 13.7 %copy-start.47 = (f32[8,16]{1,0:T(8,128)S(1)}, f32[8,16]{1,0:T(8,128)}, u32[]{:S(2)}) copy-start(f32[8,16]{1,0:T(8,128)} %copy-done.46) | copy-start | bytes 1540
  235.6 15.0 %copy-start.48 = (f32[128,8]{0,1:T(8,128)S(1)}, f32[128,8]{0,1:T(8,128)}, u32[]{:S(2)}) copy-start(f32[128,8]{0,1:T(8,128)} %get-tuple-element.13) | copy-start | bytes 12292
  235.6 59.4 %collective-permute-start.14 = (f32[2,2,2,2,2,2,2,2,1024]{8,7,6,5,4,3,2,1,0:T(2,128)}, f32[2,2,2,2,2,2,2,2,1024]{8,7,6,5,4,3,2,1,0:T(2,128)}, u32[]{:S(2)}, u32[]{:S(2)}) collective-permute-start(f32[2,2,2,2,2,2,2,2,1024]{8,7,6,5,4,3,2,1,0:T(2,128)} %bitcast.341), channel_id=1, source_target_pairs={{0,1},{1,0},{2,3},{3,2},{4,5},{5,4},{6,7},{7,6},{8,9},{9,8},{10,11... | collective-permute-start | bytes 3145736 | tf_op jit(solution)/shard_map/ppermute | solution.py:134
  242.0 5.7 %copy-start.35 = (bf16[2,8,640]{2,1,0:T(8,128)(2,1)}, bf16[2,8,640]{2,1,0:T(8,128)(2,1)S(1)}, u32[]{:S(2)}) copy-start(bf16[2,8,640]{2,1,0:T(8,128)(2,1)S(1)} %fusion.100) | copy-start | bytes 61444
  242.6 12.0 %collective-permute-start.7 = (bf16[8,640]{1,0:T(8,128)(2,1)}, bf16[8,640]{1,0:T(8,128)(2,1)}, u32[]{:S(2)}, u32[]{:S(2)}) collective-permute-start(bf16[8,640]{1,0:T(8,128)(2,1)} %slice_bitcast_fusion.6), channel_id=1, source_target_pairs={{0,256},{4,260},{8,264},{12,268},{16,272},{20,276},{24,280},{28,28... | collective-permute-start | bytes 30728 | tf_op jit(solution)/shard_map/ppermute | solution.py:16
  247.7 5.4 %copy-start.2 = (bf16[1024,8,64]{0,2,1:T(8,128)(2,1)S(1)}, bf16[1024,8,64]{0,2,1:T(8,128)(2,1)}, u32[]{:S(2)}) copy-start(bf16[1024,8,64]{0,2,1:T(8,128)(2,1)} %copy.1159) | copy-start | bytes 3145732
  250.6 3.9 copy-start.49
  250.6 13.1 %copy-start.9 = (bf16[128,512]{0,1:T(8,128)(2,1)S(1)}, bf16[128,512]{0,1:T(8,128)(2,1)}, u32[]{:S(2)}) copy-start(bf16[128,512]{0,1:T(8,128)(2,1)} %get-tuple-element.90) | copy-start | bytes 393220
  253.1 10.6 %copy-start.29 = (f32[2,8,8,64]{3,1,0,2:T(8,128)S(1)}, f32[2,8,8,64]{3,1,0,2:T(8,128)}, u32[]{:S(2)}) copy-start(f32[2,8,8,64]{3,1,0,2:T(8,128)} %fusion.29) | copy-start | bytes 98308
  253.1 11.5 %copy-start.30 = (f32[8,64,128]{2,1,0:T(8,128)S(1)}, f32[8,64,128]{2,1,0:T(8,128)}, u32[]{:S(2)}) copy-start(f32[8,64,128]{2,1,0:T(8,128)} %fusion.17) | copy-start | bytes 786436
  254.5 11.9 %copy-start.7 = (bf16[1,2,64,8,512]{4,3,2,1,0:T(8,128)(2,1)S(1)}, bf16[1,2,64,8,512]{4,3,2,1,0:T(8,128)(2,1)}, u32[]{:S(2)}) copy-start(bf16[1,2,64,8,512]{4,3,2,1,0:T(8,128)(2,1)} %get-tuple-element.18) | copy-start | bytes 3145732
  255.4 17.0 %collective-permute-start.8 = (bf16[3,1,8,640]{3,2,0,1:T(8,128)(2,1)S(1)}, bf16[3,1,8,640]{3,2,0,1:T(8,128)(2,1)S(1)}, u32[]{:S(2)}, u32[]{:S(2)}) collective-permute-start(bf16[3,1,8,640]{3,2,0,1:T(8,128)(2,1)S(1)} %fusion.129), channel_id=1, source_target_pairs={{0,16},{4,20},{8,24},{12,28},{16,0},{20,4},{24,8},{28,12},{32,48},... | collective-permute-start | bytes 92168 | tf_op jit(solution)/shard_map/ppermute | solution.py:16
  267.5 2.3 copy-start.6
  272.4 22.6 %copy-start.8 = (f32[2,2,2,2,2,2,2,2,1,1024]{9,8,7,6,5,4,3,2,1,0:T(1,128)S(1)}, f32[2,2,2,2,2,2,2,2,1,1024]{9,8,7,6,5,4,3,2,1,0:T(1,128)}, u32[]{:S(2)}) copy-start(f32[2,2,2,2,2,2,2,2,1,1024]{9,8,7,6,5,4,3,2,1,0:T(1,128)} %get-tuple-element.24) | copy-start | bytes 3145732
  273.0 8.7 %collective-permute-start.9 = (bf16[3,2,8,640]{3,2,0,1:T(8,128)(2,1)S(1)}, bf16[3,2,8,640]{3,2,0,1:T(8,128)(2,1)S(1)}, u32[]{:S(2)}, u32[]{:S(2)}) collective-permute-start(bf16[3,2,8,640]{3,2,0,1:T(8,128)(2,1)S(1)} %pad_maximum_fusion.23), channel_id=1, source_target_pairs={{0,8},{4,12},{8,0},{12,4},{16,24},{20,28},{24,16},{28,20},{32,40},... | collective-permute-start | bytes 184328 | tf_op jit(solution)/shard_map/ppermute | solution.py:16
  282.5 8.3 %collective-permute-start.10 = (bf16[3,4,8,640]{3,2,0,1:T(8,128)(2,1)S(1)}, bf16[3,4,8,640]{3,2,0,1:T(8,128)(2,1)S(1)}, u32[]{:S(2)}, u32[]{:S(2)}) collective-permute-start(bf16[3,4,8,640]{3,2,0,1:T(8,128)(2,1)S(1)} %pad_maximum_fusion.21), channel_id=1, source_target_pairs={{0,64},{4,68},{8,72},{12,76},{16,80},{20,84},{24,88},{28,92},{32,9... | collective-permute-start | bytes 368648 | tf_op jit(solution)/shard_map/ppermute | solution.py:16
  292.6 15.9 %collective-permute-start.11 = (bf16[320,640]{0,1:T(8,128)(2,1)S(1)}, bf16[320,640]{0,1:T(8,128)(2,1)S(1)}, u32[]{:S(2)}, u32[]{:S(2)}) collective-permute-start(bf16[320,640]{0,1:T(8,128)(2,1)S(1)} %pad_maximum_fusion.2), channel_id=1, source_target_pairs={{0,4},{4,0},{8,12},{12,8},{16,20},{20,16},{24,28},{28,24},{32,36},... | collective-permute-start | bytes 1228808 | tf_op jit(solution)/shard_map/ppermute | solution.py:16
  295.0 7.4 %copy-start.26 = (bf16[3,4,8,640]{3,2,0,1:T(8,128)(2,1)S(1)}, bf16[3,4,8,640]{3,2,0,1:T(8,128)(2,1)}, u32[]{:S(2)}) copy-start(bf16[3,4,8,640]{3,2,0,1:T(8,128)(2,1)} %copy-done.25) | copy-start | bytes 368644
  297.9 17.7 %collective-permute-start.15 = (f32[2,2,2,2,2,2,2,1024]{7,6,5,4,3,2,1,0:T(2,128)}, f32[2,2,2,2,2,2,2,1024]{7,6,5,4,3,2,1,0:T(2,128)S(1)}, u32[]{:S(2)}, u32[]{:S(2)}) collective-permute-start(f32[2,2,2,2,2,2,2,1024]{7,6,5,4,3,2,1,0:T(2,128)} %dynamic-slice_bitcast_fusion), channel_id=1, source_target_pairs={{0,4},{1,5},{2,6},{3,7},{4,0},{5,1},{6,2},{7,3},{8,12},{9,13},{10,... | collective-permute-start | bytes 1572872 | tf_op jit(solution)/shard_map/ppermute | solution.py:134
  310.5 34.9 %copy-start.11 = (bf16[1,128,512]{1,2,0:T(8,128)(2,1)S(1)}, bf16[1,128,512]{1,2,0:T(8,128)(2,1)}, u32[]{:S(2)}) copy-start(bf16[1,128,512]{1,2,0:T(8,128)(2,1)} %copy-done.10) | copy-start | bytes 393220
  310.5 35.0 %copy-start.17 = (bf16[1,128,512]{1,2,0:T(8,128)(2,1)S(1)}, bf16[1,128,512]{1,2,0:T(8,128)(2,1)}, u32[]{:S(2)}) copy-start(bf16[1,128,512]{1,2,0:T(8,128)(2,1)} %copy-done.16) | copy-start | bytes 393220
  310.5 35.0 %copy-start.18 = (bf16[128,512]{0,1:T(8,128)(2,1)S(1)}, bf16[128,512]{0,1:T(8,128)(2,1)}, u32[]{:S(2)}) copy-start(bf16[128,512]{0,1:T(8,128)(2,1)} %copy.1188) | copy-start | bytes 393220
  310.5 41.4 %collective-permute-start.12 = (bf16[3,16,8,640]{3,2,1,0:T(8,128)(2,1)}, bf16[3,16,8,640]{3,2,1,0:T(8,128)(2,1)S(1)}, u32[]{:S(2)}, u32[]{:S(2)}) collective-permute-start(bf16[3,16,8,640]{3,2,1,0:T(8,128)(2,1)} %get-tuple-element.46), channel_id=1, source_target_pairs={{0,32},{4,36},{8,40},{12,44},{16,48},{20,52},{24,56},{28,60},{32,0... | collective-permute-start | bytes 1474568 | tf_op jit(solution)/shard_map/ppermute | solution.py:16
  316.0 11.2 %collective-permute-start.16 = (f32[2,2,2,2,2,2,1024]{6,5,4,3,2,1,0:T(2,128)S(1)}, f32[2,2,2,2,2,2,1024]{6,5,4,3,2,1,0:T(2,128)S(1)}, u32[]{:S(2)}, u32[]{:S(2)}) collective-permute-start(f32[2,2,2,2,2,2,1024]{6,5,4,3,2,1,0:T(2,128)S(1)} %dynamic-slice_bitcast_fusion.1), channel_id=1, source_target_pairs={{0,32},{1,33},{2,34},{3,35},{4,36},{5,37},{6,38},{7,39},{8,40},{9,... | collective-permute-start | bytes 786440 | tf_op jit(solution)/shard_map/ppermute | solution.py:134
  327.4 6.9 %collective-permute-start.17 = (f32[2,2,2,2,2,1024]{5,4,3,2,1,0:T(2,128)S(1)}, f32[2,2,2,2,2,1024]{5,4,3,2,1,0:T(2,128)S(1)}, u32[]{:S(2)}, u32[]{:S(2)}) collective-permute-start(f32[2,2,2,2,2,1024]{5,4,3,2,1,0:T(2,128)S(1)} %dynamic-slice_bitcast_fusion.2), channel_id=1, source_target_pairs={{0,128},{1,129},{2,130},{3,131},{4,132},{5,133},{6,134},{7,135},{8... | collective-permute-start | bytes 393224 | tf_op jit(solution)/shard_map/ppermute | solution.py:134
  330.0 29.3 %copy-start.15 = (bf16[1,128,512]{1,2,0:T(8,128)(2,1)S(1)}, bf16[1,128,512]{1,2,0:T(8,128)(2,1)}, u32[]{:S(2)}) copy-start(bf16[1,128,512]{1,2,0:T(8,128)(2,1)} %copy.1153) | copy-start | bytes 393220
  330.0 29.3 %copy-start.19 = (bf16[128,512]{0,1:T(8,128)(2,1)S(1)}, bf16[128,512]{0,1:T(8,128)(2,1)}, u32[]{:S(2)}) copy-start(bf16[128,512]{0,1:T(8,128)(2,1)} %copy.1188) | copy-start | bytes 393220
  334.3 7.8 %collective-permute-start.18 = (f32[2,2,2,2,1024]{4,3,2,1,0:T(2,128)S(1)}, f32[2,2,2,2,1024]{4,3,2,1,0:T(2,128)S(1)}, u32[]{:S(2)}, u32[]{:S(2)}) collective-permute-start(f32[2,2,2,2,1024]{4,3,2,1,0:T(2,128)S(1)} %dynamic-slice_bitcast_fusion.3), channel_id=1, source_target_pairs={{0,8},{1,9},{2,10},{3,11},{4,12},{5,13},{6,14},{7,15},{8,0},{9,1},... | collective-permute-start | bytes 196616 | tf_op jit(solution)/shard_map/ppermute | solution.py:134
  342.1 7.3 %collective-permute-start.19 = (f32[2,2,2,1024]{3,2,1,0:T(2,128)S(1)}, f32[2,2,2,1024]{3,2,1,0:T(2,128)S(1)}, u32[]{:S(2)}, u32[]{:S(2)}) collective-permute-start(f32[2,2,2,1024]{3,2,1,0:T(2,128)S(1)} %dynamic-slice_bitcast_fusion.4), channel_id=1, source_target_pairs={{0,64},{1,65},{2,66},{3,67},{4,68},{5,69},{6,70},{7,71},{8,72},{9,... | collective-permute-start | bytes 98312 | tf_op jit(solution)/shard_map/ppermute | solution.py:134
  349.5 7.4 %collective-permute-start.20 = (f32[2,2,1024]{2,1,0:T(2,128)S(1)}, f32[2,2,1024]{2,1,0:T(2,128)S(1)}, u32[]{:S(2)}, u32[]{:S(2)}) collective-permute-start(f32[2,2,1024]{2,1,0:T(2,128)S(1)} %dynamic-slice_bitcast_fusion.5), channel_id=1, source_target_pairs={{0,256},{1,257},{2,258},{3,259},{4,260},{5,261},{6,262},{7,263},{8... | collective-permute-start | bytes 49160 | tf_op jit(solution)/shard_map/ppermute | solution.py:134
  353.0 28.2 %collective-permute-start.13 = (bf16[3,32,8,640]{3,2,1,0:T(8,128)(2,1)}, bf16[3,32,8,640]{3,2,1,0:T(8,128)(2,1)}, u32[]{:S(2)}, u32[]{:S(2)}) collective-permute-start(bf16[3,32,8,640]{3,2,1,0:T(8,128)(2,1)} %get-tuple-element.39), channel_id=1, source_target_pairs={{0,128},{4,132},{8,136},{12,140},{16,144},{20,148},{24,152},{28,15... | collective-permute-start | bytes 2949128 | tf_op jit(solution)/shard_map/ppermute | solution.py:16
  356.9 9.5 %collective-permute-start.21 = (f32[2,1024]{1,0:T(2,128)S(1)}, f32[2,1024]{1,0:T(2,128)S(1)}, u32[]{:S(2)}, u32[]{:S(2)}) collective-permute-start(f32[2,1024]{1,0:T(2,128)S(1)} %dynamic-slice_bitcast_fusion.6), channel_id=1, source_target_pairs={{0,16},{1,17},{2,18},{3,19},{4,20},{5,21},{6,22},{7,23},{8,24},{9,... | collective-permute-start | bytes 24584 | tf_op jit(solution)/shard_map/ppermute | solution.py:134
  366.4 14.2 %collective-permute-start.22 = (f32[1024]{0:T(1024)S(1)}, f32[1024]{0:T(1024)S(1)}, u32[]{:S(2)}, u32[]{:S(2)}) collective-permute-start(f32[1024]{0:T(1024)S(1)} %bitcast.433), channel_id=1, source_target_pairs={{0,2},{1,3},{2,0},{3,1},{4,6},{5,7},{6,4},{7,5},{8,10},{9,11},{10,... | collective-permute-start | bytes 12296 | tf_op jit(solution)/shard_map/ppermute | solution.py:134
  392.4 2.7 copy-start.37
  404.3 2.9 copy-start.1
  (15 other events, 17.4 us)

commit v6 on v4

--- a/solution.py
+++ b/solution.py
@@ -227,7 +227,7 @@
     devices = lax.axis_size("tm")
     bit_count = devices.bit_length() - 1
     top_bit = bit_count - 1
-    near_first = {0: 3, 1: 1, 2: 0, 3: 4, 4: 2, 5: 5}
+    near_first = {0: 1, 1: 2, 2: 0, 3: 4, 4: 3, 5: 5}
     low_bits = sorted(range(top_bit), key=lambda b: near_first.get(b, b))
     wide = features + 128
 

time: 381 us -> 394 us (1.034)
  starting transfers between devices: 89.5 us -> 97.4 us
  waiting for transfers between devices: 108 us -> 114 us
    ppermute x14, starting transfers between devices: 64.5 us -> 69.5 us  [partner(): return lax.ppermute(value, axis, pairs)]
    unnamed x139 -> x136, local copies, waits for them, and re-layouts: 15.3 us -> 16.3 us
  transfers between devices with their start and end apart: 23 -> 23, of which waited for: 18 -> 19; matrix products, arithmetic and copies ran while one was open for 27% -> 27% of each run, Pallas kernels for 0% -> 0%
where the time goes in v6:
time: 394 us; the launch traced here: 391 us
  local copies, waits for them, and re-layouts  116 us (29%)
  waiting for transfers between devices  114 us (29%)
  starting transfers between devices  97.4 us (25%)
  other arithmetic  33.7 us (9%)
  matrix products  28 us (7%)
    ppermute x14, waiting for transfers between devices, partner(): return lax.ppermute(value, axis, pairs)  84.1 us
    ppermute x14, starting transfers between devices, partner(): return lax.ppermute(value, axis, pairs)  69.5 us
    another operation x18, local copies, waits for them, and re-layouts, heads_view(): return matrix.reshape(matrix.shape[0], HEADS, HD)  37.2 us
    ppermute x9, waiting for transfers between devices, scatter_sum(): block = keep + lax.ppermute(send, axes, pairs)  29.7 us
    ppermute x9, starting transfers between devices, scatter_sum(): block = keep + lax.ppermute(send, axes, pairs)  27.9 us
    unnamed x136, local copies, waits for them, and re-layouts  16.3 us
    mul x26, local copies, waits for them, and re-layouts, spread_rows(): values[:, None] * chooser  14.3 us
  transfers between devices with their start and end apart: 23, of which 19 were waited for; matrix products, arithmetic and copies ran while one was open for 27% of the time, Pallas kernels for 0%

profile of v6, /device:TPU:6, one launch (start us, length us, event | category | flops | bytes accessed | tf_op | source)
XLA Modules:
  0.0 390.7 jit_solution(335744825354562129)
XLA Ops:
  6.0 9.1 %collective-permute-start = (bf16[3,2,1,8,512]{4,3,1,0,2:T(8,128)(2,1)S(1)}, bf16[3,2,1,8,512]{4,3,1,0,2:T(8,128)(2,1)S(1)}, u32[]{:S(2)}, u32[]{:S(2)}) collective-permute-start(bf16[3,2,1,8,512]{4,3,1,0,2:T(8,128)(2,1)S(1)} %bitcast.396), channel_id=1, source_target_pairs={{0,16},{4,20},{8,24},{12,28},{16,0},{20,4},{24,8},{28,12},{32,48},... | collective-permute-start | bytes 147464 | tf_op jit(solution)/shard_map/ppermute | solution.py:16
  15.2 2.0 collective-permute-done
  17.3 3.8 collective-permute-start.1
  21.1 10.4 %collective-permute-done.1 = bf16[480,512]{1,0:T(8,128)(2,1)S(1)} collective-permute-done((bf16[480,512]{1,0:T(8,128)(2,1)S(1)}, bf16[480,512]{1,0:T(8,128)(2,1)S(1)}, u32[]{:S(2)}, u32[]{:S(2)}) %collective-permute-start.1) | collective-permute-done | bytes 491552 | tf_op jit(solution)/shard_map/ppermute | solution.py:16
  31.5 6.8 %collective-permute-start.2 = (bf16[3,2,4,8,512]{4,3,2,1,0:T(8,128)(2,1)S(1)}, bf16[3,2,4,8,512]{4,3,2,1,0:T(8,128)(2,1)S(1)}, u32[]{:S(2)}, u32[]{:S(2)}) collective-permute-start(bf16[3,2,4,8,512]{4,3,2,1,0:T(8,128)(2,1)S(1)} %pad_maximum_fusion.11), channel_id=1, source_target_pairs={{0,8},{4,12},{8,0},{12,4},{16,24},{20,28},{24,16},{28,20},{32,40},... | collective-permute-start | bytes 589832 | tf_op jit(solution)/shard_map/ppermute | solution.py:16
  39.0 7.9 %collective-permute-done.2 = bf16[3,2,4,8,512]{4,3,2,1,0:T(8,128)(2,1)S(1)} collective-permute-done((bf16[3,2,4,8,512]{4,3,2,1,0:T(8,128)(2,1)S(1)}, bf16[3,2,4,8,512]{4,3,2,1,0:T(8,128)(2,1)S(1)}, u32[]{:S(2)}, u32[]{:S(2)}) %collective-permute-start.2) | collective-permute-done | bytes 196640 | tf_op jit(solution)/shard_map/ppermute | solution.py:16
  46.9 3.3 collective-permute-start.3
  52.3 8.1 %collective-permute-done.3 = bf16[3,2,8,8,512]{4,3,2,1,0:T(8,128)(2,1)S(1)} collective-permute-done((bf16[3,2,8,8,512]{4,3,2,1,0:T(8,128)(2,1)S(1)}, bf16[3,2,8,8,512]{4,3,2,1,0:T(8,128)(2,1)S(1)}, u32[]{:S(2)}, u32[]{:S(2)}) %collective-permute-start.3) | collective-permute-done | bytes 393248 | tf_op jit(solution)/shard_map/ppermute | solution.py:16
  61.4 2.9 collective-permute-start.4
  64.3 16.8 %collective-permute-done.4 = bf16[3,2,16,8,512]{4,3,2,1,0:T(8,128)(2,1)S(1)} collective-permute-done((bf16[3,2,16,8,512]{4,3,2,1,0:T(8,128)(2,1)S(1)}, bf16[3,2,16,8,512]{4,3,2,1,0:T(8,128)(2,1)S(1)}, u32[]{:S(2)}, u32[]{:S(2)}) %collective-permute-start.4) | collective-permute-done | bytes 786464 | tf_op jit(solution)/shard_map/ppermute | solution.py:16
  82.3 3.5 collective-permute-start.5
  96.9 21.2 %collective-permute-done.5 = bf16[3,2,32,8,512]{4,3,2,1,0:T(8,128)(2,1)} collective-permute-done((bf16[3,2,32,8,512]{4,3,2,1,0:T(8,128)(2,1)}, bf16[3,2,32,8,512]{4,3,2,1,0:T(8,128)(2,1)}, u32[]{:S(2)}, u32[]{:S(2)}) %collective-permute-start.5) | collective-permute-done | bytes 1572896 | tf_op jit(solution)/shard_map/ppermute | solution.py:16
  118.1 2.8 constant_dynamic-update-slice_fusion.11
  120.9 2.7 slice_bitcast_fusion
  123.6 5.3 %collective-permute-start.6 = (bf16[3,64,8,512]{3,2,1,0:T(8,128)(2,1)}, bf16[3,64,8,512]{3,2,1,0:T(8,128)(2,1)}, u32[]{:S(2)}, u32[]{:S(2)}) collective-permute-start(bf16[3,64,8,512]{3,2,1,0:T(8,128)(2,1)} %slice_bitcast_fusion), channel_id=1, source_target_pairs={{0,256},{4,260},{8,264},{12,268},{16,272},{20,276},{24,280},{28,28... | collective-permute-start | bytes 4718600 | tf_op jit(solution)/shard_map/ppermute | solution.py:16
  128.9 3.5 fusion.133
  132.3 2.1 reshape_reshape_squeeze.6
  134.4 2.5 copy.976
  137.0 4.2 %reshape_reshape_squeeze.14 = bf16[1024,8,64]{2,1,0:T(8,128)(2,1)} reshape(bf16[1,2,64,8,512]{4,3,2,1,0:T(8,128)(2,1)} %get-tuple-element.21) | data formatting | bytes 2097152 | tf_op jit(solution)/shard_map/reshape;reshape;squeeze | solution.py:140
  141.1 3.3 copy.985
  149.7 3.9 reshape_reshape_squeeze.15
  153.6 3.3 copy.1041
  157.0 2.3 slice_bitcast_fusion.3
  159.9 2.3 slice_bitcast_fusion.2
  163.4 2.1 reshape_reshape.28
  165.5 2.5 copy.981
  171.4 3.9 reshape_reshape.29
  175.3 3.4 copy.988
  183.1 1.9 copy.993
  188.4 2.8 fusion.65
  197.8 1.9 fusion.55
  201.4 3.2 constant_dynamic-slice_fusion.3
  206.3 2.0 collective-permute-start.14
  216.2 8.7 %collective-permute-start.7 = (bf16[2,1,8,640]{3,2,0,1:T(8,128)(2,1)}, bf16[2,1,8,640]{3,2,0,1:T(8,128)(2,1)}, u32[]{:S(2)}, u32[]{:S(2)}) collective-permute-start(bf16[2,1,8,640]{3,2,0,1:T(8,128)(2,1)} %bitcast.78), channel_id=1, source_target_pairs={{0,16},{4,20},{8,24},{12,28},{16,0},{20,4},{24,8},{28,12},{32,48},... | collective-permute-start | bytes 61448 | tf_op jit(solution)/shard_map/ppermute | solution.py:16
  225.5 3.0 fusion.29
  229.8 2.4 fusion.17
  232.3 2.0 fusion.35
  243.0 6.2 %collective-permute-start.8 = (bf16[160,640]{0,1:T(8,128)(2,1)S(1)}, bf16[160,640]{0,1:T(8,128)(2,1)S(1)}, u32[]{:S(2)}, u32[]{:S(2)}) collective-permute-start(bf16[160,640]{0,1:T(8,128)(2,1)S(1)} %pad_maximum_fusion.6), channel_id=1, source_target_pairs={{0,4},{4,0},{8,12},{12,8},{16,20},{20,16},{24,28},{28,24},{32,36},... | collective-permute-start | bytes 614408 | tf_op jit(solution)/shard_map/ppermute | solution.py:16
  250.6 6.7 %collective-permute-done.8 = bf16[160,640]{0,1:T(8,128)(2,1)S(1)} collective-permute-done((bf16[160,640]{0,1:T(8,128)(2,1)S(1)}, bf16[160,640]{0,1:T(8,128)(2,1)S(1)}, u32[]{:S(2)}, u32[]{:S(2)}) %collective-permute-start.8) | collective-permute-done | bytes 204832 | tf_op jit(solution)/shard_map/ppermute | solution.py:16
  258.3 5.3 %collective-permute-start.9 = (bf16[2,4,8,640]{3,2,1,0:T(8,128)(2,1)S(1)}, bf16[2,4,8,640]{3,2,1,0:T(8,128)(2,1)S(1)}, u32[]{:S(2)}, u32[]{:S(2)}) collective-permute-start(bf16[2,4,8,640]{3,2,1,0:T(8,128)(2,1)S(1)} %pad_maximum_fusion.24), channel_id=1, source_target_pairs={{0,8},{4,12},{8,0},{12,4},{16,24},{20,28},{24,16},{28,20},{32,40},... | collective-permute-start | bytes 245768 | tf_op jit(solution)/shard_map/ppermute | solution.py:16
  265.2 2.5 collective-permute-done.9
  268.4 3.3 collective-permute-start.10
  273.3 3.9 collective-permute-done.10
  277.9 2.7 collective-permute-start.11
  284.0 3.2 collective-permute-done.11
  289.1 3.7 collective-permute-start.12
  294.8 2.1 bitcast_add_fusion
  297.8 4.2 %collective-permute-start.15 = (f32[2,2,2,2,2,2,2,1024]{7,6,5,4,3,2,1,0:T(2,128)}, f32[2,2,2,2,2,2,2,1024]{7,6,5,4,3,2,1,0:T(2,128)}, u32[]{:S(2)}, u32[]{:S(2)}) collective-permute-start(f32[2,2,2,2,2,2,2,1024]{7,6,5,4,3,2,1,0:T(2,128)} %dynamic-slice_bitcast_fusion), channel_id=1, source_target_pairs={{0,4},{1,5},{2,6},{3,7},{4,0},{5,1},{6,2},{7,3},{8,12},{9,13},{10,... | collective-permute-start | bytes 1572872 | tf_op jit(solution)/shard_map/ppermute | solution.py:134
  308.2 3.7 collective-permute-done.15
  313.4 2.7 collective-permute-start.16
  317.8 3.9 collective-permute-done.16
  321.9 2.4 collective-permute-start.17
  325.1 3.6 collective-permute-done.17
  328.8 5.3 %collective-permute-start.18 = (f32[2,2,2,2,1024]{4,3,2,1,0:T(2,128)S(1)}, f32[2,2,2,2,1024]{4,3,2,1,0:T(2,128)S(1)}, u32[]{:S(2)}, u32[]{:S(2)}) collective-permute-start(f32[2,2,2,2,1024]{4,3,2,1,0:T(2,128)S(1)} %dynamic-slice_bitcast_fusion.3), channel_id=1, source_target_pairs={{0,8},{1,9},{2,10},{3,11},{4,12},{5,13},{6,14},{7,15},{8,0},{9,1},... | collective-permute-start | bytes 196616 | tf_op jit(solution)/shard_map/ppermute | solution.py:134
  334.9 1.9 copy.1038
  336.9 4.8 %collective-permute-start.13 = (bf16[64,8,640]{2,1,0:T(8,128)(2,1)}, bf16[64,8,640]{2,1,0:T(8,128)(2,1)}, u32[]{:S(2)}, u32[]{:S(2)}) collective-permute-start(bf16[64,8,640]{2,1,0:T(8,128)(2,1)} %slice_bitcast_fusion.1), channel_id=1, source_target_pairs={{0,256},{4,260},{8,264},{12,268},{16,272},{20,276},{24,280},{28,28... | collective-permute-start | bytes 1966088 | tf_op jit(solution)/shard_map/ppermute | solution.py:16
  341.7 3.3 collective-permute-start.19
  345.1 2.3 fusion.11
  349.1 2.5 collective-permute-start.20
  352.4 3.8 collective-permute-done.20
  356.3 3.5 collective-permute-start.21
  361.7 4.1 %collective-permute-done.21 = f32[2,1024]{1,0:T(2,128)S(1)} collective-permute-done((f32[2,1024]{1,0:T(2,128)S(1)}, f32[2,1024]{1,0:T(2,128)S(1)}, u32[]{:S(2)}, u32[]{:S(2)}) %collective-permute-start.21) | collective-permute-done | bytes 8224 | tf_op jit(solution)/shard_map/ppermute | solution.py:134
  371.0 9.0 %collective-permute-done.22 = f32[1024]{0:T(1024)S(1)} collective-permute-done((f32[1024]{0:T(1024)S(1)}, f32[1024]{0:T(1024)S(1)}, u32[]{:S(2)}, u32[]{:S(2)}) %collective-permute-start.22) | collective-permute-done | bytes 4128 | tf_op jit(solution)/shard_map/ppermute | solution.py:134
  388.5 2.2 add_convert_fusion
  (330 shorter events, 112.0 us)
Async XLA Ops:
  0.6 3.7 copy-start.60
  0.7 3.1 copy-start.17
  0.7 3.3 copy-start.16
  6.0 11.2 %collective-permute-start = (bf16[3,2,1,8,512]{4,3,1,0,2:T(8,128)(2,1)S(1)}, bf16[3,2,1,8,512]{4,3,1,0,2:T(8,128)(2,1)S(1)}, u32[]{:S(2)}, u32[]{:S(2)}) collective-permute-start(bf16[3,2,1,8,512]{4,3,1,0,2:T(8,128)(2,1)S(1)} %bitcast.396), channel_id=1, source_target_pairs={{0,16},{4,20},{8,24},{12,28},{16,0},{20,4},{24,8},{28,12},{32,48},... | collective-permute-start | bytes 147464 | tf_op jit(solution)/shard_map/ppermute | solution.py:16
  17.3 14.2 %collective-permute-start.1 = (bf16[480,512]{1,0:T(8,128)(2,1)S(1)}, bf16[480,512]{1,0:T(8,128)(2,1)S(1)}, u32[]{:S(2)}, u32[]{:S(2)}) collective-permute-start(bf16[480,512]{1,0:T(8,128)(2,1)S(1)} %pad_maximum_fusion.3), channel_id=1, source_target_pairs={{0,4},{4,0},{8,12},{12,8},{16,20},{20,16},{24,28},{28,24},{32,36},... | collective-permute-start | bytes 1474568 | tf_op jit(solution)/shard_map/ppermute | solution.py:16
  31.5 15.3 %collective-permute-start.2 = (bf16[3,2,4,8,512]{4,3,2,1,0:T(8,128)(2,1)S(1)}, bf16[3,2,4,8,512]{4,3,2,1,0:T(8,128)(2,1)S(1)}, u32[]{:S(2)}, u32[]{:S(2)}) collective-permute-start(bf16[3,2,4,8,512]{4,3,2,1,0:T(8,128)(2,1)S(1)} %pad_maximum_fusion.11), channel_id=1, source_target_pairs={{0,8},{4,12},{8,0},{12,4},{16,24},{20,28},{24,16},{28,20},{32,40},... | collective-permute-start | bytes 589832 | tf_op jit(solution)/shard_map/ppermute | solution.py:16
  46.9 13.5 %collective-permute-start.3 = (bf16[3,2,8,8,512]{4,3,2,1,0:T(8,128)(2,1)S(1)}, bf16[3,2,8,8,512]{4,3,2,1,0:T(8,128)(2,1)S(1)}, u32[]{:S(2)}, u32[]{:S(2)}) collective-permute-start(bf16[3,2,8,8,512]{4,3,2,1,0:T(8,128)(2,1)S(1)} %pad_maximum_fusion.5), channel_id=1, source_target_pairs={{0,64},{4,68},{8,72},{12,76},{16,80},{20,84},{24,88},{28,92},{32,9... | collective-permute-start | bytes 1179656 | tf_op jit(solution)/shard_map/ppermute | solution.py:16
  61.4 25.5 %copy-start.35 = (bf16[8,2,512]{2,1,0:T(2,128)(2,1)S(1)}, bf16[8,2,512]{2,1,0:T(2,128)(2,1)}, u32[]{:S(2)}) copy-start(bf16[8,2,512]{2,1,0:T(2,128)(2,1)} %copy-done.34) | copy-start | bytes 49156
  61.4 26.3 %copy-start.53 = (f32[8,8]{0,1:T(8,128)S(1)}, f32[8,8]{0,1:T(8,128)}, u32[]{:S(2)}) copy-start(f32[8,8]{0,1:T(8,128)} %constant.249.clone) | copy-start | bytes 772
  61.4 26.4 %copy-start.51 = (f32[16,8]{0,1:T(8,128)S(1)}, f32[16,8]{0,1:T(8,128)}, u32[]{:S(2)}) copy-start(f32[16,8]{0,1:T(8,128)} %constant.250.clone) | copy-start | bytes 1540
  61.4 26.5 %copy-start.40 = (bf16[16,8,64]{2,1,0:T(8,128)(2,1)S(1)}, bf16[16,8,64]{2,1,0:T(8,128)(2,1)}, u32[]{:S(2)}) copy-start(bf16[16,8,64]{2,1,0:T(8,128)(2,1)} %get-tuple-element.7) | copy-start | bytes 49156
  61.4 19.7 %collective-permute-start.4 = (bf16[3,2,16,8,512]{4,3,2,1,0:T(8,128)(2,1)S(1)}, bf16[3,2,16,8,512]{4,3,2,1,0:T(8,128)(2,1)S(1)}, u32[]{:S(2)}, u32[]{:S(2)}) collective-permute-start(bf16[3,2,16,8,512]{4,3,2,1,0:T(8,128)(2,1)S(1)} %get-tuple-element.41), channel_id=1, source_target_pairs={{0,32},{4,36},{8,40},{12,44},{16,48},{20,52},{24,56},{28,60},{32,0... | collective-permute-start | bytes 2359304 | tf_op jit(solution)/shard_map/ppermute | solution.py:16
  82.3 35.8 %collective-permute-start.5 = (bf16[3,2,32,8,512]{4,3,2,1,0:T(8,128)(2,1)}, bf16[3,2,32,8,512]{4,3,2,1,0:T(8,128)(2,1)}, u32[]{:S(2)}, u32[]{:S(2)}) collective-permute-start(bf16[3,2,32,8,512]{4,3,2,1,0:T(8,128)(2,1)} %get-tuple-element.31), channel_id=1, source_target_pairs={{0,128},{4,132},{8,136},{12,140},{16,144},{20,148},{24,152},{28,15... | collective-permute-start | bytes 4718600 | tf_op jit(solution)/shard_map/ppermute | solution.py:16
  86.0 9.7 %copy-start.21 = (bf16[1,128,512]{1,2,0:T(8,128)(2,1)}, bf16[1,128,512]{1,2,0:T(8,128)(2,1)S(1)}, u32[]{:S(2)}) copy-start(bf16[1,128,512]{1,2,0:T(8,128)(2,1)S(1)} %copy.959) | copy-start | bytes 393220
  86.1 9.6 %copy-start.14 = (bf16[1,128,512]{1,2,0:T(8,128)(2,1)}, bf16[1,128,512]{1,2,0:T(8,128)(2,1)S(1)}, u32[]{:S(2)}) copy-start(bf16[1,128,512]{1,2,0:T(8,128)(2,1)S(1)} %copy.963) | copy-start | bytes 393220
  87.8 8.3 %copy-start.43 = (f32[128,8]{0,1:T(8,128)}, f32[128,8]{0,1:T(8,128)S(1)}, u32[]{:S(2)}) copy-start(f32[128,8]{0,1:T(8,128)S(1)} %mul.636) | copy-start | bytes 12292
  87.9 8.2 %copy-start.45 = (f32[128,8]{0,1:T(8,128)}, f32[128,8]{0,1:T(8,128)S(1)}, u32[]{:S(2)}) copy-start(f32[128,8]{0,1:T(8,128)S(1)} %mul.646) | copy-start | bytes 12292
  88.0 8.1 %copy-start.41 = (bf16[2,8,512]{2,1,0:T(8,128)(2,1)}, bf16[2,8,512]{2,1,0:T(8,128)(2,1)S(1)}, u32[]{:S(2)}) copy-start(bf16[2,8,512]{2,1,0:T(8,128)(2,1)S(1)} %get-tuple-element.77) | copy-start | bytes 49156
  94.2 26.7 %copy-start.29 = (bf16[128,512]{0,1:T(8,128)(2,1)}, bf16[128,512]{0,1:T(8,128)(2,1)S(1)}, u32[]{:S(2)}) copy-start(bf16[128,512]{0,1:T(8,128)(2,1)S(1)} %copy.962) | copy-start | bytes 393220
  96.1 24.8 %copy-start.50 = (f32[8,128]{1,0:T(8,128)}, f32[8,128]{1,0:T(8,128)S(1)}, u32[]{:S(2)}) copy-start(f32[8,128]{1,0:T(8,128)S(1)} %get-tuple-element.100) | copy-start | bytes 12292
  123.6 36.3 %collective-permute-start.6 = (bf16[3,64,8,512]{3,2,1,0:T(8,128)(2,1)}, bf16[3,64,8,512]{3,2,1,0:T(8,128)(2,1)}, u32[]{:S(2)}, u32[]{:S(2)}) collective-permute-start(bf16[3,64,8,512]{3,2,1,0:T(8,128)(2,1)} %slice_bitcast_fusion), channel_id=1, source_target_pairs={{0,256},{4,260},{8,264},{12,268},{16,272},{20,276},{24,280},{28,28... | collective-permute-start | bytes 4718600 | tf_op jit(solution)/shard_map/ppermute | solution.py:16
  136.9 7.5 %copy-start.3 = (bf16[1024,8,64]{0,2,1:T(8,128)(2,1)}, bf16[1024,8,64]{0,2,1:T(8,128)(2,1)S(1)}, u32[]{:S(2)}) copy-start(bf16[1024,8,64]{0,2,1:T(8,128)(2,1)S(1)} %copy.976) | copy-start | bytes 3145732
  165.5 3.8 copy-start.52
  178.7 9.8 %copy-start.44 = (f32[128,8]{0,1:T(8,128)S(1)}, f32[128,8]{0,1:T(8,128)}, u32[]{:S(2)}) copy-start(f32[128,8]{0,1:T(8,128)} %copy-done.43) | copy-start | bytes 12292
  178.7 9.8 %copy-start.46 = (f32[128,8]{0,1:T(8,128)S(1)}, f32[128,8]{0,1:T(8,128)}, u32[]{:S(2)}) copy-start(f32[128,8]{0,1:T(8,128)} %copy-done.45) | copy-start | bytes 12292
  197.8 3.0 copy-start.36
  204.7 3.7 copy-start.32
  204.7 3.7 copy-start.33
  204.7 3.7 copy-start.54
  206.3 23.5 %copy-start.19 = (bf16[1,128,512]{1,2,0:T(8,128)(2,1)S(1)}, bf16[1,128,512]{1,2,0:T(8,128)(2,1)}, u32[]{:S(2)}) copy-start(bf16[1,128,512]{1,2,0:T(8,128)(2,1)} %copy.982) | copy-start | bytes 393220
  206.3 23.5 %copy-start.47 = (f32[128,8]{0,1:T(8,128)S(1)}, f32[128,8]{0,1:T(8,128)}, u32[]{:S(2)}) copy-start(f32[128,8]{0,1:T(8,128)} %get-tuple-element.15) | copy-start | bytes 12292
  206.3 88.5 %collective-permute-start.14 = (f32[2,2,2,2,2,2,2,2,1024]{8,7,6,5,4,3,2,1,0:T(2,128)}, f32[2,2,2,2,2,2,2,2,1024]{8,7,6,5,4,3,2,1,0:T(2,128)}, u32[]{:S(2)}, u32[]{:S(2)}) collective-permute-start(f32[2,2,2,2,2,2,2,2,1024]{8,7,6,5,4,3,2,1,0:T(2,128)} %bitcast.359), channel_id=1, source_target_pairs={{0,1},{1,0},{2,3},{3,2},{4,5},{5,4},{6,7},{7,6},{8,9},{9,8},{10,11... | collective-permute-start | bytes 3145736 | tf_op jit(solution)/shard_map/ppermute | solution.py:134
  216.2 24.8 %collective-permute-start.7 = (bf16[2,1,8,640]{3,2,0,1:T(8,128)(2,1)}, bf16[2,1,8,640]{3,2,0,1:T(8,128)(2,1)}, u32[]{:S(2)}, u32[]{:S(2)}) collective-permute-start(bf16[2,1,8,640]{3,2,0,1:T(8,128)(2,1)} %bitcast.78), channel_id=1, source_target_pairs={{0,16},{4,20},{8,24},{12,28},{16,0},{20,4},{24,8},{28,12},{32,48},... | collective-permute-start | bytes 61448 | tf_op jit(solution)/shard_map/ppermute | solution.py:16
  225.5 6.7 %copy-start.2 = (bf16[1024,8,64]{0,2,1:T(8,128)(2,1)S(1)}, bf16[1024,8,64]{0,2,1:T(8,128)(2,1)}, u32[]{:S(2)}) copy-start(bf16[1024,8,64]{0,2,1:T(8,128)(2,1)} %copy.988) | copy-start | bytes 3145732
  228.5 3.8 copy-start.56
  234.3 2.3 copy-start.31
  234.3 3.1 copy-start.38
  239.5 24.2 %copy-start.49 = (f32[8,128]{1,0:T(8,128)S(1)}, f32[8,128]{1,0:T(8,128)}, u32[]{:S(2)}) copy-start(f32[8,128]{1,0:T(8,128)} %get-tuple-element.19) | copy-start | bytes 12292
  239.5 24.2 %copy-start.15 = (bf16[1,128,512]{1,2,0:T(8,128)(2,1)S(1)}, bf16[1,128,512]{1,2,0:T(8,128)(2,1)}, u32[]{:S(2)}) copy-start(bf16[1,128,512]{1,2,0:T(8,128)(2,1)} %copy-done.14) | copy-start | bytes 393220
  243.0 37.7 %copy-start.55 = (f32[128,8]{0,1:T(8,128)S(1)}, f32[128,8]{0,1:T(8,128)}, u32[]{:S(2)}) copy-start(f32[128,8]{0,1:T(8,128)} %mul.660) | copy-start | bytes 12292
  243.0 37.7 %copy-start.20 = (bf16[1,128,512]{1,2,0:T(8,128)(2,1)S(1)}, bf16[1,128,512]{1,2,0:T(8,128)(2,1)}, u32[]{:S(2)}) copy-start(bf16[1,128,512]{1,2,0:T(8,128)(2,1)} %copy.982) | copy-start | bytes 393220
  243.0 37.7 %copy-start.23 = (bf16[128,512]{0,1:T(8,128)(2,1)S(1)}, bf16[128,512]{0,1:T(8,128)(2,1)}, u32[]{:S(2)}) copy-start(bf16[128,512]{0,1:T(8,128)(2,1)} %copy.1017) | copy-start | bytes 393220
  243.0 14.3 %collective-permute-start.8 = (bf16[160,640]{0,1:T(8,128)(2,1)S(1)}, bf16[160,640]{0,1:T(8,128)(2,1)S(1)}, u32[]{:S(2)}, u32[]{:S(2)}) collective-permute-start(bf16[160,640]{0,1:T(8,128)(2,1)S(1)} %pad_maximum_fusion.6), channel_id=1, source_target_pairs={{0,4},{4,0},{8,12},{12,8},{16,20},{20,16},{24,28},{28,24},{32,36},... | collective-permute-start | bytes 614408 | tf_op jit(solution)/shard_map/ppermute | solution.py:16
  258.3 9.4 %collective-permute-start.9 = (bf16[2,4,8,640]{3,2,1,0:T(8,128)(2,1)S(1)}, bf16[2,4,8,640]{3,2,1,0:T(8,128)(2,1)S(1)}, u32[]{:S(2)}, u32[]{:S(2)}) collective-permute-start(bf16[2,4,8,640]{3,2,1,0:T(8,128)(2,1)S(1)} %pad_maximum_fusion.24), channel_id=1, source_target_pairs={{0,8},{4,12},{8,0},{12,4},{16,24},{20,28},{24,16},{28,20},{32,40},... | collective-permute-start | bytes 245768 | tf_op jit(solution)/shard_map/ppermute | solution.py:16
  268.4 8.7 %collective-permute-start.10 = (bf16[2,8,8,640]{3,2,1,0:T(8,128)(2,1)S(1)}, bf16[2,8,8,640]{3,2,1,0:T(8,128)(2,1)S(1)}, u32[]{:S(2)}, u32[]{:S(2)}) collective-permute-start(bf16[2,8,8,640]{3,2,1,0:T(8,128)(2,1)S(1)} %pad_maximum_fusion.22), channel_id=1, source_target_pairs={{0,64},{4,68},{8,72},{12,76},{16,80},{20,84},{24,88},{28,92},{32,9... | collective-permute-start | bytes 491528 | tf_op jit(solution)/shard_map/ppermute | solution.py:16
  272.5 8.2 %copy-start.22 = (bf16[128,512]{0,1:T(8,128)(2,1)}, bf16[128,512]{0,1:T(8,128)(2,1)S(1)}, u32[]{:S(2)}) copy-start(bf16[128,512]{0,1:T(8,128)(2,1)S(1)} %slice.208) | copy-start | bytes 393220
  277.9 9.3 %collective-permute-start.11 = (bf16[2,16,8,640]{3,2,1,0:T(8,128)(2,1)}, bf16[2,16,8,640]{3,2,1,0:T(8,128)(2,1)}, u32[]{:S(2)}, u32[]{:S(2)}) collective-permute-start(bf16[2,16,8,640]{3,2,1,0:T(8,128)(2,1)} %get-tuple-element.53), channel_id=1, source_target_pairs={{0,32},{4,36},{8,40},{12,44},{16,48},{20,52},{24,56},{28,60},{32,0... | collective-permute-start | bytes 983048 | tf_op jit(solution)/shard_map/ppermute | solution.py:16
  282.1 12.7 %copy-start.6 = (f32[2,2,2,2,2,2,2,2,1,1024]{9,8,7,6,5,4,3,2,1,0:T(1,128)S(1)}, f32[2,2,2,2,2,2,2,2,1,1024]{9,8,7,6,5,4,3,2,1,0:T(1,128)}, u32[]{:S(2)}) copy-start(f32[2,2,2,2,2,2,2,2,1,1024]{9,8,7,6,5,4,3,2,1,0:T(1,128)} %get-tuple-element.26) | copy-start | bytes 3145732
  289.1 13.7 %collective-permute-start.12 = (bf16[2,32,8,640]{3,2,1,0:T(8,128)(2,1)}, bf16[2,32,8,640]{3,2,1,0:T(8,128)(2,1)}, u32[]{:S(2)}, u32[]{:S(2)}) collective-permute-start(bf16[2,32,8,640]{3,2,1,0:T(8,128)(2,1)} %get-tuple-element.42), channel_id=1, source_target_pairs={{0,128},{4,132},{8,136},{12,140},{16,144},{20,148},{24,152},{28,15... | collective-permute-start | bytes 1966088 | tf_op jit(solution)/shard_map/ppermute | solution.py:16
  294.8 8.0 %copy-start.7 = (bf16[2,64,8,640]{3,2,1,0:T(8,128)(2,1)S(1)}, bf16[2,64,8,640]{3,2,1,0:T(8,128)(2,1)}, u32[]{:S(2)}) copy-start(bf16[2,64,8,640]{3,2,1,0:T(8,128)(2,1)} %get-tuple-element.43) | copy-start | bytes 3932164
  297.8 14.1 %collective-permute-start.15 = (f32[2,2,2,2,2,2,2,1024]{7,6,5,4,3,2,1,0:T(2,128)}, f32[2,2,2,2,2,2,2,1024]{7,6,5,4,3,2,1,0:T(2,128)}, u32[]{:S(2)}, u32[]{:S(2)}) collective-permute-start(f32[2,2,2,2,2,2,2,1024]{7,6,5,4,3,2,1,0:T(2,128)} %dynamic-slice_bitcast_fusion), channel_id=1, source_target_pairs={{0,4},{1,5},{2,6},{3,7},{4,0},{5,1},{6,2},{7,3},{8,12},{9,13},{10,... | collective-permute-start | bytes 1572872 | tf_op jit(solution)/shard_map/ppermute | solution.py:134
  305.1 11.0 %copy-start.9 = (bf16[2,64,8,640]{3,2,1,0:T(8,128)(2,1)S(1)}, bf16[2,64,8,640]{3,2,1,0:T(8,128)(2,1)}, u32[]{:S(2)}) copy-start(bf16[2,64,8,640]{3,2,1,0:T(8,128)(2,1)} %copy-done.8) | copy-start | bytes 3932164
  313.4 8.3 %collective-permute-start.16 = (f32[2,2,2,2,2,2,1024]{6,5,4,3,2,1,0:T(2,128)S(1)}, f32[2,2,2,2,2,2,1024]{6,5,4,3,2,1,0:T(2,128)S(1)}, u32[]{:S(2)}, u32[]{:S(2)}) collective-permute-start(f32[2,2,2,2,2,2,1024]{6,5,4,3,2,1,0:T(2,128)S(1)} %dynamic-slice_bitcast_fusion.1), channel_id=1, source_target_pairs={{0,32},{1,33},{2,34},{3,35},{4,36},{5,37},{6,38},{7,39},{8,40},{9,... | collective-permute-start | bytes 786440 | tf_op jit(solution)/shard_map/ppermute | solution.py:134
  321.9 6.9 %collective-permute-start.17 = (f32[2,2,2,2,2,1024]{5,4,3,2,1,0:T(2,128)S(1)}, f32[2,2,2,2,2,1024]{5,4,3,2,1,0:T(2,128)S(1)}, u32[]{:S(2)}, u32[]{:S(2)}) collective-permute-start(f32[2,2,2,2,2,1024]{5,4,3,2,1,0:T(2,128)S(1)} %dynamic-slice_bitcast_fusion.2), channel_id=1, source_target_pairs={{0,128},{1,129},{2,130},{3,131},{4,132},{5,133},{6,134},{7,135},{8... | collective-permute-start | bytes 393224 | tf_op jit(solution)/shard_map/ppermute | solution.py:134
  328.8 12.8 %collective-permute-start.18 = (f32[2,2,2,2,1024]{4,3,2,1,0:T(2,128)S(1)}, f32[2,2,2,2,1024]{4,3,2,1,0:T(2,128)S(1)}, u32[]{:S(2)}, u32[]{:S(2)}) collective-permute-start(f32[2,2,2,2,1024]{4,3,2,1,0:T(2,128)S(1)} %dynamic-slice_bitcast_fusion.3), channel_id=1, source_target_pairs={{0,8},{1,9},{2,10},{3,11},{4,12},{5,13},{6,14},{7,15},{8,0},{9,1},... | collective-permute-start | bytes 196616 | tf_op jit(solution)/shard_map/ppermute | solution.py:134
  334.9 10.2 %copy-start.39 = (bf16[16,8,64]{2,1,0:T(8,128)(2,1)S(1)}, bf16[16,8,64]{2,1,0:T(8,128)(2,1)}, u32[]{:S(2)}) copy-start(bf16[16,8,64]{2,1,0:T(8,128)(2,1)} %reshape_reshape_squeeze_stack.11) | copy-start | bytes 49156
  336.8 22.9 %copy-start.37 = (bf16[16,8,64]{2,1,0:T(8,128)(2,1)S(1)}, bf16[16,8,64]{2,1,0:T(8,128)(2,1)}, u32[]{:S(2)}) copy-start(bf16[16,8,64]{2,1,0:T(8,128)(2,1)} %reshape_reshape_squeeze_stack.12) | copy-start | bytes 49156
  336.9 43.7 %collective-permute-start.13 = (bf16[64,8,640]{2,1,0:T(8,128)(2,1)}, bf16[64,8,640]{2,1,0:T(8,128)(2,1)}, u32[]{:S(2)}, u32[]{:S(2)}) collective-permute-start(bf16[64,8,640]{2,1,0:T(8,128)(2,1)} %slice_bitcast_fusion.1), channel_id=1, source_target_pairs={{0,256},{4,260},{8,264},{12,268},{16,272},{20,276},{24,280},{28,28... | collective-permute-start | bytes 1966088 | tf_op jit(solution)/shard_map/ppermute | solution.py:16
  341.7 7.3 %collective-permute-start.19 = (f32[2,2,2,1024]{3,2,1,0:T(2,128)S(1)}, f32[2,2,2,1024]{3,2,1,0:T(2,128)S(1)}, u32[]{:S(2)}, u32[]{:S(2)}) collective-permute-start(f32[2,2,2,1024]{3,2,1,0:T(2,128)S(1)} %dynamic-slice_bitcast_fusion.4), channel_id=1, source_target_pairs={{0,64},{1,65},{2,66},{3,67},{4,68},{5,69},{6,70},{7,71},{8,72},{9,... | collective-permute-start | bytes 98312 | tf_op jit(solution)/shard_map/ppermute | solution.py:134
  349.1 7.1 %collective-permute-start.20 = (f32[2,2,1024]{2,1,0:T(2,128)S(1)}, f32[2,2,1024]{2,1,0:T(2,128)S(1)}, u32[]{:S(2)}, u32[]{:S(2)}) collective-permute-start(f32[2,2,1024]{2,1,0:T(2,128)S(1)} %dynamic-slice_bitcast_fusion.5), channel_id=1, source_target_pairs={{0,256},{1,257},{2,258},{3,259},{4,260},{5,261},{6,262},{7,263},{8... | collective-permute-start | bytes 49160 | tf_op jit(solution)/shard_map/ppermute | solution.py:134
  356.3 9.5 %collective-permute-start.21 = (f32[2,1024]{1,0:T(2,128)S(1)}, f32[2,1024]{1,0:T(2,128)S(1)}, u32[]{:S(2)}, u32[]{:S(2)}) collective-permute-start(f32[2,1024]{1,0:T(2,128)S(1)} %dynamic-slice_bitcast_fusion.6), channel_id=1, source_target_pairs={{0,16},{1,17},{2,18},{3,19},{4,20},{5,21},{6,22},{7,23},{8,24},{9,... | collective-permute-start | bytes 24584 | tf_op jit(solution)/shard_map/ppermute | solution.py:134
  365.7 14.2 %collective-permute-start.22 = (f32[1024]{0:T(1024)S(1)}, f32[1024]{0:T(1024)S(1)}, u32[]{:S(2)}, u32[]{:S(2)}) collective-permute-start(f32[1024]{0:T(1024)S(1)} %bitcast.449), channel_id=1, source_target_pairs={{0,2},{1,3},{2,0},{3,1},{4,6},{5,7},{6,4},{7,5},{8,10},{9,11},{10,... | collective-permute-start | bytes 12296 | tf_op jit(solution)/shard_map/ppermute | solution.py:134
  369.1 11.5 %copy-start.10 = (bf16[64,8,640]{2,1,0:T(8,128)(2,1)S(1)}, bf16[64,8,640]{2,1,0:T(8,128)(2,1)}, u32[]{:S(2)}) copy-start(bf16[64,8,640]{2,1,0:T(8,128)(2,1)} %slice_bitcast_fusion.1) | copy-start | bytes 1966084
  387.4 3.2 copy-start.1
  (20 other events, 27.4 us)

commit v7 on v4

--- a/solution.py
+++ b/solution.py
@@ -229,24 +229,21 @@
     top_bit = bit_count - 1
     near_first = {0: 3, 1: 1, 2: 0, 3: 4, 4: 2, 5: 5}
     low_bits = sorted(range(top_bit), key=lambda b: near_first.get(b, b))
-    wide = features + 128
+    wide = 2 * features + 128
 
     qkv = jnp.stack([by_parity(pick_rows(m, R2)) for m in (queries, keys_all, values_all)], 0)
     per_par = qkv.shape[2]
-    own, other_qkv = gather_with_rider(
-        qkv[:, :, None], 2, low_bits, jnp.stack([queries, keys_all, values_all], 0)
+    own, other_kv = gather_with_rider(
+        qkv[1:, :, None], 2, low_bits, jnp.stack([keys_all, values_all], 0)
     )
     far = partner(own[:, 0], "tm", top_bit)
-    other_q = other_qkv[0]
-    keys_one = jnp.concatenate([keys_all, other_qkv[1]], 0)
-    values_one = jnp.concatenate([values_all, other_qkv[2]], 0)
+    keys_one = jnp.concatenate([keys_all, other_kv[0]], 0)
+    values_one = jnp.concatenate([values_all, other_kv[1]], 0)
     part_one, lse_one = attend(queries, keys_one, values_one, inv_root)
-    q_seg2 = own[0].reshape(-1, features)
-    k_seg2 = own[1].reshape(-1, features)
-    v_seg2 = own[2].reshape(-1, features)
-    q_seg3 = jnp.concatenate([own[0, 0], far[0]], 0).reshape(-1, features)
-    k_seg3 = jnp.concatenate([own[1, 0], far[1]], 0).reshape(-1, features)
-    v_seg3 = jnp.concatenate([own[2, 0], far[2]], 0).reshape(-1, features)
+    k_seg2 = own[0].reshape(-1, features)
+    v_seg2 = own[1].reshape(-1, features)
+    k_seg3 = jnp.concatenate([own[0, 0], far[0]], 0).reshape(-1, features)
+    v_seg3 = jnp.concatenate([own[1, 0], far[1]], 0).reshape(-1, features)
     q_two = qkv[0].reshape(-1, features)
     q_three = qkv[0, 0]
     part_two, lse_two = attend(q_two, k_seg2, v_seg2, inv_root)
@@ -284,7 +281,8 @@
 
     grad_one = grad_of(weights[0], grad_attn)
     offset_one = weights[0] * rowdot
-    packed_one = jnp.concatenate([grad_one, split_exact(jnp.concatenate([lse_one, offset_one], 1))], 1)
+    stats_one = split_exact(jnp.concatenate([lse_one, offset_one], 1))
+    packed_one = jnp.concatenate([queries, grad_one, stats_one], 1)
 
     ga_par = by_parity(pick_rows(grad_attn, R2))
     w_two = by_parity(pick_stats(weights[1], R2))
@@ -295,15 +293,16 @@
     lse3_par = jnp.stack([lse_three, no_level], 0)
     w3_par = jnp.stack([w_three, no_level], 0)
     stats_par = jnp.concatenate([lse_two_par, w_two, lse3_par, w3_par, rd_two], -1)
-    packed = pad_lanes(jnp.concatenate([ga_par, split_exact(stats_par)], -1), wide)
+    packed = pad_lanes(jnp.concatenate([qkv[0], ga_par, split_exact(stats_par)], -1), wide)
     own_b, other_one = gather_with_rider(packed[:, None], 1, low_bits, pad_lanes(packed_one, wide))
-    other_stats = join_exact(other_one[:, features : features + 6 * HEADS])
+    other_q = other_one[:, :features]
+    other_stats = join_exact(other_one[:, 2 * features : 2 * features + 6 * HEADS])
     total_q = spread_rows(
         near_grad(queries, keys_one, values_one, grad_one, lse_one, offset_one, inv_root), 1
     )
     k_g1, v_g1 = far_grad(
         jnp.concatenate([queries, other_q], 0),
-        jnp.concatenate([grad_one, other_one[:, :features]], 0),
+        jnp.concatenate([grad_one, other_one[:, features : 2 * features]], 0),
         jnp.concatenate([lse_one, other_stats[:, :HEADS]], 0),
         jnp.concatenate([offset_one, other_stats[:, HEADS:]], 0),
         keys_all,
@@ -317,13 +316,13 @@
 
     def unpack(rows):
         rows = rows.reshape(-1, wide)
-        stats = join_exact(rows[:, features : features + 3 * stat_w])
-        return rows[:, :features], stats.reshape(-1, 5, HEADS)
+        stats = join_exact(rows[:, 2 * features : 2 * features + 3 * stat_w])
+        return rows[:, :features], rows[:, features : 2 * features], stats.reshape(-1, 5, HEADS)
 
     g_two = grad_of(w_two.reshape(-1, HEADS), ga_par.reshape(-1, features))
     c_two = w_two.reshape(-1, HEADS) * rd_two.reshape(-1, HEADS)
     grad_q2 = near_grad(q_two, k_seg2, v_seg2, g_two, lse_two, c_two, inv_root)
-    ga_seg2, st_seg2 = unpack(own_b)
+    q_seg2, ga_seg2, st_seg2 = unpack(own_b)
     k_g2, v_g2 = far_grad(
         q_seg2,
         grad_of(st_seg2[:, 1], ga_seg2),
@@ -337,7 +336,7 @@
     g_three = grad_of(w_three, ga_par[0])
     c_three = w_three * rd_two[0]
     grad_q3 = near_grad(q_three, k_seg3, v_seg3, g_three, lse_three, c_three, inv_root)
-    ga_seg3, st_seg3 = unpack(jnp.concatenate([own_b[0], far_b], 0))
+    q_seg3, ga_seg3, st_seg3 = unpack(jnp.concatenate([own_b[0], far_b], 0))
     k_g3, v_g3 = far_grad(
         q_seg3,
         grad_of(st_seg3[:, 3], ga_seg3),

time: 381 us -> 394 us (1.034)
  local copies, waits for them, and re-layouts: 117 us -> 150 us
  waiting for transfers between devices: 108 us -> 78 us
  other arithmetic: 34.2 us -> 38.8 us
    ppermute x14, waiting for transfers between devices: 81.1 us -> 53.1 us  [partner(): return lax.ppermute(value, axis, pairs)]
    another operation x18 -> x14, local copies, waits for them, and re-layouts: 37.9 us -> 27.9 us  [heads_view(): return matrix.reshape(matrix.shape[0], HEADS, HD)]
    unnamed x139 -> x124, local copies, waits for them, and re-layouts: 15.3 us -> 24.4 us
    mul x26, local copies, waits for them, and re-layouts: 14.3 us -> 23 us  [spread_rows(): values[:, None] * chooser]
    ppermute x9, starting transfers between devices: 24.9 us -> 30.6 us  [scatter_sum(): block = keep + lax.ppermute(send, axes, pairs)]
    slice x6 -> x7, local copies, waits for them, and re-layouts: 5.14 us -> 9.97 us  [the longest x2 3.32 us: on_device(): values_one = jnp.concatenate([values_all, other_kv[1]], 0)]
  transfers between devices with their start and end apart: 23 -> 23, of which waited for: 18 -> 16; matrix products, arithmetic and copies ran while one was open for 27% -> 30% of each run, Pallas kernels for 0% -> 0%
where the time goes in v7:
time: 394 us; the launch traced here: 389 us
  local copies, waits for them, and re-layouts  150 us (38%)
  starting transfers between devices  93.2 us (24%)
  waiting for transfers between devices  78 us (20%)
  other arithmetic  38.8 us (10%)
  matrix products  27.6 us (7%)
    ppermute x14, starting transfers between devices, partner(): return lax.ppermute(value, axis, pairs)  62.6 us
    ppermute x14, waiting for transfers between devices, partner(): return lax.ppermute(value, axis, pairs)  53.1 us
    ppermute x9, starting transfers between devices, scatter_sum(): block = keep + lax.ppermute(send, axes, pairs)  30.6 us
    another operation x14, local copies, waits for them, and re-layouts, heads_view(): return matrix.reshape(matrix.shape[0], HEADS, HD)  27.9 us
    ppermute x9, waiting for transfers between devices, scatter_sum(): block = keep + lax.ppermute(send, axes, pairs)  24.9 us
    unnamed x124, local copies, waits for them, and re-layouts  24.4 us
    mul x26, local copies, waits for them, and re-layouts, spread_rows(): values[:, None] * chooser  23 us
  transfers between devices with their start and end apart: 23, of which 16 were waited for; matrix products, arithmetic and copies ran while one was open for 30% of the time, Pallas kernels for 0%

profile of v7, /device:TPU:6, one launch (start us, length us, event | category | flops | bytes accessed | tf_op | source)
XLA Modules:
  0.0 389.5 jit_solution(13576777680031982615)
XLA Ops:
  5.6 9.1 %collective-permute-start = (bf16[2,2,1,8,512]{4,3,1,0,2:T(8,128)(2,1)S(1)}, bf16[2,2,1,8,512]{4,3,1,0,2:T(8,128)(2,1)S(1)}, u32[]{:S(2)}, u32[]{:S(2)}) collective-permute-start(bf16[2,2,1,8,512]{4,3,1,0,2:T(8,128)(2,1)S(1)} %bitcast.398), channel_id=1, source_target_pairs={{0,16},{4,20},{8,24},{12,28},{16,0},{20,4},{24,8},{28,12},{32,48},... | collective-permute-start | bytes 98312 | tf_op jit(solution)/shard_map/ppermute | solution.py:16
  16.6 5.2 %collective-permute-start.1 = (bf16[2,2,2,8,512]{4,3,1,0,2:T(8,128)(2,1)S(1)}, bf16[2,2,2,8,512]{4,3,1,0,2:T(8,128)(2,1)S(1)}, u32[]{:S(2)}, u32[]{:S(2)}) collective-permute-start(bf16[2,2,2,8,512]{4,3,1,0,2:T(8,128)(2,1)S(1)} %pad_maximum_fusion.23), channel_id=1, source_target_pairs={{0,8},{4,12},{8,0},{12,4},{16,24},{20,28},{24,16},{28,20},{32,40},... | collective-permute-start | bytes 196616 | tf_op jit(solution)/shard_map/ppermute | solution.py:16
  21.8 3.6 collective-permute-done.1
  25.5 3.3 collective-permute-start.2
  29.4 4.4 %collective-permute-done.2 = bf16[2,2,4,8,512]{4,3,1,0,2:T(8,128)(2,1)S(1)} collective-permute-done((bf16[2,2,4,8,512]{4,3,1,0,2:T(8,128)(2,1)S(1)}, bf16[2,2,4,8,512]{4,3,1,0,2:T(8,128)(2,1)S(1)}, u32[]{:S(2)}, u32[]{:S(2)}) %collective-permute-start.2) | collective-permute-done | bytes 131104 | tf_op jit(solution)/shard_map/ppermute | solution.py:16
  33.9 2.4 collective-permute-start.3
  38.3 7.6 %collective-permute-done.3 = bf16[512,512]{1,0:T(8,128)(2,1)S(1)} collective-permute-done((bf16[512,512]{1,0:T(8,128)(2,1)S(1)}, bf16[512,512]{1,0:T(8,128)(2,1)S(1)}, u32[]{:S(2)}, u32[]{:S(2)}) %collective-permute-start.3) | collective-permute-done | bytes 524320 | tf_op jit(solution)/shard_map/ppermute | solution.py:16
  48.6 2.7 collective-permute-start.4
  69.0 1.9 constant_dynamic-update-slice_fusion.4
  70.9 3.5 collective-permute-start.5
  82.7 11.0 %collective-permute-done.5 = bf16[2,2,32,8,512]{4,3,2,1,0:T(8,128)(2,1)} collective-permute-done((bf16[2,2,32,8,512]{4,3,2,1,0:T(8,128)(2,1)}, bf16[2,2,32,8,512]{4,3,2,1,0:T(8,128)(2,1)}, u32[]{:S(2)}, u32[]{:S(2)}) %collective-permute-start.5) | collective-permute-done | bytes 1048608 | tf_op jit(solution)/shard_map/ppermute | solution.py:16
  97.9 5.3 %collective-permute-start.6 = (bf16[2,64,8,512]{3,2,1,0:T(8,128)(2,1)}, bf16[2,64,8,512]{3,2,1,0:T(8,128)(2,1)}, u32[]{:S(2)}, u32[]{:S(2)}) collective-permute-start(bf16[2,64,8,512]{3,2,1,0:T(8,128)(2,1)} %slice_bitcast_fusion.1), channel_id=1, source_target_pairs={{0,256},{4,260},{8,264},{12,268},{16,272},{20,276},{24,280},{28,28... | collective-permute-start | bytes 3145736 | tf_op jit(solution)/shard_map/ppermute | solution.py:16
  103.2 2.1 reshape_reshape_squeeze.4
  105.3 2.5 copy.867
  109.0 3.9 %reshape_reshape_squeeze.10 = bf16[1024,8,64]{2,1,0:T(8,128)(2,1)} reshape(bf16[1,2,64,8,512]{4,3,2,1,0:T(8,128)(2,1)} %get-tuple-element.24) | data formatting | bytes 2097152 | tf_op jit(solution)/shard_map/reshape;reshape;squeeze | solution.py:140
  112.9 3.4 copy.876
  126.8 2.1 reshape_reshape.24
  128.9 2.5 copy.872
  137.4 3.9 reshape_reshape.25
  141.3 3.3 copy.879
  147.1 1.9 mul.644
  149.0 1.9 copy.884
  155.7 2.3 fusion.63
  188.4 10.0 %collective-permute-start.7 = (bf16[2,1,8,1152]{3,2,0,1:T(8,128)(2,1)}, bf16[2,1,8,1152]{3,2,0,1:T(8,128)(2,1)}, u32[]{:S(2)}, u32[]{:S(2)}) collective-permute-start(bf16[2,1,8,1152]{3,2,0,1:T(8,128)(2,1)} %pad_bitcast_fusion), channel_id=1, source_target_pairs={{0,16},{4,20},{8,24},{12,28},{16,0},{20,4},{24,8},{28,12},{32,48},... | collective-permute-start | bytes 110600 | tf_op jit(solution)/shard_map/ppermute | solution.py:16
  203.3 2.1 fusion.55
  205.3 2.5 fusion.18
  208.6 2.2 fusion.30
  211.4 5.5 %constant_dynamic-slice_fusion.3 = (f32[2,2,2,2,2,2,2,2,1,1024]{9,8,7,6,5,4,3,2,1,0:T(1,128)S(1)}, f32[2,2,2,2,2,2,2,2,1,1024]{9,8,7,6,5,4,3,2,1,0:T(1,128)}) fusion(f32[2,2,2,2,2,2,2,2,2,1024]{9,8,7,6,5,4,3,2,1,0:T(2,128)} %fusion.55, s32[]{:T(128)S(6)} %select_n.151, s32[]{:T(128)S(6)} %select_n.152), kind=kLoop, calls=%fused_computation.260 | loop fusion | bytes 4194312 | tf_op jit(solution)/shard_map/jit(dynamic_index_in_dim)/dynamic_slice | solution.py:131
  219.8 2.1 mul.683
  223.5 1.9 mul.698
  225.4 2.9 copy.1012
  228.2 1.9 collective-permute-start.14
  231.0 6.2 %collective-permute-start.8 = (bf16[2,2,8,1152]{3,2,0,1:T(8,128)(2,1)S(1)}, bf16[2,2,8,1152]{3,2,0,1:T(8,128)(2,1)S(1)}, u32[]{:S(2)}, u32[]{:S(2)}) collective-permute-start(bf16[2,2,8,1152]{3,2,0,1:T(8,128)(2,1)S(1)} %pad_maximum_fusion.22), channel_id=1, source_target_pairs={{0,8},{4,12},{8,0},{12,4},{16,24},{20,28},{24,16},{28,20},{32,40},... | collective-permute-start | bytes 221192 | tf_op jit(solution)/shard_map/ppermute | solution.py:16
  238.6 3.1 collective-permute-done.8
  242.5 3.0 collective-permute-start.9
  246.2 5.4 %collective-permute-done.9 = bf16[2,4,8,1152]{3,2,0,1:T(8,128)(2,1)S(1)} collective-permute-done((bf16[2,4,8,1152]{3,2,0,1:T(8,128)(2,1)S(1)}, bf16[2,4,8,1152]{3,2,0,1:T(8,128)(2,1)S(1)}, u32[]{:S(2)}, u32[]{:S(2)}) %collective-permute-start.9) | collective-permute-done | bytes 147488 | tf_op jit(solution)/shard_map/ppermute | solution.py:16
  256.0 2.7 collective-permute-start.10
  258.8 2.1 bitcast_add_fusion
  261.8 3.1 collective-permute-start.15
  265.7 8.5 %collective-permute-done.10 = bf16[256,1152]{0,1:T(8,128)(2,1)S(1)} collective-permute-done((bf16[256,1152]{0,1:T(8,128)(2,1)S(1)}, bf16[256,1152]{0,1:T(8,128)(2,1)S(1)}, u32[]{:S(2)}, u32[]{:S(2)}) %collective-permute-start.10) | collective-permute-done | bytes 589856 | tf_op jit(solution)/shard_map/ppermute | solution.py:16
  280.3 3.3 collective-permute-done.15
  285.0 3.1 collective-permute-start.16
  288.1 2.8 collective-permute-start.11
  292.5 3.5 collective-permute-done.16
  296.2 2.6 collective-permute-start.17
  298.8 4.2 %collective-permute-done.17 = f32[2,2,2,2,2,1024]{5,4,3,2,1,0:T(2,128)S(1)} collective-permute-done((f32[2,2,2,2,2,1024]{5,4,3,2,1,0:T(2,128)S(1)}, f32[2,2,2,2,2,1024]{5,4,3,2,1,0:T(2,128)S(1)}, u32[]{:S(2)}, u32[]{:S(2)}) %collective-permute-start.17) | collective-permute-done | bytes 131104 | tf_op jit(solution)/shard_map/ppermute | solution.py:134
  303.2 4.5 %collective-permute-start.18 = (f32[2,2,2,2,1024]{4,3,2,1,0:T(2,128)S(1)}, f32[2,2,2,2,1024]{4,3,2,1,0:T(2,128)S(1)}, u32[]{:S(2)}, u32[]{:S(2)}) collective-permute-start(f32[2,2,2,2,1024]{4,3,2,1,0:T(2,128)S(1)} %dynamic-slice_bitcast_fusion.3), channel_id=1, source_target_pairs={{0,8},{1,9},{2,10},{3,11},{4,12},{5,13},{6,14},{7,15},{8,0},{9,1},... | collective-permute-start | bytes 196616 | tf_op jit(solution)/shard_map/ppermute | solution.py:134
  310.3 2.7 collective-permute-start.19
  313.6 4.0 %collective-permute-done.19 = f32[2,2,2,1024]{3,2,1,0:T(2,128)S(1)} collective-permute-done((f32[2,2,2,1024]{3,2,1,0:T(2,128)S(1)}, f32[2,2,2,1024]{3,2,1,0:T(2,128)S(1)}, u32[]{:S(2)}, u32[]{:S(2)}) %collective-permute-start.19) | collective-permute-done | bytes 32800 | tf_op jit(solution)/shard_map/ppermute | solution.py:134
  317.7 4.7 %collective-permute-start.20 = (f32[2,2,1024]{2,1,0:T(2,128)S(1)}, f32[2,2,1024]{2,1,0:T(2,128)S(1)}, u32[]{:S(2)}, u32[]{:S(2)}) collective-permute-start(f32[2,2,1024]{2,1,0:T(2,128)S(1)} %dynamic-slice_bitcast_fusion.5), channel_id=1, source_target_pairs={{0,256},{1,257},{2,258},{3,259},{4,260},{5,261},{6,262},{7,263},{8... | collective-permute-start | bytes 49160 | tf_op jit(solution)/shard_map/ppermute | solution.py:134
  323.3 2.6 collective-permute-start.12
  326.6 1.9 collective-permute-start.21
  328.5 2.5 fusion.19
  330.9 5.4 %collective-permute-done.21 = f32[2,1024]{1,0:T(2,128)} collective-permute-done((f32[2,1024]{1,0:T(2,128)}, f32[2,1024]{1,0:T(2,128)}, u32[]{:S(2)}, u32[]{:S(2)}) %collective-permute-start.21) | collective-permute-done | bytes 8224 | tf_op jit(solution)/shard_map/ppermute | solution.py:134
  337.0 6.1 %collective-permute-start.22 = (f32[1024]{0:T(1024)S(1)}, f32[1024]{0:T(1024)S(1)}, u32[]{:S(2)}, u32[]{:S(2)}) collective-permute-start(f32[1024]{0:T(1024)S(1)} %bitcast.441), channel_id=1, source_target_pairs={{0,2},{1,3},{2,0},{3,1},{4,6},{5,7},{6,4},{7,5},{8,10},{9,11},{10,... | collective-permute-start | bytes 12296 | tf_op jit(solution)/shard_map/ppermute | solution.py:134
  343.1 1.9 fusion.43
  348.7 2.6 collective-permute-done.22
  354.4 2.0 slice_convert_fusion.1
  357.0 3.8 collective-permute-start.13
  360.8 1.9 copy.931
  369.2 7.6 %collective-permute-done.13 = bf16[64,8,1152]{2,1,0:T(8,128)(2,1)} collective-permute-done((bf16[64,8,1152]{2,1,0:T(8,128)(2,1)}, bf16[64,8,1152]{2,1,0:T(8,128)(2,1)}, u32[]{:S(2)}, u32[]{:S(2)}) %collective-permute-start.13) | collective-permute-done | bytes 1179680 | tf_op jit(solution)/shard_map/ppermute | solution.py:16
  379.3 2.0 slice_convert_fusion
  381.3 1.9 copy.940
  387.3 2.2 add_convert_fusion
  (316 shorter events, 152.6 us)
Async XLA Ops:
  0.6 1.4 copy-start
  0.6 3.7 copy-start.52
  0.7 3.1 copy-start.27
  0.7 3.3 copy-start.13
  2.0 2.2 copy-start.14
  3.4 22.0 %copy-start.11 = (bf16[128,512]{0,1:T(8,128)(2,1)}, bf16[128,512]{0,1:T(8,128)(2,1)S(1)}, u32[]{:S(2)}) copy-start(bf16[128,512]{0,1:T(8,128)(2,1)S(1)} %convolution_convert_fusion.1) | copy-start | bytes 393220
  5.5 32.8 %copy-start.30 = (bf16[8,2,512]{2,1,0:T(2,128)(2,1)}, bf16[8,2,512]{2,1,0:T(2,128)(2,1)S(1)}, u32[]{:S(2)}) copy-start(bf16[8,2,512]{2,1,0:T(2,128)(2,1)S(1)} %reshape_reshape.21) | copy-start | bytes 49156
  5.6 11.0 %collective-permute-start = (bf16[2,2,1,8,512]{4,3,1,0,2:T(8,128)(2,1)S(1)}, bf16[2,2,1,8,512]{4,3,1,0,2:T(8,128)(2,1)S(1)}, u32[]{:S(2)}, u32[]{:S(2)}) collective-permute-start(bf16[2,2,1,8,512]{4,3,1,0,2:T(8,128)(2,1)S(1)} %bitcast.398), channel_id=1, source_target_pairs={{0,16},{4,20},{8,24},{12,28},{16,0},{20,4},{24,8},{28,12},{32,48},... | collective-permute-start | bytes 98312 | tf_op jit(solution)/shard_map/ppermute | solution.py:16
  16.6 8.8 %collective-permute-start.1 = (bf16[2,2,2,8,512]{4,3,1,0,2:T(8,128)(2,1)S(1)}, bf16[2,2,2,8,512]{4,3,1,0,2:T(8,128)(2,1)S(1)}, u32[]{:S(2)}, u32[]{:S(2)}) collective-permute-start(bf16[2,2,2,8,512]{4,3,1,0,2:T(8,128)(2,1)S(1)} %pad_maximum_fusion.23), channel_id=1, source_target_pairs={{0,8},{4,12},{8,0},{12,4},{16,24},{20,28},{24,16},{28,20},{32,40},... | collective-permute-start | bytes 196616 | tf_op jit(solution)/shard_map/ppermute | solution.py:16
  25.5 8.4 %collective-permute-start.2 = (bf16[2,2,4,8,512]{4,3,1,0,2:T(8,128)(2,1)S(1)}, bf16[2,2,4,8,512]{4,3,1,0,2:T(8,128)(2,1)S(1)}, u32[]{:S(2)}, u32[]{:S(2)}) collective-permute-start(bf16[2,2,4,8,512]{4,3,1,0,2:T(8,128)(2,1)S(1)} %pad_maximum_fusion.21), channel_id=1, source_target_pairs={{0,64},{4,68},{8,72},{12,76},{16,80},{20,84},{24,88},{28,92},{32,9... | collective-permute-start | bytes 393224 | tf_op jit(solution)/shard_map/ppermute | solution.py:16
  33.9 12.0 %collective-permute-start.3 = (bf16[512,512]{1,0:T(8,128)(2,1)S(1)}, bf16[512,512]{1,0:T(8,128)(2,1)S(1)}, u32[]{:S(2)}, u32[]{:S(2)}) collective-permute-start(bf16[512,512]{1,0:T(8,128)(2,1)S(1)} %pad_maximum_fusion.2), channel_id=1, source_target_pairs={{0,4},{4,0},{8,12},{12,8},{16,20},{20,16},{24,28},{28,24},{32,36},... | collective-permute-start | bytes 1572872 | tf_op jit(solution)/shard_map/ppermute | solution.py:16
  48.6 20.4 %collective-permute-start.4 = (bf16[2,2,16,8,512]{4,3,2,1,0:T(8,128)(2,1)}, bf16[2,2,16,8,512]{4,3,2,1,0:T(8,128)(2,1)}, u32[]{:S(2)}, u32[]{:S(2)}) collective-permute-start(bf16[2,2,16,8,512]{4,3,2,1,0:T(8,128)(2,1)} %get-tuple-element.46), channel_id=1, source_target_pairs={{0,32},{4,36},{8,40},{12,44},{16,48},{20,52},{24,56},{28,60},{32,0... | collective-permute-start | bytes 1572872 | tf_op jit(solution)/shard_map/ppermute | solution.py:16
  59.7 20.8 %copy-start.15 = (bf16[1,128,512]{1,2,0:T(8,128)(2,1)S(1)}, bf16[1,128,512]{1,2,0:T(8,128)(2,1)}, u32[]{:S(2)}) copy-start(bf16[1,128,512]{1,2,0:T(8,128)(2,1)} %copy.848) | copy-start | bytes 393220
  69.0 6.8 %copy-start.39 = (bf16[2,8,512]{2,1,0:T(8,128)(2,1)}, bf16[2,8,512]{2,1,0:T(8,128)(2,1)S(1)}, u32[]{:S(2)}) copy-start(bf16[2,8,512]{2,1,0:T(8,128)(2,1)S(1)} %get-tuple-element.76) | copy-start | bytes 49156
  70.9 9.6 %copy-start.4 = (bf16[2,2,64,8,512]{4,3,2,1,0:T(8,128)(2,1)}, bf16[2,2,64,8,512]{4,3,2,1,0:T(8,128)(2,1)S(1)}, u32[]{:S(2)}) copy-start(bf16[2,2,64,8,512]{4,3,2,1,0:T(8,128)(2,1)S(1)} %get-tuple-element.40) | copy-start | bytes 6291460
  70.9 22.8 %collective-permute-start.5 = (bf16[2,2,32,8,512]{4,3,2,1,0:T(8,128)(2,1)}, bf16[2,2,32,8,512]{4,3,2,1,0:T(8,128)(2,1)}, u32[]{:S(2)}, u32[]{:S(2)}) collective-permute-start(bf16[2,2,32,8,512]{4,3,2,1,0:T(8,128)(2,1)} %get-tuple-element.39), channel_id=1, source_target_pairs={{0,128},{4,132},{8,136},{12,140},{16,144},{20,148},{24,152},{28,15... | collective-permute-start | bytes 3145736 | tf_op jit(solution)/shard_map/ppermute | solution.py:16
  80.5 13.2 %copy-start.5 = (bf16[2,2,64,8,512]{4,3,2,1,0:T(8,128)(2,1)S(1)}, bf16[2,2,64,8,512]{4,3,2,1,0:T(8,128)(2,1)}, u32[]{:S(2)}) copy-start(bf16[2,2,64,8,512]{4,3,2,1,0:T(8,128)(2,1)} %copy-done.4) | copy-start | bytes 6291460
  81.9 14.2 %copy-start.47 = (f32[8,128]{1,0:T(8,128)}, f32[8,128]{1,0:T(8,128)S(1)}, u32[]{:S(2)}) copy-start(f32[8,128]{1,0:T(8,128)S(1)} %get-tuple-element.98) | copy-start | bytes 12292
  95.0 1.6 copy-start.6
  97.9 26.5 %collective-permute-start.6 = (bf16[2,64,8,512]{3,2,1,0:T(8,128)(2,1)}, bf16[2,64,8,512]{3,2,1,0:T(8,128)(2,1)}, u32[]{:S(2)}, u32[]{:S(2)}) collective-permute-start(bf16[2,64,8,512]{3,2,1,0:T(8,128)(2,1)} %slice_bitcast_fusion.1), channel_id=1, source_target_pairs={{0,256},{4,260},{8,264},{12,268},{16,272},{20,276},{24,280},{28,28... | collective-permute-start | bytes 3145736 | tf_op jit(solution)/shard_map/ppermute | solution.py:16
  105.3 2.5 copy-start.36
  107.9 5.1 %copy-start.3 = (bf16[1024,8,64]{0,2,1:T(8,128)(2,1)}, bf16[1024,8,64]{0,2,1:T(8,128)(2,1)S(1)}, u32[]{:S(2)}) copy-start(bf16[1024,8,64]{0,2,1:T(8,128)(2,1)S(1)} %copy.867) | copy-start | bytes 3145732
  112.9 5.6 %copy-start.49 = (f32[8,8]{0,1:T(8,128)S(1)}, f32[8,8]{0,1:T(8,128)}, u32[]{:S(2)}) copy-start(f32[8,8]{0,1:T(8,128)} %constant.249.clone) | copy-start | bytes 772
  117.6 3.5 copy-start.42
  155.7 2.9 copy-start.44
  177.4 23.6 %copy-start.32 = (f32[8,128]{1,0:T(8,128)S(1)}, f32[8,128]{1,0:T(8,128)}, u32[]{:S(2)}) copy-start(f32[8,128]{1,0:T(8,128)} %get-tuple-element.17) | copy-start | bytes 12292
  177.4 23.6 %copy-start.38 = (f32[128,8]{0,1:T(8,128)S(1)}, f32[128,8]{0,1:T(8,128)}, u32[]{:S(2)}) copy-start(f32[128,8]{0,1:T(8,128)} %mul.660) | copy-start | bytes 12292
  187.0 16.2 %copy-start.31 = (bf16[1,128,1024]{2,1,0:T(8,128)(2,1)S(1)}, bf16[1,128,1024]{2,1,0:T(8,128)(2,1)}, u32[]{:S(2)}) copy-start(bf16[1,128,1024]{2,1,0:T(8,128)(2,1)} %param.34) | copy-start | bytes 786436
  188.4 41.8 %collective-permute-start.7 = (bf16[2,1,8,1152]{3,2,0,1:T(8,128)(2,1)}, bf16[2,1,8,1152]{3,2,0,1:T(8,128)(2,1)}, u32[]{:S(2)}, u32[]{:S(2)}) collective-permute-start(bf16[2,1,8,1152]{3,2,0,1:T(8,128)(2,1)} %pad_bitcast_fusion), channel_id=1, source_target_pairs={{0,16},{4,20},{8,24},{12,28},{16,0},{20,4},{24,8},{28,12},{32,48},... | collective-permute-start | bytes 110600 | tf_op jit(solution)/shard_map/ppermute | solution.py:16
  203.3 5.3 %copy-start.43 = (f32[8,16]{1,0:T(8,128)S(1)}, f32[8,16]{1,0:T(8,128)}, u32[]{:S(2)}) copy-start(f32[8,16]{1,0:T(8,128)} %copy-done.42) | copy-start | bytes 1540
  205.3 5.4 %copy-start.2 = (bf16[1024,8,64]{0,2,1:T(8,128)(2,1)S(1)}, bf16[1024,8,64]{0,2,1:T(8,128)(2,1)}, u32[]{:S(2)}) copy-start(bf16[1024,8,64]{0,2,1:T(8,128)(2,1)} %copy.879) | copy-start | bytes 3145732
  205.3 5.4 %copy-start.37 = (f32[8,8]{1,0:T(8,128)S(1)}, f32[8,8]{1,0:T(8,128)}, u32[]{:S(2)}) copy-start(f32[8,8]{1,0:T(8,128)} %log_add_fusion) | copy-start | bytes 772
  207.9 3.0 copy-start.34
  207.9 3.0 copy-start.46
  207.9 3.0 copy-start.50
  211.4 6.1 %copy-start.29 = (f32[8,64,128]{2,1,0:T(8,128)S(1)}, f32[8,64,128]{2,1,0:T(8,128)}, u32[]{:S(2)}) copy-start(f32[8,64,128]{2,1,0:T(8,128)} %fusion.18) | copy-start | bytes 786436
  219.8 17.4 %copy-start.7 = (bf16[2,64,8,1152]{3,2,1,0:T(8,128)(2,1)S(1)}, bf16[2,64,8,1152]{3,2,1,0:T(8,128)(2,1)}, u32[]{:S(2)}) copy-start(bf16[2,64,8,1152]{3,2,1,0:T(8,128)(2,1)} %get-tuple-element.67) | copy-start | bytes 7077892
  225.4 4.8 %copy-start.23 = (bf16[2,1,8,1152]{3,2,0,1:T(8,128)(2,1)S(1)}, bf16[2,1,8,1152]{3,2,0,1:T(8,128)(2,1)}, u32[]{:S(2)}) copy-start(bf16[2,1,8,1152]{3,2,0,1:T(8,128)(2,1)} %pad_bitcast_fusion) | copy-start | bytes 110596
  228.2 30.5 %collective-permute-start.14 = (f32[2,2,2,2,2,2,2,2,1024]{8,7,6,5,4,3,2,1,0:T(2,128)}, f32[2,2,2,2,2,2,2,2,1024]{8,7,6,5,4,3,2,1,0:T(2,128)}, u32[]{:S(2)}, u32[]{:S(2)}) collective-permute-start(f32[2,2,2,2,2,2,2,2,1024]{8,7,6,5,4,3,2,1,0:T(2,128)} %bitcast.350), channel_id=1, source_target_pairs={{0,1},{1,0},{2,3},{3,2},{4,5},{5,4},{6,7},{7,6},{8,9},{9,8},{10,11... | collective-permute-start | bytes 3145736 | tf_op jit(solution)/shard_map/ppermute | solution.py:134
  231.0 10.7 %collective-permute-start.8 = (bf16[2,2,8,1152]{3,2,0,1:T(8,128)(2,1)S(1)}, bf16[2,2,8,1152]{3,2,0,1:T(8,128)(2,1)S(1)}, u32[]{:S(2)}, u32[]{:S(2)}) collective-permute-start(bf16[2,2,8,1152]{3,2,0,1:T(8,128)(2,1)S(1)} %pad_maximum_fusion.22), channel_id=1, source_target_pairs={{0,8},{4,12},{8,0},{12,4},{16,24},{20,28},{24,16},{28,20},{32,40},... | collective-permute-start | bytes 221192 | tf_op jit(solution)/shard_map/ppermute | solution.py:16
  242.5 9.1 %collective-permute-start.9 = (bf16[2,4,8,1152]{3,2,0,1:T(8,128)(2,1)S(1)}, bf16[2,4,8,1152]{3,2,0,1:T(8,128)(2,1)S(1)}, u32[]{:S(2)}, u32[]{:S(2)}) collective-permute-start(bf16[2,4,8,1152]{3,2,0,1:T(8,128)(2,1)S(1)} %pad_maximum_fusion.20), channel_id=1, source_target_pairs={{0,64},{4,68},{8,72},{12,76},{16,80},{20,84},{24,88},{28,92},{32,9... | collective-permute-start | bytes 442376 | tf_op jit(solution)/shard_map/ppermute | solution.py:16
  251.5 1.6 copy-start.24
  256.0 18.2 %collective-permute-start.10 = (bf16[256,1152]{0,1:T(8,128)(2,1)S(1)}, bf16[256,1152]{0,1:T(8,128)(2,1)S(1)}, u32[]{:S(2)}, u32[]{:S(2)}) collective-permute-start(bf16[256,1152]{0,1:T(8,128)(2,1)S(1)} %fusion.38), channel_id=1, source_target_pairs={{0,4},{4,0},{8,12},{12,8},{16,20},{20,16},{24,28},{28,24},{32,36},... | collective-permute-start | bytes 1769480 | tf_op jit(solution)/shard_map/ppermute | solution.py:16
  258.8 6.2 %copy-start.25 = (bf16[2,4,8,1152]{3,2,0,1:T(8,128)(2,1)S(1)}, bf16[2,4,8,1152]{3,2,0,1:T(8,128)(2,1)}, u32[]{:S(2)}) copy-start(bf16[2,4,8,1152]{3,2,0,1:T(8,128)(2,1)} %copy-done.24) | copy-start | bytes 442372
  260.8 4.9 %copy-start.9 = (f32[2,2,2,2,2,2,2,2,1024]{8,7,6,5,4,3,2,1,0:T(2,128)}, f32[2,2,2,2,2,2,2,2,1024]{8,7,6,5,4,3,2,1,0:T(2,128)S(1)}, u32[]{:S(2)}) copy-start(f32[2,2,2,2,2,2,2,2,1024]{8,7,6,5,4,3,2,1,0:T(2,128)S(1)} %bitcast_add_fusion) | copy-start | bytes 3145732
  261.8 21.7 %collective-permute-start.15 = (f32[2,2,2,2,2,2,2,1024]{7,6,5,4,3,2,1,0:T(2,128)}, f32[2,2,2,2,2,2,2,1024]{7,6,5,4,3,2,1,0:T(2,128)}, u32[]{:S(2)}, u32[]{:S(2)}) collective-permute-start(f32[2,2,2,2,2,2,2,1024]{7,6,5,4,3,2,1,0:T(2,128)} %dynamic-slice_bitcast_fusion), channel_id=1, source_target_pairs={{0,4},{1,5},{2,6},{3,7},{4,0},{5,1},{6,2},{7,3},{8,12},{9,13},{10,... | collective-permute-start | bytes 1572872 | tf_op jit(solution)/shard_map/ppermute | solution.py:134
  275.0 8.5 %copy-start.10 = (f32[2,2,2,2,2,2,2,2,1024]{8,7,6,5,4,3,2,1,0:T(2,128)S(1)}, f32[2,2,2,2,2,2,2,2,1024]{8,7,6,5,4,3,2,1,0:T(2,128)}, u32[]{:S(2)}) copy-start(f32[2,2,2,2,2,2,2,2,1024]{8,7,6,5,4,3,2,1,0:T(2,128)} %copy-done.9) | copy-start | bytes 3145732
  280.3 7.8 %copy-start.51 = (bf16[2,16,8,1152]{3,2,1,0:T(8,128)(2,1)S(1)}, bf16[2,16,8,1152]{3,2,1,0:T(8,128)(2,1)}, u32[]{:S(2)}) copy-start(bf16[2,16,8,1152]{3,2,1,0:T(8,128)(2,1)} %get-tuple-element.43) | copy-start | bytes 1769476
  280.3 27.5 %copy-start.16 = (bf16[1,128,512]{1,2,0:T(8,128)(2,1)S(1)}, bf16[1,128,512]{1,2,0:T(8,128)(2,1)}, u32[]{:S(2)}) copy-start(bf16[1,128,512]{1,2,0:T(8,128)(2,1)} %copy.848) | copy-start | bytes 393220
  285.0 11.1 %collective-permute-start.16 = (f32[2,2,2,2,2,2,1024]{6,5,4,3,2,1,0:T(2,128)S(1)}, f32[2,2,2,2,2,2,1024]{6,5,4,3,2,1,0:T(2,128)S(1)}, u32[]{:S(2)}, u32[]{:S(2)}) collective-permute-start(f32[2,2,2,2,2,2,1024]{6,5,4,3,2,1,0:T(2,128)S(1)} %dynamic-slice_bitcast_fusion.1), channel_id=1, source_target_pairs={{0,32},{1,33},{2,34},{3,35},{4,36},{5,37},{6,38},{7,39},{8,40},{9,... | collective-permute-start | bytes 786440 | tf_op jit(solution)/shard_map/ppermute | solution.py:134
  288.1 34.3 %collective-permute-start.11 = (bf16[2,16,8,1152]{3,2,1,0:T(8,128)(2,1)S(1)}, bf16[2,16,8,1152]{3,2,1,0:T(8,128)(2,1)S(1)}, u32[]{:S(2)}, u32[]{:S(2)}) collective-permute-start(bf16[2,16,8,1152]{3,2,1,0:T(8,128)(2,1)S(1)} %copy-done.51), channel_id=1, source_target_pairs={{0,32},{4,36},{8,40},{12,44},{16,48},{20,52},{24,56},{28,60},{32,0... | collective-permute-start | bytes 1769480 | tf_op jit(solution)/shard_map/ppermute | solution.py:16
  292.5 30.8 %copy-start.17 = (bf16[128,512]{0,1:T(8,128)(2,1)}, bf16[128,512]{0,1:T(8,128)(2,1)S(1)}, u32[]{:S(2)}) copy-start(bf16[128,512]{0,1:T(8,128)(2,1)S(1)} %get-tuple-element.31) | copy-start | bytes 393220
  296.2 6.9 %collective-permute-start.17 = (f32[2,2,2,2,2,1024]{5,4,3,2,1,0:T(2,128)S(1)}, f32[2,2,2,2,2,1024]{5,4,3,2,1,0:T(2,128)S(1)}, u32[]{:S(2)}, u32[]{:S(2)}) collective-permute-start(f32[2,2,2,2,2,1024]{5,4,3,2,1,0:T(2,128)S(1)} %dynamic-slice_bitcast_fusion.2), channel_id=1, source_target_pairs={{0,128},{1,129},{2,130},{3,131},{4,132},{5,133},{6,134},{7,135},{8... | collective-permute-start | bytes 393224 | tf_op jit(solution)/shard_map/ppermute | solution.py:134
  303.2 7.1 %collective-permute-start.18 = (f32[2,2,2,2,1024]{4,3,2,1,0:T(2,128)S(1)}, f32[2,2,2,2,1024]{4,3,2,1,0:T(2,128)S(1)}, u32[]{:S(2)}, u32[]{:S(2)}) collective-permute-start(f32[2,2,2,2,1024]{4,3,2,1,0:T(2,128)S(1)} %dynamic-slice_bitcast_fusion.3), channel_id=1, source_target_pairs={{0,8},{1,9},{2,10},{3,11},{4,12},{5,13},{6,14},{7,15},{8,0},{9,1},... | collective-permute-start | bytes 196616 | tf_op jit(solution)/shard_map/ppermute | solution.py:134
  310.3 7.3 %collective-permute-start.19 = (f32[2,2,2,1024]{3,2,1,0:T(2,128)S(1)}, f32[2,2,2,1024]{3,2,1,0:T(2,128)S(1)}, u32[]{:S(2)}, u32[]{:S(2)}) collective-permute-start(f32[2,2,2,1024]{3,2,1,0:T(2,128)S(1)} %dynamic-slice_bitcast_fusion.4), channel_id=1, source_target_pairs={{0,64},{1,65},{2,66},{3,67},{4,68},{5,69},{6,70},{7,71},{8,72},{9,... | collective-permute-start | bytes 98312 | tf_op jit(solution)/shard_map/ppermute | solution.py:134
  317.7 8.3 %collective-permute-start.20 = (f32[2,2,1024]{2,1,0:T(2,128)S(1)}, f32[2,2,1024]{2,1,0:T(2,128)S(1)}, u32[]{:S(2)}, u32[]{:S(2)}) collective-permute-start(f32[2,2,1024]{2,1,0:T(2,128)S(1)} %dynamic-slice_bitcast_fusion.5), channel_id=1, source_target_pairs={{0,256},{1,257},{2,258},{3,259},{4,260},{5,261},{6,262},{7,263},{8... | collective-permute-start | bytes 49160 | tf_op jit(solution)/shard_map/ppermute | solution.py:134
  323.3 28.5 %collective-permute-start.12 = (bf16[2,32,8,1152]{3,2,1,0:T(8,128)(2,1)}, bf16[2,32,8,1152]{3,2,1,0:T(8,128)(2,1)}, u32[]{:S(2)}, u32[]{:S(2)}) collective-permute-start(bf16[2,32,8,1152]{3,2,1,0:T(8,128)(2,1)} %get-tuple-element.32), channel_id=1, source_target_pairs={{0,128},{4,132},{8,136},{12,140},{16,144},{20,148},{24,152},{28,15... | collective-permute-start | bytes 3538952 | tf_op jit(solution)/shard_map/ppermute | solution.py:16
  326.6 9.8 %collective-permute-start.21 = (f32[2,1024]{1,0:T(2,128)}, f32[2,1024]{1,0:T(2,128)}, u32[]{:S(2)}, u32[]{:S(2)}) collective-permute-start(f32[2,1024]{1,0:T(2,128)} %dynamic-slice_bitcast_fusion.6), channel_id=1, source_target_pairs={{0,16},{1,17},{2,18},{3,19},{4,20},{5,21},{6,22},{7,23},{8,24},{9,... | collective-permute-start | bytes 24584 | tf_op jit(solution)/shard_map/ppermute | solution.py:134
  337.0 14.2 %collective-permute-start.22 = (f32[1024]{0:T(1024)S(1)}, f32[1024]{0:T(1024)S(1)}, u32[]{:S(2)}, u32[]{:S(2)}) collective-permute-start(f32[1024]{0:T(1024)S(1)} %bitcast.441), channel_id=1, source_target_pairs={{0,2},{1,3},{2,0},{3,1},{4,6},{5,7},{6,4},{7,5},{8,10},{9,11},{10,... | collective-permute-start | bytes 12296 | tf_op jit(solution)/shard_map/ppermute | solution.py:134
  357.0 19.9 %collective-permute-start.13 = (bf16[64,8,1152]{2,1,0:T(8,128)(2,1)}, bf16[64,8,1152]{2,1,0:T(8,128)(2,1)}, u32[]{:S(2)}, u32[]{:S(2)}) collective-permute-start(bf16[64,8,1152]{2,1,0:T(8,128)(2,1)} %slice_bitcast_fusion), channel_id=1, source_target_pairs={{0,256},{4,260},{8,264},{12,268},{16,272},{20,276},{24,280},{28,28... | collective-permute-start | bytes 3538952 | tf_op jit(solution)/shard_map/ppermute | solution.py:16
  362.7 1.5 copy-start.35
  364.3 1.5 copy-start.33
  383.3 1.5 copy-start.45
  386.2 3.3 copy-start.1
  (13 other events, 11.6 us)

commit v8 on v4

--- a/solution.py
+++ b/solution.py
@@ -125,7 +125,7 @@
     size = 1 << bit_count
     block = matrix.reshape((2,) * bit_count + matrix.shape[1:])
     dims = [bit_count - 1 - j for j in range(bit_count)]
-    for bit_pos in bit_order:
+    for bit_pos in bit_order[:-2]:
         axis_pos = dims.index(bit_pos)
         my_bit = index // (1 << bit_pos) % 2
         keep = lax.dynamic_index_in_dim(block, my_bit, axis_pos, keepdims=False)
@@ -133,7 +133,16 @@
         pairs = [(source, source ^ (1 << bit_pos)) for source in range(size)]
         block = keep + lax.ppermute(send, axes, pairs)
         dims.pop(axis_pos)
-    return block.reshape((1,) + matrix.shape[1:])
+    high_bit, low_bit = dims
+    block = block.reshape((4,) + matrix.shape[1:])
+    mine = index // (1 << high_bit) % 2 * 2 + index // (1 << low_bit) % 2
+    total = lax.dynamic_index_in_dim(block, mine, 0, keepdims=False)
+    for flip in range(1, 4):
+        mask = (flip // 2 << high_bit) | (flip % 2 << low_bit)
+        send = lax.dynamic_index_in_dim(block, mine ^ flip, 0, keepdims=False)
+        pairs = [(source, source ^ mask) for source in range(size)]
+        total = total + lax.ppermute(send, axes, pairs)
+    return total.reshape((1,) + matrix.shape[1:])
 
 
 def heads_view(matrix):

time: 381 us -> 384 us (level)
  starting transfers between devices: 89.5 us -> 102 us
  waiting for transfers between devices: 108 us -> 102 us
    ppermute x0 -> x3, starting transfers between devices: none -> 17 us  [scatter_sum(): total = total + lax.ppermute(send, axes, pairs)]
    ppermute x9 -> x7, waiting for transfers between devices: 27.2 us -> 20.5 us  [scatter_sum(): block = keep + lax.ppermute(send, axes, pairs)]
    ppermute x9 -> x7, starting transfers between devices: 24.9 us -> 20.7 us  [scatter_sum(): block = keep + lax.ppermute(send, axes, pairs)]
  transfers between devices with their start and end apart: 23 -> 24, of which waited for: 18 -> 16; matrix products, arithmetic and copies ran while one was open for 27% -> 26% of each run, Pallas kernels for 0% -> 0%
where the time goes in v8:
time: 384 us; the launch traced here: 380 us
  local copies, waits for them, and re-layouts  115 us (30%)
  starting transfers between devices  102 us (27%)
  waiting for transfers between devices  102 us (27%)
  other arithmetic  33 us (9%)
  matrix products  25.8 us (7%)
    ppermute x14, waiting for transfers between devices, partner(): return lax.ppermute(value, axis, pairs)  82 us
    ppermute x14, starting transfers between devices, partner(): return lax.ppermute(value, axis, pairs)  64.6 us
    another operation x18, local copies, waits for them, and re-layouts, heads_view(): return matrix.reshape(matrix.shape[0], HEADS, HD)  37.9 us
    ppermute x7, starting transfers between devices, scatter_sum(): block = keep + lax.ppermute(send, axes, pairs)  20.7 us
    ppermute x7, waiting for transfers between devices, scatter_sum(): block = keep + lax.ppermute(send, axes, pairs)  20.5 us
    ppermute x3, starting transfers between devices, scatter_sum(): total = total + lax.ppermute(send, axes, pairs)  17 us
    unnamed x139, local copies, waits for them, and re-layouts  14.3 us
    mul x26, local copies, waits for them, and re-layouts, spread_rows(): values[:, None] * chooser  14.2 us
  transfers between devices with their start and end apart: 24, of which 16 were waited for; matrix products, arithmetic and copies ran while one was open for 26% of the time, Pallas kernels for 0%

profile of v8, /device:TPU:6, one launch (start us, length us, event | category | flops | bytes accessed | tf_op | source)
XLA Modules:
  0.0 380.2 jit_solution(1176087575292730624)
XLA Ops:
  5.1 9.1 %collective-permute-start = (bf16[3,2,1,8,512]{4,3,1,0,2:T(8,128)(2,1)S(1)}, bf16[3,2,1,8,512]{4,3,1,0,2:T(8,128)(2,1)S(1)}, u32[]{:S(2)}, u32[]{:S(2)}) collective-permute-start(bf16[3,2,1,8,512]{4,3,1,0,2:T(8,128)(2,1)S(1)} %bitcast.380), channel_id=1, source_target_pairs={{0,16},{4,20},{8,24},{12,28},{16,0},{20,4},{24,8},{28,12},{32,48},... | collective-permute-start | bytes 147464 | tf_op jit(solution)/shard_map/ppermute | solution.py:16
  14.2 2.1 collective-permute-done
  16.3 5.3 %collective-permute-start.1 = (bf16[3,2,2,8,512]{4,3,1,0,2:T(8,128)(2,1)S(1)}, bf16[3,2,2,8,512]{4,3,1,0,2:T(8,128)(2,1)S(1)}, u32[]{:S(2)}, u32[]{:S(2)}) collective-permute-start(bf16[3,2,2,8,512]{4,3,1,0,2:T(8,128)(2,1)S(1)} %pad_maximum_fusion.23), channel_id=1, source_target_pairs={{0,8},{4,12},{8,0},{12,4},{16,24},{20,28},{24,16},{28,20},{32,40},... | collective-permute-start | bytes 294920 | tf_op jit(solution)/shard_map/ppermute | solution.py:16
  21.6 5.0 %collective-permute-done.1 = bf16[3,2,2,8,512]{4,3,1,0,2:T(8,128)(2,1)S(1)} collective-permute-done((bf16[3,2,2,8,512]{4,3,1,0,2:T(8,128)(2,1)S(1)}, bf16[3,2,2,8,512]{4,3,1,0,2:T(8,128)(2,1)S(1)}, u32[]{:S(2)}, u32[]{:S(2)}) %collective-permute-start.1) | collective-permute-done | bytes 98336 | tf_op jit(solution)/shard_map/ppermute | solution.py:16
  26.7 3.3 collective-permute-start.2
  30.1 5.7 %collective-permute-done.2 = bf16[3,2,4,8,512]{4,3,1,0,2:T(8,128)(2,1)S(1)} collective-permute-done((bf16[3,2,4,8,512]{4,3,1,0,2:T(8,128)(2,1)S(1)}, bf16[3,2,4,8,512]{4,3,1,0,2:T(8,128)(2,1)S(1)}, u32[]{:S(2)}, u32[]{:S(2)}) %collective-permute-start.2) | collective-permute-done | bytes 196640 | tf_op jit(solution)/shard_map/ppermute | solution.py:16
  35.9 3.8 collective-permute-start.3
  42.5 14.0 %collective-permute-done.3 = bf16[768,512]{1,0:T(8,128)(2,1)S(1)} collective-permute-done((bf16[768,512]{1,0:T(8,128)(2,1)S(1)}, bf16[768,512]{1,0:T(8,128)(2,1)S(1)}, u32[]{:S(2)}, u32[]{:S(2)}) %collective-permute-start.3) | collective-permute-done | bytes 786464 | tf_op jit(solution)/shard_map/ppermute | solution.py:16
  57.6 2.9 collective-permute-start.4
  60.4 17.0 %collective-permute-done.4 = bf16[3,2,16,8,512]{4,3,2,1,0:T(8,128)(2,1)S(1)} collective-permute-done((bf16[3,2,16,8,512]{4,3,2,1,0:T(8,128)(2,1)S(1)}, bf16[3,2,16,8,512]{4,3,2,1,0:T(8,128)(2,1)S(1)}, u32[]{:S(2)}, u32[]{:S(2)}) %collective-permute-start.4) | collective-permute-done | bytes 786464 | tf_op jit(solution)/shard_map/ppermute | solution.py:16
  78.7 3.5 collective-permute-start.5
  93.8 20.9 %collective-permute-done.5 = bf16[3,2,32,8,512]{4,3,2,1,0:T(8,128)(2,1)} collective-permute-done((bf16[3,2,32,8,512]{4,3,2,1,0:T(8,128)(2,1)}, bf16[3,2,32,8,512]{4,3,2,1,0:T(8,128)(2,1)}, u32[]{:S(2)}, u32[]{:S(2)}) %collective-permute-start.5) | collective-permute-done | bytes 1572896 | tf_op jit(solution)/shard_map/ppermute | solution.py:16
  114.6 2.8 constant_dynamic-update-slice_fusion.9
  117.4 2.7 slice_bitcast_fusion
  120.1 5.3 %collective-permute-start.6 = (bf16[3,64,8,512]{3,2,1,0:T(8,128)(2,1)}, bf16[3,64,8,512]{3,2,1,0:T(8,128)(2,1)}, u32[]{:S(2)}, u32[]{:S(2)}) collective-permute-start(bf16[3,64,8,512]{3,2,1,0:T(8,128)(2,1)} %slice_bitcast_fusion), channel_id=1, source_target_pairs={{0,256},{4,260},{8,264},{12,268},{16,272},{20,276},{24,280},{28,28... | collective-permute-start | bytes 4718600 | tf_op jit(solution)/shard_map/ppermute | solution.py:16
  125.4 3.5 fusion.133
  128.9 2.1 reshape_reshape_squeeze.6
  131.0 2.5 copy.1008
  133.5 4.2 %reshape_reshape_squeeze.14 = bf16[1024,8,64]{2,1,0:T(8,128)(2,1)} reshape(bf16[1,2,64,8,512]{4,3,2,1,0:T(8,128)(2,1)} %get-tuple-element.19) | data formatting | bytes 2097152 | tf_op jit(solution)/shard_map/reshape;reshape;squeeze | solution.py:149
  137.7 3.3 copy.1017
  146.3 3.9 %reshape_reshape_squeeze.15 = bf16[1024,8,64]{2,1,0:T(8,128)(2,1)} reshape(bf16[1,2,64,8,512]{4,3,2,1,0:T(8,128)(2,1)} %get-tuple-element.18) | data formatting | bytes 2097152 | tf_op jit(solution)/shard_map/reshape;reshape;squeeze | solution.py:149
  150.2 3.3 copy.1075
  153.5 2.3 slice_bitcast_fusion.3
  156.7 2.3 slice_bitcast_fusion.2
  160.2 2.1 reshape_reshape.28
  162.2 2.5 copy.1013
  169.4 3.9 %reshape_reshape.29 = bf16[1024,8,64]{2,1,0:T(8,128)(2,1)} reshape(bf16[128,8,512]{2,1,0:T(8,128)(2,1)} %get-tuple-element.103) | data formatting | bytes 2097152 | tf_op jit(solution)/shard_map/reshape;reshape | solution.py:149
  173.3 3.4 copy.1020
  181.1 1.9 copy.1025
  186.4 2.8 fusion.65
  196.4 1.9 fusion.55
  200.1 3.2 constant_dynamic-slice_fusion.5
  205.0 2.0 collective-permute-start.14
  212.8 8.4 %collective-permute-start.7 = (bf16[2,1,8,640]{3,2,0,1:T(8,128)(2,1)}, bf16[2,1,8,640]{3,2,0,1:T(8,128)(2,1)}, u32[]{:S(2)}, u32[]{:S(2)}) collective-permute-start(bf16[2,1,8,640]{3,2,0,1:T(8,128)(2,1)} %fusion.129), channel_id=1, source_target_pairs={{0,16},{4,20},{8,24},{12,28},{16,0},{20,4},{24,8},{28,12},{32,48},... | collective-permute-start | bytes 61448 | tf_op jit(solution)/shard_map/ppermute | solution.py:16
  221.8 3.0 fusion.29
  226.0 2.4 fusion.17
  228.4 2.0 fusion.35
  233.2 5.7 %collective-permute-start.8 = (bf16[2,2,8,640]{3,2,0,1:T(8,128)(2,1)}, bf16[2,2,8,640]{3,2,0,1:T(8,128)(2,1)S(1)}, u32[]{:S(2)}, u32[]{:S(2)}) collective-permute-start(bf16[2,2,8,640]{3,2,0,1:T(8,128)(2,1)} %pad_maximum_fusion.26), channel_id=1, source_target_pairs={{0,8},{4,12},{8,0},{12,4},{16,24},{20,28},{24,16},{28,20},{32,40},... | collective-permute-start | bytes 122888 | tf_op jit(solution)/shard_map/ppermute | solution.py:16
  245.8 3.3 collective-permute-start.9
  250.5 3.1 collective-permute-done.9
  255.6 2.8 collective-permute-start.10
  259.8 6.1 %collective-permute-done.10 = bf16[256,640]{0,1:T(8,128)(2,1)S(1)} collective-permute-done((bf16[256,640]{0,1:T(8,128)(2,1)S(1)}, bf16[256,640]{0,1:T(8,128)(2,1)S(1)}, u32[]{:S(2)}, u32[]{:S(2)}) %collective-permute-start.10) | collective-permute-done | bytes 327712 | tf_op jit(solution)/shard_map/ppermute | solution.py:16
  267.0 2.7 collective-permute-start.11
  273.8 2.9 collective-permute-done.11
  278.5 3.7 collective-permute-start.12
  285.0 2.1 bitcast_add_fusion
  287.2 2.8 collective-permute-start.15
  290.0 4.3 %collective-permute-done.12 = bf16[2,32,8,640]{3,2,1,0:T(8,128)(2,1)} collective-permute-done((bf16[2,32,8,640]{3,2,1,0:T(8,128)(2,1)}, bf16[2,32,8,640]{3,2,1,0:T(8,128)(2,1)}, u32[]{:S(2)}, u32[]{:S(2)}) %collective-permute-start.12) | collective-permute-done | bytes 655392 | tf_op jit(solution)/shard_map/ppermute | solution.py:16
  297.2 2.4 collective-permute-done.15
  301.0 2.7 collective-permute-start.16
  304.3 1.9 copy.1072
  306.2 2.1 slice_bitcast_fusion.1
  308.3 4.9 %collective-permute-start.13 = (bf16[64,8,640]{2,1,0:T(8,128)(2,1)}, bf16[64,8,640]{2,1,0:T(8,128)(2,1)}, u32[]{:S(2)}, u32[]{:S(2)}) collective-permute-start(bf16[64,8,640]{2,1,0:T(8,128)(2,1)} %slice_bitcast_fusion.1), channel_id=1, source_target_pairs={{0,256},{4,260},{8,264},{12,268},{16,272},{20,276},{24,280},{28,28... | collective-permute-start | bytes 1966088 | tf_op jit(solution)/shard_map/ppermute | solution.py:16
  314.5 2.0 collective-permute-start.17
  316.6 9.9 %collective-permute-done.17 = f32[2,2,2,2,2,1024]{5,4,3,2,1,0:T(2,128)S(1)} collective-permute-done((f32[2,2,2,2,2,1024]{5,4,3,2,1,0:T(2,128)S(1)}, f32[2,2,2,2,2,1024]{5,4,3,2,1,0:T(2,128)S(1)}, u32[]{:S(2)}, u32[]{:S(2)}) %collective-permute-start.17) | collective-permute-done | bytes 131104 | tf_op jit(solution)/shard_map/ppermute | solution.py:134
  326.6 4.5 %collective-permute-start.18 = (f32[2,2,2,2,1024]{4,3,2,1,0:T(2,128)S(1)}, f32[2,2,2,2,1024]{4,3,2,1,0:T(2,128)S(1)}, u32[]{:S(2)}, u32[]{:S(2)}) collective-permute-start(f32[2,2,2,2,1024]{4,3,2,1,0:T(2,128)S(1)} %dynamic-slice_bitcast_fusion.3), channel_id=1, source_target_pairs={{0,8},{1,9},{2,10},{3,11},{4,12},{5,13},{6,14},{7,15},{8,0},{9,1},... | collective-permute-start | bytes 196616 | tf_op jit(solution)/shard_map/ppermute | solution.py:134
  332.1 2.2 collective-permute-done.18
  334.4 3.0 collective-permute-start.19
  337.4 4.3 %collective-permute-done.19 = f32[2,2,2,1024]{3,2,1,0:T(2,128)S(1)} collective-permute-done((f32[2,2,2,1024]{3,2,1,0:T(2,128)S(1)}, f32[2,2,2,1024]{3,2,1,0:T(2,128)S(1)}, u32[]{:S(2)}, u32[]{:S(2)}) %collective-permute-start.19) | collective-permute-done | bytes 32800 | tf_op jit(solution)/shard_map/ppermute | solution.py:134
  341.8 3.6 collective-permute-start.20
  350.9 4.5 %collective-permute-start.22 = (f32[1024]{0:T(1024)S(1)}, f32[1024]{0:T(1024)S(1)}, u32[]{:S(2)}, u32[]{:S(2)}) collective-permute-start(f32[1024]{0:T(1024)S(1)} %bitcast.431), channel_id=1, source_target_pairs={{0,16},{1,17},{2,18},{3,19},{4,20},{5,21},{6,22},{7,23},{8,24},{9,... | collective-permute-start | bytes 12296 | tf_op jit(solution)/shard_map/ppermute | solution.py:144
  355.4 10.6 %collective-permute-start.23 = (f32[1024]{0:T(1024)S(1)}, f32[1024]{0:T(1024)S(1)}, u32[]{:S(2)}, u32[]{:S(2)}) collective-permute-start(f32[1024]{0:T(1024)S(1)} %bitcast.430), channel_id=1, source_target_pairs={{0,18},{1,19},{2,16},{3,17},{4,22},{5,23},{6,20},{7,21},{8,26},{9,... | collective-permute-start | bytes 12296 | tf_op jit(solution)/shard_map/ppermute | solution.py:144
  373.5 1.9 copy.1082
  378.0 2.2 add_convert_fusion
  (335 shorter events, 105.5 us)
Async XLA Ops:
  0.6 3.7 copy-start.62
  0.7 3.3 copy-start.16
  5.1 11.2 %collective-permute-start = (bf16[3,2,1,8,512]{4,3,1,0,2:T(8,128)(2,1)S(1)}, bf16[3,2,1,8,512]{4,3,1,0,2:T(8,128)(2,1)S(1)}, u32[]{:S(2)}, u32[]{:S(2)}) collective-permute-start(bf16[3,2,1,8,512]{4,3,1,0,2:T(8,128)(2,1)S(1)} %bitcast.380), channel_id=1, source_target_pairs={{0,16},{4,20},{8,24},{12,28},{16,0},{20,4},{24,8},{28,12},{32,48},... | collective-permute-start | bytes 147464 | tf_op jit(solution)/shard_map/ppermute | solution.py:16
  16.3 10.4 %collective-permute-start.1 = (bf16[3,2,2,8,512]{4,3,1,0,2:T(8,128)(2,1)S(1)}, bf16[3,2,2,8,512]{4,3,1,0,2:T(8,128)(2,1)S(1)}, u32[]{:S(2)}, u32[]{:S(2)}) collective-permute-start(bf16[3,2,2,8,512]{4,3,1,0,2:T(8,128)(2,1)S(1)} %pad_maximum_fusion.23), channel_id=1, source_target_pairs={{0,8},{4,12},{8,0},{12,4},{16,24},{20,28},{24,16},{28,20},{32,40},... | collective-permute-start | bytes 294920 | tf_op jit(solution)/shard_map/ppermute | solution.py:16
  26.7 9.1 %collective-permute-start.2 = (bf16[3,2,4,8,512]{4,3,1,0,2:T(8,128)(2,1)S(1)}, bf16[3,2,4,8,512]{4,3,1,0,2:T(8,128)(2,1)S(1)}, u32[]{:S(2)}, u32[]{:S(2)}) collective-permute-start(bf16[3,2,4,8,512]{4,3,1,0,2:T(8,128)(2,1)S(1)} %pad_maximum_fusion.11), channel_id=1, source_target_pairs={{0,64},{4,68},{8,72},{12,76},{16,80},{20,84},{24,88},{28,92},{32,9... | collective-permute-start | bytes 589832 | tf_op jit(solution)/shard_map/ppermute | solution.py:16
  35.9 20.6 %collective-permute-start.3 = (bf16[768,512]{1,0:T(8,128)(2,1)S(1)}, bf16[768,512]{1,0:T(8,128)(2,1)S(1)}, u32[]{:S(2)}, u32[]{:S(2)}) collective-permute-start(bf16[768,512]{1,0:T(8,128)(2,1)S(1)} %pad_maximum_fusion.3), channel_id=1, source_target_pairs={{0,4},{4,0},{8,12},{12,8},{16,20},{20,16},{24,28},{28,24},{32,36},... | collective-permute-start | bytes 2359304 | tf_op jit(solution)/shard_map/ppermute | solution.py:16
  57.6 27.1 %copy-start.49 = (f32[8,8]{0,1:T(8,128)S(1)}, f32[8,8]{0,1:T(8,128)}, u32[]{:S(2)}) copy-start(f32[8,8]{0,1:T(8,128)} %constant.246.clone) | copy-start | bytes 772
  57.6 27.2 %copy-start.48 = (f32[16,8]{0,1:T(8,128)S(1)}, f32[16,8]{0,1:T(8,128)}, u32[]{:S(2)}) copy-start(f32[16,8]{0,1:T(8,128)} %constant.247.clone) | copy-start | bytes 1540
  57.6 19.8 %collective-permute-start.4 = (bf16[3,2,16,8,512]{4,3,2,1,0:T(8,128)(2,1)S(1)}, bf16[3,2,16,8,512]{4,3,2,1,0:T(8,128)(2,1)S(1)}, u32[]{:S(2)}, u32[]{:S(2)}) collective-permute-start(bf16[3,2,16,8,512]{4,3,2,1,0:T(8,128)(2,1)S(1)} %get-tuple-element.39), channel_id=1, source_target_pairs={{0,32},{4,36},{8,40},{12,44},{16,48},{20,52},{24,56},{28,60},{32,0... | collective-permute-start | bytes 2359304 | tf_op jit(solution)/shard_map/ppermute | solution.py:16
  78.7 36.0 %collective-permute-start.5 = (bf16[3,2,32,8,512]{4,3,2,1,0:T(8,128)(2,1)}, bf16[3,2,32,8,512]{4,3,2,1,0:T(8,128)(2,1)}, u32[]{:S(2)}, u32[]{:S(2)}) collective-permute-start(bf16[3,2,32,8,512]{4,3,2,1,0:T(8,128)(2,1)} %get-tuple-element.32), channel_id=1, source_target_pairs={{0,128},{4,132},{8,136},{12,140},{16,144},{20,148},{24,152},{28,15... | collective-permute-start | bytes 4718600 | tf_op jit(solution)/shard_map/ppermute | solution.py:16
  82.3 10.4 %copy-start.21 = (bf16[1,128,512]{1,2,0:T(8,128)(2,1)}, bf16[1,128,512]{1,2,0:T(8,128)(2,1)S(1)}, u32[]{:S(2)}) copy-start(bf16[1,128,512]{1,2,0:T(8,128)(2,1)S(1)} %copy.989) | copy-start | bytes 393220
  82.4 10.2 %copy-start.14 = (bf16[1,128,512]{1,2,0:T(8,128)(2,1)}, bf16[1,128,512]{1,2,0:T(8,128)(2,1)S(1)}, u32[]{:S(2)}) copy-start(bf16[1,128,512]{1,2,0:T(8,128)(2,1)S(1)} %copy.993) | copy-start | bytes 393220
  84.8 6.2 %copy-start.41 = (f32[128,8]{0,1:T(8,128)}, f32[128,8]{0,1:T(8,128)S(1)}, u32[]{:S(2)}) copy-start(f32[128,8]{0,1:T(8,128)S(1)} %mul.639) | copy-start | bytes 12292
  84.9 6.1 %copy-start.42 = (f32[128,8]{0,1:T(8,128)}, f32[128,8]{0,1:T(8,128)S(1)}, u32[]{:S(2)}) copy-start(f32[128,8]{0,1:T(8,128)S(1)} %mul.649) | copy-start | bytes 12292
  91.1 26.3 %copy-start.29 = (bf16[128,512]{0,1:T(8,128)(2,1)}, bf16[128,512]{0,1:T(8,128)(2,1)S(1)}, u32[]{:S(2)}) copy-start(bf16[128,512]{0,1:T(8,128)(2,1)S(1)} %copy.992) | copy-start | bytes 393220
  93.0 24.4 %copy-start.47 = (f32[8,128]{1,0:T(8,128)}, f32[8,128]{1,0:T(8,128)S(1)}, u32[]{:S(2)}) copy-start(f32[8,128]{1,0:T(8,128)S(1)} %get-tuple-element.99) | copy-start | bytes 12292
  120.1 36.5 %collective-permute-start.6 = (bf16[3,64,8,512]{3,2,1,0:T(8,128)(2,1)}, bf16[3,64,8,512]{3,2,1,0:T(8,128)(2,1)}, u32[]{:S(2)}, u32[]{:S(2)}) collective-permute-start(bf16[3,64,8,512]{3,2,1,0:T(8,128)(2,1)} %slice_bitcast_fusion), channel_id=1, source_target_pairs={{0,256},{4,260},{8,264},{12,268},{16,272},{20,276},{24,280},{28,28... | collective-permute-start | bytes 4718600 | tf_op jit(solution)/shard_map/ppermute | solution.py:16
  133.5 7.5 %copy-start.4 = (bf16[1024,8,64]{0,2,1:T(8,128)(2,1)}, bf16[1024,8,64]{0,2,1:T(8,128)(2,1)S(1)}, u32[]{:S(2)}) copy-start(bf16[1024,8,64]{0,2,1:T(8,128)(2,1)S(1)} %copy.1008) | copy-start | bytes 3145732
  137.7 3.3 copy-start.38
  142.2 4.1 %copy-start.43 = (f32[8,16]{1,0:T(8,128)}, f32[8,16]{1,0:T(8,128)S(1)}, u32[]{:S(2)}) copy-start(f32[8,16]{1,0:T(8,128)S(1)} %log_add_fusion.1) | copy-start | bytes 1540
  203.4 3.7 copy-start.32
  203.4 3.7 copy-start.33
  203.4 3.7 copy-start.51
  205.0 21.0 %copy-start.19 = (bf16[1,128,512]{1,2,0:T(8,128)(2,1)S(1)}, bf16[1,128,512]{1,2,0:T(8,128)(2,1)}, u32[]{:S(2)}) copy-start(bf16[1,128,512]{1,2,0:T(8,128)(2,1)} %copy.1014) | copy-start | bytes 393220
  205.0 80.0 %collective-permute-start.14 = (f32[2,2,2,2,2,2,2,2,1024]{8,7,6,5,4,3,2,1,0:T(2,128)}, f32[2,2,2,2,2,2,2,2,1024]{8,7,6,5,4,3,2,1,0:T(2,128)}, u32[]{:S(2)}, u32[]{:S(2)}) collective-permute-start(f32[2,2,2,2,2,2,2,2,1024]{8,7,6,5,4,3,2,1,0:T(2,128)} %bitcast.346), channel_id=1, source_target_pairs={{0,1},{1,0},{2,3},{3,2},{4,5},{5,4},{6,7},{7,6},{8,9},{9,8},{10,11... | collective-permute-start | bytes 3145736 | tf_op jit(solution)/shard_map/ppermute | solution.py:134
  209.9 11.2 %copy-start.45 = (f32[8,8]{0,1:T(8,128)}, f32[8,8]{0,1:T(8,128)S(1)}, u32[]{:S(2)}) copy-start(f32[8,8]{0,1:T(8,128)S(1)} %multiply_reduce_fusion.6) | copy-start | bytes 772
  212.1 9.1 %copy-start.52 = (bf16[2,8,40]{2,1,0:T(8,128)(2,1)}, bf16[2,8,40]{2,1,0:T(8,128)(2,1)S(1)}, u32[]{:S(2)}) copy-start(bf16[2,8,40]{2,1,0:T(8,128)(2,1)S(1)} %get-tuple-element.86) | copy-start | bytes 3844
  212.1 9.1 %copy-start.54 = (bf16[2,8,40]{2,1,0:T(8,128)(2,1)}, bf16[2,8,40]{2,1,0:T(8,128)(2,1)S(1)}, u32[]{:S(2)}) copy-start(bf16[2,8,40]{2,1,0:T(8,128)(2,1)S(1)} %get-tuple-element.87) | copy-start | bytes 3844
  212.1 9.1 %copy-start.56 = (bf16[2,8,40]{2,1,0:T(8,128)(2,1)}, bf16[2,8,40]{2,1,0:T(8,128)(2,1)S(1)}, u32[]{:S(2)}) copy-start(bf16[2,8,40]{2,1,0:T(8,128)(2,1)S(1)} %get-tuple-element.88) | copy-start | bytes 3844
  212.8 19.1 %collective-permute-start.7 = (bf16[2,1,8,640]{3,2,0,1:T(8,128)(2,1)}, bf16[2,1,8,640]{3,2,0,1:T(8,128)(2,1)}, u32[]{:S(2)}, u32[]{:S(2)}) collective-permute-start(bf16[2,1,8,640]{3,2,0,1:T(8,128)(2,1)} %fusion.129), channel_id=1, source_target_pairs={{0,16},{4,20},{8,24},{12,28},{16,0},{20,4},{24,8},{28,12},{32,48},... | collective-permute-start | bytes 61448 | tf_op jit(solution)/shard_map/ppermute | solution.py:16
  221.8 6.7 %copy-start.2 = (bf16[1024,8,64]{0,2,1:T(8,128)(2,1)S(1)}, bf16[1024,8,64]{0,2,1:T(8,128)(2,1)}, u32[]{:S(2)}) copy-start(bf16[1024,8,64]{0,2,1:T(8,128)(2,1)} %copy.1020) | copy-start | bytes 3145732
  230.5 8.4 %copy-start.53 = (bf16[2,8,40]{2,1,0:T(8,128)(2,1)S(1)}, bf16[2,8,40]{2,1,0:T(8,128)(2,1)}, u32[]{:S(2)}) copy-start(bf16[2,8,40]{2,1,0:T(8,128)(2,1)} %copy-done.52) | copy-start | bytes 3844
  230.5 8.4 %copy-start.55 = (bf16[2,8,40]{2,1,0:T(8,128)(2,1)S(1)}, bf16[2,8,40]{2,1,0:T(8,128)(2,1)}, u32[]{:S(2)}) copy-start(bf16[2,8,40]{2,1,0:T(8,128)(2,1)} %copy-done.54) | copy-start | bytes 3844
  230.5 8.4 %copy-start.57 = (bf16[2,8,40]{2,1,0:T(8,128)(2,1)S(1)}, bf16[2,8,40]{2,1,0:T(8,128)(2,1)}, u32[]{:S(2)}) copy-start(bf16[2,8,40]{2,1,0:T(8,128)(2,1)} %copy-done.56) | copy-start | bytes 3844
  230.5 9.2 %copy-start.30 = (f32[2,8,8,64]{3,1,0,2:T(8,128)S(1)}, f32[2,8,8,64]{3,1,0,2:T(8,128)}, u32[]{:S(2)}) copy-start(f32[2,8,8,64]{3,1,0,2:T(8,128)} %fusion.29) | copy-start | bytes 98308
  230.5 10.1 %copy-start.31 = (f32[8,64,128]{2,1,0:T(8,128)S(1)}, f32[8,64,128]{2,1,0:T(8,128)}, u32[]{:S(2)}) copy-start(f32[8,64,128]{2,1,0:T(8,128)} %fusion.17) | copy-start | bytes 786436
  230.6 10.9 %copy-start.36 = (f32[8,8,64]{2,0,1:T(8,128)S(1)}, f32[8,8,64]{2,0,1:T(8,128)}, u32[]{:S(2)}) copy-start(f32[8,8,64]{2,0,1:T(8,128)} %fusion.35) | copy-start | bytes 49156
  233.2 11.7 %collective-permute-start.8 = (bf16[2,2,8,640]{3,2,0,1:T(8,128)(2,1)}, bf16[2,2,8,640]{3,2,0,1:T(8,128)(2,1)S(1)}, u32[]{:S(2)}, u32[]{:S(2)}) collective-permute-start(bf16[2,2,8,640]{3,2,0,1:T(8,128)(2,1)} %pad_maximum_fusion.26), channel_id=1, source_target_pairs={{0,8},{4,12},{8,0},{12,4},{16,24},{20,28},{24,16},{28,20},{32,40},... | collective-permute-start | bytes 122888 | tf_op jit(solution)/shard_map/ppermute | solution.py:16
  244.9 24.8 %copy-start.46 = (f32[8,128]{1,0:T(8,128)S(1)}, f32[8,128]{1,0:T(8,128)}, u32[]{:S(2)}) copy-start(f32[8,128]{1,0:T(8,128)} %get-tuple-element.17) | copy-start | bytes 12292
  244.9 24.8 %copy-start.15 = (bf16[1,128,512]{1,2,0:T(8,128)(2,1)S(1)}, bf16[1,128,512]{1,2,0:T(8,128)(2,1)}, u32[]{:S(2)}) copy-start(bf16[1,128,512]{1,2,0:T(8,128)(2,1)} %copy-done.14) | copy-start | bytes 393220
  244.9 24.8 %copy-start.22 = (bf16[1,128,512]{1,2,0:T(8,128)(2,1)S(1)}, bf16[1,128,512]{1,2,0:T(8,128)(2,1)}, u32[]{:S(2)}) copy-start(bf16[1,128,512]{1,2,0:T(8,128)(2,1)} %copy-done.21) | copy-start | bytes 393220
  245.0 24.8 %copy-start.23 = (bf16[128,512]{0,1:T(8,128)(2,1)S(1)}, bf16[128,512]{0,1:T(8,128)(2,1)}, u32[]{:S(2)}) copy-start(bf16[128,512]{0,1:T(8,128)(2,1)} %copy.1049) | copy-start | bytes 393220
  245.8 7.8 %collective-permute-start.9 = (bf16[2,4,8,640]{3,2,0,1:T(8,128)(2,1)S(1)}, bf16[2,4,8,640]{3,2,0,1:T(8,128)(2,1)S(1)}, u32[]{:S(2)}, u32[]{:S(2)}) collective-permute-start(bf16[2,4,8,640]{3,2,0,1:T(8,128)(2,1)S(1)} %pad_maximum_fusion.24), channel_id=1, source_target_pairs={{0,64},{4,68},{8,72},{12,76},{16,80},{20,84},{24,88},{28,92},{32,9... | collective-permute-start | bytes 245768 | tf_op jit(solution)/shard_map/ppermute | solution.py:16
  254.6 15.9 %copy-start.58 = (f32[128,8]{0,1:T(8,128)S(1)}, f32[128,8]{0,1:T(8,128)}, u32[]{:S(2)}) copy-start(f32[128,8]{0,1:T(8,128)} %mul.663) | copy-start | bytes 12292
  254.6 15.9 %copy-start.20 = (bf16[1,128,512]{1,2,0:T(8,128)(2,1)S(1)}, bf16[1,128,512]{1,2,0:T(8,128)(2,1)}, u32[]{:S(2)}) copy-start(bf16[1,128,512]{1,2,0:T(8,128)(2,1)} %copy.1014) | copy-start | bytes 393220
  255.6 10.3 %collective-permute-start.10 = (bf16[256,640]{0,1:T(8,128)(2,1)S(1)}, bf16[256,640]{0,1:T(8,128)(2,1)S(1)}, u32[]{:S(2)}, u32[]{:S(2)}) collective-permute-start(bf16[256,640]{0,1:T(8,128)(2,1)S(1)} %pad_maximum_fusion.6), channel_id=1, source_target_pairs={{0,4},{4,0},{8,12},{12,8},{16,20},{20,16},{24,28},{28,24},{32,36},... | collective-permute-start | bytes 983048 | tf_op jit(solution)/shard_map/ppermute | solution.py:16
  267.0 9.7 %collective-permute-start.11 = (bf16[2,16,8,640]{3,2,1,0:T(8,128)(2,1)}, bf16[2,16,8,640]{3,2,1,0:T(8,128)(2,1)}, u32[]{:S(2)}, u32[]{:S(2)}) collective-permute-start(bf16[2,16,8,640]{3,2,1,0:T(8,128)(2,1)} %get-tuple-element.51), channel_id=1, source_target_pairs={{0,32},{4,36},{8,40},{12,44},{16,48},{20,52},{24,56},{28,60},{32,0... | collective-permute-start | bytes 983048 | tf_op jit(solution)/shard_map/ppermute | solution.py:16
  271.9 13.1 %copy-start.7 = (f32[2,2,2,2,2,2,2,2,1,1024]{9,8,7,6,5,4,3,2,1,0:T(1,128)S(1)}, f32[2,2,2,2,2,2,2,2,1,1024]{9,8,7,6,5,4,3,2,1,0:T(1,128)}, u32[]{:S(2)}) copy-start(f32[2,2,2,2,2,2,2,2,1,1024]{9,8,7,6,5,4,3,2,1,0:T(1,128)} %get-tuple-element.24) | copy-start | bytes 3145732
  278.5 15.8 %collective-permute-start.12 = (bf16[2,32,8,640]{3,2,1,0:T(8,128)(2,1)}, bf16[2,32,8,640]{3,2,1,0:T(8,128)(2,1)}, u32[]{:S(2)}, u32[]{:S(2)}) collective-permute-start(bf16[2,32,8,640]{3,2,1,0:T(8,128)(2,1)} %get-tuple-element.40), channel_id=1, source_target_pairs={{0,128},{4,132},{8,136},{12,140},{16,144},{20,148},{24,152},{28,15... | collective-permute-start | bytes 1966088 | tf_op jit(solution)/shard_map/ppermute | solution.py:16
  285.0 9.3 %copy-start.8 = (bf16[2,64,8,640]{3,2,1,0:T(8,128)(2,1)S(1)}, bf16[2,64,8,640]{3,2,1,0:T(8,128)(2,1)}, u32[]{:S(2)}) copy-start(bf16[2,64,8,640]{3,2,1,0:T(8,128)(2,1)} %get-tuple-element.41) | copy-start | bytes 3932164
  287.2 12.4 %collective-permute-start.15 = (f32[2,2,2,2,2,2,2,1024]{7,6,5,4,3,2,1,0:T(2,128)S(1)}, f32[2,2,2,2,2,2,2,1024]{7,6,5,4,3,2,1,0:T(2,128)S(1)}, u32[]{:S(2)}, u32[]{:S(2)}) collective-permute-start(f32[2,2,2,2,2,2,2,1024]{7,6,5,4,3,2,1,0:T(2,128)S(1)} %dynamic-slice_bitcast_fusion), channel_id=1, source_target_pairs={{0,4},{1,5},{2,6},{3,7},{4,0},{5,1},{6,2},{7,3},{8,12},{9,13},{10,... | collective-permute-start | bytes 1572872 | tf_op jit(solution)/shard_map/ppermute | solution.py:134
  295.5 4.6 %copy-start.9 = (bf16[2,64,8,640]{3,2,1,0:T(8,128)(2,1)}, bf16[2,64,8,640]{3,2,1,0:T(8,128)(2,1)S(1)}, u32[]{:S(2)}) copy-start(bf16[2,64,8,640]{3,2,1,0:T(8,128)(2,1)S(1)} %constant_dynamic-update-slice_fusion.26) | copy-start | bytes 3932164
  301.0 12.3 %collective-permute-start.16 = (f32[2,2,2,2,2,2,1024]{6,5,4,3,2,1,0:T(2,128)}, f32[2,2,2,2,2,2,1024]{6,5,4,3,2,1,0:T(2,128)}, u32[]{:S(2)}, u32[]{:S(2)}) collective-permute-start(f32[2,2,2,2,2,2,1024]{6,5,4,3,2,1,0:T(2,128)} %dynamic-slice_bitcast_fusion.1), channel_id=1, source_target_pairs={{0,32},{1,33},{2,34},{3,35},{4,36},{5,37},{6,38},{7,39},{8,40},{9,... | collective-permute-start | bytes 786440 | tf_op jit(solution)/shard_map/ppermute | solution.py:134
  306.2 24.9 %copy-start.3 = (bf16[1024,8,64]{0,2,1:T(8,128)(2,1)S(1)}, bf16[1024,8,64]{0,2,1:T(8,128)(2,1)}, u32[]{:S(2)}) copy-start(bf16[1024,8,64]{0,2,1:T(8,128)(2,1)} %copy.1075) | copy-start | bytes 3145732
  306.2 24.9 %copy-start.37 = (bf16[16,8,64]{2,1,0:T(8,128)(2,1)S(1)}, bf16[16,8,64]{2,1,0:T(8,128)(2,1)}, u32[]{:S(2)}) copy-start(bf16[16,8,64]{2,1,0:T(8,128)(2,1)} %reshape_reshape_squeeze_stack.11) | copy-start | bytes 49156
  308.3 37.0 %copy-start.35 = (bf16[16,8,64]{2,1,0:T(8,128)(2,1)S(1)}, bf16[16,8,64]{2,1,0:T(8,128)(2,1)}, u32[]{:S(2)}) copy-start(bf16[16,8,64]{2,1,0:T(8,128)(2,1)} %reshape_reshape_squeeze_stack.12) | copy-start | bytes 49156
  308.3 61.6 %collective-permute-start.13 = (bf16[64,8,640]{2,1,0:T(8,128)(2,1)}, bf16[64,8,640]{2,1,0:T(8,128)(2,1)}, u32[]{:S(2)}, u32[]{:S(2)}) collective-permute-start(bf16[64,8,640]{2,1,0:T(8,128)(2,1)} %slice_bitcast_fusion.1), channel_id=1, source_target_pairs={{0,256},{4,260},{8,264},{12,268},{16,272},{20,276},{24,280},{28,28... | collective-permute-start | bytes 1966088 | tf_op jit(solution)/shard_map/ppermute | solution.py:16
  314.5 12.0 %collective-permute-start.17 = (f32[2,2,2,2,2,1024]{5,4,3,2,1,0:T(2,128)S(1)}, f32[2,2,2,2,2,1024]{5,4,3,2,1,0:T(2,128)S(1)}, u32[]{:S(2)}, u32[]{:S(2)}) collective-permute-start(f32[2,2,2,2,2,1024]{5,4,3,2,1,0:T(2,128)S(1)} %dynamic-slice_bitcast_fusion.2), channel_id=1, source_target_pairs={{0,128},{1,129},{2,130},{3,131},{4,132},{5,133},{6,134},{7,135},{8... | collective-permute-start | bytes 393224 | tf_op jit(solution)/shard_map/ppermute | solution.py:134
  326.6 7.8 %collective-permute-start.18 = (f32[2,2,2,2,1024]{4,3,2,1,0:T(2,128)S(1)}, f32[2,2,2,2,1024]{4,3,2,1,0:T(2,128)S(1)}, u32[]{:S(2)}, u32[]{:S(2)}) collective-permute-start(f32[2,2,2,2,1024]{4,3,2,1,0:T(2,128)S(1)} %dynamic-slice_bitcast_fusion.3), channel_id=1, source_target_pairs={{0,8},{1,9},{2,10},{3,11},{4,12},{5,13},{6,14},{7,15},{8,0},{9,1},... | collective-permute-start | bytes 196616 | tf_op jit(solution)/shard_map/ppermute | solution.py:134
  334.4 7.3 %collective-permute-start.19 = (f32[2,2,2,1024]{3,2,1,0:T(2,128)S(1)}, f32[2,2,2,1024]{3,2,1,0:T(2,128)S(1)}, u32[]{:S(2)}, u32[]{:S(2)}) collective-permute-start(f32[2,2,2,1024]{3,2,1,0:T(2,128)S(1)} %dynamic-slice_bitcast_fusion.4), channel_id=1, source_target_pairs={{0,64},{1,65},{2,66},{3,67},{4,68},{5,69},{6,70},{7,71},{8,72},{9,... | collective-permute-start | bytes 98312 | tf_op jit(solution)/shard_map/ppermute | solution.py:134
  341.8 7.1 %collective-permute-start.20 = (f32[2,2,1024]{2,1,0:T(2,128)S(1)}, f32[2,2,1024]{2,1,0:T(2,128)S(1)}, u32[]{:S(2)}, u32[]{:S(2)}) collective-permute-start(f32[2,2,1024]{2,1,0:T(2,128)S(1)} %dynamic-slice_bitcast_fusion.5), channel_id=1, source_target_pairs={{0,256},{1,257},{2,258},{3,259},{4,260},{5,261},{6,262},{7,263},{8... | collective-permute-start | bytes 49160 | tf_op jit(solution)/shard_map/ppermute | solution.py:134
  349.0 20.3 %collective-permute-start.21 = (f32[1024]{0:T(1024)S(1)}, f32[1024]{0:T(1024)S(1)}, u32[]{:S(2)}, u32[]{:S(2)}) collective-permute-start(f32[1024]{0:T(1024)S(1)} %bitcast.432), channel_id=1, source_target_pairs={{0,2},{1,3},{2,0},{3,1},{4,6},{5,7},{6,4},{7,5},{8,10},{9,11},{10,... | collective-permute-start | bytes 12296 | tf_op jit(solution)/shard_map/ppermute | solution.py:144
  350.9 18.4 %collective-permute-start.22 = (f32[1024]{0:T(1024)S(1)}, f32[1024]{0:T(1024)S(1)}, u32[]{:S(2)}, u32[]{:S(2)}) collective-permute-start(f32[1024]{0:T(1024)S(1)} %bitcast.431), channel_id=1, source_target_pairs={{0,16},{1,17},{2,18},{3,19},{4,20},{5,21},{6,22},{7,23},{8,24},{9,... | collective-permute-start | bytes 12296 | tf_op jit(solution)/shard_map/ppermute | solution.py:144
  355.4 13.9 %collective-permute-start.23 = (f32[1024]{0:T(1024)S(1)}, f32[1024]{0:T(1024)S(1)}, u32[]{:S(2)}, u32[]{:S(2)}) collective-permute-start(f32[1024]{0:T(1024)S(1)} %bitcast.430), channel_id=1, source_target_pairs={{0,18},{1,19},{2,16},{3,17},{4,22},{5,23},{6,20},{7,21},{8,26},{9,... | collective-permute-start | bytes 12296 | tf_op jit(solution)/shard_map/ppermute | solution.py:144
  (23 other events, 36.8 us)
